TPU v7x, 32 devices: a whole 2x2x4 slice. The times are simulated.
32 devices in a mesh: groups: 2 (over y), context: 8 (over z, x), tensor: 2 (over core).
Axes of the slice: x: 2, y: 2, z: 4, core: 2. Of those that a mesh axis runs over, the one named last changes fastest.
Arguments:
- inputs: bfloat16 [8192, 2048], P('tensor', ('groups', 'context')), parts along dimension 1, may hold values from -12 to 12, as said below
- gate_medium: bfloat16 [8192, 2048], P('tensor', ('groups', 'context')), parts along dimension 1, may hold values from -6 to 6
- key_medium: bfloat16 [8192, 2048], P('tensor', ('groups', 'context')), parts along dimension 1, may hold values from -6 to 6
- gate_long: bfloat16 [8192, 2048], P('tensor', ('groups', 'context')), parts along dimension 1, may hold values from -6 to 6
- key_long: bfloat16 [8192, 2048], P('tensor', ('groups', 'context')), parts along dimension 1, may hold values from -6 to 6
- medium_taps: bfloat16 [512, 128], P('tensor'), may hold values from -0.5 to 0.5
- log_decay: float32 [8192, 16], P('tensor'), may hold values from 9.765625e-05 to 0.0768, as said below
- residues: float32 [8192, 16], P('tensor'), may hold values from -1.5 to 1.5
- norm_gain: float32 [8192], P('tensor'), may hold values from 0.1 to 1.9
Outputs:
- output: bfloat16 [8192, 2048], P('tensor', ('groups', 'context')), parts along dimension 1
There are 2 independent parts, one for each index of `groups`. A program takes and returns all parts, laid end to end along the dimension named above; an argument that names none is the same for every part. Nothing has to cross between parts.
Inputs may be any that keep to these rules, and one draw needn't show every extreme that they name: `inputs`: block input; channel and token scales vary. `log_decay`: decay per token of each pole.
All inputs are finite; a program needn't handle non-finite values.
Results may differ from a plain program's by a relative error of at most 0.0045.
Values may be sent and summed in bfloat16 or wider, within the bound.
No kernel may reach another device: no remote copies, remote signals or barrier semaphores. Data moves between devices by JAX's collectives and lax.ppermute only.
A program may use at most 256 MiB of HBM per device.

v0:
```python
import math

import jax
import jax.numpy as jnp
from jax import lax
from jax.sharding import PartitionSpec as P

D = 8192


HIGHEST_MODE = lax.Precision.HIGHEST


def shifted(block, axis, distance):
    devices = range(lax.axis_size(axis))
    route = [(i - distance, i) for i in devices if i - distance in devices]
    return lax.ppermute(block, axis, route)


def toeplitz_taps(taps):
    filters, length = taps.shape
    padded = jnp.concatenate([taps, jnp.zeros((filters, 2 * length), taps.dtype)], axis=1)
    tiled = jnp.tile(padded, (1, 2 * length))[:, : 2 * length * (3 * length - 1)]
    return tiled.reshape(filters, 2 * length, 3 * length - 1)[:, :, length : 2 * length]


def eigenmode_panel(signal, damping_ratios, weights, initial, block_size):
    channels, length = signal.shape
    count_blocks = length // block_size
    offsets = jnp.arange(block_size, dtype=jnp.float32)
    rescaled_entries = weights * jnp.sqrt(2.0 * damping_ratios)
    powers = jnp.exp(-damping_ratios[:, :, None] * offsets)
    impulse_response = jnp.einsum("gj,gju->gu", rescaled_entries, powers, precision=HIGHEST_MODE)
    padded_response = jnp.concatenate([impulse_response, jnp.zeros_like(impulse_response)], axis=1)
    tiled = jnp.tile(padded_response, (1, block_size))[:, : block_size * (2 * block_size - 1)]
    toeplitz = tiled.reshape(channels, block_size, 2 * block_size - 1)[:, :, :block_size]
    blocks = signal.reshape(channels, count_blocks, block_size)
    inside = jnp.einsum("cbs,cst->cbt", blocks, toeplitz, precision=HIGHEST_MODE)
    closing = jnp.exp(-damping_ratios[:, :, None] * (block_size - 1.0 - offsets))
    finals = jnp.einsum("cbs,cms->cbm", blocks, closing, precision=HIGHEST_MODE)
    block_ids = jnp.arange(count_blocks, dtype=jnp.float32)
    block_gap = block_ids[:, None] - block_ids[None, :]
    decay_matrix = jnp.where(
        block_gap[None, None] >= 0.0,
        jnp.exp(
            -damping_ratios[:, :, None, None] * block_size * jnp.maximum(block_gap, 0.0)[None, None]
        ),
        0.0,
    )
    running = jnp.einsum("cmab,cbm->cam", decay_matrix, finals, precision=HIGHEST_MODE)
    running = (
        running
        + jnp.exp(-damping_ratios[:, None, :] * block_size * (block_ids[None, :, None] + 1.0))
        * initial[:, None, :]
    )
    before = jnp.concatenate([initial[:, None, :], running[:, :-1]], axis=1)
    opening = rescaled_entries[:, :, None] * jnp.exp(-damping_ratios[:, :, None] * (offsets + 1.0))
    carried_over_state = jnp.einsum("cbm,cmt->cbt", before, opening, precision=HIGHEST_MODE)
    return ((inside + carried_over_state).reshape(channels, length), running[:, -1])


def on_device(
    inputs,
    gate_medium,
    key_medium,
    gate_long,
    key_long,
    medium_taps,
    log_decay,
    residues,
    norm_gain,
):
    channels, length = inputs.shape
    tap_count = medium_taps.shape[1]
    filter_count = medium_taps.shape[0]
    per_group = channels // filter_count
    source = inputs.astype(jnp.float32)
    values_medium = (key_medium.astype(jnp.float32) * source).astype(jnp.bfloat16)
    rim_cells = shifted(values_medium, "context", 1)
    padded = jnp.concatenate([rim_cells, values_medium], axis=1)
    tile_count = length // tap_count
    leading = padded[:, :length].reshape(channels, tile_count, tap_count)
    trailing = padded[:, tap_count:].reshape(channels, tile_count, tap_count)
    windows = jnp.concatenate([leading, trailing], axis=2).reshape(
        filter_count, per_group, tile_count, 2 * tap_count
    )
    medium_out = jnp.einsum(
        "gjis,gst->gjit", windows, toeplitz_taps(medium_taps), preferred_element_type=jnp.float32
    ).reshape(channels, length)
    after_medium = source + gate_medium.astype(jnp.float32) * medium_out
    partial_value = jnp.sum(after_medium * after_medium, axis=0, keepdims=True)
    totals = lax.psum(partial_value, "tensor")
    normed = after_medium * lax.rsqrt(totals / D + 1e-05) * norm_gain[:, None]
    values_long = (key_long.astype(jnp.float32) * normed).astype(jnp.bfloat16)
    spread = lax.all_to_all(values_long, "context", split_axis=0, concat_axis=1, tiled=True)
    span_width = spread.shape[0]
    seq_length = spread.shape[1]
    position = lax.axis_index("context") * span_width
    damping_ratios = lax.dynamic_slice_in_dim(log_decay, position, span_width, 0)
    weights = lax.dynamic_slice_in_dim(residues, position, span_width, 0)
    initial = jnp.zeros(damping_ratios.shape, jnp.float32)
    convolved, unused_state = eigenmode_panel(
        spread.astype(jnp.float32), damping_ratios, weights, initial, math.gcd(seq_length, 128)
    )
    long_out = lax.all_to_all(
        convolved.astype(jnp.bfloat16), "context", split_axis=1, concat_axis=0, tiled=True
    )
    return (after_medium + gate_long.astype(jnp.float32) * long_out.astype(jnp.float32)).astype(
        jnp.bfloat16
    )


def solution(mesh):
    return jax.shard_map(
        on_device,
        mesh=mesh,
        in_specs=(
            P("tensor", ("groups", "context")),
            P("tensor", ("groups", "context")),
            P("tensor", ("groups", "context")),
            P("tensor", ("groups", "context")),
            P("tensor", ("groups", "context")),
            P("tensor", None),
            P("tensor", None),
            P("tensor", None),
            P("tensor"),
        ),
        out_specs=P("tensor", ("groups", "context")),
        check_vma=False,
    )
```

profile of v0, /device:TPU:0, one launch (start us, length us, event | category | flops | bytes accessed | tf_op | source)
XLA Modules:
  0.0 560.1 jit_solution(13348192044033509353)
XLA Ops:
  0.0 1.8 fusion.15
  1.9 0.0 copy-start.6
  1.9 4.9 collective-permute-start
  6.8 0.0 copy-done.10
  6.8 16.3 %tile.8 = bf16[256,256,384]{2,1,0:T(8,128)(2,1)} broadcast(bf16[256,384]{1,0:T(8,128)(2,1)S(1)} %concatenate.20), dimensions={0,2} | broadcast | bytes 50528256 | tf_op jit(solution)/shard_map/tile | solution.py:23
  23.1 0.0 copy-done.6
  23.1 50.5 %copy.49 = bf16[32,8,256,384]{3,1,2,0:T(8,128)(2,1)} copy(bf16[32,8,256,384]{3,2,1,0:T(8,128)(2,1)} %bitcast.48) | data formatting | bytes 100663296
  73.6 33.4 %slice.20 = bf16[256,98048]{1,0:T(8,128)(2,1)} slice(bf16[256,98304]{1,0:T(8,128)(2,1)} %bitcast.49), slice={[0:256], [0:98048]} | slice | bytes 100401152 | tf_op jit(solution)/shard_map/slice | solution.py:23
  107.0 129.2 %reshape.88 = bf16[256,256,383]{2,1,0:T(8,128)(2,1)} reshape(bf16[256,98048]{1,0:T(8,128)(2,1)} %slice.20) | data formatting | bytes 100401152 | tf_op jit(solution)/shard_map/reshape | solution.py:24
  236.2 0.0 collective-permute-done
  236.2 1.0 copy-done.8
  237.2 8.8 %fusion.2 = f32[256,16,128]{2,1,0:T(8,128)S(1)} fusion(bf16[256,256,383]{2,1,0:T(8,128)(2,1)} %reshape.88, bf16[256,16,1,128]{3,1,0,2:T(8,128)(2,1)} %bitcast.50, bf16[256,16,1,128]{3,1,0,2:T(8,128)(2,1)} %bitcast.52), kind=kOutput, calls=%fused_computation.2 | convolution fusion | flops 272629760 | bytes 20971520 | tf_op jit(solution)/shard_map/gjis,gst->gjit/dot_general | solution.py:87
  246.0 0.0 copy-done.2
  246.0 0.0 copy-done.4
  246.0 0.0 copy-start
  246.1 0.0 copy-start.11
  246.1 0.6 multiply_reduce_fusion.1
  246.6 2.5 psum.7
  249.1 0.0 copy-done
  249.1 0.0 copy-done.11
  249.1 2.8 multiply_convert_fusion
  251.9 5.0 all-to-all-start
  256.9 0.8 broadcast_multiply_fusion
  257.7 0.1 copy.32
  257.9 0.0 copy-start.9
  257.9 0.8 copy.33
  258.7 0.1 copy.36
  258.8 4.2 fusion.11
  263.1 21.2 %tile.20 = f32[512,128,256]{2,1,0:T(8,128)} broadcast(f32[512,256]{1,0:T(8,128)S(1)} %concatenate.21), dimensions={0,2} | broadcast | bytes 67633152 | tf_op jit(solution)/shard_map/tile | solution.py:35
  284.3 56.3 %copy.50 = f32[64,8,128,256]{3,1,2,0:T(8,128)} copy(f32[64,8,128,256]{3,2,1,0:T(8,128)} %bitcast.19) | data formatting | bytes 134217728
  340.6 44.7 %slice.22 = f32[512,32640]{1,0:T(8,128)} slice(f32[512,32768]{1,0:T(8,128)} %bitcast.20), slice={[0:512], [0:32640]} | slice | bytes 133693440 | tf_op jit(solution)/shard_map/slice | solution.py:35
  385.3 107.2 %reshape.90 = f32[512,128,255]{2,1,0:T(8,128)} reshape(f32[512,32640]{1,0:T(8,128)} %slice.22) | data formatting | bytes 133693440 | tf_op jit(solution)/shard_map/reshape | solution.py:36
  492.6 0.0 all-to-all-done
  492.6 4.0 fusion.27
  496.6 0.8 copy.46
  497.3 0.9 multiply_reduce_fusion
  498.3 0.2 copy.60
  498.4 0.1 slice_add_fusion
  498.5 0.7 copy.47
  499.3 6.5 %fusion.4 = f32[512,8,128]{2,1,0:T(8,128)S(1)} fusion(f32[512,7,16]{2,1,0:T(8,128)S(1)} %copy.47, f32[128]{0:T(128)S(1)} %iota_add_fusion, f32[512,16]{1,0:T(8,128)} %copy.33, f32[512,16]{1,0:T(8,128)} %copy-done.9), kind=kOutput, calls=%fused_computation.4 | convolution fusion | flops 102760448 | bytes 2392576 | tf_op jit(solution)/shard_map/cbm,cmt->cbt/dot_general | solution.py:58
  505.8 0.0 copy-start.7
  505.8 20.5 %add_convert_fusion = bf16[512,8,128]{2,1,0:T(8,128)(2,1)S(1)} fusion(f32[512,8,128]{2,1,0:T(8,128)S(1)} %fusion.4, f32[512,128,255]{2,1,0:T(8,128)} %reshape.90, bf16[8,512,128]{2,1,0:T(8,128)(2,1)S(1)} %all-to-all-done), kind=kOutput, calls=%fused_computation.27 | convolution fusion | flops 806354944 | bytes 37748736 | tf_op jit(solution)/shard_map/cbs,cst->cbt/dot_general | solution.py:38
  526.3 0.0 copy-start.3
  526.3 0.0 copy-start.5
  526.3 0.1 copy.35
  526.5 31.6 %all_to_all.26 = bf16[512,8,128]{2,0,1:T(8,128)(2,1)S(1)} all-to-all(bf16[512,8,128]{2,0,1:T(8,128)(2,1)S(1)} %copy.35), channel_id=1, replica_groups=mesh['groups'=2,'context'=8,'tensor'=2] {'context'}, dimensions={1} | all-to-all | bytes 2097152 | tf_op jit(solution)/shard_map/all_to_all | solution.py:105
  558.1 0.0 copy-done.1
  558.1 1.6 fusion.20
  (17 shorter events, 0.1 us)
Async XLA Ops:
  0.0 6.8 %copy-start.10 = (bf16[256,128]{1,0:T(8,128)(2,1)S(1)}, bf16[256,128]{1,0:T(8,128)(2,1)}, u32[]{:S(2)}) copy-start(bf16[256,128]{1,0:T(8,128)(2,1)} %param.14) | copy-start | bytes 196612
  1.9 21.2 %copy-start.6 = (bf16[4096,128]{1,0:T(8,128)(2,1)}, bf16[4096,128]{1,0:T(8,128)(2,1)S(1)}, u32[]{:S(2)}) copy-start(bf16[4096,128]{1,0:T(8,128)(2,1)S(1)} %fusion.15) | copy-start | bytes 3145732
  1.9 234.3 %collective-permute-start = (bf16[4096,128]{1,0:T(8,128)(2,1)S(1)}, bf16[4096,128]{1,0:T(8,128)(2,1)S(1)}, u32[]{:S(2)}, u32[]{:S(2)}) collective-permute-start(bf16[4096,128]{1,0:T(8,128)(2,1)S(1)} %fusion.15), channel_id=1, source_target_pairs={{0,2},{2,4},{4,6},{6,8},{8,10},{10,12},{12,14},{1,3},{3,5},{5,7},{... | collective-permute-start | bytes 3145736 | tf_op jit(solution)/shard_map/ppermute | solution.py:17
  236.2 1.0 copy-start.8
  237.2 8.8 %copy-start.2 = (bf16[4096,128]{1,0:T(8,128)(2,1)S(1)}, bf16[4096,128]{1,0:T(8,128)(2,1)}, u32[]{:S(2)}) copy-start(bf16[4096,128]{1,0:T(8,128)(2,1)} %param.9) | copy-start | bytes 3145732
  237.2 8.9 %copy-start.4 = (bf16[4096,128]{1,0:T(8,128)(2,1)S(1)}, bf16[4096,128]{1,0:T(8,128)(2,1)}, u32[]{:S(2)}) copy-start(bf16[4096,128]{1,0:T(8,128)(2,1)} %param.10) | copy-start | bytes 3145732
  246.0 3.1 copy-start
  246.1 3.0 copy-start.11
  251.9 240.7 %all-to-all-start = ((bf16[8,512,128]{2,1,0:T(8,128)(2,1)}), bf16[8,512,128]{2,1,0:T(8,128)(2,1)S(1)}, u32[]{:S(2)}, u32[]{:S(2)}) async-start(bf16[8,512,128]{2,1,0:T(8,128)(2,1)} %bitcast.51), calls=%async_computation | async-start | bytes 2097152 | tf_op jit(solution)/shard_map/all_to_all | solution.py:95
  257.9 234.7 %copy-start.9 = (f32[512,16]{1,0:T(8,128)}, f32[512,16]{1,0:T(8,128)S(1)}, u32[]{:S(2)}) copy-start(f32[512,16]{1,0:T(8,128)S(1)} %copy.32) | copy-start | bytes 98308
  505.8 52.3 %copy-start.7 = (bf16[4096,128]{1,0:T(8,128)(2,1)S(1)}, bf16[4096,128]{1,0:T(8,128)(2,1)}, u32[]{:S(2)}) copy-start(bf16[4096,128]{1,0:T(8,128)(2,1)} %param.12) | copy-start | bytes 3145732
  526.3 31.8 %copy-start.1 = (f32[256,16,128]{2,1,0:T(8,128)S(1)}, f32[256,16,128]{2,1,0:T(8,128)}, u32[]{:S(2)}) copy-start(f32[256,16,128]{2,1,0:T(8,128)} %copy-done) | copy-start | bytes 6291460
  526.3 31.8 %copy-start.3 = (bf16[4096,128]{1,0:T(8,128)(2,1)S(1)}, bf16[4096,128]{1,0:T(8,128)(2,1)}, u32[]{:S(2)}) copy-start(bf16[4096,128]{1,0:T(8,128)(2,1)} %param.9) | copy-start | bytes 3145732
  526.3 31.8 %copy-start.5 = (bf16[4096,128]{1,0:T(8,128)(2,1)S(1)}, bf16[4096,128]{1,0:T(8,128)(2,1)}, u32[]{:S(2)}) copy-start(bf16[4096,128]{1,0:T(8,128)(2,1)} %param.10) | copy-start | bytes 3145732
where the time goes:
time: 568 us; the launch traced here: 560 us
  local copies, waits for them, and re-layouts  463 us (82%)
  matrix products  43.9 us (8%)
  blocking collectives  34.1 us (6%)
  starting transfers between devices  9.92 us (2%)
  other arithmetic  8.68 us (2%)
    reshape x1, local copies, waits for them, and re-layouts, toeplitz_taps(): tiled.reshape(filters, 2 * length, 3 * length - 1)[:, :, length:2 * length]  129 us
    unnamed x28, local copies, waits for them, and re-layouts  109 us
    reshape x1, local copies, waits for them, and re-layouts, eigenmode_panel(): tiled.reshape(channels, block_size, 2 * block_size - 1)[:, :, :block_size]  107 us
    slice x1, local copies, waits for them, and re-layouts, eigenmode_panel(): jnp.tile(padded_response, (1, block_size))  44.7 us
    slice x1, local copies, waits for them, and re-layouts, toeplitz_taps(): tiled = jnp.tile(padded, (1, 2 * length))[:, :2 * length * (3 * length - 1)]  33.4 us
    all_to_all x1, blocking collectives, on_device(): lax.all_to_all(convolved.astype(jnp.bfloat16), 'context', split_axis=1, c...  31.6 us
    another operation x1, local copies, waits for them, and re-layouts, eigenmode_panel(): jnp.tile(padded_response, (1, block_size))  21.2 us
    dot_general x1, matrix products, eigenmode_panel(): jnp.einsum('cbs,cst->cbt', blocks, toeplitz, precision=HIGHEST_MODE)  20.5 us
  transfers between devices with their start and end apart: 2, of which 0 were waited for; matrix products, arithmetic and copies ran while one was open for 83% of the time, Pallas kernels for 0%

commit v1 on v0

v1 whole, which is shorter than its diff:
```python
import functools

import jax
import jax.numpy as jnp
from jax import lax
from jax.experimental import pallas as pl
from jax.experimental.pallas import tpu as pltpu
from jax.sharding import PartitionSpec as P

F32 = jnp.float32
BF16 = jnp.bfloat16
EPS = 1e-05
SUB, LANE = 8, 128
TILE = SUB * LANE


def shifted(block, axis, distance):
    devices = range(lax.axis_size(axis))
    route = [(i - distance, i) for i in devices if i - distance in devices]
    return lax.ppermute(block, axis, route)


def medium_kernel(x_ref, gm_ref, km_ref, rim_ref, taps_ref, am_ref, ss_ref):
    rows, length = x_ref.shape
    groups = taps_ref.shape[0]
    per_group = rows // groups
    row = lax.broadcasted_iota(jnp.int32, (length, length), 0)
    col = lax.broadcasted_iota(jnp.int32, (length, length), 1)
    upper = col >= row

    @pl.when(pl.program_id(0) == 0)
    def _():
        ss_ref[...] = jnp.zeros_like(ss_ref)

    acc = jnp.zeros((1, length), F32)
    for g in range(groups):
        lo, hi = g * per_group, (g + 1) * per_group
        taps = jnp.broadcast_to(taps_ref[g : g + 1, :].astype(F32), (length, length))
        rolled = pltpu.roll(taps, 0, 1, stride=1, stride_axis=0)
        t_cur = jnp.where(upper, rolled, 0.0).astype(BF16)
        t_rim = jnp.where(upper, 0.0, rolled).astype(BF16)
        x = x_ref[lo:hi, :].astype(F32)
        vm = (km_ref[lo:hi, :].astype(F32) * x).astype(BF16)
        conv = jnp.dot(vm, t_cur, preferred_element_type=F32) + jnp.dot(
            rim_ref[lo:hi, :], t_rim, preferred_element_type=F32
        )
        am = x + gm_ref[lo:hi, :].astype(F32) * conv
        am_ref[lo:hi, :] = am
        acc = acc + jnp.sum(am * am, axis=0, keepdims=True)
    ss_ref[...] += acc


def medium_call(inputs, gate_medium, key_medium, rim, taps):
    channels, length = inputs.shape
    per_group = channels // taps.shape[0]
    block = 256
    tap_block = block // per_group
    big = pl.BlockSpec((block, length), lambda b: (b, 0))
    return pl.pallas_call(
        medium_kernel,
        grid=(channels // block,),
        in_specs=[big, big, big, big, pl.BlockSpec((tap_block, length), lambda b: (b, 0))],
        out_specs=[big, pl.BlockSpec((1, length), lambda b: (0, 0))],
        out_shape=[
            jax.ShapeDtypeStruct((channels, length), F32),
            jax.ShapeDtypeStruct((1, length), F32),
        ],
        compiler_params=pltpu.CompilerParams(dimension_semantics=("arbitrary",)),
    )(inputs, gate_medium, key_medium, rim, taps)


def final_state_kernel(vt_ref, lam_ref, f_ref):
    modes = lam_ref.shape[0]
    length = vt_ref.shape[0]
    lam = [lam_ref[m] for m in range(modes)]

    def body(t, h):
        v = vt_ref[t].astype(F32)
        return tuple(lam[m] * h[m] + v for m in range(modes))

    h = lax.fori_loop(0, length, body, tuple(jnp.zeros((SUB, LANE), F32) for _ in range(modes)), unroll=8)
    for m in range(modes):
        f_ref[m] = h[m]


def output_kernel(vt_ref, lam_ref, w_ref, h0_ref, yt_ref):
    modes = lam_ref.shape[0]
    length = vt_ref.shape[0]
    lam = [lam_ref[m] for m in range(modes)]
    w = [w_ref[m] for m in range(modes)]

    def body(t, h):
        v = vt_ref[t].astype(F32)
        h = tuple(lam[m] * h[m] + v for m in range(modes))
        y = w[0] * h[0]
        for m in range(1, modes):
            y = y + w[m] * h[m]
        yt_ref[t] = y
        return h

    lax.fori_loop(0, length, body, tuple(h0_ref[m] for m in range(modes)), unroll=8)


def tiled_spec(lead):
    return pl.BlockSpec((lead, None, SUB, LANE), lambda b: (0, b, 0, 0))


def final_state_call(vt, lam):
    length, blocks = vt.shape[0], vt.shape[1]
    modes = lam.shape[0]
    return pl.pallas_call(
        final_state_kernel,
        grid=(blocks,),
        in_specs=[tiled_spec(length), tiled_spec(modes)],
        out_specs=tiled_spec(modes),
        out_shape=jax.ShapeDtypeStruct(lam.shape, F32),
    )(vt, lam)


def output_call(vt, lam, w, h0):
    length, blocks = vt.shape[0], vt.shape[1]
    modes = lam.shape[0]
    return pl.pallas_call(
        output_kernel,
        grid=(blocks,),
        in_specs=[tiled_spec(length), tiled_spec(modes), tiled_spec(modes), tiled_spec(modes)],
        out_specs=tiled_spec(length),
        out_shape=jax.ShapeDtypeStruct(vt.shape, F32),
    )(vt, lam, w, h0)


def to_tiles(a):
    channels, k = a.shape
    return a.T.reshape(k, channels // TILE, SUB, LANE)


def on_device(
    inputs,
    gate_medium,
    key_medium,
    gate_long,
    key_long,
    medium_taps,
    log_decay,
    residues,
    norm_gain,
):
    channels, length = inputs.shape
    assert length == medium_taps.shape[1]
    width = channels * lax.axis_size("tensor")
    source = inputs.astype(F32)
    values_medium = (key_medium.astype(F32) * source).astype(BF16)
    rim = shifted(values_medium, "context", 1)
    after_medium, partial = medium_call(inputs, gate_medium, key_medium, rim, medium_taps)
    totals = lax.psum(partial, "tensor")
    normed = after_medium * lax.rsqrt(totals / width + EPS) * norm_gain[:, None]
    values_long = (key_long.astype(F32) * normed).astype(BF16)

    vt = to_tiles(values_long)
    a_t = to_tiles(log_decay)
    lam = jnp.exp(-a_t)
    w = to_tiles(residues * jnp.sqrt(2.0 * log_decay))
    finals = final_state_call(vt, lam)

    carried = shifted(finals, "context", 1)
    distance = 1
    while distance < lax.axis_size("context"):
        decay = jnp.exp(-(length * distance) * a_t)
        carried = carried + decay * shifted(carried, "context", distance)
        distance *= 2

    yt = output_call(vt, lam, w, carried)
    long_out = yt.reshape(length, channels).T.astype(BF16)
    return (after_medium + gate_long.astype(F32) * long_out.astype(F32)).astype(BF16)


def solution(mesh):
    return jax.shard_map(
        on_device,
        mesh=mesh,
        in_specs=(
            P("tensor", ("groups", "context")),
            P("tensor", ("groups", "context")),
            P("tensor", ("groups", "context")),
            P("tensor", ("groups", "context")),
            P("tensor", ("groups", "context")),
            P("tensor", None),
            P("tensor", None),
            P("tensor", None),
            P("tensor"),
        ),
        out_specs=P("tensor", ("groups", "context")),
        check_vma=False,
    )
```

time: 568 us -> 117 us (0.21)
  the two profiles are of different devices: /device:TPU:0 before, /device:TPU:24 now
where the time goes in v1:
time: 117 us; the launch traced here: 115 us
  waiting for transfers between devices  59.6 us (51%)
  Pallas kernels  24.4 us (21%)
  other arithmetic  10.8 us (9%)
  starting transfers between devices  10.4 us (9%)
  local copies, waits for them, and re-layouts  7.48 us (6%)
  blocking collectives  2.57 us (2%)
    ppermute x5, waiting for transfers between devices, shifted(): return lax.ppermute(block, axis, route)  59.6 us
    pallas_call x1, Pallas kernels, medium_call(): pl.pallas_call(medium_kernel, grid=(channels // block,), in_specs=[big, b...  13.1 us
    ppermute x5, starting transfers between devices, shifted(): return lax.ppermute(block, axis, route)  10.4 us
    pallas_call x1, Pallas kernels, output_call(): pl.pallas_call(output_kernel, grid=(blocks,), in_specs=[tiled_spec(length...  6.87 us
    pallas_call x1, Pallas kernels, final_state_call(): pl.pallas_call(final_state_kernel, grid=(blocks,), in_specs=[tiled_spec(l...  4.44 us
    convert_element_type x1, local copies, waits for them, and re-layouts, on_device(): long_out.astype(F32)  3.13 us
    convert_element_type x1, other arithmetic, on_device(): long_out.astype(F32)  3.08 us
    convert_element_type x1, other arithmetic, on_device(): (after_medium + gate_long.astype(F32) * long_out.astype(F32)).astype(BF16)  2.83 us
  transfers between devices with their start and end apart: 5, of which 5 were waited for; matrix products, arithmetic and copies ran while one was open for 2% of the time, Pallas kernels for 0%

profile of v1, /device:TPU:24, one launch (start us, length us, event | category | flops | bytes accessed | tf_op | source)
XLA Modules:
  0.0 115.3 jit_solution(554090307426255913)
XLA Ops:
  0.0 0.0 copy-start.5
  0.0 0.0 copy-start.4
  0.0 1.9 %multiply_convert_fusion.1 = bf16[4096,128]{1,0:T(8,128)(2,1)S(1)} fusion(bf16[4096,128]{1,0:T(8,128)(2,1)} %x_ref.1, bf16[4096,128]{1,0:T(8,128)(2,1)} %km_ref.1), kind=kLoop, calls=%fused_computation.4 | loop fusion | flops 2097152 | bytes 3145728 | tf_op jit(solution)/shard_map/convert_element_type | solution.py:152
  1.9 3.4 %collective-permute-start = (bf16[4096,128]{1,0:T(8,128)(2,1)S(1)}, bf16[4096,128]{1,0:T(8,128)(2,1)S(1)}, u32[]{:S(2)}, u32[]{:S(2)}) collective-permute-start(bf16[4096,128]{1,0:T(8,128)(2,1)S(1)} %multiply_convert_fusion.1), channel_id=1, source_target_pairs={{0,2},{2,4},{4,6},{6,8},{8,10},{10,12},{12,14},{1,3},{3,5},{5,7},{... | collective-permute-start | bytes 3145736 | tf_op jit(solution)/shard_map/ppermute | solution.py:20
  5.3 0.0 copy-done.5
  5.3 0.0 copy-done.4
  5.3 0.2 exponential_bitcast_fusion
  5.5 0.8 copy.14
  6.3 0.0 copy-start.1
  6.3 0.0 copy-start.6
  6.3 23.3 %collective-permute-done.rim_ref = bf16[4096,128]{1,0:T(8,128)(2,1)S(1)} collective-permute-done((bf16[4096,128]{1,0:T(8,128)(2,1)S(1)}, bf16[4096,128]{1,0:T(8,128)(2,1)S(1)}, u32[]{:S(2)}, u32[]{:S(2)}) %collective-permute-start) | collective-permute-done | bytes 1048608 | tf_op jit(solution)/shard_map/ppermute | solution.py:20
  29.6 0.0 copy-start.3
  29.6 1.0 copy-done.3
  30.5 13.1 %shard_map.91 = (f32[4096,128]{1,0:T(8,128)}, f32[1,128]{1,0:T(1,128)}) custom-call(bf16[4096,128]{1,0:T(8,128)(2,1)} %x_ref.1, bf16[4096,128]{1,0:T(8,128)(2,1)} %gm_ref.1, bf16[4096,128]{1,0:T(8,128)(2,1)} %km_ref.1, bf16[4096,128]{1,0:T(8,128)(2,1)} %copy-done.3, bf16[256,128]{1,0:T(8,128)(2,1)} %taps_ref.1), custom_call_target="tpu_custom_call" | custom-call | tf_op jit(solution)/shard_map/pallas_call | solution.py:59
  43.7 2.6 %psum.7 = f32[1,128]{1,0:T(1,128)S(1)} all-reduce(f32[1,128]{1,0:T(1,128)} %get-tuple-element.8), channel_id=1, replica_groups=mesh['groups'=2,'context'=8,'tensor'=2] {'tensor'}, use_global_device_ids=true, to_apply=%region_0.0 | all-reduce | flops 128 | bytes 1024 | tf_op jit(solution)/shard_map/psum | solution.py:155
  46.3 0.0 copy-done.1
  46.3 0.0 copy-done.6
  46.3 1.9 %multiply_convert_fusion = bf16[4096,128]{1,0:T(8,128)(2,1)S(1)} fusion(f32[4096,128]{1,0:T(8,128)} %get-tuple-element.7, bf16[4096,128]{1,0:T(8,128)(2,1)S(1)} %copy-done.1, f32[4096]{0:T(1024)S(1)} %copy-done.6, f32[128]{0:T(128)S(1)} %rsqrt_bitcast_fusion), kind=kLoop, calls=%fused_computation.3 | loop fusion | flops 2621440 | bytes 4211200 | tf_op jit(solution)/shard_map/convert_element_type | solution.py:157
  48.2 1.7 %copy.12.vt_ref = bf16[128,4,8,128]{3,2,1,0:T(8,128)(2,1)} copy(bf16[128,4,8,128]{0,3,2,1:T(8,128)(2,1)S(1)} %bitcast.38) | data formatting | bytes 2097152 | tf_op jit(solution)/shard_map/reshape | solution.py:134
  49.9 4.4 %shard_map.92 = f32[16,4,8,128]{3,2,1,0:T(8,128)} custom-call(bf16[128,4,8,128]{3,2,1,0:T(8,128)(2,1)} %copy.12.vt_ref, f32[16,4,8,128]{3,2,1,0:T(8,128)} %bitcast.39), custom_call_target="tpu_custom_call" | custom-call | tf_op jit(solution)/shard_map/pallas_call | solution.py:111
  54.3 2.5 %collective-permute-start.1 = (f32[16,4,8,128]{3,2,1,0:T(8,128)}, f32[16,4,8,128]{3,2,1,0:T(8,128)S(1)}, u32[]{:S(2)}, u32[]{:S(2)}) collective-permute-start(f32[16,4,8,128]{3,2,1,0:T(8,128)} %shard_map.92), channel_id=1, source_target_pairs={{0,2},{2,4},{4,6},{6,8},{8,10},{10,12},{12,14},{1,3},{3,5},{5,7},{... | collective-permute-start | bytes 786440 | tf_op jit(solution)/shard_map/ppermute | solution.py:20
  56.8 8.9 %collective-permute-done.1 = f32[16,4,8,128]{3,2,1,0:T(8,128)S(1)} collective-permute-done((f32[16,4,8,128]{3,2,1,0:T(8,128)}, f32[16,4,8,128]{3,2,1,0:T(8,128)S(1)}, u32[]{:S(2)}, u32[]{:S(2)}) %collective-permute-start.1) | collective-permute-done | bytes 262176 | tf_op jit(solution)/shard_map/ppermute | solution.py:20
  65.7 1.9 %collective-permute-start.2 = (f32[16,4,8,128]{3,2,1,0:T(8,128)S(1)}, f32[16,4,8,128]{3,2,1,0:T(8,128)S(1)}, u32[]{:S(2)}, u32[]{:S(2)}) collective-permute-start(f32[16,4,8,128]{3,2,1,0:T(8,128)S(1)} %collective-permute-done.1), channel_id=1, source_target_pairs={{0,2},{2,4},{4,6},{6,8},{8,10},{10,12},{12,14},{1,3},{3,5},{5,7},{... | collective-permute-start | bytes 786440 | tf_op jit(solution)/shard_map/ppermute | solution.py:20
  67.6 0.1 copy.16
  67.7 8.4 %collective-permute-done.2 = f32[16,4,8,128]{3,2,1,0:T(8,128)S(1)} collective-permute-done((f32[16,4,8,128]{3,2,1,0:T(8,128)S(1)}, f32[16,4,8,128]{3,2,1,0:T(8,128)S(1)}, u32[]{:S(2)}, u32[]{:S(2)}) %collective-permute-start.2) | collective-permute-done | bytes 262176 | tf_op jit(solution)/shard_map/ppermute | solution.py:20
  76.0 0.1 multiply_add_fusion.2
  76.1 1.3 %collective-permute-start.3 = (f32[16,4,8,128]{3,2,1,0:T(8,128)S(1)}, f32[16,4,8,128]{3,2,1,0:T(8,128)S(1)}, u32[]{:S(2)}, u32[]{:S(2)}) collective-permute-start(f32[16,4,8,128]{3,2,1,0:T(8,128)S(1)} %multiply_add_fusion.2), channel_id=1, source_target_pairs={{0,4},{2,6},{4,8},{6,10},{8,12},{10,14},{1,5},{3,7},{5,9},{7,11},{... | collective-permute-start | bytes 786440 | tf_op jit(solution)/shard_map/ppermute | solution.py:20
  77.4 0.1 copy.17
  77.4 7.2 %collective-permute-done.3 = f32[16,4,8,128]{3,2,1,0:T(8,128)S(1)} collective-permute-done((f32[16,4,8,128]{3,2,1,0:T(8,128)S(1)}, f32[16,4,8,128]{3,2,1,0:T(8,128)S(1)}, u32[]{:S(2)}, u32[]{:S(2)}) %collective-permute-start.3) | collective-permute-done | bytes 262176 | tf_op jit(solution)/shard_map/ppermute | solution.py:20
  84.6 0.1 multiply_add_fusion.1
  84.7 1.3 %collective-permute-start.4 = (f32[16,4,8,128]{3,2,1,0:T(8,128)S(1)}, f32[16,4,8,128]{3,2,1,0:T(8,128)S(1)}, u32[]{:S(2)}, u32[]{:S(2)}) collective-permute-start(f32[16,4,8,128]{3,2,1,0:T(8,128)S(1)} %multiply_add_fusion.1), channel_id=1, source_target_pairs={{0,8},{2,10},{4,12},{6,14},{1,9},{3,11},{5,13},{7,15},{16,24},{18,... | collective-permute-start | bytes 786440 | tf_op jit(solution)/shard_map/ppermute | solution.py:20
  86.0 0.1 copy.18
  86.0 0.8 copy.15
  86.8 11.9 %collective-permute-done.4 = f32[16,4,8,128]{3,2,1,0:T(8,128)S(1)} collective-permute-done((f32[16,4,8,128]{3,2,1,0:T(8,128)S(1)}, f32[16,4,8,128]{3,2,1,0:T(8,128)S(1)}, u32[]{:S(2)}, u32[]{:S(2)}) %collective-permute-start.4) | collective-permute-done | bytes 262176 | tf_op jit(solution)/shard_map/ppermute | solution.py:20
  98.7 0.8 multiply_add_fusion.h0_ref
  99.4 6.9 %shard_map.93 = f32[128,4,8,128]{3,2,1,0:T(8,128)} custom-call(bf16[128,4,8,128]{3,2,1,0:T(8,128)(2,1)} %copy.12.vt_ref, f32[16,4,8,128]{3,2,1,0:T(8,128)} %bitcast.40, f32[16,4,8,128]{3,2,1,0:T(8,128)} %bitcast.44, f32[16,4,8,128]{3,2,1,0:T(8,128)} %multiply_add_fusion.h0_ref), custom_call_target="tpu_custom_call" | custom-call | tf_op jit(solution)/shard_map/pallas_call | solution.py:123
  106.3 3.1 %convert_convert_fusion = f32[128,4,8,128]{3,2,1,0:T(8,128)} fusion(f32[128,4,8,128]{3,2,1,0:T(8,128)} %shard_map.93), kind=kLoop, calls=%fused_computation.5 | loop fusion | flops 1048576 | bytes 4194304 | tf_op jit(solution)/shard_map/convert_element_type | solution.py:174
  109.4 0.0 copy-start
  109.4 0.0 copy-start.2
  109.4 3.1 %copy.13 = f32[128,4,8,128]{0,3,2,1:T(8,128)} copy(f32[128,4,8,128]{3,2,1,0:T(8,128)} %convert_convert_fusion) | data formatting | bytes 4194304 | tf_op jit(solution)/shard_map/convert_element_type | solution.py:174
  112.5 0.0 copy-done
  112.5 0.0 copy-done.2
  112.5 2.8 %fusion.1 = bf16[4096,128]{1,0:T(8,128)(2,1)} fusion(f32[4096,128]{1,0:T(8,128)S(1)} %copy-done, f32[128,4,8,128]{0,3,2,1:T(8,128)} %copy.13, bf16[4096,128]{1,0:T(8,128)(2,1)S(1)} %copy-done.2), kind=kLoop, calls=%fused_computation.2 | loop fusion | flops 2097152 | bytes 6291456 | tf_op jit(solution)/shard_map/convert_element_type | solution.py:174
  (1 shorter events, 0.0 us)
Async XLA Ops:
  0.0 5.3 %copy-start.5 = (f32[4096,16]{0,1:T(8,128)S(1)}, f32[4096,16]{0,1:T(8,128)}, u32[]{:S(2)}) copy-start(f32[4096,16]{0,1:T(8,128)} %param.16) | copy-start | bytes 786436
  0.0 5.3 %copy-start.4 = (f32[4096,16]{0,1:T(8,128)S(1)}, f32[4096,16]{0,1:T(8,128)}, u32[]{:S(2)}) copy-start(f32[4096,16]{0,1:T(8,128)} %param.15) | copy-start | bytes 786436
  1.9 27.7 %collective-permute-start = (bf16[4096,128]{1,0:T(8,128)(2,1)S(1)}, bf16[4096,128]{1,0:T(8,128)(2,1)S(1)}, u32[]{:S(2)}, u32[]{:S(2)}) collective-permute-start(bf16[4096,128]{1,0:T(8,128)(2,1)S(1)} %multiply_convert_fusion.1), channel_id=1, source_target_pairs={{0,2},{2,4},{4,6},{6,8},{8,10},{10,12},{12,14},{1,3},{3,5},{5,7},{... | collective-permute-start | bytes 3145736 | tf_op jit(solution)/shard_map/ppermute | solution.py:20
  6.3 40.0 %copy-start.1 = (bf16[4096,128]{1,0:T(8,128)(2,1)S(1)}, bf16[4096,128]{1,0:T(8,128)(2,1)}, u32[]{:S(2)}) copy-start(bf16[4096,128]{1,0:T(8,128)(2,1)} %param.13) | copy-start | bytes 3145732
  6.3 40.0 %copy-start.6 = (f32[4096]{0:T(1024)S(1)}, f32[4096]{0:T(1024)}, u32[]{:S(2)}) copy-start(f32[4096]{0:T(1024)} %param.17) | copy-start | bytes 49156
  29.6 1.0 copy-start.3
  54.3 11.4 %collective-permute-start.1 = (f32[16,4,8,128]{3,2,1,0:T(8,128)}, f32[16,4,8,128]{3,2,1,0:T(8,128)S(1)}, u32[]{:S(2)}, u32[]{:S(2)}) collective-permute-start(f32[16,4,8,128]{3,2,1,0:T(8,128)} %shard_map.92), channel_id=1, source_target_pairs={{0,2},{2,4},{4,6},{6,8},{8,10},{10,12},{12,14},{1,3},{3,5},{5,7},{... | collective-permute-start | bytes 786440 | tf_op jit(solution)/shard_map/ppermute | solution.py:20
  65.7 10.3 %collective-permute-start.2 = (f32[16,4,8,128]{3,2,1,0:T(8,128)S(1)}, f32[16,4,8,128]{3,2,1,0:T(8,128)S(1)}, u32[]{:S(2)}, u32[]{:S(2)}) collective-permute-start(f32[16,4,8,128]{3,2,1,0:T(8,128)S(1)} %collective-permute-done.1), channel_id=1, source_target_pairs={{0,2},{2,4},{4,6},{6,8},{8,10},{10,12},{12,14},{1,3},{3,5},{5,7},{... | collective-permute-start | bytes 786440 | tf_op jit(solution)/shard_map/ppermute | solution.py:20
  76.1 8.5 %collective-permute-start.3 = (f32[16,4,8,128]{3,2,1,0:T(8,128)S(1)}, f32[16,4,8,128]{3,2,1,0:T(8,128)S(1)}, u32[]{:S(2)}, u32[]{:S(2)}) collective-permute-start(f32[16,4,8,128]{3,2,1,0:T(8,128)S(1)} %multiply_add_fusion.2), channel_id=1, source_target_pairs={{0,4},{2,6},{4,8},{6,10},{8,12},{10,14},{1,5},{3,7},{5,9},{7,11},{... | collective-permute-start | bytes 786440 | tf_op jit(solution)/shard_map/ppermute | solution.py:20
  84.7 14.0 %collective-permute-start.4 = (f32[16,4,8,128]{3,2,1,0:T(8,128)S(1)}, f32[16,4,8,128]{3,2,1,0:T(8,128)S(1)}, u32[]{:S(2)}, u32[]{:S(2)}) collective-permute-start(f32[16,4,8,128]{3,2,1,0:T(8,128)S(1)} %multiply_add_fusion.1), channel_id=1, source_target_pairs={{0,8},{2,10},{4,12},{6,14},{1,9},{3,11},{5,13},{7,15},{16,24},{18,... | collective-permute-start | bytes 786440 | tf_op jit(solution)/shard_map/ppermute | solution.py:20
  109.4 3.1 %copy-start = (f32[4096,128]{1,0:T(8,128)S(1)}, f32[4096,128]{1,0:T(8,128)}, u32[]{:S(2)}) copy-start(f32[4096,128]{1,0:T(8,128)} %get-tuple-element.7) | copy-start | bytes 6291460
  109.4 3.1 %copy-start.2 = (bf16[4096,128]{1,0:T(8,128)(2,1)S(1)}, bf16[4096,128]{1,0:T(8,128)(2,1)}, u32[]{:S(2)}) copy-start(bf16[4096,128]{1,0:T(8,128)(2,1)} %param.12) | copy-start | bytes 3145732

commit v2 on v1

--- a/solution.py
+++ b/solution.py
@@ -132,6 +132,22 @@
 def to_tiles(a):
     channels, k = a.shape
     return a.T.reshape(k, channels // TILE, SUB, LANE)
+
+
+def exclusive_scan(finals, a_t, length, count, first=4, radix=2):
+    first = min(first, count)
+    carried = shifted(finals, "context", 1)
+    for j in range(2, first + 1):
+        carried = carried + jnp.exp(-(length * (j - 1)) * a_t) * shifted(finals, "context", j)
+    window = first
+    while window < count:
+        step = carried
+        for j in range(1, radix):
+            if j * window < count:
+                decay = jnp.exp(-(length * j * window) * a_t)
+                carried = carried + decay * shifted(step, "context", j * window)
+        window *= radix
+    return carried
 
 
 def on_device(
@@ -162,12 +178,7 @@
     w = to_tiles(residues * jnp.sqrt(2.0 * log_decay))
     finals = final_state_call(vt, lam)
 
-    carried = shifted(finals, "context", 1)
-    distance = 1
-    while distance < lax.axis_size("context"):
-        decay = jnp.exp(-(length * distance) * a_t)
-        carried = carried + decay * shifted(carried, "context", distance)
-        distance *= 2
+    carried = exclusive_scan(finals, a_t, length, lax.axis_size("context"))
 
     yt = output_call(vt, lam, w, carried)
     long_out = yt.reshape(length, channels).T.astype(BF16)

time: 117 us -> 124 us (1.060)
  the two profiles are of different devices: /device:TPU:24 before, /device:TPU:0 now
where the time goes in v2:
time: 124 us; the launch traced here: 122 us
  starting transfers between devices  41.5 us (33%)
  waiting for transfers between devices  35.4 us (29%)
  Pallas kernels  24.4 us (20%)
  other arithmetic  10.9 us (9%)
  local copies, waits for them, and re-layouts  7.52 us (6%)
  blocking collectives  2.57 us (2%)
    ppermute x6, starting transfers between devices, shifted(): return lax.ppermute(block, axis, route)  41.5 us
    ppermute x6, waiting for transfers between devices, shifted(): return lax.ppermute(block, axis, route)  35.4 us
    pallas_call x1, Pallas kernels, medium_call(): pl.pallas_call(medium_kernel, grid=(channels // block,), in_specs=[big, b...  13.1 us
    pallas_call x1, Pallas kernels, output_call(): pl.pallas_call(output_kernel, grid=(blocks,), in_specs=[tiled_spec(length...  6.86 us
    pallas_call x1, Pallas kernels, final_state_call(): pl.pallas_call(final_state_kernel, grid=(blocks,), in_specs=[tiled_spec(l...  4.44 us
    convert_element_type x1, local copies, waits for them, and re-layouts, on_device(): long_out.astype(F32)  3.13 us
    convert_element_type x1, other arithmetic, on_device(): long_out.astype(F32)  3.07 us
    convert_element_type x1, other arithmetic, on_device(): (after_medium + gate_long.astype(F32) * long_out.astype(F32)).astype(BF16)  2.83 us
  transfers between devices with their start and end apart: 6, of which 4 were waited for; matrix products, arithmetic and copies ran while one was open for 2% of the time, Pallas kernels for 0%

profile of v2, /device:TPU:0, one launch (start us, length us, event | category | flops | bytes accessed | tf_op | source)
XLA Modules:
  0.0 122.5 jit_solution(13265233332928257655)
XLA Ops:
  0.0 0.0 copy-start.5
  0.0 0.0 copy-start.4
  0.0 1.9 %multiply_convert_fusion.1 = bf16[4096,128]{1,0:T(8,128)(2,1)S(1)} fusion(bf16[4096,128]{1,0:T(8,128)(2,1)} %x_ref.1, bf16[4096,128]{1,0:T(8,128)(2,1)} %km_ref.1), kind=kLoop, calls=%fused_computation.4 | loop fusion | flops 2097152 | bytes 3145728 | tf_op jit(solution)/shard_map/convert_element_type | solution.py:168
  1.9 4.9 %collective-permute-start = (bf16[4096,128]{1,0:T(8,128)(2,1)S(1)}, bf16[4096,128]{1,0:T(8,128)(2,1)S(1)}, u32[]{:S(2)}, u32[]{:S(2)}) collective-permute-start(bf16[4096,128]{1,0:T(8,128)(2,1)S(1)} %multiply_convert_fusion.1), channel_id=1, source_target_pairs={{0,2},{2,4},{4,6},{6,8},{8,10},{10,12},{12,14},{1,3},{3,5},{5,7},{... | collective-permute-start | bytes 3145736 | tf_op jit(solution)/shard_map/ppermute | solution.py:20
  6.8 0.0 copy-done.5
  6.8 0.0 copy-done.4
  6.8 0.2 exponential_bitcast_fusion
  7.0 0.8 copy.14
  7.8 0.0 copy-start.1
  7.8 0.0 copy-start.6
  7.8 21.3 %collective-permute-done.rim_ref = bf16[4096,128]{1,0:T(8,128)(2,1)S(1)} collective-permute-done((bf16[4096,128]{1,0:T(8,128)(2,1)S(1)}, bf16[4096,128]{1,0:T(8,128)(2,1)S(1)}, u32[]{:S(2)}, u32[]{:S(2)}) %collective-permute-start) | collective-permute-done | bytes 1048608 | tf_op jit(solution)/shard_map/ppermute | solution.py:20
  29.1 0.0 copy-start.3
  29.1 1.0 copy-done.3
  30.1 13.1 %shard_map.91 = (f32[4096,128]{1,0:T(8,128)}, f32[1,128]{1,0:T(1,128)}) custom-call(bf16[4096,128]{1,0:T(8,128)(2,1)} %x_ref.1, bf16[4096,128]{1,0:T(8,128)(2,1)} %gm_ref.1, bf16[4096,128]{1,0:T(8,128)(2,1)} %km_ref.1, bf16[4096,128]{1,0:T(8,128)(2,1)} %copy-done.3, bf16[256,128]{1,0:T(8,128)(2,1)} %taps_ref.1), custom_call_target="tpu_custom_call" | custom-call | tf_op jit(solution)/shard_map/pallas_call | solution.py:59
  43.2 2.6 %psum.7 = f32[1,128]{1,0:T(1,128)S(1)} all-reduce(f32[1,128]{1,0:T(1,128)} %get-tuple-element.8), channel_id=1, replica_groups=mesh['groups'=2,'context'=8,'tensor'=2] {'tensor'}, use_global_device_ids=true, to_apply=%region_0.0 | all-reduce | flops 128 | bytes 1024 | tf_op jit(solution)/shard_map/psum | solution.py:171
  45.8 0.0 copy-done.1
  45.8 0.0 copy-done.6
  45.8 1.9 %multiply_convert_fusion = bf16[4096,128]{1,0:T(8,128)(2,1)S(1)} fusion(f32[4096,128]{1,0:T(8,128)} %get-tuple-element.7, bf16[4096,128]{1,0:T(8,128)(2,1)S(1)} %copy-done.1, f32[4096]{0:T(1024)S(1)} %copy-done.6, f32[128]{0:T(128)S(1)} %rsqrt_bitcast_fusion), kind=kLoop, calls=%fused_computation.3 | loop fusion | flops 2621440 | bytes 4211200 | tf_op jit(solution)/shard_map/convert_element_type | solution.py:173
  47.8 1.7 %copy.12.vt_ref = bf16[128,4,8,128]{3,2,1,0:T(8,128)(2,1)} copy(bf16[128,4,8,128]{0,3,2,1:T(8,128)(2,1)S(1)} %bitcast.43) | data formatting | bytes 2097152 | tf_op jit(solution)/shard_map/reshape | solution.py:134
  49.5 4.4 %shard_map.92 = f32[16,4,8,128]{3,2,1,0:T(8,128)} custom-call(bf16[128,4,8,128]{3,2,1,0:T(8,128)(2,1)} %copy.12.vt_ref, f32[16,4,8,128]{3,2,1,0:T(8,128)} %bitcast.44), custom_call_target="tpu_custom_call" | custom-call | tf_op jit(solution)/shard_map/pallas_call | solution.py:111
  53.9 6.4 %collective-permute-start.4 = (f32[16,4,8,128]{3,2,1,0:T(8,128)}, f32[16,4,8,128]{3,2,1,0:T(8,128)S(1)}, u32[]{:S(2)}, u32[]{:S(2)}) collective-permute-start(f32[16,4,8,128]{3,2,1,0:T(8,128)} %shard_map.92), channel_id=1, source_target_pairs={{0,8},{2,10},{4,12},{6,14},{1,9},{3,11},{5,13},{7,15},{16,24},{18,... | collective-permute-start | bytes 786440 | tf_op jit(solution)/shard_map/ppermute | solution.py:20
  60.3 3.5 %collective-permute-start.3 = (f32[16,4,8,128]{3,2,1,0:T(8,128)}, f32[16,4,8,128]{3,2,1,0:T(8,128)S(1)}, u32[]{:S(2)}, u32[]{:S(2)}) collective-permute-start(f32[16,4,8,128]{3,2,1,0:T(8,128)} %shard_map.92), channel_id=1, source_target_pairs={{0,6},{2,8},{4,10},{6,12},{8,14},{1,7},{3,9},{5,11},{7,13},{9,15},... | collective-permute-start | bytes 786440 | tf_op jit(solution)/shard_map/ppermute | solution.py:20
  63.8 1.3 %collective-permute-start.2 = (f32[16,4,8,128]{3,2,1,0:T(8,128)}, f32[16,4,8,128]{3,2,1,0:T(8,128)S(1)}, u32[]{:S(2)}, u32[]{:S(2)}) collective-permute-start(f32[16,4,8,128]{3,2,1,0:T(8,128)} %shard_map.92), channel_id=1, source_target_pairs={{0,4},{2,6},{4,8},{6,10},{8,12},{10,14},{1,5},{3,7},{5,9},{7,11},{... | collective-permute-start | bytes 786440 | tf_op jit(solution)/shard_map/ppermute | solution.py:20
  65.1 3.3 %collective-permute-start.1 = (f32[16,4,8,128]{3,2,1,0:T(8,128)}, f32[16,4,8,128]{3,2,1,0:T(8,128)S(1)}, u32[]{:S(2)}, u32[]{:S(2)}) collective-permute-start(f32[16,4,8,128]{3,2,1,0:T(8,128)} %shard_map.92), channel_id=1, source_target_pairs={{0,2},{2,4},{4,6},{6,8},{8,10},{10,12},{12,14},{1,3},{3,5},{5,7},{... | collective-permute-start | bytes 786440 | tf_op jit(solution)/shard_map/ppermute | solution.py:20
  68.5 0.1 copy.17
  68.5 0.1 copy.16
  68.6 0.1 copy.18
  68.7 0.0 collective-permute-done.4
  68.7 4.3 %collective-permute-done.3 = f32[16,4,8,128]{3,2,1,0:T(8,128)S(1)} collective-permute-done((f32[16,4,8,128]{3,2,1,0:T(8,128)}, f32[16,4,8,128]{3,2,1,0:T(8,128)S(1)}, u32[]{:S(2)}, u32[]{:S(2)}) %collective-permute-start.3) | collective-permute-done | bytes 262176 | tf_op jit(solution)/shard_map/ppermute | solution.py:20
  73.0 4.8 %collective-permute-done.2 = f32[16,4,8,128]{3,2,1,0:T(8,128)S(1)} collective-permute-done((f32[16,4,8,128]{3,2,1,0:T(8,128)}, f32[16,4,8,128]{3,2,1,0:T(8,128)S(1)}, u32[]{:S(2)}, u32[]{:S(2)}) %collective-permute-start.2) | collective-permute-done | bytes 262176 | tf_op jit(solution)/shard_map/ppermute | solution.py:20
  77.8 0.0 collective-permute-done.1
  77.8 0.2 multiply_add_fusion.1
  78.0 22.0 %collective-permute-start.5 = (f32[16,4,8,128]{3,2,1,0:T(8,128)S(1)}, f32[16,4,8,128]{3,2,1,0:T(8,128)S(1)}, u32[]{:S(2)}, u32[]{:S(2)}) collective-permute-start(f32[16,4,8,128]{3,2,1,0:T(8,128)S(1)} %multiply_add_fusion.1), channel_id=1, source_target_pairs={{0,8},{2,10},{4,12},{6,14},{1,9},{3,11},{5,13},{7,15},{16,24},{18,... | collective-permute-start | bytes 786440 | tf_op jit(solution)/shard_map/ppermute | solution.py:20
  100.0 0.1 copy.19
  100.1 0.8 copy.15
  100.8 4.9 %collective-permute-done.5 = f32[16,4,8,128]{3,2,1,0:T(8,128)S(1)} collective-permute-done((f32[16,4,8,128]{3,2,1,0:T(8,128)S(1)}, f32[16,4,8,128]{3,2,1,0:T(8,128)S(1)}, u32[]{:S(2)}, u32[]{:S(2)}) %collective-permute-start.5) | collective-permute-done | bytes 262176 | tf_op jit(solution)/shard_map/ppermute | solution.py:20
  105.8 0.8 multiply_add_fusion.h0_ref
  106.5 6.9 %shard_map.93 = f32[128,4,8,128]{3,2,1,0:T(8,128)} custom-call(bf16[128,4,8,128]{3,2,1,0:T(8,128)(2,1)} %copy.12.vt_ref, f32[16,4,8,128]{3,2,1,0:T(8,128)} %bitcast.45, f32[16,4,8,128]{3,2,1,0:T(8,128)} %bitcast.50, f32[16,4,8,128]{3,2,1,0:T(8,128)} %multiply_add_fusion.h0_ref), custom_call_target="tpu_custom_call" | custom-call | tf_op jit(solution)/shard_map/pallas_call | solution.py:123
  113.4 3.1 %convert_convert_fusion = f32[128,4,8,128]{3,2,1,0:T(8,128)} fusion(f32[128,4,8,128]{3,2,1,0:T(8,128)} %shard_map.93), kind=kLoop, calls=%fused_computation.5 | loop fusion | flops 1048576 | bytes 4194304 | tf_op jit(solution)/shard_map/convert_element_type | solution.py:185
  116.5 0.0 copy-start
  116.5 0.0 copy-start.2
  116.5 3.1 %copy.13 = f32[128,4,8,128]{0,3,2,1:T(8,128)} copy(f32[128,4,8,128]{3,2,1,0:T(8,128)} %convert_convert_fusion) | data formatting | bytes 4194304 | tf_op jit(solution)/shard_map/convert_element_type | solution.py:185
  119.6 0.0 copy-done
  119.6 0.0 copy-done.2
  119.6 2.8 %fusion.1 = bf16[4096,128]{1,0:T(8,128)(2,1)} fusion(f32[4096,128]{1,0:T(8,128)S(1)} %copy-done, f32[128,4,8,128]{0,3,2,1:T(8,128)} %copy.13, bf16[4096,128]{1,0:T(8,128)(2,1)S(1)} %copy-done.2), kind=kLoop, calls=%fused_computation.2 | loop fusion | flops 2097152 | bytes 6291456 | tf_op jit(solution)/shard_map/convert_element_type | solution.py:185
  (1 shorter events, 0.0 us)
Async XLA Ops:
  0.0 6.8 %copy-start.5 = (f32[4096,16]{0,1:T(8,128)S(1)}, f32[4096,16]{0,1:T(8,128)}, u32[]{:S(2)}) copy-start(f32[4096,16]{0,1:T(8,128)} %param.16) | copy-start | bytes 786436
  0.0 6.8 %copy-start.4 = (f32[4096,16]{0,1:T(8,128)S(1)}, f32[4096,16]{0,1:T(8,128)}, u32[]{:S(2)}) copy-start(f32[4096,16]{0,1:T(8,128)} %param.15) | copy-start | bytes 786436
  1.9 27.2 %collective-permute-start = (bf16[4096,128]{1,0:T(8,128)(2,1)S(1)}, bf16[4096,128]{1,0:T(8,128)(2,1)S(1)}, u32[]{:S(2)}, u32[]{:S(2)}) collective-permute-start(bf16[4096,128]{1,0:T(8,128)(2,1)S(1)} %multiply_convert_fusion.1), channel_id=1, source_target_pairs={{0,2},{2,4},{4,6},{6,8},{8,10},{10,12},{12,14},{1,3},{3,5},{5,7},{... | collective-permute-start | bytes 3145736 | tf_op jit(solution)/shard_map/ppermute | solution.py:20
  7.8 38.0 %copy-start.1 = (bf16[4096,128]{1,0:T(8,128)(2,1)S(1)}, bf16[4096,128]{1,0:T(8,128)(2,1)}, u32[]{:S(2)}) copy-start(bf16[4096,128]{1,0:T(8,128)(2,1)} %param.13) | copy-start | bytes 3145732
  7.8 38.0 %copy-start.6 = (f32[4096]{0:T(1024)S(1)}, f32[4096]{0:T(1024)}, u32[]{:S(2)}) copy-start(f32[4096]{0:T(1024)} %param.17) | copy-start | bytes 49156
  29.1 1.0 copy-start.3
  53.9 14.8 %collective-permute-start.4 = (f32[16,4,8,128]{3,2,1,0:T(8,128)}, f32[16,4,8,128]{3,2,1,0:T(8,128)S(1)}, u32[]{:S(2)}, u32[]{:S(2)}) collective-permute-start(f32[16,4,8,128]{3,2,1,0:T(8,128)} %shard_map.92), channel_id=1, source_target_pairs={{0,8},{2,10},{4,12},{6,14},{1,9},{3,11},{5,13},{7,15},{16,24},{18,... | collective-permute-start | bytes 786440 | tf_op jit(solution)/shard_map/ppermute | solution.py:20
  60.3 12.7 %collective-permute-start.3 = (f32[16,4,8,128]{3,2,1,0:T(8,128)}, f32[16,4,8,128]{3,2,1,0:T(8,128)S(1)}, u32[]{:S(2)}, u32[]{:S(2)}) collective-permute-start(f32[16,4,8,128]{3,2,1,0:T(8,128)} %shard_map.92), channel_id=1, source_target_pairs={{0,6},{2,8},{4,10},{6,12},{8,14},{1,7},{3,9},{5,11},{7,13},{9,15},... | collective-permute-start | bytes 786440 | tf_op jit(solution)/shard_map/ppermute | solution.py:20
  63.8 14.0 %collective-permute-start.2 = (f32[16,4,8,128]{3,2,1,0:T(8,128)}, f32[16,4,8,128]{3,2,1,0:T(8,128)S(1)}, u32[]{:S(2)}, u32[]{:S(2)}) collective-permute-start(f32[16,4,8,128]{3,2,1,0:T(8,128)} %shard_map.92), channel_id=1, source_target_pairs={{0,4},{2,6},{4,8},{6,10},{8,12},{10,14},{1,5},{3,7},{5,9},{7,11},{... | collective-permute-start | bytes 786440 | tf_op jit(solution)/shard_map/ppermute | solution.py:20
  65.1 12.7 %collective-permute-start.1 = (f32[16,4,8,128]{3,2,1,0:T(8,128)}, f32[16,4,8,128]{3,2,1,0:T(8,128)S(1)}, u32[]{:S(2)}, u32[]{:S(2)}) collective-permute-start(f32[16,4,8,128]{3,2,1,0:T(8,128)} %shard_map.92), channel_id=1, source_target_pairs={{0,2},{2,4},{4,6},{6,8},{8,10},{10,12},{12,14},{1,3},{3,5},{5,7},{... | collective-permute-start | bytes 786440 | tf_op jit(solution)/shard_map/ppermute | solution.py:20
  78.0 27.8 %collective-permute-start.5 = (f32[16,4,8,128]{3,2,1,0:T(8,128)S(1)}, f32[16,4,8,128]{3,2,1,0:T(8,128)S(1)}, u32[]{:S(2)}, u32[]{:S(2)}) collective-permute-start(f32[16,4,8,128]{3,2,1,0:T(8,128)S(1)} %multiply_add_fusion.1), channel_id=1, source_target_pairs={{0,8},{2,10},{4,12},{6,14},{1,9},{3,11},{5,13},{7,15},{16,24},{18,... | collective-permute-start | bytes 786440 | tf_op jit(solution)/shard_map/ppermute | solution.py:20
  116.5 3.1 %copy-start = (f32[4096,128]{1,0:T(8,128)S(1)}, f32[4096,128]{1,0:T(8,128)}, u32[]{:S(2)}) copy-start(f32[4096,128]{1,0:T(8,128)} %get-tuple-element.7) | copy-start | bytes 6291460
  116.5 3.1 %copy-start.2 = (bf16[4096,128]{1,0:T(8,128)(2,1)S(1)}, bf16[4096,128]{1,0:T(8,128)(2,1)}, u32[]{:S(2)}) copy-start(bf16[4096,128]{1,0:T(8,128)(2,1)} %param.12) | copy-start | bytes 3145732

commit v3 on v2

--- a/solution.py
+++ b/solution.py
@@ -148,6 +148,16 @@
                 carried = carried + decay * shifted(step, "context", j * window)
         window *= radix
     return carried
+
+
+def gathered_scan(finals, a_t, length):
+    count = lax.axis_size("context")
+    everyone = lax.all_gather(finals, "context")
+    gap = lax.axis_index("context") - 1 - jnp.arange(count)
+    inside = (gap >= 0).reshape((count,) + (1,) * a_t.ndim)
+    distance = (length * jnp.maximum(gap, 0)).astype(F32).reshape(inside.shape)
+    decay = jnp.where(inside, jnp.exp(-distance * a_t[None]), 0.0)
+    return jnp.sum(decay * everyone, axis=0)
 
 
 def on_device(
@@ -178,7 +188,7 @@
     w = to_tiles(residues * jnp.sqrt(2.0 * log_decay))
     finals = final_state_call(vt, lam)
 
-    carried = exclusive_scan(finals, a_t, length, lax.axis_size("context"))
+    carried = gathered_scan(finals, a_t, length)
 
     yt = output_call(vt, lam, w, carried)
     long_out = yt.reshape(length, channels).T.astype(BF16)

time: 124 us -> 139 us (1.12)
  waiting for transfers between devices: 35.4 us -> 72.3 us
  starting transfers between devices: 41.5 us -> 4.91 us
  between operations: 0.14 us -> 13.5 us
  other arithmetic: 10.9 us -> 13.4 us
    all_gather x0 -> x1, waiting for transfers between devices: none -> 50.8 us  [gathered_scan(): everyone = lax.all_gather(finals, 'context')]
    ppermute x6 -> x1, starting transfers between devices: 41.5 us -> 4.91 us  [shifted(): return lax.ppermute(block, axis, route)]
    ppermute x6 -> x1, waiting for transfers between devices: 35.4 us -> 21.5 us  [shifted(): return lax.ppermute(block, axis, route)]
    reduce_sum x0 -> x1, other arithmetic: none -> 2.82 us  [gathered_scan(): return jnp.sum(decay * everyone, axis=0)]
  transfers between devices with their start and end apart: 6 -> 2, of which waited for: 4 -> 2; matrix products, arithmetic and copies ran while one was open for 2% -> 1% of each run, Pallas kernels for 0% -> 0%
where the time goes in v3:
time: 139 us; the launch traced here: 138 us
  waiting for transfers between devices  72.3 us (52%)
  Pallas kernels  24.5 us (18%)
  between operations  13.5 us (10%)
  other arithmetic  13.4 us (10%)
  local copies, waits for them, and re-layouts  6.63 us (5%)
  starting transfers between devices  4.91 us (4%)
  blocking collectives  2.57 us (2%)
    all_gather x1, waiting for transfers between devices, gathered_scan(): everyone = lax.all_gather(finals, 'context')  50.8 us
    ppermute x1, waiting for transfers between devices, shifted(): return lax.ppermute(block, axis, route)  21.5 us
    pallas_call x1, Pallas kernels, medium_call(): pl.pallas_call(medium_kernel, grid=(channels // block,), in_specs=[big, b...  13.2 us
    pallas_call x1, Pallas kernels, output_call(): pl.pallas_call(output_kernel, grid=(blocks,), in_specs=[tiled_spec(length...  6.87 us
    ppermute x1, starting transfers between devices, shifted(): return lax.ppermute(block, axis, route)  4.91 us
    pallas_call x1, Pallas kernels, final_state_call(): pl.pallas_call(final_state_kernel, grid=(blocks,), in_specs=[tiled_spec(l...  4.46 us
    convert_element_type x1, local copies, waits for them, and re-layouts, on_device(): long_out.astype(F32)  3.14 us
    convert_element_type x1, other arithmetic, on_device(): long_out.astype(F32)  3.07 us
  transfers between devices with their start and end apart: 2, of which 2 were waited for; matrix products, arithmetic and copies ran while one was open for 1% of the time, Pallas kernels for 0%

profile of v3, /device:TPU:0, one launch (start us, length us, event | category | flops | bytes accessed | tf_op | source)
XLA Modules:
  0.0 137.8 jit_solution(16786487569483018988)
XLA Ops:
  6.5 0.0 copy-start.2
  6.5 0.0 all-gather.3.cloned.1.call-start
  6.5 1.9 %multiply_convert_fusion.1 = bf16[4096,128]{1,0:T(8,128)(2,1)S(1)} fusion(bf16[4096,128]{1,0:T(8,128)(2,1)} %x_ref.1, bf16[4096,128]{1,0:T(8,128)(2,1)} %km_ref.1), kind=kLoop, calls=%fused_computation.5 | loop fusion | flops 2097152 | bytes 3145728 | tf_op jit(solution)/shard_map/convert_element_type | solution.py:178
  8.4 4.9 %collective-permute-start = (bf16[4096,128]{1,0:T(8,128)(2,1)S(1)}, bf16[4096,128]{1,0:T(8,128)(2,1)S(1)}, u32[]{:S(2)}, u32[]{:S(2)}) collective-permute-start(bf16[4096,128]{1,0:T(8,128)(2,1)S(1)} %multiply_convert_fusion.1), channel_id=1, source_target_pairs={{0,2},{2,4},{4,6},{6,8},{8,10},{10,12},{12,14},{1,3},{3,5},{5,7},{... | collective-permute-start | bytes 3145736 | tf_op jit(solution)/shard_map/ppermute | solution.py:20
  13.3 0.0 copy-done.2
  13.3 0.1 copy.16
  13.4 0.7 negate_exponential_fusion.lam_ref
  14.1 0.0 copy-start.1
  14.1 0.0 copy-start.6
  14.1 21.5 %collective-permute-done.rim_ref = bf16[4096,128]{1,0:T(8,128)(2,1)S(1)} collective-permute-done((bf16[4096,128]{1,0:T(8,128)(2,1)S(1)}, bf16[4096,128]{1,0:T(8,128)(2,1)S(1)}, u32[]{:S(2)}, u32[]{:S(2)}) %collective-permute-start) | collective-permute-done | bytes 1048608 | tf_op jit(solution)/shard_map/ppermute | solution.py:20
  35.6 0.0 copy-start.4
  35.7 1.0 copy-done.4
  36.6 13.2 %shard_map.91 = (f32[4096,128]{1,0:T(8,128)}, f32[1,128]{1,0:T(1,128)}) custom-call(bf16[4096,128]{1,0:T(8,128)(2,1)} %x_ref.1, bf16[4096,128]{1,0:T(8,128)(2,1)} %gm_ref.1, bf16[4096,128]{1,0:T(8,128)(2,1)} %km_ref.1, bf16[4096,128]{1,0:T(8,128)(2,1)} %copy-done.4, bf16[256,128]{1,0:T(8,128)(2,1)} %taps_ref.1), custom_call_target="tpu_custom_call" | custom-call | tf_op jit(solution)/shard_map/pallas_call | solution.py:59
  49.8 2.6 %psum.7 = f32[1,128]{1,0:T(1,128)S(1)} all-reduce(f32[1,128]{1,0:T(1,128)} %get-tuple-element.8), channel_id=1, replica_groups=mesh['groups'=2,'context'=8,'tensor'=2] {'tensor'}, use_global_device_ids=true, to_apply=%region_0.0 | all-reduce | flops 128 | bytes 1024 | tf_op jit(solution)/shard_map/psum | solution.py:181
  52.4 0.0 copy-done.1
  52.4 0.0 copy-done.6
  52.4 1.9 %multiply_convert_fusion = bf16[4096,128]{1,0:T(8,128)(2,1)S(1)} fusion(f32[4096,128]{1,0:T(8,128)} %get-tuple-element.7, bf16[4096,128]{1,0:T(8,128)(2,1)S(1)} %copy-done.1, f32[4096]{0:T(1024)S(1)} %copy-done.6, f32[128]{0:T(128)S(1)} %rsqrt_bitcast_fusion), kind=kLoop, calls=%fused_computation.4 | loop fusion | flops 2621440 | bytes 4211200 | tf_op jit(solution)/shard_map/convert_element_type | solution.py:183
  54.3 0.0 copy-start.5
  54.3 1.7 %copy.14.vt_ref = bf16[128,4,8,128]{3,2,1,0:T(8,128)(2,1)} copy(bf16[128,4,8,128]{0,3,2,1:T(8,128)(2,1)S(1)} %bitcast.23) | data formatting | bytes 2097152 | tf_op jit(solution)/shard_map/reshape | solution.py:134
  56.0 4.5 %shard_map.92 = f32[16,4,8,128]{3,2,1,0:T(8,128)} custom-call(bf16[128,4,8,128]{3,2,1,0:T(8,128)(2,1)} %copy.14.vt_ref, f32[16,4,8,128]{3,2,1,0:T(8,128)} %negate_exponential_fusion.lam_ref), custom_call_target="tpu_custom_call" | custom-call | tf_op jit(solution)/shard_map/pallas_call | solution.py:111
  60.5 0.0 all-gather.3.cloned.1.call-update
  60.5 0.0 copy-done.5
  60.5 0.1 multiply_bitcast_fusion
  60.6 0.8 copy.17
  61.4 50.8 %all-gather.3.cloned.1.call-done = f32[128,4,8,128]{3,2,1,0:T(8,128)} async-done(((f32[16,4,8,128]{3,2,1,0:T(8,128)}), f32[128,4,8,128]{3,2,1,0:T(8,128)}) %all-gather.3.cloned.1.call-update) | async-done | bytes 2097168 | tf_op jit(solution)/shard_map/all_gather | solution.py:155
  112.2 2.8 %multiply_reduce_fusion.h0_ref = f32[16,4,8,128]{3,2,1,0:T(8,128)} fusion(f32[8,16,4,8,128]{4,3,2,1,0:T(8,128)} %bitcast.26, f32[16,4,8,128]{3,2,1,0:T(8,128)S(1)} %bitcast.25, f32[8]{0:T(128)S(1)} %convert_negate_fusion, pred[8]{0:T(512)(128)(4,1)S(1)} %fusion.2), kind=kLoop, calls=%fused_computation.3 | loop fusion | flops 2031616 | bytes 2621480 | tf_op jit(solution)/shard_map/reduce_sum | solution.py:160
  115.0 6.9 %shard_map.93 = f32[128,4,8,128]{3,2,1,0:T(8,128)} custom-call(bf16[128,4,8,128]{3,2,1,0:T(8,128)(2,1)} %copy.14.vt_ref, f32[16,4,8,128]{3,2,1,0:T(8,128)} %negate_exponential_fusion.lam_ref, f32[16,4,8,128]{3,2,1,0:T(8,128)} %bitcast.28, f32[16,4,8,128]{3,2,1,0:T(8,128)} %multiply_reduce_fusion.h0_ref), custom_call_target="tpu_custom_call" | custom-call | tf_op jit(solution)/shard_map/pallas_call | solution.py:123
  121.9 3.1 %convert_convert_fusion = f32[128,4,8,128]{3,2,1,0:T(8,128)} fusion(f32[128,4,8,128]{3,2,1,0:T(8,128)} %shard_map.93), kind=kLoop, calls=%fused_computation.6 | loop fusion | flops 1048576 | bytes 4194304 | tf_op jit(solution)/shard_map/convert_element_type | solution.py:195
  124.9 0.0 copy-start
  124.9 0.0 copy-start.3
  124.9 3.1 %copy.15 = f32[128,4,8,128]{0,3,2,1:T(8,128)} copy(f32[128,4,8,128]{3,2,1,0:T(8,128)} %convert_convert_fusion) | data formatting | bytes 4194304 | tf_op jit(solution)/shard_map/convert_element_type | solution.py:195
  128.1 0.0 copy-done
  128.1 0.0 copy-done.3
  128.1 2.8 %fusion.1 = bf16[4096,128]{1,0:T(8,128)(2,1)} fusion(f32[4096,128]{1,0:T(8,128)S(1)} %copy-done, f32[128,4,8,128]{0,3,2,1:T(8,128)} %copy.15, bf16[4096,128]{1,0:T(8,128)(2,1)S(1)} %copy-done.3), kind=kLoop, calls=%fused_computation.2 | loop fusion | flops 2097152 | bytes 6291456 | tf_op jit(solution)/shard_map/convert_element_type | solution.py:195
  (3 shorter events, 0.0 us)
Async XLA Ops:
  6.5 6.8 %copy-start.2 = (f32[4096,16]{0,1:T(8,128)S(1)}, f32[4096,16]{0,1:T(8,128)}, u32[]{:S(2)}) copy-start(f32[4096,16]{0,1:T(8,128)} %param.15) | copy-start | bytes 786436
  6.5 105.6 %all-gather.3.cloned.1.call-start = ((), (), s32[]{:S(2)}) async-start(), calls=%async_computation | async-start | bytes 2359296 | tf_op jit(solution)/shard_map/all_gather | solution.py:155
  8.4 27.2 %collective-permute-start = (bf16[4096,128]{1,0:T(8,128)(2,1)S(1)}, bf16[4096,128]{1,0:T(8,128)(2,1)S(1)}, u32[]{:S(2)}, u32[]{:S(2)}) collective-permute-start(bf16[4096,128]{1,0:T(8,128)(2,1)S(1)} %multiply_convert_fusion.1), channel_id=1, source_target_pairs={{0,2},{2,4},{4,6},{6,8},{8,10},{10,12},{12,14},{1,3},{3,5},{5,7},{... | collective-permute-start | bytes 3145736 | tf_op jit(solution)/shard_map/ppermute | solution.py:20
  14.1 38.2 %copy-start.1 = (bf16[4096,128]{1,0:T(8,128)(2,1)S(1)}, bf16[4096,128]{1,0:T(8,128)(2,1)}, u32[]{:S(2)}) copy-start(bf16[4096,128]{1,0:T(8,128)(2,1)} %param.13) | copy-start | bytes 3145732
  14.1 38.2 %copy-start.6 = (f32[4096]{0:T(1024)S(1)}, f32[4096]{0:T(1024)}, u32[]{:S(2)}) copy-start(f32[4096]{0:T(1024)} %param.17) | copy-start | bytes 49156
  35.6 1.0 copy-start.4
  54.3 6.2 %copy-start.5 = (f32[4096,16]{0,1:T(8,128)S(1)}, f32[4096,16]{0,1:T(8,128)}, u32[]{:S(2)}) copy-start(f32[4096,16]{0,1:T(8,128)} %param.16) | copy-start | bytes 786436
  124.9 3.1 %copy-start = (f32[4096,128]{1,0:T(8,128)S(1)}, f32[4096,128]{1,0:T(8,128)}, u32[]{:S(2)}) copy-start(f32[4096,128]{1,0:T(8,128)} %get-tuple-element.7) | copy-start | bytes 6291460
  124.9 3.1 %copy-start.3 = (bf16[4096,128]{1,0:T(8,128)(2,1)S(1)}, bf16[4096,128]{1,0:T(8,128)(2,1)}, u32[]{:S(2)}) copy-start(bf16[4096,128]{1,0:T(8,128)(2,1)} %param.12) | copy-start | bytes 3145732
Sparse Core Ops, SparseCore 0:
  60.6 51.5 all-gather.2

commit v4 on v1

--- a/solution.py
+++ b/solution.py
@@ -41,9 +41,8 @@
         t_rim = jnp.where(upper, 0.0, rolled).astype(BF16)
         x = x_ref[lo:hi, :].astype(F32)
         vm = (km_ref[lo:hi, :].astype(F32) * x).astype(BF16)
-        conv = jnp.dot(vm, t_cur, preferred_element_type=F32) + jnp.dot(
-            rim_ref[lo:hi, :], t_rim, preferred_element_type=F32
-        )
+        ext = jnp.concatenate([rim_ref[lo:hi, :], vm], axis=1)
+        conv = jnp.dot(ext, jnp.concatenate([t_rim, t_cur], axis=0), preferred_element_type=F32)
         am = x + gm_ref[lo:hi, :].astype(F32) * conv
         am_ref[lo:hi, :] = am
         acc = acc + jnp.sum(am * am, axis=0, keepdims=True)
@@ -69,13 +68,27 @@
     )(inputs, gate_medium, key_medium, rim, taps)
 
 
-def final_state_kernel(vt_ref, lam_ref, f_ref):
+def load_values(am_ref, kl_ref, g_ref, r_ref, vt_ref):
+    r = r_ref[...]
+    for i in range(SUB):
+        rows = slice(i * LANE, (i + 1) * LANE)
+        normed = am_ref[rows, :] * r * g_ref[rows, :]
+        v = (kl_ref[rows, :].astype(F32) * normed).astype(BF16).astype(F32)
+        vt_ref[pl.ds(i, LANE, stride=SUB), :] = v.T
+
+
+def token_tile(ref, t):
+    return ref[pl.ds(pl.multiple_of(t * SUB, SUB), SUB), :]
+
+
+def final_state_kernel(am_ref, kl_ref, g_ref, r_ref, lam_ref, f_ref, vt_ref):
     modes = lam_ref.shape[0]
-    length = vt_ref.shape[0]
+    length = am_ref.shape[1]
+    load_values(am_ref, kl_ref, g_ref, r_ref, vt_ref)
     lam = [lam_ref[m] for m in range(modes)]
 
     def body(t, h):
-        v = vt_ref[t].astype(F32)
+        v = token_tile(vt_ref, t)
         return tuple(lam[m] * h[m] + v for m in range(modes))
 
     h = lax.fori_loop(0, length, body, tuple(jnp.zeros((SUB, LANE), F32) for _ in range(modes)), unroll=8)
@@ -83,50 +96,59 @@
         f_ref[m] = h[m]
 
 
-def output_kernel(vt_ref, lam_ref, w_ref, h0_ref, yt_ref):
+def output_kernel(am_ref, kl_ref, gl_ref, g_ref, r_ref, lam_ref, w_ref, h0_ref, out_ref, vt_ref, yt_ref):
     modes = lam_ref.shape[0]
-    length = vt_ref.shape[0]
+    length = am_ref.shape[1]
+    load_values(am_ref, kl_ref, g_ref, r_ref, vt_ref)
     lam = [lam_ref[m] for m in range(modes)]
     w = [w_ref[m] for m in range(modes)]
 
     def body(t, h):
-        v = vt_ref[t].astype(F32)
+        v = token_tile(vt_ref, t)
         h = tuple(lam[m] * h[m] + v for m in range(modes))
         y = w[0] * h[0]
         for m in range(1, modes):
             y = y + w[m] * h[m]
-        yt_ref[t] = y
+        yt_ref[pl.ds(pl.multiple_of(t * SUB, SUB), SUB), :] = y
         return h
 
     lax.fori_loop(0, length, body, tuple(h0_ref[m] for m in range(modes)), unroll=8)
+    for i in range(SUB):
+        rows = slice(i * LANE, (i + 1) * LANE)
+        long_out = yt_ref[pl.ds(i, LANE, stride=SUB), :].T.astype(BF16).astype(F32)
+        out_ref[rows, :] = (am_ref[rows, :] + gl_ref[rows, :].astype(F32) * long_out).astype(BF16)
 
 
 def tiled_spec(lead):
     return pl.BlockSpec((lead, None, SUB, LANE), lambda b: (0, b, 0, 0))
 
 
-def final_state_call(vt, lam):
-    length, blocks = vt.shape[0], vt.shape[1]
+def final_state_call(am, kl, gain, r, lam):
+    channels, length = am.shape
     modes = lam.shape[0]
+    big = pl.BlockSpec((TILE, length), lambda b: (b, 0))
     return pl.pallas_call(
         final_state_kernel,
-        grid=(blocks,),
-        in_specs=[tiled_spec(length), tiled_spec(modes)],
+        grid=(channels // TILE,),
+        in_specs=[big, big, pl.BlockSpec((TILE, 1), lambda b: (b, 0)), pl.BlockSpec((1, length), lambda b: (0, 0)), tiled_spec(modes)],
         out_specs=tiled_spec(modes),
         out_shape=jax.ShapeDtypeStruct(lam.shape, F32),
-    )(vt, lam)
-
-
-def output_call(vt, lam, w, h0):
-    length, blocks = vt.shape[0], vt.shape[1]
+        scratch_shapes=[pltpu.VMEM((length * SUB, LANE), F32)],
+    )(am, kl, gain, r, lam)
+
+
+def output_call(am, kl, gl, gain, r, lam, w, h0):
+    channels, length = am.shape
     modes = lam.shape[0]
+    big = pl.BlockSpec((TILE, length), lambda b: (b, 0))
     return pl.pallas_call(
         output_kernel,
-        grid=(blocks,),
-        in_specs=[tiled_spec(length), tiled_spec(modes), tiled_spec(modes), tiled_spec(modes)],
-        out_specs=tiled_spec(length),
-        out_shape=jax.ShapeDtypeStruct(vt.shape, F32),
-    )(vt, lam, w, h0)
+        grid=(channels // TILE,),
+        in_specs=[big, big, big, pl.BlockSpec((TILE, 1), lambda b: (b, 0)), pl.BlockSpec((1, length), lambda b: (0, 0)), tiled_spec(modes), tiled_spec(modes), tiled_spec(modes)],
+        out_specs=big,
+        out_shape=jax.ShapeDtypeStruct((channels, length), BF16),
+        scratch_shapes=[pltpu.VMEM((length * SUB, LANE), F32), pltpu.VMEM((length * SUB, LANE), F32)],
+    )(am, kl, gl, gain, r, lam, w, h0)
 
 
 def to_tiles(a):
@@ -153,14 +175,12 @@
     rim = shifted(values_medium, "context", 1)
     after_medium, partial = medium_call(inputs, gate_medium, key_medium, rim, medium_taps)
     totals = lax.psum(partial, "tensor")
-    normed = after_medium * lax.rsqrt(totals / width + EPS) * norm_gain[:, None]
-    values_long = (key_long.astype(F32) * normed).astype(BF16)
-
-    vt = to_tiles(values_long)
+    r = lax.rsqrt(totals / width + EPS)
+    gain = norm_gain[:, None]
     a_t = to_tiles(log_decay)
     lam = jnp.exp(-a_t)
     w = to_tiles(residues * jnp.sqrt(2.0 * log_decay))
-    finals = final_state_call(vt, lam)
+    finals = final_state_call(after_medium, key_long, gain, r, lam)
 
     carried = shifted(finals, "context", 1)
     distance = 1
@@ -169,9 +189,7 @@
         carried = carried + decay * shifted(carried, "context", distance)
         distance *= 2
 
-    yt = output_call(vt, lam, w, carried)
-    long_out = yt.reshape(length, channels).T.astype(BF16)
-    return (after_medium + gate_long.astype(F32) * long_out.astype(F32)).astype(BF16)
+    return output_call(after_medium, key_long, gate_long, gain, r, lam, w, carried)
 
 
 def solution(mesh):

time: 117 us -> 108 us (0.923)
  other arithmetic: 10.8 us -> 3.53 us
  Pallas kernels: 24.4 us -> 28.3 us
  local copies, waits for them, and re-layouts: 7.48 us -> 4.66 us
  waiting for transfers between devices: 59.6 us -> 57.6 us
    convert_element_type x3 -> x0, other arithmetic: 7.85 us -> none  [the longest x1 3.08 us: on_device(): long_out.astype(F32)]
    pallas_call x2, Pallas kernels: 11.3 us -> 16.2 us  [the longest x1 9.83 us: output_call(): pl.pallas_call(output_kernel, grid=(channels // TILE,), in_specs=[big, bi...]
    convert_element_type x1 -> x0, local copies, waits for them, and re-layouts: 3.13 us -> none  [on_device(): long_out.astype(F32)]
    ppermute x5, waiting for transfers between devices: 59.6 us -> 57.6 us  [shifted(): return lax.ppermute(block, axis, route)]
    broadcast_in_dim x0 -> x1, local copies, waits for them, and re-layouts: none -> 2 us  [on_device(): gain = norm_gain[:, None]]
    reshape x1 -> x0, local copies, waits for them, and re-layouts: 1.68 us -> none  [to_tiles(): return a.T.reshape(k, channels // TILE, SUB, LANE)]
    unnamed x19 -> x13, local copies, waits for them, and re-layouts: 2.67 us -> 2.67 us
  transfers between devices with their start and end apart: 5 -> 5, of which waited for: 5 -> 5; matrix products, arithmetic and copies ran while one was open for 2% -> 4% of each run, Pallas kernels for 0% -> 0%
where the time goes in v4:
time: 108 us; the launch traced here: 107 us
  waiting for transfers between devices  57.6 us (53%)
  Pallas kernels  28.3 us (26%)
  starting transfers between devices  10.4 us (10%)
  local copies, waits for them, and re-layouts  4.66 us (4%)
  other arithmetic  3.53 us (3%)
  blocking collectives  2.45 us (2%)
    ppermute x5, waiting for transfers between devices, shifted(): return lax.ppermute(block, axis, route)  57.6 us
    pallas_call x1, Pallas kernels, medium_call(): pl.pallas_call(medium_kernel, grid=(channels // block,), in_specs=[big, b...  12.1 us
    ppermute x5, starting transfers between devices, shifted(): return lax.ppermute(block, axis, route)  10.4 us
    pallas_call x1, Pallas kernels, output_call(): pl.pallas_call(output_kernel, grid=(channels // TILE,), in_specs=[big, bi...  9.83 us
    pallas_call x1, Pallas kernels, final_state_call(): pl.pallas_call(final_state_kernel, grid=(channels // TILE,), in_specs=[bi...  6.34 us
    unnamed x13, local copies, waits for them, and re-layouts  2.67 us
    psum x1, blocking collectives, on_device(): totals = lax.psum(partial, 'tensor')  2.45 us
  transfers between devices with their start and end apart: 5, of which 5 were waited for; matrix products, arithmetic and copies ran while one was open for 4% of the time, Pallas kernels for 0%

profile of v4, /device:TPU:24, one launch (start us, length us, event | category | flops | bytes accessed | tf_op | source)
XLA Modules:
  0.0 107.0 jit_solution(3569376455979666843)
XLA Ops:
  0.0 0.0 copy-start.2
  0.0 0.0 copy-start.1
  0.0 0.0 copy-start.3
  0.0 1.9 %multiply_convert_fusion = bf16[4096,128]{1,0:T(8,128)(2,1)S(1)} fusion(bf16[4096,128]{1,0:T(8,128)(2,1)} %x_ref.1, bf16[4096,128]{1,0:T(8,128)(2,1)} %km_ref.1), kind=kLoop, calls=%fused_computation | loop fusion | flops 2097152 | bytes 3145728 | tf_op jit(solution)/shard_map/convert_element_type | solution.py:174
  1.9 3.4 %collective-permute-start = (bf16[4096,128]{1,0:T(8,128)(2,1)S(1)}, bf16[4096,128]{1,0:T(8,128)(2,1)S(1)}, u32[]{:S(2)}, u32[]{:S(2)}) collective-permute-start(bf16[4096,128]{1,0:T(8,128)(2,1)S(1)} %multiply_convert_fusion), channel_id=1, source_target_pairs={{0,2},{2,4},{4,6},{6,8},{8,10},{10,12},{12,14},{1,3},{3,5},{5,7},{... | collective-permute-start | bytes 3145736 | tf_op jit(solution)/shard_map/ppermute | solution.py:20
  5.3 0.0 copy-done.2
  5.3 0.0 copy-done.1
  5.3 0.2 exponential_bitcast_fusion
  5.5 0.8 copy.12
  6.3 0.0 copy-done.3
  6.3 2.0 %copy.11.g_ref = f32[4096,1]{1,0:T(8,128)} copy(f32[4096,1]{0,1:T(1,128)S(1)} %bitcast.32) | data formatting | bytes 32768 | tf_op jit(solution)/shard_map/broadcast_in_dim | solution.py:179
  8.3 21.3 %collective-permute-done.rim_ref = bf16[4096,128]{1,0:T(8,128)(2,1)S(1)} collective-permute-done((bf16[4096,128]{1,0:T(8,128)(2,1)S(1)}, bf16[4096,128]{1,0:T(8,128)(2,1)S(1)}, u32[]{:S(2)}, u32[]{:S(2)}) %collective-permute-start) | collective-permute-done | bytes 1048608 | tf_op jit(solution)/shard_map/ppermute | solution.py:20
  29.6 0.0 copy-start
  29.6 1.0 copy-done
  30.5 12.1 %shard_map.91 = (f32[4096,128]{1,0:T(8,128)}, f32[1,128]{1,0:T(1,128)}) custom-call(bf16[4096,128]{1,0:T(8,128)(2,1)} %x_ref.1, bf16[4096,128]{1,0:T(8,128)(2,1)} %gm_ref.1, bf16[4096,128]{1,0:T(8,128)(2,1)} %km_ref.1, bf16[4096,128]{1,0:T(8,128)(2,1)} %copy-done, bf16[256,128]{1,0:T(8,128)(2,1)} %taps_ref.1), custom_call_target="tpu_custom_call" | custom-call | tf_op jit(solution)/shard_map/pallas_call | solution.py:58
  42.6 2.4 %psum.7 = f32[1,128]{1,0:T(1,128)S(1)} all-reduce(f32[1,128]{1,0:T(1,128)} %get-tuple-element.8), channel_id=1, replica_groups=mesh['groups'=2,'context'=8,'tensor'=2] {'tensor'}, use_global_device_ids=true, to_apply=%region_0.0 | all-reduce | flops 128 | bytes 1024 | tf_op jit(solution)/shard_map/psum | solution.py:177
  45.1 0.6 add_rsqrt_fusion.r_ref
  45.7 6.3 %shard_map.92 = f32[16,4,8,128]{3,2,1,0:T(8,128)} custom-call(f32[4096,128]{1,0:T(8,128)} %get-tuple-element.7.am_ref, bf16[4096,128]{1,0:T(8,128)(2,1)} %kl_ref.3, f32[4096,1]{1,0:T(8,128)} %copy.11.g_ref, f32[1,128]{1,0:T(1,128)} %add_rsqrt_fusion.r_ref, f32[16,4,8,128]{3,2,1,0:T(8,128)} %bitcast.26), custom_call_target="tpu_custom_call" | custom-call | tf_op jit(solution)/shard_map/pallas_call | solution.py:130
  52.0 2.5 %collective-permute-start.1 = (f32[16,4,8,128]{3,2,1,0:T(8,128)}, f32[16,4,8,128]{3,2,1,0:T(8,128)S(1)}, u32[]{:S(2)}, u32[]{:S(2)}) collective-permute-start(f32[16,4,8,128]{3,2,1,0:T(8,128)} %shard_map.92), channel_id=1, source_target_pairs={{0,2},{2,4},{4,6},{6,8},{8,10},{10,12},{12,14},{1,3},{3,5},{5,7},{... | collective-permute-start | bytes 786440 | tf_op jit(solution)/shard_map/ppermute | solution.py:20
  54.5 8.9 %collective-permute-done.1 = f32[16,4,8,128]{3,2,1,0:T(8,128)S(1)} collective-permute-done((f32[16,4,8,128]{3,2,1,0:T(8,128)}, f32[16,4,8,128]{3,2,1,0:T(8,128)S(1)}, u32[]{:S(2)}, u32[]{:S(2)}) %collective-permute-start.1) | collective-permute-done | bytes 262176 | tf_op jit(solution)/shard_map/ppermute | solution.py:20
  63.4 1.9 %collective-permute-start.2 = (f32[16,4,8,128]{3,2,1,0:T(8,128)S(1)}, f32[16,4,8,128]{3,2,1,0:T(8,128)S(1)}, u32[]{:S(2)}, u32[]{:S(2)}) collective-permute-start(f32[16,4,8,128]{3,2,1,0:T(8,128)S(1)} %collective-permute-done.1), channel_id=1, source_target_pairs={{0,2},{2,4},{4,6},{6,8},{8,10},{10,12},{12,14},{1,3},{3,5},{5,7},{... | collective-permute-start | bytes 786440 | tf_op jit(solution)/shard_map/ppermute | solution.py:20
  65.3 0.1 copy.14
  65.4 8.4 %collective-permute-done.2 = f32[16,4,8,128]{3,2,1,0:T(8,128)S(1)} collective-permute-done((f32[16,4,8,128]{3,2,1,0:T(8,128)S(1)}, f32[16,4,8,128]{3,2,1,0:T(8,128)S(1)}, u32[]{:S(2)}, u32[]{:S(2)}) %collective-permute-start.2) | collective-permute-done | bytes 262176 | tf_op jit(solution)/shard_map/ppermute | solution.py:20
  73.7 0.1 multiply_add_fusion.2
  73.8 1.3 %collective-permute-start.3 = (f32[16,4,8,128]{3,2,1,0:T(8,128)S(1)}, f32[16,4,8,128]{3,2,1,0:T(8,128)S(1)}, u32[]{:S(2)}, u32[]{:S(2)}) collective-permute-start(f32[16,4,8,128]{3,2,1,0:T(8,128)S(1)} %multiply_add_fusion.2), channel_id=1, source_target_pairs={{0,4},{2,6},{4,8},{6,10},{8,12},{10,14},{1,5},{3,7},{5,9},{7,11},{... | collective-permute-start | bytes 786440 | tf_op jit(solution)/shard_map/ppermute | solution.py:20
  75.1 0.1 copy.15
  75.1 7.2 %collective-permute-done.3 = f32[16,4,8,128]{3,2,1,0:T(8,128)S(1)} collective-permute-done((f32[16,4,8,128]{3,2,1,0:T(8,128)S(1)}, f32[16,4,8,128]{3,2,1,0:T(8,128)S(1)}, u32[]{:S(2)}, u32[]{:S(2)}) %collective-permute-start.3) | collective-permute-done | bytes 262176 | tf_op jit(solution)/shard_map/ppermute | solution.py:20
  82.3 0.1 multiply_add_fusion.1
  82.3 1.3 %collective-permute-start.4 = (f32[16,4,8,128]{3,2,1,0:T(8,128)S(1)}, f32[16,4,8,128]{3,2,1,0:T(8,128)S(1)}, u32[]{:S(2)}, u32[]{:S(2)}) collective-permute-start(f32[16,4,8,128]{3,2,1,0:T(8,128)S(1)} %multiply_add_fusion.1), channel_id=1, source_target_pairs={{0,8},{2,10},{4,12},{6,14},{1,9},{3,11},{5,13},{7,15},{16,24},{18,... | collective-permute-start | bytes 786440 | tf_op jit(solution)/shard_map/ppermute | solution.py:20
  83.6 0.1 copy.16
  83.7 0.8 copy.13
  84.5 11.9 %collective-permute-done.4 = f32[16,4,8,128]{3,2,1,0:T(8,128)S(1)} collective-permute-done((f32[16,4,8,128]{3,2,1,0:T(8,128)S(1)}, f32[16,4,8,128]{3,2,1,0:T(8,128)S(1)}, u32[]{:S(2)}, u32[]{:S(2)}) %collective-permute-start.4) | collective-permute-done | bytes 262176 | tf_op jit(solution)/shard_map/ppermute | solution.py:20
  96.3 0.8 multiply_add_fusion.h0_ref
  97.1 9.8 %shard_map.93 = bf16[4096,128]{1,0:T(8,128)(2,1)} custom-call(f32[4096,128]{1,0:T(8,128)} %get-tuple-element.7.am_ref, bf16[4096,128]{1,0:T(8,128)(2,1)} %kl_ref.3, bf16[4096,128]{1,0:T(8,128)(2,1)} %gl_ref.1, f32[4096,1]{1,0:T(8,128)} %copy.11.g_ref, f32[1,128]{1,0:T(1,128)} %add_rsqrt_fusion.r_ref, f32[16,4,8,128]{3,2,1,0:T(8,128)} %bitcast.27, ...), custom_call_target="tpu_custom_call" | custom-call | tf_op jit(solution)/shard_map/pallas_call | solution.py:144
Async XLA Ops:
  0.0 5.3 %copy-start.2 = (f32[4096,16]{0,1:T(8,128)S(1)}, f32[4096,16]{0,1:T(8,128)}, u32[]{:S(2)}) copy-start(f32[4096,16]{0,1:T(8,128)} %param.16) | copy-start | bytes 786436
  0.0 5.3 %copy-start.1 = (f32[4096,16]{0,1:T(8,128)S(1)}, f32[4096,16]{0,1:T(8,128)}, u32[]{:S(2)}) copy-start(f32[4096,16]{0,1:T(8,128)} %param.15) | copy-start | bytes 786436
  0.0 6.3 %copy-start.3 = (f32[4096]{0:T(1024)S(1)}, f32[4096]{0:T(1024)}, u32[]{:S(2)}) copy-start(f32[4096]{0:T(1024)} %param.17) | copy-start | bytes 49156
  1.9 27.7 %collective-permute-start = (bf16[4096,128]{1,0:T(8,128)(2,1)S(1)}, bf16[4096,128]{1,0:T(8,128)(2,1)S(1)}, u32[]{:S(2)}, u32[]{:S(2)}) collective-permute-start(bf16[4096,128]{1,0:T(8,128)(2,1)S(1)} %multiply_convert_fusion), channel_id=1, source_target_pairs={{0,2},{2,4},{4,6},{6,8},{8,10},{10,12},{12,14},{1,3},{3,5},{5,7},{... | collective-permute-start | bytes 3145736 | tf_op jit(solution)/shard_map/ppermute | solution.py:20
  29.6 1.0 copy-start
  52.0 11.4 %collective-permute-start.1 = (f32[16,4,8,128]{3,2,1,0:T(8,128)}, f32[16,4,8,128]{3,2,1,0:T(8,128)S(1)}, u32[]{:S(2)}, u32[]{:S(2)}) collective-permute-start(f32[16,4,8,128]{3,2,1,0:T(8,128)} %shard_map.92), channel_id=1, source_target_pairs={{0,2},{2,4},{4,6},{6,8},{8,10},{10,12},{12,14},{1,3},{3,5},{5,7},{... | collective-permute-start | bytes 786440 | tf_op jit(solution)/shard_map/ppermute | solution.py:20
  63.4 10.3 %collective-permute-start.2 = (f32[16,4,8,128]{3,2,1,0:T(8,128)S(1)}, f32[16,4,8,128]{3,2,1,0:T(8,128)S(1)}, u32[]{:S(2)}, u32[]{:S(2)}) collective-permute-start(f32[16,4,8,128]{3,2,1,0:T(8,128)S(1)} %collective-permute-done.1), channel_id=1, source_target_pairs={{0,2},{2,4},{4,6},{6,8},{8,10},{10,12},{12,14},{1,3},{3,5},{5,7},{... | collective-permute-start | bytes 786440 | tf_op jit(solution)/shard_map/ppermute | solution.py:20
  73.8 8.5 %collective-permute-start.3 = (f32[16,4,8,128]{3,2,1,0:T(8,128)S(1)}, f32[16,4,8,128]{3,2,1,0:T(8,128)S(1)}, u32[]{:S(2)}, u32[]{:S(2)}) collective-permute-start(f32[16,4,8,128]{3,2,1,0:T(8,128)S(1)} %multiply_add_fusion.2), channel_id=1, source_target_pairs={{0,4},{2,6},{4,8},{6,10},{8,12},{10,14},{1,5},{3,7},{5,9},{7,11},{... | collective-permute-start | bytes 786440 | tf_op jit(solution)/shard_map/ppermute | solution.py:20
  82.3 14.0 %collective-permute-start.4 = (f32[16,4,8,128]{3,2,1,0:T(8,128)S(1)}, f32[16,4,8,128]{3,2,1,0:T(8,128)S(1)}, u32[]{:S(2)}, u32[]{:S(2)}) collective-permute-start(f32[16,4,8,128]{3,2,1,0:T(8,128)S(1)} %multiply_add_fusion.1), channel_id=1, source_target_pairs={{0,8},{2,10},{4,12},{6,14},{1,9},{3,11},{5,13},{7,15},{16,24},{18,... | collective-permute-start | bytes 786440 | tf_op jit(solution)/shard_map/ppermute | solution.py:20

commit v5 on v4

--- a/solution.py
+++ b/solution.py
@@ -20,13 +20,34 @@
     return lax.ppermute(block, axis, route)
 
 
-def medium_kernel(x_ref, gm_ref, km_ref, rim_ref, taps_ref, am_ref, ss_ref):
+def tap_toeplitz(taps_ref, g, length, upper):
+    taps = jnp.broadcast_to(taps_ref[g : g + 1, :].astype(F32), (length, length))
+    rolled = pltpu.roll(taps, 0, 1, stride=1, stride_axis=0)
+    if upper:
+        return jnp.where(tap_mask(length), rolled, 0.0).astype(BF16)
+    return jnp.where(tap_mask(length), 0.0, rolled).astype(BF16)
+
+
+def tap_mask(length):
+    row = lax.broadcasted_iota(jnp.int32, (length, length), 0)
+    col = lax.broadcasted_iota(jnp.int32, (length, length), 1)
+    return col >= row
+
+
+def current_kernel(x_ref, km_ref, taps_ref, conv_ref):
     rows, length = x_ref.shape
     groups = taps_ref.shape[0]
     per_group = rows // groups
-    row = lax.broadcasted_iota(jnp.int32, (length, length), 0)
-    col = lax.broadcasted_iota(jnp.int32, (length, length), 1)
-    upper = col >= row
+    for g in range(groups):
+        lo, hi = g * per_group, (g + 1) * per_group
+        vm = (km_ref[lo:hi, :].astype(F32) * x_ref[lo:hi, :].astype(F32)).astype(BF16)
+        conv_ref[lo:hi, :] = jnp.dot(vm, tap_toeplitz(taps_ref, g, length, True), preferred_element_type=F32)
+
+
+def rim_kernel(conv_ref, x_ref, gm_ref, rim_ref, taps_ref, am_ref, ss_ref):
+    rows, length = x_ref.shape
+    groups = taps_ref.shape[0]
+    per_group = rows // groups
 
     @pl.when(pl.program_id(0) == 0)
     def _():
@@ -35,15 +56,10 @@
     acc = jnp.zeros((1, length), F32)
     for g in range(groups):
         lo, hi = g * per_group, (g + 1) * per_group
-        taps = jnp.broadcast_to(taps_ref[g : g + 1, :].astype(F32), (length, length))
-        rolled = pltpu.roll(taps, 0, 1, stride=1, stride_axis=0)
-        t_cur = jnp.where(upper, rolled, 0.0).astype(BF16)
-        t_rim = jnp.where(upper, 0.0, rolled).astype(BF16)
-        x = x_ref[lo:hi, :].astype(F32)
-        vm = (km_ref[lo:hi, :].astype(F32) * x).astype(BF16)
-        ext = jnp.concatenate([rim_ref[lo:hi, :], vm], axis=1)
-        conv = jnp.dot(ext, jnp.concatenate([t_rim, t_cur], axis=0), preferred_element_type=F32)
-        am = x + gm_ref[lo:hi, :].astype(F32) * conv
+        conv = conv_ref[lo:hi, :] + jnp.dot(
+            rim_ref[lo:hi, :], tap_toeplitz(taps_ref, g, length, False), preferred_element_type=F32
+        )
+        am = x_ref[lo:hi, :].astype(F32) + gm_ref[lo:hi, :].astype(F32) * conv
         am_ref[lo:hi, :] = am
         acc = acc + jnp.sum(am * am, axis=0, keepdims=True)
     ss_ref[...] += acc
@@ -55,17 +71,25 @@
     block = 256
     tap_block = block // per_group
     big = pl.BlockSpec((block, length), lambda b: (b, 0))
+    tap_spec = pl.BlockSpec((tap_block, length), lambda b: (b, 0))
+    conv = pl.pallas_call(
+        current_kernel,
+        grid=(channels // block,),
+        in_specs=[big, big, tap_spec],
+        out_specs=big,
+        out_shape=jax.ShapeDtypeStruct((channels, length), F32),
+    )(inputs, key_medium, taps)
     return pl.pallas_call(
-        medium_kernel,
+        rim_kernel,
         grid=(channels // block,),
-        in_specs=[big, big, big, big, pl.BlockSpec((tap_block, length), lambda b: (b, 0))],
+        in_specs=[big, big, big, big, tap_spec],
         out_specs=[big, pl.BlockSpec((1, length), lambda b: (0, 0))],
         out_shape=[
             jax.ShapeDtypeStruct((channels, length), F32),
             jax.ShapeDtypeStruct((1, length), F32),
         ],
         compiler_params=pltpu.CompilerParams(dimension_semantics=("arbitrary",)),
-    )(inputs, gate_medium, key_medium, rim, taps)
+    )(conv, inputs, gate_medium, rim, taps)
 
 
 def load_values(am_ref, kl_ref, g_ref, r_ref, vt_ref):

time: 108 us -> 109 us (level)
  waiting for transfers between devices: 57.6 us -> 45.3 us
  Pallas kernels: 28.3 us -> 39.9 us
    ppermute x5, waiting for transfers between devices: 57.6 us -> 45.3 us  [shifted(): return lax.ppermute(block, axis, route)]
    pallas_call x1 -> x2, Pallas kernels: 12.1 us -> 23.7 us  [the longest x1 12.3 us: medium_call(): pl.pallas_call(rim_kernel, grid=(channels // block,), in_specs=[big, big,...]
    unnamed x13 -> x11, local copies, waits for them, and re-layouts: 2.67 us -> 2.63 us
  transfers between devices with their start and end apart: 5 -> 5, of which waited for: 5 -> 5; matrix products, arithmetic and copies ran while one was open for 4% -> 4% of each run, Pallas kernels for 0% -> 11%
where the time goes in v5:
time: 109 us; the launch traced here: 107 us
  waiting for transfers between devices  45.3 us (42%)
  Pallas kernels  39.9 us (37%)
  starting transfers between devices  10.4 us (10%)
  local copies, waits for them, and re-layouts  4.63 us (4%)
  other arithmetic  4.42 us (4%)
  blocking collectives  2.57 us (2%)
    ppermute x5, waiting for transfers between devices, shifted(): return lax.ppermute(block, axis, route)  45.3 us
    pallas_call x1, Pallas kernels, medium_call(): pl.pallas_call(rim_kernel, grid=(channels // block,), in_specs=[big, big,...  12.3 us
    pallas_call x1, Pallas kernels, medium_call(): pl.pallas_call(current_kernel, grid=(channels // block,), in_specs=[big,...  11.4 us
    ppermute x5, starting transfers between devices, shifted(): return lax.ppermute(block, axis, route)  10.4 us
    pallas_call x1, Pallas kernels, output_call(): pl.pallas_call(output_kernel, grid=(channels // TILE,), in_specs=[big, bi...  9.83 us
    pallas_call x1, Pallas kernels, final_state_call(): pl.pallas_call(final_state_kernel, grid=(channels // TILE,), in_specs=[bi...  6.34 us
    unnamed x11, local copies, waits for them, and re-layouts  2.63 us
    psum x1, blocking collectives, on_device(): totals = lax.psum(partial, 'tensor')  2.57 us
  transfers between devices with their start and end apart: 5, of which 5 were waited for; matrix products, arithmetic and copies ran while one was open for 4% of the time, Pallas kernels for 11%

profile of v5, /device:TPU:24, one launch (start us, length us, event | category | flops | bytes accessed | tf_op | source)
XLA Modules:
  0.0 107.3 jit_solution(17862660205627958147)
XLA Ops:
  0.0 1.8 %multiply_convert_fusion = bf16[4096,128]{1,0:T(8,128)(2,1)S(1)} fusion(bf16[4096,128]{1,0:T(8,128)(2,1)} %x_ref.3, bf16[4096,128]{1,0:T(8,128)(2,1)} %km_ref.1), kind=kLoop, calls=%fused_computation | loop fusion | flops 2097152 | bytes 3145728 | tf_op jit(solution)/shard_map/convert_element_type | solution.py:198
  1.8 0.0 copy-start.2
  1.8 3.4 %collective-permute-start = (bf16[4096,128]{1,0:T(8,128)(2,1)S(1)}, bf16[4096,128]{1,0:T(8,128)(2,1)S(1)}, u32[]{:S(2)}, u32[]{:S(2)}) collective-permute-start(bf16[4096,128]{1,0:T(8,128)(2,1)S(1)} %multiply_convert_fusion), channel_id=1, source_target_pairs={{0,2},{2,4},{4,6},{6,8},{8,10},{10,12},{12,14},{1,3},{3,5},{5,7},{... | collective-permute-start | bytes 3145736 | tf_op jit(solution)/shard_map/ppermute | solution.py:20
  5.2 11.4 %shard_map.91.conv_ref = f32[4096,128]{1,0:T(8,128)} custom-call(bf16[4096,128]{1,0:T(8,128)(2,1)} %x_ref.3, bf16[4096,128]{1,0:T(8,128)(2,1)} %km_ref.1, bf16[256,128]{1,0:T(8,128)(2,1)} %taps_ref.3), custom_call_target="tpu_custom_call" | custom-call | tf_op jit(solution)/shard_map/pallas_call | solution.py:75
  16.6 0.0 copy-start.1
  16.6 0.0 copy-done.2
  16.6 2.0 %copy.11.g_ref = f32[4096,1]{1,0:T(8,128)} copy(f32[4096,1]{0,1:T(1,128)S(1)} %bitcast.32) | data formatting | bytes 32768 | tf_op jit(solution)/shard_map/broadcast_in_dim | solution.py:203
  18.6 0.0 copy-done.1
  18.6 1.1 %exponential_bitcast_fusion = (f32[2,8,32,128]{3,1,2,0:T(8,128)S(1)}, f32[2,8,32,128]{3,1,2,0:T(8,128)S(1)}, f32[2,8,32,128]{3,1,2,0:T(8,128)S(1)}, f32[2,8,32,128]{3,1,2,0:T(8,128)S(1)}, f32[2,8,32,128]{3,1,2,0:T(8,128)S(1)}) fusion(f32[4096,16]{0,1:T(8,128)S(1)} %copy-done.1, f32[4096,16]{0,1:T(8,128)} %param.16), kind=kLoop, calls=%fused_computation.2 | loop fusion | flops 393216 | bytes 1835008
  19.7 0.7 copy.12
  20.5 9.1 %collective-permute-done.rim_ref = bf16[4096,128]{1,0:T(8,128)(2,1)S(1)} collective-permute-done((bf16[4096,128]{1,0:T(8,128)(2,1)S(1)}, bf16[4096,128]{1,0:T(8,128)(2,1)S(1)}, u32[]{:S(2)}, u32[]{:S(2)}) %collective-permute-start) | collective-permute-done | bytes 1048608 | tf_op jit(solution)/shard_map/ppermute | solution.py:20
  29.5 0.0 copy-start
  29.5 1.0 copy-done
  30.5 12.3 %shard_map.92 = (f32[4096,128]{1,0:T(8,128)}, f32[1,128]{1,0:T(1,128)}) custom-call(f32[4096,128]{1,0:T(8,128)} %shard_map.91.conv_ref, bf16[4096,128]{1,0:T(8,128)(2,1)} %x_ref.3, bf16[4096,128]{1,0:T(8,128)(2,1)} %gm_ref.1, bf16[4096,128]{1,0:T(8,128)(2,1)} %copy-done, bf16[256,128]{1,0:T(8,128)(2,1)} %taps_ref.3), custom_call_target="tpu_custom_call" | custom-call | tf_op jit(solution)/shard_map/pallas_call | solution.py:82
  42.8 2.6 %psum.7 = f32[1,128]{1,0:T(1,128)S(1)} all-reduce(f32[1,128]{1,0:T(1,128)} %get-tuple-element.8), channel_id=1, replica_groups=mesh['groups'=2,'context'=8,'tensor'=2] {'tensor'}, use_global_device_ids=true, to_apply=%region_0.0 | all-reduce | flops 128 | bytes 1024 | tf_op jit(solution)/shard_map/psum | solution.py:201
  45.4 0.6 add_rsqrt_fusion.r_ref
  46.0 6.3 %shard_map.93 = f32[16,4,8,128]{3,2,1,0:T(8,128)} custom-call(f32[4096,128]{1,0:T(8,128)} %get-tuple-element.7.am_ref, bf16[4096,128]{1,0:T(8,128)(2,1)} %kl_ref.3, f32[4096,1]{1,0:T(8,128)} %copy.11.g_ref, f32[1,128]{1,0:T(1,128)} %add_rsqrt_fusion.r_ref, f32[16,4,8,128]{3,2,1,0:T(8,128)} %bitcast.26), custom_call_target="tpu_custom_call" | custom-call | tf_op jit(solution)/shard_map/pallas_call | solution.py:154
  52.3 2.5 %collective-permute-start.1 = (f32[16,4,8,128]{3,2,1,0:T(8,128)}, f32[16,4,8,128]{3,2,1,0:T(8,128)S(1)}, u32[]{:S(2)}, u32[]{:S(2)}) collective-permute-start(f32[16,4,8,128]{3,2,1,0:T(8,128)} %shard_map.93), channel_id=1, source_target_pairs={{0,2},{2,4},{4,6},{6,8},{8,10},{10,12},{12,14},{1,3},{3,5},{5,7},{... | collective-permute-start | bytes 786440 | tf_op jit(solution)/shard_map/ppermute | solution.py:20
  54.8 8.9 %collective-permute-done.1 = f32[16,4,8,128]{3,2,1,0:T(8,128)S(1)} collective-permute-done((f32[16,4,8,128]{3,2,1,0:T(8,128)}, f32[16,4,8,128]{3,2,1,0:T(8,128)S(1)}, u32[]{:S(2)}, u32[]{:S(2)}) %collective-permute-start.1) | collective-permute-done | bytes 262176 | tf_op jit(solution)/shard_map/ppermute | solution.py:20
  63.7 1.9 %collective-permute-start.2 = (f32[16,4,8,128]{3,2,1,0:T(8,128)S(1)}, f32[16,4,8,128]{3,2,1,0:T(8,128)S(1)}, u32[]{:S(2)}, u32[]{:S(2)}) collective-permute-start(f32[16,4,8,128]{3,2,1,0:T(8,128)S(1)} %collective-permute-done.1), channel_id=1, source_target_pairs={{0,2},{2,4},{4,6},{6,8},{8,10},{10,12},{12,14},{1,3},{3,5},{5,7},{... | collective-permute-start | bytes 786440 | tf_op jit(solution)/shard_map/ppermute | solution.py:20
  65.6 0.1 copy.14
  65.7 8.4 %collective-permute-done.2 = f32[16,4,8,128]{3,2,1,0:T(8,128)S(1)} collective-permute-done((f32[16,4,8,128]{3,2,1,0:T(8,128)S(1)}, f32[16,4,8,128]{3,2,1,0:T(8,128)S(1)}, u32[]{:S(2)}, u32[]{:S(2)}) %collective-permute-start.2) | collective-permute-done | bytes 262176 | tf_op jit(solution)/shard_map/ppermute | solution.py:20
  74.0 0.1 multiply_add_fusion.2
  74.1 1.3 %collective-permute-start.3 = (f32[16,4,8,128]{3,2,1,0:T(8,128)S(1)}, f32[16,4,8,128]{3,2,1,0:T(8,128)S(1)}, u32[]{:S(2)}, u32[]{:S(2)}) collective-permute-start(f32[16,4,8,128]{3,2,1,0:T(8,128)S(1)} %multiply_add_fusion.2), channel_id=1, source_target_pairs={{0,4},{2,6},{4,8},{6,10},{8,12},{10,14},{1,5},{3,7},{5,9},{7,11},{... | collective-permute-start | bytes 786440 | tf_op jit(solution)/shard_map/ppermute | solution.py:20
  75.4 0.1 copy.15
  75.5 7.2 %collective-permute-done.3 = f32[16,4,8,128]{3,2,1,0:T(8,128)S(1)} collective-permute-done((f32[16,4,8,128]{3,2,1,0:T(8,128)S(1)}, f32[16,4,8,128]{3,2,1,0:T(8,128)S(1)}, u32[]{:S(2)}, u32[]{:S(2)}) %collective-permute-start.3) | collective-permute-done | bytes 262176 | tf_op jit(solution)/shard_map/ppermute | solution.py:20
  82.6 0.1 multiply_add_fusion.1
  82.7 1.3 %collective-permute-start.4 = (f32[16,4,8,128]{3,2,1,0:T(8,128)S(1)}, f32[16,4,8,128]{3,2,1,0:T(8,128)S(1)}, u32[]{:S(2)}, u32[]{:S(2)}) collective-permute-start(f32[16,4,8,128]{3,2,1,0:T(8,128)S(1)} %multiply_add_fusion.1), channel_id=1, source_target_pairs={{0,8},{2,10},{4,12},{6,14},{1,9},{3,11},{5,13},{7,15},{16,24},{18,... | collective-permute-start | bytes 786440 | tf_op jit(solution)/shard_map/ppermute | solution.py:20
  84.0 0.8 copy.13
  84.7 0.1 copy.16
  84.8 11.9 %collective-permute-done.4 = f32[16,4,8,128]{3,2,1,0:T(8,128)S(1)} collective-permute-done((f32[16,4,8,128]{3,2,1,0:T(8,128)S(1)}, f32[16,4,8,128]{3,2,1,0:T(8,128)S(1)}, u32[]{:S(2)}, u32[]{:S(2)}) %collective-permute-start.4) | collective-permute-done | bytes 262176 | tf_op jit(solution)/shard_map/ppermute | solution.py:20
  96.7 0.8 multiply_add_fusion.h0_ref
  97.4 9.8 %shard_map.94 = bf16[4096,128]{1,0:T(8,128)(2,1)} custom-call(f32[4096,128]{1,0:T(8,128)} %get-tuple-element.7.am_ref, bf16[4096,128]{1,0:T(8,128)(2,1)} %kl_ref.3, bf16[4096,128]{1,0:T(8,128)(2,1)} %gl_ref.1, f32[4096,1]{1,0:T(8,128)} %copy.11.g_ref, f32[1,128]{1,0:T(1,128)} %add_rsqrt_fusion.r_ref, f32[16,4,8,128]{3,2,1,0:T(8,128)} %bitcast.27, ...), custom_call_target="tpu_custom_call" | custom-call | tf_op jit(solution)/shard_map/pallas_call | solution.py:168
Async XLA Ops:
  1.8 14.8 %copy-start.2 = (f32[4096]{0:T(1024)S(1)}, f32[4096]{0:T(1024)}, u32[]{:S(2)}) copy-start(f32[4096]{0:T(1024)} %param.17) | copy-start | bytes 49156
  1.8 27.7 %collective-permute-start = (bf16[4096,128]{1,0:T(8,128)(2,1)S(1)}, bf16[4096,128]{1,0:T(8,128)(2,1)S(1)}, u32[]{:S(2)}, u32[]{:S(2)}) collective-permute-start(bf16[4096,128]{1,0:T(8,128)(2,1)S(1)} %multiply_convert_fusion), channel_id=1, source_target_pairs={{0,2},{2,4},{4,6},{6,8},{8,10},{10,12},{12,14},{1,3},{3,5},{5,7},{... | collective-permute-start | bytes 3145736 | tf_op jit(solution)/shard_map/ppermute | solution.py:20
  16.6 2.0 %copy-start.1 = (f32[4096,16]{0,1:T(8,128)S(1)}, f32[4096,16]{0,1:T(8,128)}, u32[]{:S(2)}) copy-start(f32[4096,16]{0,1:T(8,128)} %param.15) | copy-start | bytes 786436
  29.5 1.0 copy-start
  52.3 11.4 %collective-permute-start.1 = (f32[16,4,8,128]{3,2,1,0:T(8,128)}, f32[16,4,8,128]{3,2,1,0:T(8,128)S(1)}, u32[]{:S(2)}, u32[]{:S(2)}) collective-permute-start(f32[16,4,8,128]{3,2,1,0:T(8,128)} %shard_map.93), channel_id=1, source_target_pairs={{0,2},{2,4},{4,6},{6,8},{8,10},{10,12},{12,14},{1,3},{3,5},{5,7},{... | collective-permute-start | bytes 786440 | tf_op jit(solution)/shard_map/ppermute | solution.py:20
  63.7 10.3 %collective-permute-start.2 = (f32[16,4,8,128]{3,2,1,0:T(8,128)S(1)}, f32[16,4,8,128]{3,2,1,0:T(8,128)S(1)}, u32[]{:S(2)}, u32[]{:S(2)}) collective-permute-start(f32[16,4,8,128]{3,2,1,0:T(8,128)S(1)} %collective-permute-done.1), channel_id=1, source_target_pairs={{0,2},{2,4},{4,6},{6,8},{8,10},{10,12},{12,14},{1,3},{3,5},{5,7},{... | collective-permute-start | bytes 786440 | tf_op jit(solution)/shard_map/ppermute | solution.py:20
  74.1 8.5 %collective-permute-start.3 = (f32[16,4,8,128]{3,2,1,0:T(8,128)S(1)}, f32[16,4,8,128]{3,2,1,0:T(8,128)S(1)}, u32[]{:S(2)}, u32[]{:S(2)}) collective-permute-start(f32[16,4,8,128]{3,2,1,0:T(8,128)S(1)} %multiply_add_fusion.2), channel_id=1, source_target_pairs={{0,4},{2,6},{4,8},{6,10},{8,12},{10,14},{1,5},{3,7},{5,9},{7,11},{... | collective-permute-start | bytes 786440 | tf_op jit(solution)/shard_map/ppermute | solution.py:20
  82.7 14.0 %collective-permute-start.4 = (f32[16,4,8,128]{3,2,1,0:T(8,128)S(1)}, f32[16,4,8,128]{3,2,1,0:T(8,128)S(1)}, u32[]{:S(2)}, u32[]{:S(2)}) collective-permute-start(f32[16,4,8,128]{3,2,1,0:T(8,128)S(1)} %multiply_add_fusion.1), channel_id=1, source_target_pairs={{0,8},{2,10},{4,12},{6,14},{1,9},{3,11},{5,13},{7,15},{16,24},{18,... | collective-permute-start | bytes 786440 | tf_op jit(solution)/shard_map/ppermute | solution.py:20

commit v6 on v5

--- a/solution.py
+++ b/solution.py
@@ -20,33 +20,30 @@
     return lax.ppermute(block, axis, route)
 
 
-def tap_toeplitz(taps_ref, g, length, upper):
-    taps = jnp.broadcast_to(taps_ref[g : g + 1, :].astype(F32), (length, length))
-    rolled = pltpu.roll(taps, 0, 1, stride=1, stride_axis=0)
-    if upper:
-        return jnp.where(tap_mask(length), rolled, 0.0).astype(BF16)
-    return jnp.where(tap_mask(length), 0.0, rolled).astype(BF16)
-
-
 def tap_mask(length):
     row = lax.broadcasted_iota(jnp.int32, (length, length), 0)
     col = lax.broadcasted_iota(jnp.int32, (length, length), 1)
     return col >= row
 
 
-def current_kernel(x_ref, km_ref, taps_ref, conv_ref):
+def current_kernel(x_ref, km_ref, taps_ref, conv_ref, t_rim_ref):
     rows, length = x_ref.shape
     groups = taps_ref.shape[0]
     per_group = rows // groups
+    upper = tap_mask(length)
     for g in range(groups):
         lo, hi = g * per_group, (g + 1) * per_group
+        taps = jnp.broadcast_to(taps_ref[g : g + 1, :].astype(F32), (length, length))
+        rolled = pltpu.roll(taps, 0, 1, stride=1, stride_axis=0)
+        t_cur = jnp.where(upper, rolled, 0.0).astype(BF16)
+        t_rim_ref[g * length : (g + 1) * length, :] = jnp.where(upper, 0.0, rolled).astype(BF16)
         vm = (km_ref[lo:hi, :].astype(F32) * x_ref[lo:hi, :].astype(F32)).astype(BF16)
-        conv_ref[lo:hi, :] = jnp.dot(vm, tap_toeplitz(taps_ref, g, length, True), preferred_element_type=F32)
-
-
-def rim_kernel(conv_ref, x_ref, gm_ref, rim_ref, taps_ref, am_ref, ss_ref):
+        conv_ref[lo:hi, :] = jnp.dot(vm, t_cur, preferred_element_type=F32)
+
+
+def rim_kernel(conv_ref, x_ref, gm_ref, rim_ref, t_rim_ref, am_ref, ss_ref):
     rows, length = x_ref.shape
-    groups = taps_ref.shape[0]
+    groups = t_rim_ref.shape[0] // length
     per_group = rows // groups
 
     @pl.when(pl.program_id(0) == 0)
@@ -57,7 +54,7 @@
     for g in range(groups):
         lo, hi = g * per_group, (g + 1) * per_group
         conv = conv_ref[lo:hi, :] + jnp.dot(
-            rim_ref[lo:hi, :], tap_toeplitz(taps_ref, g, length, False), preferred_element_type=F32
+            rim_ref[lo:hi, :], t_rim_ref[g * length : (g + 1) * length, :], preferred_element_type=F32
         )
         am = x_ref[lo:hi, :].astype(F32) + gm_ref[lo:hi, :].astype(F32) * conv
         am_ref[lo:hi, :] = am
@@ -67,29 +64,33 @@
 
 def medium_call(inputs, gate_medium, key_medium, rim, taps):
     channels, length = inputs.shape
-    per_group = channels // taps.shape[0]
+    filters = taps.shape[0]
+    per_group = channels // filters
     block = 256
     tap_block = block // per_group
     big = pl.BlockSpec((block, length), lambda b: (b, 0))
-    tap_spec = pl.BlockSpec((tap_block, length), lambda b: (b, 0))
-    conv = pl.pallas_call(
+    t_spec = pl.BlockSpec((tap_block * length, length), lambda b: (b, 0))
+    conv, t_rim = pl.pallas_call(
         current_kernel,
         grid=(channels // block,),
-        in_specs=[big, big, tap_spec],
-        out_specs=big,
-        out_shape=jax.ShapeDtypeStruct((channels, length), F32),
+        in_specs=[big, big, pl.BlockSpec((tap_block, length), lambda b: (b, 0))],
+        out_specs=[big, t_spec],
+        out_shape=[
+            jax.ShapeDtypeStruct((channels, length), F32),
+            jax.ShapeDtypeStruct((filters * length, length), BF16),
+        ],
     )(inputs, key_medium, taps)
     return pl.pallas_call(
         rim_kernel,
         grid=(channels // block,),
-        in_specs=[big, big, big, big, tap_spec],
+        in_specs=[big, big, big, big, t_spec],
         out_specs=[big, pl.BlockSpec((1, length), lambda b: (0, 0))],
         out_shape=[
             jax.ShapeDtypeStruct((channels, length), F32),
             jax.ShapeDtypeStruct((1, length), F32),
         ],
         compiler_params=pltpu.CompilerParams(dimension_semantics=("arbitrary",)),
-    )(conv, inputs, gate_medium, rim, taps)
+    )(conv, inputs, gate_medium, rim, t_rim)
 
 
 def load_values(am_ref, kl_ref, g_ref, r_ref, vt_ref):

time: 109 us -> 110 us (level)
  Pallas kernels: 39.9 us -> 41.5 us
    pallas_call x1, Pallas kernels: 12.3 us -> 13.5 us  [medium_call(): pl.pallas_call(rim_kernel, grid=(channels // block,), in_specs=[big, big,...]
where the time goes in v6:
time: 110 us; the launch traced here: 108 us
  waiting for transfers between devices  44.6 us (41%)
  Pallas kernels  41.5 us (38%)
  starting transfers between devices  10.5 us (10%)
  local copies, waits for them, and re-layouts  4.69 us (4%)
  other arithmetic  4.39 us (4%)
  blocking collectives  2.57 us (2%)
    ppermute x5, waiting for transfers between devices, shifted(): return lax.ppermute(block, axis, route)  44.6 us
    pallas_call x1, Pallas kernels, medium_call(): pl.pallas_call(rim_kernel, grid=(channels // block,), in_specs=[big, big,...  13.5 us
    pallas_call x1, Pallas kernels, medium_call(): pl.pallas_call(current_kernel, grid=(channels // block,), in_specs=[big,...  12 us
    ppermute x5, starting transfers between devices, shifted(): return lax.ppermute(block, axis, route)  10.5 us
    pallas_call x1, Pallas kernels, output_call(): pl.pallas_call(output_kernel, grid=(channels // TILE,), in_specs=[big, bi...  9.78 us
    pallas_call x1, Pallas kernels, final_state_call(): pl.pallas_call(final_state_kernel, grid=(channels // TILE,), in_specs=[bi...  6.31 us
    unnamed x11, local copies, waits for them, and re-layouts  2.67 us
    psum x1, blocking collectives, on_device(): totals = lax.psum(partial, 'tensor')  2.57 us
  transfers between devices with their start and end apart: 5, of which 5 were waited for; matrix products, arithmetic and copies ran while one was open for 4% of the time, Pallas kernels for 11%

profile of v6, /device:TPU:24, one launch (start us, length us, event | category | flops | bytes accessed | tf_op | source)
XLA Modules:
  0.0 108.4 jit_solution(3430626474008000814)
XLA Ops:
  0.0 0.0 copy-start.2
  0.0 1.8 %multiply_convert_fusion = bf16[4096,128]{1,0:T(8,128)(2,1)S(1)} fusion(bf16[4096,128]{1,0:T(8,128)(2,1)} %x_ref.3, bf16[4096,128]{1,0:T(8,128)(2,1)} %km_ref.1), kind=kLoop, calls=%fused_computation | loop fusion | flops 2097152 | bytes 3145728 | tf_op jit(solution)/shard_map/convert_element_type | solution.py:199
  1.8 0.0 copy-start.1
  1.8 3.5 %collective-permute-start = (bf16[4096,128]{1,0:T(8,128)(2,1)S(1)}, bf16[4096,128]{1,0:T(8,128)(2,1)S(1)}, u32[]{:S(2)}, u32[]{:S(2)}) collective-permute-start(bf16[4096,128]{1,0:T(8,128)(2,1)S(1)} %multiply_convert_fusion), channel_id=1, source_target_pairs={{0,2},{2,4},{4,6},{6,8},{8,10},{10,12},{12,14},{1,3},{3,5},{5,7},{... | collective-permute-start | bytes 3145736 | tf_op jit(solution)/shard_map/ppermute | solution.py:20
  5.4 12.0 %shard_map.91 = (f32[4096,128]{1,0:T(8,128)}, bf16[32768,128]{1,0:T(8,128)(2,1)}) custom-call(bf16[4096,128]{1,0:T(8,128)(2,1)} %x_ref.3, bf16[4096,128]{1,0:T(8,128)(2,1)} %km_ref.1, bf16[256,128]{1,0:T(8,128)(2,1)} %taps_ref.1), custom_call_target="tpu_custom_call" | custom-call | tf_op jit(solution)/shard_map/pallas_call | solution.py:73
  17.4 0.0 copy-done.2
  17.4 2.0 %copy.11.g_ref = f32[4096,1]{1,0:T(8,128)} copy(f32[4096,1]{0,1:T(1,128)S(1)} %bitcast.32) | data formatting | bytes 32768 | tf_op jit(solution)/shard_map/broadcast_in_dim | solution.py:204
  19.4 0.0 copy-done.1
  19.4 1.1 %exponential_bitcast_fusion = (f32[2,8,32,128]{3,1,2,0:T(8,128)S(1)}, f32[2,8,32,128]{3,1,2,0:T(8,128)S(1)}, f32[2,8,32,128]{3,1,2,0:T(8,128)S(1)}, f32[2,8,32,128]{3,1,2,0:T(8,128)S(1)}, f32[2,8,32,128]{3,1,2,0:T(8,128)S(1)}) fusion(f32[4096,16]{0,1:T(8,128)S(1)} %copy-done.1, f32[4096,16]{0,1:T(8,128)} %param.16), kind=kLoop, calls=%fused_computation.2 | loop fusion | flops 393216 | bytes 1835008
  20.5 0.8 copy.12
  21.3 8.4 %collective-permute-done.rim_ref = bf16[4096,128]{1,0:T(8,128)(2,1)S(1)} collective-permute-done((bf16[4096,128]{1,0:T(8,128)(2,1)S(1)}, bf16[4096,128]{1,0:T(8,128)(2,1)S(1)}, u32[]{:S(2)}, u32[]{:S(2)}) %collective-permute-start) | collective-permute-done | bytes 1048608 | tf_op jit(solution)/shard_map/ppermute | solution.py:20
  29.7 0.0 copy-start
  29.7 1.0 copy-done
  30.6 13.5 %shard_map.92 = (f32[4096,128]{1,0:T(8,128)}, f32[1,128]{1,0:T(1,128)}) custom-call(f32[4096,128]{1,0:T(8,128)} %get-tuple-element.9.conv_ref, bf16[4096,128]{1,0:T(8,128)(2,1)} %x_ref.3, bf16[4096,128]{1,0:T(8,128)(2,1)} %gm_ref.1, bf16[4096,128]{1,0:T(8,128)(2,1)} %copy-done, bf16[32768,128]{1,0:T(8,128)(2,1)} %get-tuple-element.10.t_rim_ref), custom_call_target="tpu_custom_call" | custom-call | tf_op jit(solution)/shard_map/pallas_call | solution.py:83
  44.1 2.6 %psum.7 = f32[1,128]{1,0:T(1,128)S(1)} all-reduce(f32[1,128]{1,0:T(1,128)} %get-tuple-element.12), channel_id=1, replica_groups=mesh['groups'=2,'context'=8,'tensor'=2] {'tensor'}, use_global_device_ids=true, to_apply=%region_0.0 | all-reduce | flops 128 | bytes 1024 | tf_op jit(solution)/shard_map/psum | solution.py:202
  46.7 0.5 add_rsqrt_fusion.r_ref
  47.2 6.3 %shard_map.93 = f32[16,4,8,128]{3,2,1,0:T(8,128)} custom-call(f32[4096,128]{1,0:T(8,128)} %get-tuple-element.11.am_ref, bf16[4096,128]{1,0:T(8,128)(2,1)} %kl_ref.3, f32[4096,1]{1,0:T(8,128)} %copy.11.g_ref, f32[1,128]{1,0:T(1,128)} %add_rsqrt_fusion.r_ref, f32[16,4,8,128]{3,2,1,0:T(8,128)} %bitcast.26), custom_call_target="tpu_custom_call" | custom-call | tf_op jit(solution)/shard_map/pallas_call | solution.py:155
  53.5 2.5 %collective-permute-start.1 = (f32[16,4,8,128]{3,2,1,0:T(8,128)}, f32[16,4,8,128]{3,2,1,0:T(8,128)S(1)}, u32[]{:S(2)}, u32[]{:S(2)}) collective-permute-start(f32[16,4,8,128]{3,2,1,0:T(8,128)} %shard_map.93), channel_id=1, source_target_pairs={{0,2},{2,4},{4,6},{6,8},{8,10},{10,12},{12,14},{1,3},{3,5},{5,7},{... | collective-permute-start | bytes 786440 | tf_op jit(solution)/shard_map/ppermute | solution.py:20
  56.0 8.9 %collective-permute-done.1 = f32[16,4,8,128]{3,2,1,0:T(8,128)S(1)} collective-permute-done((f32[16,4,8,128]{3,2,1,0:T(8,128)}, f32[16,4,8,128]{3,2,1,0:T(8,128)S(1)}, u32[]{:S(2)}, u32[]{:S(2)}) %collective-permute-start.1) | collective-permute-done | bytes 262176 | tf_op jit(solution)/shard_map/ppermute | solution.py:20
  64.9 1.9 %collective-permute-start.2 = (f32[16,4,8,128]{3,2,1,0:T(8,128)S(1)}, f32[16,4,8,128]{3,2,1,0:T(8,128)S(1)}, u32[]{:S(2)}, u32[]{:S(2)}) collective-permute-start(f32[16,4,8,128]{3,2,1,0:T(8,128)S(1)} %collective-permute-done.1), channel_id=1, source_target_pairs={{0,2},{2,4},{4,6},{6,8},{8,10},{10,12},{12,14},{1,3},{3,5},{5,7},{... | collective-permute-start | bytes 786440 | tf_op jit(solution)/shard_map/ppermute | solution.py:20
  66.8 0.1 copy.14
  66.9 8.4 %collective-permute-done.2 = f32[16,4,8,128]{3,2,1,0:T(8,128)S(1)} collective-permute-done((f32[16,4,8,128]{3,2,1,0:T(8,128)S(1)}, f32[16,4,8,128]{3,2,1,0:T(8,128)S(1)}, u32[]{:S(2)}, u32[]{:S(2)}) %collective-permute-start.2) | collective-permute-done | bytes 262176 | tf_op jit(solution)/shard_map/ppermute | solution.py:20
  75.2 0.1 multiply_add_fusion.2
  75.3 1.3 %collective-permute-start.3 = (f32[16,4,8,128]{3,2,1,0:T(8,128)S(1)}, f32[16,4,8,128]{3,2,1,0:T(8,128)S(1)}, u32[]{:S(2)}, u32[]{:S(2)}) collective-permute-start(f32[16,4,8,128]{3,2,1,0:T(8,128)S(1)} %multiply_add_fusion.2), channel_id=1, source_target_pairs={{0,4},{2,6},{4,8},{6,10},{8,12},{10,14},{1,5},{3,7},{5,9},{7,11},{... | collective-permute-start | bytes 786440 | tf_op jit(solution)/shard_map/ppermute | solution.py:20
  76.6 0.1 copy.15
  76.6 7.2 %collective-permute-done.3 = f32[16,4,8,128]{3,2,1,0:T(8,128)S(1)} collective-permute-done((f32[16,4,8,128]{3,2,1,0:T(8,128)S(1)}, f32[16,4,8,128]{3,2,1,0:T(8,128)S(1)}, u32[]{:S(2)}, u32[]{:S(2)}) %collective-permute-start.3) | collective-permute-done | bytes 262176 | tf_op jit(solution)/shard_map/ppermute | solution.py:20
  83.8 0.1 multiply_add_fusion.1
  83.9 1.3 %collective-permute-start.4 = (f32[16,4,8,128]{3,2,1,0:T(8,128)S(1)}, f32[16,4,8,128]{3,2,1,0:T(8,128)S(1)}, u32[]{:S(2)}, u32[]{:S(2)}) collective-permute-start(f32[16,4,8,128]{3,2,1,0:T(8,128)S(1)} %multiply_add_fusion.1), channel_id=1, source_target_pairs={{0,8},{2,10},{4,12},{6,14},{1,9},{3,11},{5,13},{7,15},{16,24},{18,... | collective-permute-start | bytes 786440 | tf_op jit(solution)/shard_map/ppermute | solution.py:20
  85.2 0.8 copy.13
  85.9 0.1 copy.16
  86.0 11.9 %collective-permute-done.4 = f32[16,4,8,128]{3,2,1,0:T(8,128)S(1)} collective-permute-done((f32[16,4,8,128]{3,2,1,0:T(8,128)S(1)}, f32[16,4,8,128]{3,2,1,0:T(8,128)S(1)}, u32[]{:S(2)}, u32[]{:S(2)}) %collective-permute-start.4) | collective-permute-done | bytes 262176 | tf_op jit(solution)/shard_map/ppermute | solution.py:20
  97.9 0.8 multiply_add_fusion.h0_ref
  98.6 9.8 %shard_map.94 = bf16[4096,128]{1,0:T(8,128)(2,1)} custom-call(f32[4096,128]{1,0:T(8,128)} %get-tuple-element.11.am_ref, bf16[4096,128]{1,0:T(8,128)(2,1)} %kl_ref.3, bf16[4096,128]{1,0:T(8,128)(2,1)} %gl_ref.1, f32[4096,1]{1,0:T(8,128)} %copy.11.g_ref, f32[1,128]{1,0:T(1,128)} %add_rsqrt_fusion.r_ref, f32[16,4,8,128]{3,2,1,0:T(8,128)} %bitcast.27, ...), custom_call_target="tpu_custom_call" | custom-call | tf_op jit(solution)/shard_map/pallas_call | solution.py:169
Async XLA Ops:
  0.0 17.4 %copy-start.2 = (f32[4096]{0:T(1024)S(1)}, f32[4096]{0:T(1024)}, u32[]{:S(2)}) copy-start(f32[4096]{0:T(1024)} %param.17) | copy-start | bytes 49156
  1.8 17.6 %copy-start.1 = (f32[4096,16]{0,1:T(8,128)S(1)}, f32[4096,16]{0,1:T(8,128)}, u32[]{:S(2)}) copy-start(f32[4096,16]{0,1:T(8,128)} %param.15) | copy-start | bytes 786436
  1.8 27.8 %collective-permute-start = (bf16[4096,128]{1,0:T(8,128)(2,1)S(1)}, bf16[4096,128]{1,0:T(8,128)(2,1)S(1)}, u32[]{:S(2)}, u32[]{:S(2)}) collective-permute-start(bf16[4096,128]{1,0:T(8,128)(2,1)S(1)} %multiply_convert_fusion), channel_id=1, source_target_pairs={{0,2},{2,4},{4,6},{6,8},{8,10},{10,12},{12,14},{1,3},{3,5},{5,7},{... | collective-permute-start | bytes 3145736 | tf_op jit(solution)/shard_map/ppermute | solution.py:20
  29.7 1.0 copy-start
  53.5 11.4 %collective-permute-start.1 = (f32[16,4,8,128]{3,2,1,0:T(8,128)}, f32[16,4,8,128]{3,2,1,0:T(8,128)S(1)}, u32[]{:S(2)}, u32[]{:S(2)}) collective-permute-start(f32[16,4,8,128]{3,2,1,0:T(8,128)} %shard_map.93), channel_id=1, source_target_pairs={{0,2},{2,4},{4,6},{6,8},{8,10},{10,12},{12,14},{1,3},{3,5},{5,7},{... | collective-permute-start | bytes 786440 | tf_op jit(solution)/shard_map/ppermute | solution.py:20
  64.9 10.3 %collective-permute-start.2 = (f32[16,4,8,128]{3,2,1,0:T(8,128)S(1)}, f32[16,4,8,128]{3,2,1,0:T(8,128)S(1)}, u32[]{:S(2)}, u32[]{:S(2)}) collective-permute-start(f32[16,4,8,128]{3,2,1,0:T(8,128)S(1)} %collective-permute-done.1), channel_id=1, source_target_pairs={{0,2},{2,4},{4,6},{6,8},{8,10},{10,12},{12,14},{1,3},{3,5},{5,7},{... | collective-permute-start | bytes 786440 | tf_op jit(solution)/shard_map/ppermute | solution.py:20
  75.3 8.5 %collective-permute-start.3 = (f32[16,4,8,128]{3,2,1,0:T(8,128)S(1)}, f32[16,4,8,128]{3,2,1,0:T(8,128)S(1)}, u32[]{:S(2)}, u32[]{:S(2)}) collective-permute-start(f32[16,4,8,128]{3,2,1,0:T(8,128)S(1)} %multiply_add_fusion.2), channel_id=1, source_target_pairs={{0,4},{2,6},{4,8},{6,10},{8,12},{10,14},{1,5},{3,7},{5,9},{7,11},{... | collective-permute-start | bytes 786440 | tf_op jit(solution)/shard_map/ppermute | solution.py:20
  83.9 14.0 %collective-permute-start.4 = (f32[16,4,8,128]{3,2,1,0:T(8,128)S(1)}, f32[16,4,8,128]{3,2,1,0:T(8,128)S(1)}, u32[]{:S(2)}, u32[]{:S(2)}) collective-permute-start(f32[16,4,8,128]{3,2,1,0:T(8,128)S(1)} %multiply_add_fusion.1), channel_id=1, source_target_pairs={{0,8},{2,10},{4,12},{6,14},{1,9},{3,11},{5,13},{7,15},{16,24},{18,... | collective-permute-start | bytes 786440 | tf_op jit(solution)/shard_map/ppermute | solution.py:20

commit v7 on v4

--- a/solution.py
+++ b/solution.py
@@ -182,11 +182,11 @@
     w = to_tiles(residues * jnp.sqrt(2.0 * log_decay))
     finals = final_state_call(after_medium, key_long, gain, r, lam)
 
-    carried = shifted(finals, "context", 1)
+    carried = shifted(finals.astype(BF16), "context", 1).astype(F32)
     distance = 1
     while distance < lax.axis_size("context"):
         decay = jnp.exp(-(length * distance) * a_t)
-        carried = carried + decay * shifted(carried, "context", distance)
+        carried = carried + decay * shifted(carried.astype(BF16), "context", distance).astype(F32)
         distance *= 2
 
     return output_call(after_medium, key_long, gate_long, gain, r, lam, w, carried)

time: 108 us -> 97 us (0.90)
  waiting for transfers between devices: 57.6 us -> 45.4 us
    ppermute x5, waiting for transfers between devices: 57.6 us -> 45.4 us  [shifted(): return lax.ppermute(block, axis, route)]
    convert_element_type x0 -> x3, other arithmetic: none -> 1.1 us  [the longest x1 0.97 us: on_device(): carried = shifted(finals.astype(BF16), 'context', 1).astype(F32)]
where the time goes in v7:
time: 97 us; the launch traced here: 95.8 us
  waiting for transfers between devices  45.4 us (47%)
  Pallas kernels  28.2 us (29%)
  starting transfers between devices  10.4 us (11%)
  local copies, waits for them, and re-layouts  4.65 us (5%)
  other arithmetic  4.49 us (5%)
  blocking collectives  2.57 us (3%)
    ppermute x5, waiting for transfers between devices, shifted(): return lax.ppermute(block, axis, route)  45.4 us
    pallas_call x1, Pallas kernels, medium_call(): pl.pallas_call(medium_kernel, grid=(channels // block,), in_specs=[big, b...  12.1 us
    ppermute x5, starting transfers between devices, shifted(): return lax.ppermute(block, axis, route)  10.4 us
    pallas_call x1, Pallas kernels, output_call(): pl.pallas_call(output_kernel, grid=(channels // TILE,), in_specs=[big, bi...  9.82 us
    pallas_call x1, Pallas kernels, final_state_call(): pl.pallas_call(final_state_kernel, grid=(channels // TILE,), in_specs=[bi...  6.34 us
    unnamed x13, local copies, waits for them, and re-layouts  2.66 us
    psum x1, blocking collectives, on_device(): totals = lax.psum(partial, 'tensor')  2.57 us
    broadcast_in_dim x1, local copies, waits for them, and re-layouts, on_device(): gain = norm_gain[:, None]  1.99 us
  transfers between devices with their start and end apart: 5, of which 5 were waited for; matrix products, arithmetic and copies ran while one was open for 4% of the time, Pallas kernels for 0%

profile of v7, /device:TPU:24, one launch (start us, length us, event | category | flops | bytes accessed | tf_op | source)
XLA Modules:
  0.0 95.8 jit_solution(14624194455117309306)
XLA Ops:
  0.0 0.0 copy-start.2
  0.0 0.0 copy-start.1
  0.0 0.0 copy-start.3
  0.0 1.9 %multiply_convert_fusion = bf16[4096,128]{1,0:T(8,128)(2,1)S(1)} fusion(bf16[4096,128]{1,0:T(8,128)(2,1)} %x_ref.1, bf16[4096,128]{1,0:T(8,128)(2,1)} %km_ref.1), kind=kLoop, calls=%fused_computation | loop fusion | flops 2097152 | bytes 3145728 | tf_op jit(solution)/shard_map/convert_element_type | solution.py:174
  1.9 3.4 %collective-permute-start = (bf16[4096,128]{1,0:T(8,128)(2,1)S(1)}, bf16[4096,128]{1,0:T(8,128)(2,1)S(1)}, u32[]{:S(2)}, u32[]{:S(2)}) collective-permute-start(bf16[4096,128]{1,0:T(8,128)(2,1)S(1)} %multiply_convert_fusion), channel_id=1, source_target_pairs={{0,2},{2,4},{4,6},{6,8},{8,10},{10,12},{12,14},{1,3},{3,5},{5,7},{... | collective-permute-start | bytes 3145736 | tf_op jit(solution)/shard_map/ppermute | solution.py:20
  5.3 0.0 copy-done.2
  5.3 0.0 copy-done.1
  5.3 0.2 exponential_bitcast_fusion
  5.5 0.7 copy.12
  6.2 0.0 copy-done.3
  6.3 2.0 %copy.11.g_ref = f32[4096,1]{1,0:T(8,128)} copy(f32[4096,1]{0,1:T(1,128)S(1)} %bitcast.33) | data formatting | bytes 32768 | tf_op jit(solution)/shard_map/broadcast_in_dim | solution.py:179
  8.2 21.3 %collective-permute-done.rim_ref = bf16[4096,128]{1,0:T(8,128)(2,1)S(1)} collective-permute-done((bf16[4096,128]{1,0:T(8,128)(2,1)S(1)}, bf16[4096,128]{1,0:T(8,128)(2,1)S(1)}, u32[]{:S(2)}, u32[]{:S(2)}) %collective-permute-start) | collective-permute-done | bytes 1048608 | tf_op jit(solution)/shard_map/ppermute | solution.py:20
  29.6 0.0 copy-start
  29.6 1.0 %copy-done = bf16[4096,128]{1,0:T(8,128)(2,1)} copy-done((bf16[4096,128]{1,0:T(8,128)(2,1)}, bf16[4096,128]{1,0:T(8,128)(2,1)S(1)}, u32[]{:S(2)}) %copy-start) | copy-done | bytes 1048600
  30.5 12.1 %shard_map.91 = (f32[4096,128]{1,0:T(8,128)}, f32[1,128]{1,0:T(1,128)}) custom-call(bf16[4096,128]{1,0:T(8,128)(2,1)} %x_ref.1, bf16[4096,128]{1,0:T(8,128)(2,1)} %gm_ref.1, bf16[4096,128]{1,0:T(8,128)(2,1)} %km_ref.1, bf16[4096,128]{1,0:T(8,128)(2,1)} %copy-done, bf16[256,128]{1,0:T(8,128)(2,1)} %taps_ref.1), custom_call_target="tpu_custom_call" | custom-call | tf_op jit(solution)/shard_map/pallas_call | solution.py:58
  42.6 2.6 %psum.7 = f32[1,128]{1,0:T(1,128)S(1)} all-reduce(f32[1,128]{1,0:T(1,128)} %get-tuple-element.8), channel_id=1, replica_groups=mesh['groups'=2,'context'=8,'tensor'=2] {'tensor'}, use_global_device_ids=true, to_apply=%region_0.0 | all-reduce | flops 128 | bytes 1024 | tf_op jit(solution)/shard_map/psum | solution.py:177
  45.2 0.6 add_rsqrt_fusion.r_ref
  45.8 6.3 %shard_map.92 = f32[16,4,8,128]{3,2,1,0:T(8,128)} custom-call(f32[4096,128]{1,0:T(8,128)} %get-tuple-element.7.am_ref, bf16[4096,128]{1,0:T(8,128)(2,1)} %kl_ref.3, f32[4096,1]{1,0:T(8,128)} %copy.11.g_ref, f32[1,128]{1,0:T(1,128)} %add_rsqrt_fusion.r_ref, f32[16,4,8,128]{3,2,1,0:T(8,128)} %bitcast.26), custom_call_target="tpu_custom_call" | custom-call | tf_op jit(solution)/shard_map/pallas_call | solution.py:130
  52.1 1.0 %convert_element_type.34 = bf16[16,4,8,128]{3,2,1,0:T(8,128)(2,1)S(1)} convert(f32[16,4,8,128]{3,2,1,0:T(8,128)} %shard_map.92) | non-fusion elementwise | flops 65536 | bytes 393216 | tf_op jit(solution)/shard_map/convert_element_type | solution.py:185
  53.1 2.5 %collective-permute-start.1 = (bf16[16,4,8,128]{3,2,1,0:T(8,128)(2,1)S(1)}, bf16[16,4,8,128]{3,2,1,0:T(8,128)(2,1)S(1)}, u32[]{:S(2)}, u32[]{:S(2)}) collective-permute-start(bf16[16,4,8,128]{3,2,1,0:T(8,128)(2,1)S(1)} %convert_element_type.34), channel_id=1, source_target_pairs={{0,2},{2,4},{4,6},{6,8},{8,10},{10,12},{12,14},{1,3},{3,5},{5,7},{... | collective-permute-start | bytes 393224 | tf_op jit(solution)/shard_map/ppermute | solution.py:20
  55.6 5.9 %collective-permute-done.1 = bf16[16,4,8,128]{3,2,1,0:T(8,128)(2,1)S(1)} collective-permute-done((bf16[16,4,8,128]{3,2,1,0:T(8,128)(2,1)S(1)}, bf16[16,4,8,128]{3,2,1,0:T(8,128)(2,1)S(1)}, u32[]{:S(2)}, u32[]{:S(2)}) %collective-permute-start.1) | collective-permute-done | bytes 131104 | tf_op jit(solution)/shard_map/ppermute | solution.py:20
  61.5 1.9 %collective-permute-start.2 = (bf16[16,4,8,128]{3,2,1,0:T(8,128)(2,1)S(1)}, bf16[16,4,8,128]{3,2,1,0:T(8,128)(2,1)S(1)}, u32[]{:S(2)}, u32[]{:S(2)}) collective-permute-start(bf16[16,4,8,128]{3,2,1,0:T(8,128)(2,1)S(1)} %collective-permute-done.1), channel_id=1, source_target_pairs={{0,2},{2,4},{4,6},{6,8},{8,10},{10,12},{12,14},{1,3},{3,5},{5,7},{... | collective-permute-start | bytes 393224 | tf_op jit(solution)/shard_map/ppermute | solution.py:20
  63.4 0.1 copy.14
  63.4 5.8 %collective-permute-done.2 = bf16[16,4,8,128]{3,2,1,0:T(8,128)(2,1)S(1)} collective-permute-done((bf16[16,4,8,128]{3,2,1,0:T(8,128)(2,1)S(1)}, bf16[16,4,8,128]{3,2,1,0:T(8,128)(2,1)S(1)}, u32[]{:S(2)}, u32[]{:S(2)}) %collective-permute-start.2) | collective-permute-done | bytes 131104 | tf_op jit(solution)/shard_map/ppermute | solution.py:20
  69.3 1.3 %collective-permute-start.3 = (bf16[16,4,8,128]{3,2,1,0:T(8,128)(2,1)S(1)}, bf16[16,4,8,128]{3,2,1,0:T(8,128)(2,1)S(1)}, u32[]{:S(2)}, u32[]{:S(2)}) collective-permute-start(bf16[16,4,8,128]{3,2,1,0:T(8,128)(2,1)S(1)} %fusion), channel_id=1, source_target_pairs={{0,4},{2,6},{4,8},{6,10},{8,12},{10,14},{1,5},{3,7},{5,9},{7,11},{... | collective-permute-start | bytes 393224 | tf_op jit(solution)/shard_map/ppermute | solution.py:20
  70.6 0.1 copy.15
  70.6 5.5 %collective-permute-done.3 = bf16[16,4,8,128]{3,2,1,0:T(8,128)(2,1)S(1)} collective-permute-done((bf16[16,4,8,128]{3,2,1,0:T(8,128)(2,1)S(1)}, bf16[16,4,8,128]{3,2,1,0:T(8,128)(2,1)S(1)}, u32[]{:S(2)}, u32[]{:S(2)}) %collective-permute-start.3) | collective-permute-done | bytes 131104 | tf_op jit(solution)/shard_map/ppermute | solution.py:20
  76.1 0.1 fusion.1
  76.2 1.3 %collective-permute-start.4 = (bf16[16,4,8,128]{3,2,1,0:T(8,128)(2,1)S(1)}, bf16[16,4,8,128]{3,2,1,0:T(8,128)(2,1)S(1)}, u32[]{:S(2)}, u32[]{:S(2)}) collective-permute-start(bf16[16,4,8,128]{3,2,1,0:T(8,128)(2,1)S(1)} %get-tuple-element.9), channel_id=1, source_target_pairs={{0,8},{2,10},{4,12},{6,14},{1,9},{3,11},{5,13},{7,15},{16,24},{18,... | collective-permute-start | bytes 393224 | tf_op jit(solution)/shard_map/ppermute | solution.py:20
  77.5 0.1 copy.16
  77.6 0.8 copy.13
  78.3 6.9 %collective-permute-done.4 = bf16[16,4,8,128]{3,2,1,0:T(8,128)(2,1)S(1)} collective-permute-done((bf16[16,4,8,128]{3,2,1,0:T(8,128)(2,1)S(1)}, bf16[16,4,8,128]{3,2,1,0:T(8,128)(2,1)S(1)}, u32[]{:S(2)}, u32[]{:S(2)}) %collective-permute-start.4) | collective-permute-done | bytes 131104 | tf_op jit(solution)/shard_map/ppermute | solution.py:20
  85.3 0.8 multiply_add_fusion.h0_ref
  86.0 9.8 %shard_map.93 = bf16[4096,128]{1,0:T(8,128)(2,1)} custom-call(f32[4096,128]{1,0:T(8,128)} %get-tuple-element.7.am_ref, bf16[4096,128]{1,0:T(8,128)(2,1)} %kl_ref.3, bf16[4096,128]{1,0:T(8,128)(2,1)} %gl_ref.1, f32[4096,1]{1,0:T(8,128)} %copy.11.g_ref, f32[1,128]{1,0:T(1,128)} %add_rsqrt_fusion.r_ref, f32[16,4,8,128]{3,2,1,0:T(8,128)} %bitcast.27, ...), custom_call_target="tpu_custom_call" | custom-call | tf_op jit(solution)/shard_map/pallas_call | solution.py:144
  (1 shorter events, 0.0 us)
Async XLA Ops:
  0.0 5.3 %copy-start.2 = (f32[4096,16]{0,1:T(8,128)S(1)}, f32[4096,16]{0,1:T(8,128)}, u32[]{:S(2)}) copy-start(f32[4096,16]{0,1:T(8,128)} %param.16) | copy-start | bytes 786436
  0.0 5.3 %copy-start.1 = (f32[4096,16]{0,1:T(8,128)S(1)}, f32[4096,16]{0,1:T(8,128)}, u32[]{:S(2)}) copy-start(f32[4096,16]{0,1:T(8,128)} %param.15) | copy-start | bytes 786436
  0.0 6.2 %copy-start.3 = (f32[4096]{0:T(1024)S(1)}, f32[4096]{0:T(1024)}, u32[]{:S(2)}) copy-start(f32[4096]{0:T(1024)} %param.17) | copy-start | bytes 49156
  1.9 27.7 %collective-permute-start = (bf16[4096,128]{1,0:T(8,128)(2,1)S(1)}, bf16[4096,128]{1,0:T(8,128)(2,1)S(1)}, u32[]{:S(2)}, u32[]{:S(2)}) collective-permute-start(bf16[4096,128]{1,0:T(8,128)(2,1)S(1)} %multiply_convert_fusion), channel_id=1, source_target_pairs={{0,2},{2,4},{4,6},{6,8},{8,10},{10,12},{12,14},{1,3},{3,5},{5,7},{... | collective-permute-start | bytes 3145736 | tf_op jit(solution)/shard_map/ppermute | solution.py:20
  29.6 1.0 %copy-start = (bf16[4096,128]{1,0:T(8,128)(2,1)}, bf16[4096,128]{1,0:T(8,128)(2,1)S(1)}, u32[]{:S(2)}) copy-start(bf16[4096,128]{1,0:T(8,128)(2,1)S(1)} %collective-permute-done.rim_ref) | copy-start | bytes 3145732
  53.1 8.4 %collective-permute-start.1 = (bf16[16,4,8,128]{3,2,1,0:T(8,128)(2,1)S(1)}, bf16[16,4,8,128]{3,2,1,0:T(8,128)(2,1)S(1)}, u32[]{:S(2)}, u32[]{:S(2)}) collective-permute-start(bf16[16,4,8,128]{3,2,1,0:T(8,128)(2,1)S(1)} %convert_element_type.34), channel_id=1, source_target_pairs={{0,2},{2,4},{4,6},{6,8},{8,10},{10,12},{12,14},{1,3},{3,5},{5,7},{... | collective-permute-start | bytes 393224 | tf_op jit(solution)/shard_map/ppermute | solution.py:20
  61.5 7.7 %collective-permute-start.2 = (bf16[16,4,8,128]{3,2,1,0:T(8,128)(2,1)S(1)}, bf16[16,4,8,128]{3,2,1,0:T(8,128)(2,1)S(1)}, u32[]{:S(2)}, u32[]{:S(2)}) collective-permute-start(bf16[16,4,8,128]{3,2,1,0:T(8,128)(2,1)S(1)} %collective-permute-done.1), channel_id=1, source_target_pairs={{0,2},{2,4},{4,6},{6,8},{8,10},{10,12},{12,14},{1,3},{3,5},{5,7},{... | collective-permute-start | bytes 393224 | tf_op jit(solution)/shard_map/ppermute | solution.py:20
  69.3 6.9 %collective-permute-start.3 = (bf16[16,4,8,128]{3,2,1,0:T(8,128)(2,1)S(1)}, bf16[16,4,8,128]{3,2,1,0:T(8,128)(2,1)S(1)}, u32[]{:S(2)}, u32[]{:S(2)}) collective-permute-start(bf16[16,4,8,128]{3,2,1,0:T(8,128)(2,1)S(1)} %fusion), channel_id=1, source_target_pairs={{0,4},{2,6},{4,8},{6,10},{8,12},{10,14},{1,5},{3,7},{5,9},{7,11},{... | collective-permute-start | bytes 393224 | tf_op jit(solution)/shard_map/ppermute | solution.py:20
  76.2 9.1 %collective-permute-start.4 = (bf16[16,4,8,128]{3,2,1,0:T(8,128)(2,1)S(1)}, bf16[16,4,8,128]{3,2,1,0:T(8,128)(2,1)S(1)}, u32[]{:S(2)}, u32[]{:S(2)}) collective-permute-start(bf16[16,4,8,128]{3,2,1,0:T(8,128)(2,1)S(1)} %get-tuple-element.9), channel_id=1, source_target_pairs={{0,8},{2,10},{4,12},{6,14},{1,9},{3,11},{5,13},{7,15},{16,24},{18,... | collective-permute-start | bytes 393224 | tf_op jit(solution)/shard_map/ppermute | solution.py:20

commit v8 on v7

--- a/solution.py
+++ b/solution.py
@@ -182,8 +182,13 @@
     w = to_tiles(residues * jnp.sqrt(2.0 * log_decay))
     finals = final_state_call(after_medium, key_long, gain, r, lam)
 
-    carried = shifted(finals.astype(BF16), "context", 1).astype(F32)
+    sent = finals.astype(BF16)
+    carried = shifted(sent, "context", 1).astype(F32)
     distance = 1
+    if lax.axis_size("context") > 2:
+        decay = jnp.exp(-length * a_t)
+        carried = carried + decay * shifted(sent, "context", 2).astype(F32)
+        distance = 2
     while distance < lax.axis_size("context"):
         decay = jnp.exp(-(length * distance) * a_t)
         carried = carried + decay * shifted(carried.astype(BF16), "context", distance).astype(F32)

time: 97 us -> 91.8 us (0.946)
  waiting for transfers between devices: 45.4 us -> 40.5 us
    ppermute x5, waiting for transfers between devices: 45.4 us -> 40.5 us  [shifted(): return lax.ppermute(block, axis, route)]
where the time goes in v8:
time: 91.8 us; the launch traced here: 90.3 us
  waiting for transfers between devices  40.5 us (44%)
  Pallas kernels  28.2 us (31%)
  starting transfers between devices  9.78 us (11%)
  local copies, waits for them, and re-layouts  4.65 us (5%)
  other arithmetic  4.49 us (5%)
  blocking collectives  2.57 us (3%)
    ppermute x5, waiting for transfers between devices, shifted(): return lax.ppermute(block, axis, route)  40.5 us
    pallas_call x1, Pallas kernels, medium_call(): pl.pallas_call(medium_kernel, grid=(channels // block,), in_specs=[big, b...  12.1 us
    pallas_call x1, Pallas kernels, output_call(): pl.pallas_call(output_kernel, grid=(channels // TILE,), in_specs=[big, bi...  9.82 us
    ppermute x5, starting transfers between devices, shifted(): return lax.ppermute(block, axis, route)  9.78 us
    pallas_call x1, Pallas kernels, final_state_call(): pl.pallas_call(final_state_kernel, grid=(channels // TILE,), in_specs=[bi...  6.34 us
    unnamed x13, local copies, waits for them, and re-layouts  2.66 us
    psum x1, blocking collectives, on_device(): totals = lax.psum(partial, 'tensor')  2.57 us
    broadcast_in_dim x1, local copies, waits for them, and re-layouts, on_device(): gain = norm_gain[:, None]  1.99 us
  transfers between devices with their start and end apart: 5, of which 5 were waited for; matrix products, arithmetic and copies ran while one was open for 4% of the time, Pallas kernels for 0%

profile of v8, /device:TPU:24, one launch (start us, length us, event | category | flops | bytes accessed | tf_op | source)
XLA Modules:
  0.0 90.3 jit_solution(16647058563174253980)
XLA Ops:
  0.0 0.0 copy-start.2
  0.0 0.0 copy-start.1
  0.0 0.0 copy-start.3
  0.0 1.9 %multiply_convert_fusion = bf16[4096,128]{1,0:T(8,128)(2,1)S(1)} fusion(bf16[4096,128]{1,0:T(8,128)(2,1)} %x_ref.1, bf16[4096,128]{1,0:T(8,128)(2,1)} %km_ref.1), kind=kLoop, calls=%fused_computation | loop fusion | flops 2097152 | bytes 3145728 | tf_op jit(solution)/shard_map/convert_element_type | solution.py:174
  1.9 3.4 %collective-permute-start = (bf16[4096,128]{1,0:T(8,128)(2,1)S(1)}, bf16[4096,128]{1,0:T(8,128)(2,1)S(1)}, u32[]{:S(2)}, u32[]{:S(2)}) collective-permute-start(bf16[4096,128]{1,0:T(8,128)(2,1)S(1)} %multiply_convert_fusion), channel_id=1, source_target_pairs={{0,2},{2,4},{4,6},{6,8},{8,10},{10,12},{12,14},{1,3},{3,5},{5,7},{... | collective-permute-start | bytes 3145736 | tf_op jit(solution)/shard_map/ppermute | solution.py:20
  5.3 0.0 copy-done.2
  5.3 0.0 copy-done.1
  5.3 0.2 exponential_bitcast_fusion
  5.5 0.7 copy.12
  6.2 0.0 copy-done.3
  6.3 2.0 %copy.11.g_ref = f32[4096,1]{1,0:T(8,128)} copy(f32[4096,1]{0,1:T(1,128)S(1)} %bitcast.33) | data formatting | bytes 32768 | tf_op jit(solution)/shard_map/broadcast_in_dim | solution.py:179
  8.2 21.3 %collective-permute-done.rim_ref = bf16[4096,128]{1,0:T(8,128)(2,1)S(1)} collective-permute-done((bf16[4096,128]{1,0:T(8,128)(2,1)S(1)}, bf16[4096,128]{1,0:T(8,128)(2,1)S(1)}, u32[]{:S(2)}, u32[]{:S(2)}) %collective-permute-start) | collective-permute-done | bytes 1048608 | tf_op jit(solution)/shard_map/ppermute | solution.py:20
  29.6 0.0 copy-start
  29.6 1.0 %copy-done = bf16[4096,128]{1,0:T(8,128)(2,1)} copy-done((bf16[4096,128]{1,0:T(8,128)(2,1)}, bf16[4096,128]{1,0:T(8,128)(2,1)S(1)}, u32[]{:S(2)}) %copy-start) | copy-done | bytes 1048600
  30.5 12.1 %shard_map.91 = (f32[4096,128]{1,0:T(8,128)}, f32[1,128]{1,0:T(1,128)}) custom-call(bf16[4096,128]{1,0:T(8,128)(2,1)} %x_ref.1, bf16[4096,128]{1,0:T(8,128)(2,1)} %gm_ref.1, bf16[4096,128]{1,0:T(8,128)(2,1)} %km_ref.1, bf16[4096,128]{1,0:T(8,128)(2,1)} %copy-done, bf16[256,128]{1,0:T(8,128)(2,1)} %taps_ref.1), custom_call_target="tpu_custom_call" | custom-call | tf_op jit(solution)/shard_map/pallas_call | solution.py:58
  42.6 2.6 %psum.7 = f32[1,128]{1,0:T(1,128)S(1)} all-reduce(f32[1,128]{1,0:T(1,128)} %get-tuple-element.8), channel_id=1, replica_groups=mesh['groups'=2,'context'=8,'tensor'=2] {'tensor'}, use_global_device_ids=true, to_apply=%region_0.0 | all-reduce | flops 128 | bytes 1024 | tf_op jit(solution)/shard_map/psum | solution.py:177
  45.2 0.6 add_rsqrt_fusion.r_ref
  45.8 6.3 %shard_map.92 = f32[16,4,8,128]{3,2,1,0:T(8,128)} custom-call(f32[4096,128]{1,0:T(8,128)} %get-tuple-element.7.am_ref, bf16[4096,128]{1,0:T(8,128)(2,1)} %kl_ref.3, f32[4096,1]{1,0:T(8,128)} %copy.11.g_ref, f32[1,128]{1,0:T(1,128)} %add_rsqrt_fusion.r_ref, f32[16,4,8,128]{3,2,1,0:T(8,128)} %bitcast.26), custom_call_target="tpu_custom_call" | custom-call | tf_op jit(solution)/shard_map/pallas_call | solution.py:130
  52.1 1.0 %convert_element_type.33 = bf16[16,4,8,128]{3,2,1,0:T(8,128)(2,1)S(1)} convert(f32[16,4,8,128]{3,2,1,0:T(8,128)} %shard_map.92) | non-fusion elementwise | flops 65536 | bytes 393216 | tf_op jit(solution)/shard_map/convert_element_type | solution.py:185
  53.1 1.3 %collective-permute-start.2 = (bf16[16,4,8,128]{3,2,1,0:T(8,128)(2,1)S(1)}, bf16[16,4,8,128]{3,2,1,0:T(8,128)(2,1)S(1)}, u32[]{:S(2)}, u32[]{:S(2)}) collective-permute-start(bf16[16,4,8,128]{3,2,1,0:T(8,128)(2,1)S(1)} %convert_element_type.33), channel_id=1, source_target_pairs={{0,4},{2,6},{4,8},{6,10},{8,12},{10,14},{1,5},{3,7},{5,9},{7,11},{... | collective-permute-start | bytes 393224 | tf_op jit(solution)/shard_map/ppermute | solution.py:20
  54.4 2.5 %collective-permute-start.1 = (bf16[16,4,8,128]{3,2,1,0:T(8,128)(2,1)S(1)}, bf16[16,4,8,128]{3,2,1,0:T(8,128)(2,1)S(1)}, u32[]{:S(2)}, u32[]{:S(2)}) collective-permute-start(bf16[16,4,8,128]{3,2,1,0:T(8,128)(2,1)S(1)} %convert_element_type.33), channel_id=1, source_target_pairs={{0,2},{2,4},{4,6},{6,8},{8,10},{10,12},{12,14},{1,3},{3,5},{5,7},{... | collective-permute-start | bytes 393224 | tf_op jit(solution)/shard_map/ppermute | solution.py:20
  56.9 0.1 copy.14
  57.0 3.6 %collective-permute-done.2 = bf16[16,4,8,128]{3,2,1,0:T(8,128)(2,1)S(1)} collective-permute-done((bf16[16,4,8,128]{3,2,1,0:T(8,128)(2,1)S(1)}, bf16[16,4,8,128]{3,2,1,0:T(8,128)(2,1)S(1)}, u32[]{:S(2)}, u32[]{:S(2)}) %collective-permute-start.2) | collective-permute-done | bytes 131104 | tf_op jit(solution)/shard_map/ppermute | solution.py:20
  60.6 2.8 %collective-permute-done.1 = bf16[16,4,8,128]{3,2,1,0:T(8,128)(2,1)S(1)} collective-permute-done((bf16[16,4,8,128]{3,2,1,0:T(8,128)(2,1)S(1)}, bf16[16,4,8,128]{3,2,1,0:T(8,128)(2,1)S(1)}, u32[]{:S(2)}, u32[]{:S(2)}) %collective-permute-start.1) | collective-permute-done | bytes 131104 | tf_op jit(solution)/shard_map/ppermute | solution.py:20
  63.4 1.3 %collective-permute-start.3 = (bf16[16,4,8,128]{3,2,1,0:T(8,128)(2,1)S(1)}, bf16[16,4,8,128]{3,2,1,0:T(8,128)(2,1)S(1)}, u32[]{:S(2)}, u32[]{:S(2)}) collective-permute-start(bf16[16,4,8,128]{3,2,1,0:T(8,128)(2,1)S(1)} %fusion), channel_id=1, source_target_pairs={{0,4},{2,6},{4,8},{6,10},{8,12},{10,14},{1,5},{3,7},{5,9},{7,11},{... | collective-permute-start | bytes 393224 | tf_op jit(solution)/shard_map/ppermute | solution.py:20
  64.7 0.1 copy.15
  64.8 5.5 %collective-permute-done.3 = bf16[16,4,8,128]{3,2,1,0:T(8,128)(2,1)S(1)} collective-permute-done((bf16[16,4,8,128]{3,2,1,0:T(8,128)(2,1)S(1)}, bf16[16,4,8,128]{3,2,1,0:T(8,128)(2,1)S(1)}, u32[]{:S(2)}, u32[]{:S(2)}) %collective-permute-start.3) | collective-permute-done | bytes 131104 | tf_op jit(solution)/shard_map/ppermute | solution.py:20
  70.3 0.1 fusion.1
  70.4 1.3 %collective-permute-start.4 = (bf16[16,4,8,128]{3,2,1,0:T(8,128)(2,1)S(1)}, bf16[16,4,8,128]{3,2,1,0:T(8,128)(2,1)S(1)}, u32[]{:S(2)}, u32[]{:S(2)}) collective-permute-start(bf16[16,4,8,128]{3,2,1,0:T(8,128)(2,1)S(1)} %get-tuple-element.9), channel_id=1, source_target_pairs={{0,8},{2,10},{4,12},{6,14},{1,9},{3,11},{5,13},{7,15},{16,24},{18,... | collective-permute-start | bytes 393224 | tf_op jit(solution)/shard_map/ppermute | solution.py:20
  71.7 0.1 copy.16
  71.8 0.8 copy.13
  72.5 7.2 %collective-permute-done.4 = bf16[16,4,8,128]{3,2,1,0:T(8,128)(2,1)S(1)} collective-permute-done((bf16[16,4,8,128]{3,2,1,0:T(8,128)(2,1)S(1)}, bf16[16,4,8,128]{3,2,1,0:T(8,128)(2,1)S(1)}, u32[]{:S(2)}, u32[]{:S(2)}) %collective-permute-start.4) | collective-permute-done | bytes 131104 | tf_op jit(solution)/shard_map/ppermute | solution.py:20
  79.8 0.8 multiply_add_fusion.h0_ref
  80.5 9.8 %shard_map.93 = bf16[4096,128]{1,0:T(8,128)(2,1)} custom-call(f32[4096,128]{1,0:T(8,128)} %get-tuple-element.7.am_ref, bf16[4096,128]{1,0:T(8,128)(2,1)} %kl_ref.3, bf16[4096,128]{1,0:T(8,128)(2,1)} %gl_ref.1, f32[4096,1]{1,0:T(8,128)} %copy.11.g_ref, f32[1,128]{1,0:T(1,128)} %add_rsqrt_fusion.r_ref, f32[16,4,8,128]{3,2,1,0:T(8,128)} %bitcast.27, ...), custom_call_target="tpu_custom_call" | custom-call | tf_op jit(solution)/shard_map/pallas_call | solution.py:144
  (1 shorter events, 0.0 us)
Async XLA Ops:
  0.0 5.3 %copy-start.2 = (f32[4096,16]{0,1:T(8,128)S(1)}, f32[4096,16]{0,1:T(8,128)}, u32[]{:S(2)}) copy-start(f32[4096,16]{0,1:T(8,128)} %param.16) | copy-start | bytes 786436
  0.0 5.3 %copy-start.1 = (f32[4096,16]{0,1:T(8,128)S(1)}, f32[4096,16]{0,1:T(8,128)}, u32[]{:S(2)}) copy-start(f32[4096,16]{0,1:T(8,128)} %param.15) | copy-start | bytes 786436
  0.0 6.2 %copy-start.3 = (f32[4096]{0:T(1024)S(1)}, f32[4096]{0:T(1024)}, u32[]{:S(2)}) copy-start(f32[4096]{0:T(1024)} %param.17) | copy-start | bytes 49156
  1.9 27.7 %collective-permute-start = (bf16[4096,128]{1,0:T(8,128)(2,1)S(1)}, bf16[4096,128]{1,0:T(8,128)(2,1)S(1)}, u32[]{:S(2)}, u32[]{:S(2)}) collective-permute-start(bf16[4096,128]{1,0:T(8,128)(2,1)S(1)} %multiply_convert_fusion), channel_id=1, source_target_pairs={{0,2},{2,4},{4,6},{6,8},{8,10},{10,12},{12,14},{1,3},{3,5},{5,7},{... | collective-permute-start | bytes 3145736 | tf_op jit(solution)/shard_map/ppermute | solution.py:20
  29.6 1.0 %copy-start = (bf16[4096,128]{1,0:T(8,128)(2,1)}, bf16[4096,128]{1,0:T(8,128)(2,1)S(1)}, u32[]{:S(2)}) copy-start(bf16[4096,128]{1,0:T(8,128)(2,1)S(1)} %collective-permute-done.rim_ref) | copy-start | bytes 3145732
  53.1 7.5 %collective-permute-start.2 = (bf16[16,4,8,128]{3,2,1,0:T(8,128)(2,1)S(1)}, bf16[16,4,8,128]{3,2,1,0:T(8,128)(2,1)S(1)}, u32[]{:S(2)}, u32[]{:S(2)}) collective-permute-start(bf16[16,4,8,128]{3,2,1,0:T(8,128)(2,1)S(1)} %convert_element_type.33), channel_id=1, source_target_pairs={{0,4},{2,6},{4,8},{6,10},{8,12},{10,14},{1,5},{3,7},{5,9},{7,11},{... | collective-permute-start | bytes 393224 | tf_op jit(solution)/shard_map/ppermute | solution.py:20
  54.4 9.0 %collective-permute-start.1 = (bf16[16,4,8,128]{3,2,1,0:T(8,128)(2,1)S(1)}, bf16[16,4,8,128]{3,2,1,0:T(8,128)(2,1)S(1)}, u32[]{:S(2)}, u32[]{:S(2)}) collective-permute-start(bf16[16,4,8,128]{3,2,1,0:T(8,128)(2,1)S(1)} %convert_element_type.33), channel_id=1, source_target_pairs={{0,2},{2,4},{4,6},{6,8},{8,10},{10,12},{12,14},{1,3},{3,5},{5,7},{... | collective-permute-start | bytes 393224 | tf_op jit(solution)/shard_map/ppermute | solution.py:20
  63.4 6.9 %collective-permute-start.3 = (bf16[16,4,8,128]{3,2,1,0:T(8,128)(2,1)S(1)}, bf16[16,4,8,128]{3,2,1,0:T(8,128)(2,1)S(1)}, u32[]{:S(2)}, u32[]{:S(2)}) collective-permute-start(bf16[16,4,8,128]{3,2,1,0:T(8,128)(2,1)S(1)} %fusion), channel_id=1, source_target_pairs={{0,4},{2,6},{4,8},{6,10},{8,12},{10,14},{1,5},{3,7},{5,9},{7,11},{... | collective-permute-start | bytes 393224 | tf_op jit(solution)/shard_map/ppermute | solution.py:20
  70.4 9.4 %collective-permute-start.4 = (bf16[16,4,8,128]{3,2,1,0:T(8,128)(2,1)S(1)}, bf16[16,4,8,128]{3,2,1,0:T(8,128)(2,1)S(1)}, u32[]{:S(2)}, u32[]{:S(2)}) collective-permute-start(bf16[16,4,8,128]{3,2,1,0:T(8,128)(2,1)S(1)} %get-tuple-element.9), channel_id=1, source_target_pairs={{0,8},{2,10},{4,12},{6,14},{1,9},{3,11},{5,13},{7,15},{16,24},{18,... | collective-permute-start | bytes 393224 | tf_op jit(solution)/shard_map/ppermute | solution.py:20

commit v9 on v7

--- a/solution.py
+++ b/solution.py
@@ -154,6 +154,23 @@
 def to_tiles(a):
     channels, k = a.shape
     return a.T.reshape(k, channels // TILE, SUB, LANE)
+
+
+def decayed_scan(finals, a_t, length, count, radix=3):
+    sent = finals.astype(BF16)
+    carried = shifted(sent, "context", 1).astype(F32)
+    for j in range(2, min(radix, count) + 1):
+        decay = jnp.exp(-(length * (j - 1)) * a_t)
+        carried = carried + decay * shifted(sent, "context", j).astype(F32)
+    window = radix
+    while window < count:
+        sent = carried.astype(BF16)
+        for j in range(1, radix):
+            if j * window < count:
+                decay = jnp.exp(-(length * j * window) * a_t)
+                carried = carried + decay * shifted(sent, "context", j * window).astype(F32)
+        window *= radix
+    return carried
 
 
 def on_device(
@@ -182,12 +199,7 @@
     w = to_tiles(residues * jnp.sqrt(2.0 * log_decay))
     finals = final_state_call(after_medium, key_long, gain, r, lam)
 
-    carried = shifted(finals.astype(BF16), "context", 1).astype(F32)
-    distance = 1
-    while distance < lax.axis_size("context"):
-        decay = jnp.exp(-(length * distance) * a_t)
-        carried = carried + decay * shifted(carried.astype(BF16), "context", distance).astype(F32)
-        distance *= 2
+    carried = decayed_scan(finals, a_t, length, lax.axis_size("context"))
 
     return output_call(after_medium, key_long, gate_long, gain, r, lam, w, carried)
 

time: 97 us -> 93.5 us (0.964)
  the two profiles are of different devices: /device:TPU:24 before, /device:TPU:16 now
where the time goes in v9:
time: 93.5 us; the launch traced here: 92.3 us
  waiting for transfers between devices  38.8 us (41%)
  Pallas kernels  28.3 us (30%)
  starting transfers between devices  13.3 us (14%)
  local copies, waits for them, and re-layouts  4.69 us (5%)
  other arithmetic  4.49 us (5%)
  blocking collectives  2.57 us (3%)
    ppermute x6, waiting for transfers between devices, shifted(): return lax.ppermute(block, axis, route)  38.8 us
    ppermute x6, starting transfers between devices, shifted(): return lax.ppermute(block, axis, route)  13.3 us
    pallas_call x1, Pallas kernels, medium_call(): pl.pallas_call(medium_kernel, grid=(channels // block,), in_specs=[big, b...  12.1 us
    pallas_call x1, Pallas kernels, output_call(): pl.pallas_call(output_kernel, grid=(channels // TILE,), in_specs=[big, bi...  9.86 us
    pallas_call x1, Pallas kernels, final_state_call(): pl.pallas_call(final_state_kernel, grid=(channels // TILE,), in_specs=[bi...  6.37 us
    unnamed x14, local copies, waits for them, and re-layouts  2.71 us
    psum x1, blocking collectives, on_device(): totals = lax.psum(partial, 'tensor')  2.57 us
    broadcast_in_dim x1, local copies, waits for them, and re-layouts, on_device(): gain = norm_gain[:, None]  1.99 us
  transfers between devices with their start and end apart: 6, of which 5 were waited for; matrix products, arithmetic and copies ran while one was open for 4% of the time, Pallas kernels for 0%

profile of v9, /device:TPU:16, one launch (start us, length us, event | category | flops | bytes accessed | tf_op | source)
XLA Modules:
  0.0 92.3 jit_solution(6571009702057516755)
XLA Ops:
  0.0 0.0 copy-start.2
  0.0 0.0 copy-start.1
  0.0 1.9 %multiply_convert_fusion = bf16[4096,128]{1,0:T(8,128)(2,1)S(1)} fusion(bf16[4096,128]{1,0:T(8,128)(2,1)} %x_ref.1, bf16[4096,128]{1,0:T(8,128)(2,1)} %km_ref.1), kind=kLoop, calls=%fused_computation | loop fusion | flops 2097152 | bytes 3145728 | tf_op jit(solution)/shard_map/convert_element_type | solution.py:191
  1.9 0.0 copy-start.3
  1.9 3.4 %collective-permute-start = (bf16[4096,128]{1,0:T(8,128)(2,1)S(1)}, bf16[4096,128]{1,0:T(8,128)(2,1)S(1)}, u32[]{:S(2)}, u32[]{:S(2)}) collective-permute-start(bf16[4096,128]{1,0:T(8,128)(2,1)S(1)} %multiply_convert_fusion), channel_id=1, source_target_pairs={{0,2},{2,4},{4,6},{6,8},{8,10},{10,12},{12,14},{1,3},{3,5},{5,7},{... | collective-permute-start | bytes 3145736 | tf_op jit(solution)/shard_map/ppermute | solution.py:20
  5.3 0.0 copy-done.2
  5.3 0.0 copy-done.1
  5.3 0.2 exponential_bitcast_fusion.1
  5.5 0.7 copy.12
  6.3 0.0 copy-done.3
  6.3 2.0 %copy.11.g_ref = f32[4096,1]{1,0:T(8,128)} copy(f32[4096,1]{0,1:T(1,128)S(1)} %bitcast.38) | data formatting | bytes 32768 | tf_op jit(solution)/shard_map/broadcast_in_dim | solution.py:196
  8.3 21.3 %collective-permute-done.rim_ref = bf16[4096,128]{1,0:T(8,128)(2,1)S(1)} collective-permute-done((bf16[4096,128]{1,0:T(8,128)(2,1)S(1)}, bf16[4096,128]{1,0:T(8,128)(2,1)S(1)}, u32[]{:S(2)}, u32[]{:S(2)}) %collective-permute-start) | collective-permute-done | bytes 1048608 | tf_op jit(solution)/shard_map/ppermute | solution.py:20
  29.6 0.0 copy-start
  29.6 1.0 %copy-done = bf16[4096,128]{1,0:T(8,128)(2,1)} copy-done((bf16[4096,128]{1,0:T(8,128)(2,1)}, bf16[4096,128]{1,0:T(8,128)(2,1)S(1)}, u32[]{:S(2)}) %copy-start) | copy-done | bytes 1048600
  30.6 12.1 %shard_map.91 = (f32[4096,128]{1,0:T(8,128)}, f32[1,128]{1,0:T(1,128)}) custom-call(bf16[4096,128]{1,0:T(8,128)(2,1)} %x_ref.1, bf16[4096,128]{1,0:T(8,128)(2,1)} %gm_ref.1, bf16[4096,128]{1,0:T(8,128)(2,1)} %km_ref.1, bf16[4096,128]{1,0:T(8,128)(2,1)} %copy-done, bf16[256,128]{1,0:T(8,128)(2,1)} %taps_ref.1), custom_call_target="tpu_custom_call" | custom-call | tf_op jit(solution)/shard_map/pallas_call | solution.py:58
  42.6 2.6 %psum.7 = f32[1,128]{1,0:T(1,128)S(1)} all-reduce(f32[1,128]{1,0:T(1,128)} %get-tuple-element.8), channel_id=1, replica_groups=mesh['groups'=2,'context'=8,'tensor'=2] {'tensor'}, use_global_device_ids=true, to_apply=%region_0.0 | all-reduce | flops 128 | bytes 1024 | tf_op jit(solution)/shard_map/psum | solution.py:194
  45.2 0.6 add_rsqrt_fusion.r_ref
  45.8 6.4 %shard_map.92 = f32[16,4,8,128]{3,2,1,0:T(8,128)} custom-call(f32[4096,128]{1,0:T(8,128)} %get-tuple-element.7.am_ref, bf16[4096,128]{1,0:T(8,128)(2,1)} %kl_ref.3, f32[4096,1]{1,0:T(8,128)} %copy.11.g_ref, f32[1,128]{1,0:T(1,128)} %add_rsqrt_fusion.r_ref, f32[16,4,8,128]{3,2,1,0:T(8,128)} %bitcast.31), custom_call_target="tpu_custom_call" | custom-call | tf_op jit(solution)/shard_map/pallas_call | solution.py:130
  52.1 1.0 %convert_element_type.33 = bf16[16,4,8,128]{3,2,1,0:T(8,128)(2,1)S(1)} convert(f32[16,4,8,128]{3,2,1,0:T(8,128)} %shard_map.92) | non-fusion elementwise | flops 65536 | bytes 393216 | tf_op jit(solution)/shard_map/convert_element_type | solution.py:160
  53.1 3.5 %collective-permute-start.3 = (bf16[16,4,8,128]{3,2,1,0:T(8,128)(2,1)S(1)}, bf16[16,4,8,128]{3,2,1,0:T(8,128)(2,1)S(1)}, u32[]{:S(2)}, u32[]{:S(2)}) collective-permute-start(bf16[16,4,8,128]{3,2,1,0:T(8,128)(2,1)S(1)} %convert_element_type.33), channel_id=1, source_target_pairs={{0,6},{2,8},{4,10},{6,12},{8,14},{1,7},{3,9},{5,11},{7,13},{9,15},... | collective-permute-start | bytes 393224 | tf_op jit(solution)/shard_map/ppermute | solution.py:20
  56.6 1.9 %collective-permute-start.2 = (bf16[16,4,8,128]{3,2,1,0:T(8,128)(2,1)S(1)}, bf16[16,4,8,128]{3,2,1,0:T(8,128)(2,1)S(1)}, u32[]{:S(2)}, u32[]{:S(2)}) collective-permute-start(bf16[16,4,8,128]{3,2,1,0:T(8,128)(2,1)S(1)} %convert_element_type.33), channel_id=1, source_target_pairs={{0,4},{2,6},{4,8},{6,10},{8,12},{10,14},{1,5},{3,7},{5,9},{7,11},{... | collective-permute-start | bytes 393224 | tf_op jit(solution)/shard_map/ppermute | solution.py:20
  58.5 1.9 %collective-permute-start.1 = (bf16[16,4,8,128]{3,2,1,0:T(8,128)(2,1)S(1)}, bf16[16,4,8,128]{3,2,1,0:T(8,128)(2,1)S(1)}, u32[]{:S(2)}, u32[]{:S(2)}) collective-permute-start(bf16[16,4,8,128]{3,2,1,0:T(8,128)(2,1)S(1)} %convert_element_type.33), channel_id=1, source_target_pairs={{0,2},{2,4},{4,6},{6,8},{8,10},{10,12},{12,14},{1,3},{3,5},{5,7},{... | collective-permute-start | bytes 393224 | tf_op jit(solution)/shard_map/ppermute | solution.py:20
  60.5 0.1 copy.15
  60.5 0.1 copy.14
  60.6 1.9 %collective-permute-done.3 = bf16[16,4,8,128]{3,2,1,0:T(8,128)(2,1)S(1)} collective-permute-done((bf16[16,4,8,128]{3,2,1,0:T(8,128)(2,1)S(1)}, bf16[16,4,8,128]{3,2,1,0:T(8,128)(2,1)S(1)}, u32[]{:S(2)}, u32[]{:S(2)}) %collective-permute-start.3) | collective-permute-done | bytes 131104 | tf_op jit(solution)/shard_map/ppermute | solution.py:20
  62.5 1.3 %collective-permute-done.2 = bf16[16,4,8,128]{3,2,1,0:T(8,128)(2,1)S(1)} collective-permute-done((bf16[16,4,8,128]{3,2,1,0:T(8,128)(2,1)S(1)}, bf16[16,4,8,128]{3,2,1,0:T(8,128)(2,1)S(1)}, u32[]{:S(2)}, u32[]{:S(2)}) %collective-permute-start.2) | collective-permute-done | bytes 131104 | tf_op jit(solution)/shard_map/ppermute | solution.py:20
  63.8 8.4 %collective-permute-done.1 = bf16[16,4,8,128]{3,2,1,0:T(8,128)(2,1)S(1)} collective-permute-done((bf16[16,4,8,128]{3,2,1,0:T(8,128)(2,1)S(1)}, bf16[16,4,8,128]{3,2,1,0:T(8,128)(2,1)S(1)}, u32[]{:S(2)}, u32[]{:S(2)}) %collective-permute-start.1) | collective-permute-done | bytes 131104 | tf_op jit(solution)/shard_map/ppermute | solution.py:20
  72.2 0.1 fusion
  72.3 0.7 collective-permute-start.5
  73.0 1.9 %collective-permute-start.4 = (bf16[16,4,8,128]{3,2,1,0:T(8,128)(2,1)S(1)}, bf16[16,4,8,128]{3,2,1,0:T(8,128)(2,1)S(1)}, u32[]{:S(2)}, u32[]{:S(2)}) collective-permute-start(bf16[16,4,8,128]{3,2,1,0:T(8,128)(2,1)S(1)} %get-tuple-element.9), channel_id=1, source_target_pairs={{0,6},{2,8},{4,10},{6,12},{8,14},{1,7},{3,9},{5,11},{7,13},{9,15},... | collective-permute-start | bytes 393224 | tf_op jit(solution)/shard_map/ppermute | solution.py:20
  74.9 0.1 copy.16
  75.0 0.8 copy.13
  75.8 0.1 copy.17
  75.8 0.0 collective-permute-done.5
  75.8 5.8 %collective-permute-done.4 = bf16[16,4,8,128]{3,2,1,0:T(8,128)(2,1)S(1)} collective-permute-done((bf16[16,4,8,128]{3,2,1,0:T(8,128)(2,1)S(1)}, bf16[16,4,8,128]{3,2,1,0:T(8,128)(2,1)S(1)}, u32[]{:S(2)}, u32[]{:S(2)}) %collective-permute-start.4) | collective-permute-done | bytes 131104 | tf_op jit(solution)/shard_map/ppermute | solution.py:20
  81.7 0.8 multiply_add_fusion.h0_ref
  82.5 9.9 %shard_map.93 = bf16[4096,128]{1,0:T(8,128)(2,1)} custom-call(f32[4096,128]{1,0:T(8,128)} %get-tuple-element.7.am_ref, bf16[4096,128]{1,0:T(8,128)(2,1)} %kl_ref.3, bf16[4096,128]{1,0:T(8,128)(2,1)} %gl_ref.1, f32[4096,1]{1,0:T(8,128)} %copy.11.g_ref, f32[1,128]{1,0:T(1,128)} %add_rsqrt_fusion.r_ref, f32[16,4,8,128]{3,2,1,0:T(8,128)} %bitcast.32, ...), custom_call_target="tpu_custom_call" | custom-call | tf_op jit(solution)/shard_map/pallas_call | solution.py:144
Async XLA Ops:
  0.0 5.3 %copy-start.2 = (f32[4096,16]{0,1:T(8,128)S(1)}, f32[4096,16]{0,1:T(8,128)}, u32[]{:S(2)}) copy-start(f32[4096,16]{0,1:T(8,128)} %param.16) | copy-start | bytes 786436
  0.0 5.3 %copy-start.1 = (f32[4096,16]{0,1:T(8,128)S(1)}, f32[4096,16]{0,1:T(8,128)}, u32[]{:S(2)}) copy-start(f32[4096,16]{0,1:T(8,128)} %param.15) | copy-start | bytes 786436
  1.9 4.4 %copy-start.3 = (f32[4096]{0:T(1024)S(1)}, f32[4096]{0:T(1024)}, u32[]{:S(2)}) copy-start(f32[4096]{0:T(1024)} %param.17) | copy-start | bytes 49156
  1.9 27.7 %collective-permute-start = (bf16[4096,128]{1,0:T(8,128)(2,1)S(1)}, bf16[4096,128]{1,0:T(8,128)(2,1)S(1)}, u32[]{:S(2)}, u32[]{:S(2)}) collective-permute-start(bf16[4096,128]{1,0:T(8,128)(2,1)S(1)} %multiply_convert_fusion), channel_id=1, source_target_pairs={{0,2},{2,4},{4,6},{6,8},{8,10},{10,12},{12,14},{1,3},{3,5},{5,7},{... | collective-permute-start | bytes 3145736 | tf_op jit(solution)/shard_map/ppermute | solution.py:20
  29.6 1.0 %copy-start = (bf16[4096,128]{1,0:T(8,128)(2,1)}, bf16[4096,128]{1,0:T(8,128)(2,1)S(1)}, u32[]{:S(2)}) copy-start(bf16[4096,128]{1,0:T(8,128)(2,1)S(1)} %collective-permute-done.rim_ref) | copy-start | bytes 3145732
  53.1 9.4 %collective-permute-start.3 = (bf16[16,4,8,128]{3,2,1,0:T(8,128)(2,1)S(1)}, bf16[16,4,8,128]{3,2,1,0:T(8,128)(2,1)S(1)}, u32[]{:S(2)}, u32[]{:S(2)}) collective-permute-start(bf16[16,4,8,128]{3,2,1,0:T(8,128)(2,1)S(1)} %convert_element_type.33), channel_id=1, source_target_pairs={{0,6},{2,8},{4,10},{6,12},{8,14},{1,7},{3,9},{5,11},{7,13},{9,15},... | collective-permute-start | bytes 393224 | tf_op jit(solution)/shard_map/ppermute | solution.py:20
  56.6 7.2 %collective-permute-start.2 = (bf16[16,4,8,128]{3,2,1,0:T(8,128)(2,1)S(1)}, bf16[16,4,8,128]{3,2,1,0:T(8,128)(2,1)S(1)}, u32[]{:S(2)}, u32[]{:S(2)}) collective-permute-start(bf16[16,4,8,128]{3,2,1,0:T(8,128)(2,1)S(1)} %convert_element_type.33), channel_id=1, source_target_pairs={{0,4},{2,6},{4,8},{6,10},{8,12},{10,14},{1,5},{3,7},{5,9},{7,11},{... | collective-permute-start | bytes 393224 | tf_op jit(solution)/shard_map/ppermute | solution.py:20
  58.5 13.7 %collective-permute-start.1 = (bf16[16,4,8,128]{3,2,1,0:T(8,128)(2,1)S(1)}, bf16[16,4,8,128]{3,2,1,0:T(8,128)(2,1)S(1)}, u32[]{:S(2)}, u32[]{:S(2)}) collective-permute-start(bf16[16,4,8,128]{3,2,1,0:T(8,128)(2,1)S(1)} %convert_element_type.33), channel_id=1, source_target_pairs={{0,2},{2,4},{4,6},{6,8},{8,10},{10,12},{12,14},{1,3},{3,5},{5,7},{... | collective-permute-start | bytes 393224 | tf_op jit(solution)/shard_map/ppermute | solution.py:20
  72.3 3.5 %collective-permute-start.5 = (bf16[16,4,8,128]{3,2,1,0:T(8,128)(2,1)S(1)}, bf16[16,4,8,128]{3,2,1,0:T(8,128)(2,1)S(1)}, u32[]{:S(2)}, u32[]{:S(2)}) collective-permute-start(bf16[16,4,8,128]{3,2,1,0:T(8,128)(2,1)S(1)} %get-tuple-element.9), channel_id=1, source_target_pairs={{0,12},{2,14},{1,13},{3,15},{16,28},{18,30},{17,29},{19,31}} | collective-permute-start | bytes 393224 | tf_op jit(solution)/shard_map/ppermute | solution.py:20
  73.0 8.7 %collective-permute-start.4 = (bf16[16,4,8,128]{3,2,1,0:T(8,128)(2,1)S(1)}, bf16[16,4,8,128]{3,2,1,0:T(8,128)(2,1)S(1)}, u32[]{:S(2)}, u32[]{:S(2)}) collective-permute-start(bf16[16,4,8,128]{3,2,1,0:T(8,128)(2,1)S(1)} %get-tuple-element.9), channel_id=1, source_target_pairs={{0,6},{2,8},{4,10},{6,12},{8,14},{1,7},{3,9},{5,11},{7,13},{9,15},... | collective-permute-start | bytes 393224 | tf_op jit(solution)/shard_map/ppermute | solution.py:20

commit v10 on v8

--- a/solution.py
+++ b/solution.py
@@ -93,13 +93,12 @@
 
     h = lax.fori_loop(0, length, body, tuple(jnp.zeros((SUB, LANE), F32) for _ in range(modes)), unroll=8)
     for m in range(modes):
-        f_ref[m] = h[m]
-
-
-def output_kernel(am_ref, kl_ref, gl_ref, g_ref, r_ref, lam_ref, w_ref, h0_ref, out_ref, vt_ref, yt_ref):
+        f_ref[m] = h[m].astype(f_ref.dtype)
+
+
+def output_kernel(am_ref, vt_ref, gl_ref, lam_ref, w_ref, h0_ref, out_ref, yt_ref):
     modes = lam_ref.shape[0]
     length = am_ref.shape[1]
-    load_values(am_ref, kl_ref, g_ref, r_ref, vt_ref)
     lam = [lam_ref[m] for m in range(modes)]
     w = [w_ref[m] for m in range(modes)]
 
@@ -131,24 +130,26 @@
         final_state_kernel,
         grid=(channels // TILE,),
         in_specs=[big, big, pl.BlockSpec((TILE, 1), lambda b: (b, 0)), pl.BlockSpec((1, length), lambda b: (0, 0)), tiled_spec(modes)],
-        out_specs=tiled_spec(modes),
-        out_shape=jax.ShapeDtypeStruct(lam.shape, F32),
-        scratch_shapes=[pltpu.VMEM((length * SUB, LANE), F32)],
+        out_specs=[tiled_spec(modes), pl.BlockSpec((length * SUB, LANE), lambda b: (b, 0))],
+        out_shape=[
+            jax.ShapeDtypeStruct(lam.shape, BF16),
+            jax.ShapeDtypeStruct((channels // TILE * length * SUB, LANE), F32),
+        ],
     )(am, kl, gain, r, lam)
 
 
-def output_call(am, kl, gl, gain, r, lam, w, h0):
+def output_call(am, vt, gl, lam, w, h0):
     channels, length = am.shape
     modes = lam.shape[0]
     big = pl.BlockSpec((TILE, length), lambda b: (b, 0))
     return pl.pallas_call(
         output_kernel,
         grid=(channels // TILE,),
-        in_specs=[big, big, big, pl.BlockSpec((TILE, 1), lambda b: (b, 0)), pl.BlockSpec((1, length), lambda b: (0, 0)), tiled_spec(modes), tiled_spec(modes), tiled_spec(modes)],
+        in_specs=[big, pl.BlockSpec((length * SUB, LANE), lambda b: (b, 0)), big, tiled_spec(modes), tiled_spec(modes), tiled_spec(modes)],
         out_specs=big,
         out_shape=jax.ShapeDtypeStruct((channels, length), BF16),
-        scratch_shapes=[pltpu.VMEM((length * SUB, LANE), F32), pltpu.VMEM((length * SUB, LANE), F32)],
-    )(am, kl, gl, gain, r, lam, w, h0)
+        scratch_shapes=[pltpu.VMEM((length * SUB, LANE), F32)],
+    )(am, vt, gl, lam, w, h0)
 
 
 def to_tiles(a):
@@ -180,9 +181,9 @@
     a_t = to_tiles(log_decay)
     lam = jnp.exp(-a_t)
     w = to_tiles(residues * jnp.sqrt(2.0 * log_decay))
-    finals = final_state_call(after_medium, key_long, gain, r, lam)
-
-    sent = finals.astype(BF16)
+    finals, vt = final_state_call(after_medium, key_long, gain, r, lam)
+
+    sent = finals
     carried = shifted(sent, "context", 1).astype(F32)
     distance = 1
     if lax.axis_size("context") > 2:
@@ -194,7 +195,7 @@
         carried = carried + decay * shifted(carried.astype(BF16), "context", distance).astype(F32)
         distance *= 2
 
-    return output_call(after_medium, key_long, gate_long, gain, r, lam, w, carried)
+    return output_call(after_medium, vt, gate_long, lam, w, carried)
 
 
 def solution(mesh):

time: 91.8 us -> 89.4 us (0.974)
  Pallas kernels: 28.2 us -> 26.6 us
  other arithmetic: 4.49 us -> 3.55 us
    pallas_call x1, Pallas kernels: 9.82 us -> 7.75 us  [output_call(): pl.pallas_call(output_kernel, grid=(channels // TILE,), in_specs=[big, pl...]
    convert_element_type x1 -> x0, other arithmetic: 0.97 us -> none  [on_device(): sent = finals.astype(BF16)]
where the time goes in v10:
time: 89.4 us; the launch traced here: 87.9 us
  waiting for transfers between devices  40.7 us (46%)
  Pallas kernels  26.6 us (30%)
  starting transfers between devices  9.76 us (11%)
  local copies, waits for them, and re-layouts  4.63 us (5%)
  other arithmetic  3.55 us (4%)
  blocking collectives  2.57 us (3%)
    ppermute x5, waiting for transfers between devices, shifted(): return lax.ppermute(block, axis, route)  40.7 us
    pallas_call x1, Pallas kernels, medium_call(): pl.pallas_call(medium_kernel, grid=(channels // block,), in_specs=[big, b...  12.1 us
    ppermute x5, starting transfers between devices, shifted(): return lax.ppermute(block, axis, route)  9.76 us
    pallas_call x1, Pallas kernels, output_call(): pl.pallas_call(output_kernel, grid=(channels // TILE,), in_specs=[big, pl...  7.75 us
    pallas_call x1, Pallas kernels, final_state_call(): pl.pallas_call(final_state_kernel, grid=(channels // TILE,), in_specs=[bi...  6.72 us
    unnamed x13, local copies, waits for them, and re-layouts  2.65 us
    psum x1, blocking collectives, on_device(): totals = lax.psum(partial, 'tensor')  2.57 us
    broadcast_in_dim x1, local copies, waits for them, and re-layouts, on_device(): gain = norm_gain[:, None]  1.98 us
  transfers between devices with their start and end apart: 5, of which 5 were waited for; matrix products, arithmetic and copies ran while one was open for 4% of the time, Pallas kernels for 0%

profile of v10, /device:TPU:24, one launch (start us, length us, event | category | flops | bytes accessed | tf_op | source)
XLA Modules:
  0.0 87.9 jit_solution(14770961908526861857)
XLA Ops:
  0.0 0.0 copy-start.2
  0.0 0.0 copy-start.1
  0.0 0.0 copy-start.3
  0.0 1.9 %multiply_convert_fusion = bf16[4096,128]{1,0:T(8,128)(2,1)S(1)} fusion(bf16[4096,128]{1,0:T(8,128)(2,1)} %x_ref.1, bf16[4096,128]{1,0:T(8,128)(2,1)} %km_ref.1), kind=kLoop, calls=%fused_computation | loop fusion | flops 2097152 | bytes 3145728 | tf_op jit(solution)/shard_map/convert_element_type | solution.py:175
  1.9 3.4 %collective-permute-start = (bf16[4096,128]{1,0:T(8,128)(2,1)S(1)}, bf16[4096,128]{1,0:T(8,128)(2,1)S(1)}, u32[]{:S(2)}, u32[]{:S(2)}) collective-permute-start(bf16[4096,128]{1,0:T(8,128)(2,1)S(1)} %multiply_convert_fusion), channel_id=1, source_target_pairs={{0,2},{2,4},{4,6},{6,8},{8,10},{10,12},{12,14},{1,3},{3,5},{5,7},{... | collective-permute-start | bytes 3145736 | tf_op jit(solution)/shard_map/ppermute | solution.py:20
  5.3 0.0 copy-done.2
  5.3 0.0 copy-done.1
  5.3 0.2 exponential_bitcast_fusion
  5.5 0.8 copy.11
  6.3 0.0 copy-done.3
  6.3 2.0 %copy.10.g_ref = f32[4096,1]{1,0:T(8,128)} copy(f32[4096,1]{0,1:T(1,128)S(1)} %bitcast.33) | data formatting | bytes 32768 | tf_op jit(solution)/shard_map/broadcast_in_dim | solution.py:180
  8.2 21.3 %collective-permute-done.rim_ref = bf16[4096,128]{1,0:T(8,128)(2,1)S(1)} collective-permute-done((bf16[4096,128]{1,0:T(8,128)(2,1)S(1)}, bf16[4096,128]{1,0:T(8,128)(2,1)S(1)}, u32[]{:S(2)}, u32[]{:S(2)}) %collective-permute-start) | collective-permute-done | bytes 1048608 | tf_op jit(solution)/shard_map/ppermute | solution.py:20
  29.6 0.0 copy-start
  29.6 1.0 %copy-done = bf16[4096,128]{1,0:T(8,128)(2,1)} copy-done((bf16[4096,128]{1,0:T(8,128)(2,1)}, bf16[4096,128]{1,0:T(8,128)(2,1)S(1)}, u32[]{:S(2)}) %copy-start) | copy-done | bytes 1048600
  30.5 12.1 %shard_map.91 = (f32[4096,128]{1,0:T(8,128)}, f32[1,128]{1,0:T(1,128)}) custom-call(bf16[4096,128]{1,0:T(8,128)(2,1)} %x_ref.1, bf16[4096,128]{1,0:T(8,128)(2,1)} %gm_ref.1, bf16[4096,128]{1,0:T(8,128)(2,1)} %km_ref.1, bf16[4096,128]{1,0:T(8,128)(2,1)} %copy-done, bf16[256,128]{1,0:T(8,128)(2,1)} %taps_ref.1), custom_call_target="tpu_custom_call" | custom-call | tf_op jit(solution)/shard_map/pallas_call | solution.py:58
  42.6 2.6 %psum.7 = f32[1,128]{1,0:T(1,128)S(1)} all-reduce(f32[1,128]{1,0:T(1,128)} %get-tuple-element.10), channel_id=1, replica_groups=mesh['groups'=2,'context'=8,'tensor'=2] {'tensor'}, use_global_device_ids=true, to_apply=%region_0.0 | all-reduce | flops 128 | bytes 1024 | tf_op jit(solution)/shard_map/psum | solution.py:178
  45.2 0.6 add_rsqrt_fusion.r_ref
  45.8 6.7 %shard_map.92 = (bf16[16,4,8,128]{3,2,1,0:T(8,128)(2,1)}, f32[4096,128]{1,0:T(8,128)}) custom-call(f32[4096,128]{1,0:T(8,128)} %get-tuple-element.9.am_ref, bf16[4096,128]{1,0:T(8,128)(2,1)} %kl_ref.1, f32[4096,1]{1,0:T(8,128)} %copy.10.g_ref, f32[1,128]{1,0:T(1,128)} %add_rsqrt_fusion.r_ref, f32[16,4,8,128]{3,2,1,0:T(8,128)} %bitcast.26), custom_call_target="tpu_custom_call" | custom-call | tf_op jit(solution)/shard_map/pallas_call | solution.py:129
  52.5 1.3 %collective-permute-start.2 = (bf16[16,4,8,128]{3,2,1,0:T(8,128)(2,1)}, bf16[16,4,8,128]{3,2,1,0:T(8,128)(2,1)S(1)}, u32[]{:S(2)}, u32[]{:S(2)}) collective-permute-start(bf16[16,4,8,128]{3,2,1,0:T(8,128)(2,1)} %get-tuple-element.12), channel_id=1, source_target_pairs={{0,4},{2,6},{4,8},{6,10},{8,12},{10,14},{1,5},{3,7},{5,9},{7,11},{... | collective-permute-start | bytes 393224 | tf_op jit(solution)/shard_map/ppermute | solution.py:20
  53.8 2.5 %collective-permute-start.1 = (bf16[16,4,8,128]{3,2,1,0:T(8,128)(2,1)}, bf16[16,4,8,128]{3,2,1,0:T(8,128)(2,1)S(1)}, u32[]{:S(2)}, u32[]{:S(2)}) collective-permute-start(bf16[16,4,8,128]{3,2,1,0:T(8,128)(2,1)} %get-tuple-element.12), channel_id=1, source_target_pairs={{0,2},{2,4},{4,6},{6,8},{8,10},{10,12},{12,14},{1,3},{3,5},{5,7},{... | collective-permute-start | bytes 393224 | tf_op jit(solution)/shard_map/ppermute | solution.py:20
  56.3 0.1 copy.13
  56.4 3.8 %collective-permute-done.2 = bf16[16,4,8,128]{3,2,1,0:T(8,128)(2,1)S(1)} collective-permute-done((bf16[16,4,8,128]{3,2,1,0:T(8,128)(2,1)}, bf16[16,4,8,128]{3,2,1,0:T(8,128)(2,1)S(1)}, u32[]{:S(2)}, u32[]{:S(2)}) %collective-permute-start.2) | collective-permute-done | bytes 131104 | tf_op jit(solution)/shard_map/ppermute | solution.py:20
  60.2 2.8 %collective-permute-done.1 = bf16[16,4,8,128]{3,2,1,0:T(8,128)(2,1)S(1)} collective-permute-done((bf16[16,4,8,128]{3,2,1,0:T(8,128)(2,1)}, bf16[16,4,8,128]{3,2,1,0:T(8,128)(2,1)S(1)}, u32[]{:S(2)}, u32[]{:S(2)}) %collective-permute-start.1) | collective-permute-done | bytes 131104 | tf_op jit(solution)/shard_map/ppermute | solution.py:20
  63.1 1.3 %collective-permute-start.3 = (bf16[16,4,8,128]{3,2,1,0:T(8,128)(2,1)S(1)}, bf16[16,4,8,128]{3,2,1,0:T(8,128)(2,1)S(1)}, u32[]{:S(2)}, u32[]{:S(2)}) collective-permute-start(bf16[16,4,8,128]{3,2,1,0:T(8,128)(2,1)S(1)} %fusion), channel_id=1, source_target_pairs={{0,4},{2,6},{4,8},{6,10},{8,12},{10,14},{1,5},{3,7},{5,9},{7,11},{... | collective-permute-start | bytes 393224 | tf_op jit(solution)/shard_map/ppermute | solution.py:20
  64.4 0.1 copy.14
  64.4 5.5 %collective-permute-done.3 = bf16[16,4,8,128]{3,2,1,0:T(8,128)(2,1)S(1)} collective-permute-done((bf16[16,4,8,128]{3,2,1,0:T(8,128)(2,1)S(1)}, bf16[16,4,8,128]{3,2,1,0:T(8,128)(2,1)S(1)}, u32[]{:S(2)}, u32[]{:S(2)}) %collective-permute-start.3) | collective-permute-done | bytes 131104 | tf_op jit(solution)/shard_map/ppermute | solution.py:20
  69.9 0.1 fusion.1
  70.0 1.3 %collective-permute-start.4 = (bf16[16,4,8,128]{3,2,1,0:T(8,128)(2,1)S(1)}, bf16[16,4,8,128]{3,2,1,0:T(8,128)(2,1)S(1)}, u32[]{:S(2)}, u32[]{:S(2)}) collective-permute-start(bf16[16,4,8,128]{3,2,1,0:T(8,128)(2,1)S(1)} %get-tuple-element.13), channel_id=1, source_target_pairs={{0,8},{2,10},{4,12},{6,14},{1,9},{3,11},{5,13},{7,15},{16,24},{18,... | collective-permute-start | bytes 393224 | tf_op jit(solution)/shard_map/ppermute | solution.py:20
  71.3 0.1 copy.15
  71.4 0.7 copy.12
  72.1 7.3 %collective-permute-done.4 = bf16[16,4,8,128]{3,2,1,0:T(8,128)(2,1)S(1)} collective-permute-done((bf16[16,4,8,128]{3,2,1,0:T(8,128)(2,1)S(1)}, bf16[16,4,8,128]{3,2,1,0:T(8,128)(2,1)S(1)}, u32[]{:S(2)}, u32[]{:S(2)}) %collective-permute-start.4) | collective-permute-done | bytes 131104 | tf_op jit(solution)/shard_map/ppermute | solution.py:20
  79.4 0.8 multiply_add_fusion.h0_ref
  80.2 7.8 %shard_map.93 = bf16[4096,128]{1,0:T(8,128)(2,1)} custom-call(f32[4096,128]{1,0:T(8,128)} %get-tuple-element.9.am_ref, f32[4096,128]{1,0:T(8,128)} %get-tuple-element.11.vt_ref, bf16[4096,128]{1,0:T(8,128)(2,1)} %gl_ref.1, f32[16,4,8,128]{3,2,1,0:T(8,128)} %bitcast.27, f32[16,4,8,128]{3,2,1,0:T(8,128)} %bitcast.30, f32[16,4,8,128]{3,2,1,0:T(8,128)} %multiply_add_fusion.h0_ref), custom_call_target="tpu_custom_call" | custom-call | tf_op jit(solution)/shard_map/pallas_call | solution.py:145
  (1 shorter events, 0.0 us)
Async XLA Ops:
  0.0 5.3 %copy-start.2 = (f32[4096,16]{0,1:T(8,128)S(1)}, f32[4096,16]{0,1:T(8,128)}, u32[]{:S(2)}) copy-start(f32[4096,16]{0,1:T(8,128)} %param.16) | copy-start | bytes 786436
  0.0 5.3 %copy-start.1 = (f32[4096,16]{0,1:T(8,128)S(1)}, f32[4096,16]{0,1:T(8,128)}, u32[]{:S(2)}) copy-start(f32[4096,16]{0,1:T(8,128)} %param.15) | copy-start | bytes 786436
  0.0 6.3 %copy-start.3 = (f32[4096]{0:T(1024)S(1)}, f32[4096]{0:T(1024)}, u32[]{:S(2)}) copy-start(f32[4096]{0:T(1024)} %param.17) | copy-start | bytes 49156
  1.9 27.7 %collective-permute-start = (bf16[4096,128]{1,0:T(8,128)(2,1)S(1)}, bf16[4096,128]{1,0:T(8,128)(2,1)S(1)}, u32[]{:S(2)}, u32[]{:S(2)}) collective-permute-start(bf16[4096,128]{1,0:T(8,128)(2,1)S(1)} %multiply_convert_fusion), channel_id=1, source_target_pairs={{0,2},{2,4},{4,6},{6,8},{8,10},{10,12},{12,14},{1,3},{3,5},{5,7},{... | collective-permute-start | bytes 3145736 | tf_op jit(solution)/shard_map/ppermute | solution.py:20
  29.6 1.0 %copy-start = (bf16[4096,128]{1,0:T(8,128)(2,1)}, bf16[4096,128]{1,0:T(8,128)(2,1)S(1)}, u32[]{:S(2)}) copy-start(bf16[4096,128]{1,0:T(8,128)(2,1)S(1)} %collective-permute-done.rim_ref) | copy-start | bytes 3145732
  52.5 7.7 %collective-permute-start.2 = (bf16[16,4,8,128]{3,2,1,0:T(8,128)(2,1)}, bf16[16,4,8,128]{3,2,1,0:T(8,128)(2,1)S(1)}, u32[]{:S(2)}, u32[]{:S(2)}) collective-permute-start(bf16[16,4,8,128]{3,2,1,0:T(8,128)(2,1)} %get-tuple-element.12), channel_id=1, source_target_pairs={{0,4},{2,6},{4,8},{6,10},{8,12},{10,14},{1,5},{3,7},{5,9},{7,11},{... | collective-permute-start | bytes 393224 | tf_op jit(solution)/shard_map/ppermute | solution.py:20
  53.8 9.2 %collective-permute-start.1 = (bf16[16,4,8,128]{3,2,1,0:T(8,128)(2,1)}, bf16[16,4,8,128]{3,2,1,0:T(8,128)(2,1)S(1)}, u32[]{:S(2)}, u32[]{:S(2)}) collective-permute-start(bf16[16,4,8,128]{3,2,1,0:T(8,128)(2,1)} %get-tuple-element.12), channel_id=1, source_target_pairs={{0,2},{2,4},{4,6},{6,8},{8,10},{10,12},{12,14},{1,3},{3,5},{5,7},{... | collective-permute-start | bytes 393224 | tf_op jit(solution)/shard_map/ppermute | solution.py:20
  63.1 6.9 %collective-permute-start.3 = (bf16[16,4,8,128]{3,2,1,0:T(8,128)(2,1)S(1)}, bf16[16,4,8,128]{3,2,1,0:T(8,128)(2,1)S(1)}, u32[]{:S(2)}, u32[]{:S(2)}) collective-permute-start(bf16[16,4,8,128]{3,2,1,0:T(8,128)(2,1)S(1)} %fusion), channel_id=1, source_target_pairs={{0,4},{2,6},{4,8},{6,10},{8,12},{10,14},{1,5},{3,7},{5,9},{7,11},{... | collective-permute-start | bytes 393224 | tf_op jit(solution)/shard_map/ppermute | solution.py:20
  70.0 9.4 %collective-permute-start.4 = (bf16[16,4,8,128]{3,2,1,0:T(8,128)(2,1)S(1)}, bf16[16,4,8,128]{3,2,1,0:T(8,128)(2,1)S(1)}, u32[]{:S(2)}, u32[]{:S(2)}) collective-permute-start(bf16[16,4,8,128]{3,2,1,0:T(8,128)(2,1)S(1)} %get-tuple-element.13), channel_id=1, source_target_pairs={{0,8},{2,10},{4,12},{6,14},{1,9},{3,11},{5,13},{7,15},{16,24},{18,... | collective-permute-start | bytes 393224 | tf_op jit(solution)/shard_map/ppermute | solution.py:20

commit v11 on v10

--- a/solution.py
+++ b/solution.py
@@ -52,7 +52,7 @@
 def medium_call(inputs, gate_medium, key_medium, rim, taps):
     channels, length = inputs.shape
     per_group = channels // taps.shape[0]
-    block = 256
+    block = 512
     tap_block = block // per_group
     big = pl.BlockSpec((block, length), lambda b: (b, 0))
     return pl.pallas_call(

time: 89.4 us -> 84.6 us (0.946)
  Pallas kernels: 26.6 us -> 22.4 us
    pallas_call x1, Pallas kernels: 12.1 us -> 7.91 us  [medium_call(): pl.pallas_call(medium_kernel, grid=(channels // block,), in_specs=[big, b...]
  transfers between devices with their start and end apart: 5 -> 5, of which waited for: 5 -> 5; matrix products, arithmetic and copies ran while one was open for 4% -> 5% of each run, Pallas kernels for 0% -> 0%
where the time goes in v11:
time: 84.6 us; the launch traced here: 83.7 us
  waiting for transfers between devices  40.7 us (48%)
  Pallas kernels  22.4 us (26%)
  starting transfers between devices  9.76 us (12%)
  local copies, waits for them, and re-layouts  4.63 us (5%)
  other arithmetic  3.55 us (4%)
  blocking collectives  2.57 us (3%)
    ppermute x5, waiting for transfers between devices, shifted(): return lax.ppermute(block, axis, route)  40.7 us
    ppermute x5, starting transfers between devices, shifted(): return lax.ppermute(block, axis, route)  9.76 us
    pallas_call x1, Pallas kernels, medium_call(): pl.pallas_call(medium_kernel, grid=(channels // block,), in_specs=[big, b...  7.91 us
    pallas_call x1, Pallas kernels, output_call(): pl.pallas_call(output_kernel, grid=(channels // TILE,), in_specs=[big, pl...  7.75 us
    pallas_call x1, Pallas kernels, final_state_call(): pl.pallas_call(final_state_kernel, grid=(channels // TILE,), in_specs=[bi...  6.72 us
    unnamed x13, local copies, waits for them, and re-layouts  2.65 us
    psum x1, blocking collectives, on_device(): totals = lax.psum(partial, 'tensor')  2.57 us
    broadcast_in_dim x1, local copies, waits for them, and re-layouts, on_device(): gain = norm_gain[:, None]  1.98 us
  transfers between devices with their start and end apart: 5, of which 5 were waited for; matrix products, arithmetic and copies ran while one was open for 5% of the time, Pallas kernels for 0%

profile of v11, /device:TPU:24, one launch (start us, length us, event | category | flops | bytes accessed | tf_op | source)
XLA Modules:
  0.0 83.7 jit_solution(5702675877514963478)
XLA Ops:
  0.0 0.0 copy-start.2
  0.0 0.0 copy-start.1
  0.0 0.0 copy-start.3
  0.0 1.9 %multiply_convert_fusion = bf16[4096,128]{1,0:T(8,128)(2,1)S(1)} fusion(bf16[4096,128]{1,0:T(8,128)(2,1)} %x_ref.1, bf16[4096,128]{1,0:T(8,128)(2,1)} %km_ref.1), kind=kLoop, calls=%fused_computation | loop fusion | flops 2097152 | bytes 3145728 | tf_op jit(solution)/shard_map/convert_element_type | solution.py:175
  1.9 3.4 %collective-permute-start = (bf16[4096,128]{1,0:T(8,128)(2,1)S(1)}, bf16[4096,128]{1,0:T(8,128)(2,1)S(1)}, u32[]{:S(2)}, u32[]{:S(2)}) collective-permute-start(bf16[4096,128]{1,0:T(8,128)(2,1)S(1)} %multiply_convert_fusion), channel_id=1, source_target_pairs={{0,2},{2,4},{4,6},{6,8},{8,10},{10,12},{12,14},{1,3},{3,5},{5,7},{... | collective-permute-start | bytes 3145736 | tf_op jit(solution)/shard_map/ppermute | solution.py:20
  5.3 0.0 copy-done.2
  5.3 0.0 copy-done.1
  5.3 0.2 exponential_bitcast_fusion
  5.5 0.8 copy.11
  6.3 0.0 copy-done.3
  6.3 2.0 %copy.10.g_ref = f32[4096,1]{1,0:T(8,128)} copy(f32[4096,1]{0,1:T(1,128)S(1)} %bitcast.33) | data formatting | bytes 32768 | tf_op jit(solution)/shard_map/broadcast_in_dim | solution.py:180
  8.2 21.3 %collective-permute-done.rim_ref = bf16[4096,128]{1,0:T(8,128)(2,1)S(1)} collective-permute-done((bf16[4096,128]{1,0:T(8,128)(2,1)S(1)}, bf16[4096,128]{1,0:T(8,128)(2,1)S(1)}, u32[]{:S(2)}, u32[]{:S(2)}) %collective-permute-start) | collective-permute-done | bytes 1048608 | tf_op jit(solution)/shard_map/ppermute | solution.py:20
  29.6 0.0 copy-start
  29.6 1.0 %copy-done = bf16[4096,128]{1,0:T(8,128)(2,1)} copy-done((bf16[4096,128]{1,0:T(8,128)(2,1)}, bf16[4096,128]{1,0:T(8,128)(2,1)S(1)}, u32[]{:S(2)}) %copy-start) | copy-done | bytes 1048600
  30.5 7.9 %shard_map.91 = (f32[4096,128]{1,0:T(8,128)}, f32[1,128]{1,0:T(1,128)}) custom-call(bf16[4096,128]{1,0:T(8,128)(2,1)} %x_ref.1, bf16[4096,128]{1,0:T(8,128)(2,1)} %gm_ref.1, bf16[4096,128]{1,0:T(8,128)(2,1)} %km_ref.1, bf16[4096,128]{1,0:T(8,128)(2,1)} %copy-done, bf16[256,128]{1,0:T(8,128)(2,1)} %taps_ref.1), custom_call_target="tpu_custom_call" | custom-call | tf_op jit(solution)/shard_map/pallas_call | solution.py:58
  38.5 2.6 %psum.7 = f32[1,128]{1,0:T(1,128)S(1)} all-reduce(f32[1,128]{1,0:T(1,128)} %get-tuple-element.10), channel_id=1, replica_groups=mesh['groups'=2,'context'=8,'tensor'=2] {'tensor'}, use_global_device_ids=true, to_apply=%region_0.0 | all-reduce | flops 128 | bytes 1024 | tf_op jit(solution)/shard_map/psum | solution.py:178
  41.0 0.6 add_rsqrt_fusion.r_ref
  41.6 6.7 %shard_map.92 = (bf16[16,4,8,128]{3,2,1,0:T(8,128)(2,1)}, f32[4096,128]{1,0:T(8,128)}) custom-call(f32[4096,128]{1,0:T(8,128)} %get-tuple-element.9.am_ref, bf16[4096,128]{1,0:T(8,128)(2,1)} %kl_ref.1, f32[4096,1]{1,0:T(8,128)} %copy.10.g_ref, f32[1,128]{1,0:T(1,128)} %add_rsqrt_fusion.r_ref, f32[16,4,8,128]{3,2,1,0:T(8,128)} %bitcast.26), custom_call_target="tpu_custom_call" | custom-call | tf_op jit(solution)/shard_map/pallas_call | solution.py:129
  48.4 1.3 %collective-permute-start.2 = (bf16[16,4,8,128]{3,2,1,0:T(8,128)(2,1)}, bf16[16,4,8,128]{3,2,1,0:T(8,128)(2,1)S(1)}, u32[]{:S(2)}, u32[]{:S(2)}) collective-permute-start(bf16[16,4,8,128]{3,2,1,0:T(8,128)(2,1)} %get-tuple-element.12), channel_id=1, source_target_pairs={{0,4},{2,6},{4,8},{6,10},{8,12},{10,14},{1,5},{3,7},{5,9},{7,11},{... | collective-permute-start | bytes 393224 | tf_op jit(solution)/shard_map/ppermute | solution.py:20
  49.6 2.5 %collective-permute-start.1 = (bf16[16,4,8,128]{3,2,1,0:T(8,128)(2,1)}, bf16[16,4,8,128]{3,2,1,0:T(8,128)(2,1)S(1)}, u32[]{:S(2)}, u32[]{:S(2)}) collective-permute-start(bf16[16,4,8,128]{3,2,1,0:T(8,128)(2,1)} %get-tuple-element.12), channel_id=1, source_target_pairs={{0,2},{2,4},{4,6},{6,8},{8,10},{10,12},{12,14},{1,3},{3,5},{5,7},{... | collective-permute-start | bytes 393224 | tf_op jit(solution)/shard_map/ppermute | solution.py:20
  52.1 0.1 copy.13
  52.2 3.8 %collective-permute-done.2 = bf16[16,4,8,128]{3,2,1,0:T(8,128)(2,1)S(1)} collective-permute-done((bf16[16,4,8,128]{3,2,1,0:T(8,128)(2,1)}, bf16[16,4,8,128]{3,2,1,0:T(8,128)(2,1)S(1)}, u32[]{:S(2)}, u32[]{:S(2)}) %collective-permute-start.2) | collective-permute-done | bytes 131104 | tf_op jit(solution)/shard_map/ppermute | solution.py:20
  56.0 2.8 %collective-permute-done.1 = bf16[16,4,8,128]{3,2,1,0:T(8,128)(2,1)S(1)} collective-permute-done((bf16[16,4,8,128]{3,2,1,0:T(8,128)(2,1)}, bf16[16,4,8,128]{3,2,1,0:T(8,128)(2,1)S(1)}, u32[]{:S(2)}, u32[]{:S(2)}) %collective-permute-start.1) | collective-permute-done | bytes 131104 | tf_op jit(solution)/shard_map/ppermute | solution.py:20
  58.9 1.3 %collective-permute-start.3 = (bf16[16,4,8,128]{3,2,1,0:T(8,128)(2,1)S(1)}, bf16[16,4,8,128]{3,2,1,0:T(8,128)(2,1)S(1)}, u32[]{:S(2)}, u32[]{:S(2)}) collective-permute-start(bf16[16,4,8,128]{3,2,1,0:T(8,128)(2,1)S(1)} %fusion), channel_id=1, source_target_pairs={{0,4},{2,6},{4,8},{6,10},{8,12},{10,14},{1,5},{3,7},{5,9},{7,11},{... | collective-permute-start | bytes 393224 | tf_op jit(solution)/shard_map/ppermute | solution.py:20
  60.2 0.1 copy.14
  60.3 5.5 %collective-permute-done.3 = bf16[16,4,8,128]{3,2,1,0:T(8,128)(2,1)S(1)} collective-permute-done((bf16[16,4,8,128]{3,2,1,0:T(8,128)(2,1)S(1)}, bf16[16,4,8,128]{3,2,1,0:T(8,128)(2,1)S(1)}, u32[]{:S(2)}, u32[]{:S(2)}) %collective-permute-start.3) | collective-permute-done | bytes 131104 | tf_op jit(solution)/shard_map/ppermute | solution.py:20
  65.8 0.1 fusion.1
  65.8 1.3 %collective-permute-start.4 = (bf16[16,4,8,128]{3,2,1,0:T(8,128)(2,1)S(1)}, bf16[16,4,8,128]{3,2,1,0:T(8,128)(2,1)S(1)}, u32[]{:S(2)}, u32[]{:S(2)}) collective-permute-start(bf16[16,4,8,128]{3,2,1,0:T(8,128)(2,1)S(1)} %get-tuple-element.13), channel_id=1, source_target_pairs={{0,8},{2,10},{4,12},{6,14},{1,9},{3,11},{5,13},{7,15},{16,24},{18,... | collective-permute-start | bytes 393224 | tf_op jit(solution)/shard_map/ppermute | solution.py:20
  67.1 0.1 copy.15
  67.2 0.7 copy.12
  68.0 7.3 %collective-permute-done.4 = bf16[16,4,8,128]{3,2,1,0:T(8,128)(2,1)S(1)} collective-permute-done((bf16[16,4,8,128]{3,2,1,0:T(8,128)(2,1)S(1)}, bf16[16,4,8,128]{3,2,1,0:T(8,128)(2,1)S(1)}, u32[]{:S(2)}, u32[]{:S(2)}) %collective-permute-start.4) | collective-permute-done | bytes 131104 | tf_op jit(solution)/shard_map/ppermute | solution.py:20
  75.2 0.8 multiply_add_fusion.h0_ref
  76.0 7.8 %shard_map.93 = bf16[4096,128]{1,0:T(8,128)(2,1)} custom-call(f32[4096,128]{1,0:T(8,128)} %get-tuple-element.9.am_ref, f32[4096,128]{1,0:T(8,128)} %get-tuple-element.11.vt_ref, bf16[4096,128]{1,0:T(8,128)(2,1)} %gl_ref.1, f32[16,4,8,128]{3,2,1,0:T(8,128)} %bitcast.27, f32[16,4,8,128]{3,2,1,0:T(8,128)} %bitcast.30, f32[16,4,8,128]{3,2,1,0:T(8,128)} %multiply_add_fusion.h0_ref), custom_call_target="tpu_custom_call" | custom-call | tf_op jit(solution)/shard_map/pallas_call | solution.py:145
  (1 shorter events, 0.0 us)
Async XLA Ops:
  0.0 5.3 %copy-start.2 = (f32[4096,16]{0,1:T(8,128)S(1)}, f32[4096,16]{0,1:T(8,128)}, u32[]{:S(2)}) copy-start(f32[4096,16]{0,1:T(8,128)} %param.16) | copy-start | bytes 786436
  0.0 5.3 %copy-start.1 = (f32[4096,16]{0,1:T(8,128)S(1)}, f32[4096,16]{0,1:T(8,128)}, u32[]{:S(2)}) copy-start(f32[4096,16]{0,1:T(8,128)} %param.15) | copy-start | bytes 786436
  0.0 6.3 %copy-start.3 = (f32[4096]{0:T(1024)S(1)}, f32[4096]{0:T(1024)}, u32[]{:S(2)}) copy-start(f32[4096]{0:T(1024)} %param.17) | copy-start | bytes 49156
  1.9 27.7 %collective-permute-start = (bf16[4096,128]{1,0:T(8,128)(2,1)S(1)}, bf16[4096,128]{1,0:T(8,128)(2,1)S(1)}, u32[]{:S(2)}, u32[]{:S(2)}) collective-permute-start(bf16[4096,128]{1,0:T(8,128)(2,1)S(1)} %multiply_convert_fusion), channel_id=1, source_target_pairs={{0,2},{2,4},{4,6},{6,8},{8,10},{10,12},{12,14},{1,3},{3,5},{5,7},{... | collective-permute-start | bytes 3145736 | tf_op jit(solution)/shard_map/ppermute | solution.py:20
  29.6 1.0 %copy-start = (bf16[4096,128]{1,0:T(8,128)(2,1)}, bf16[4096,128]{1,0:T(8,128)(2,1)S(1)}, u32[]{:S(2)}) copy-start(bf16[4096,128]{1,0:T(8,128)(2,1)S(1)} %collective-permute-done.rim_ref) | copy-start | bytes 3145732
  48.4 7.7 %collective-permute-start.2 = (bf16[16,4,8,128]{3,2,1,0:T(8,128)(2,1)}, bf16[16,4,8,128]{3,2,1,0:T(8,128)(2,1)S(1)}, u32[]{:S(2)}, u32[]{:S(2)}) collective-permute-start(bf16[16,4,8,128]{3,2,1,0:T(8,128)(2,1)} %get-tuple-element.12), channel_id=1, source_target_pairs={{0,4},{2,6},{4,8},{6,10},{8,12},{10,14},{1,5},{3,7},{5,9},{7,11},{... | collective-permute-start | bytes 393224 | tf_op jit(solution)/shard_map/ppermute | solution.py:20
  49.6 9.2 %collective-permute-start.1 = (bf16[16,4,8,128]{3,2,1,0:T(8,128)(2,1)}, bf16[16,4,8,128]{3,2,1,0:T(8,128)(2,1)S(1)}, u32[]{:S(2)}, u32[]{:S(2)}) collective-permute-start(bf16[16,4,8,128]{3,2,1,0:T(8,128)(2,1)} %get-tuple-element.12), channel_id=1, source_target_pairs={{0,2},{2,4},{4,6},{6,8},{8,10},{10,12},{12,14},{1,3},{3,5},{5,7},{... | collective-permute-start | bytes 393224 | tf_op jit(solution)/shard_map/ppermute | solution.py:20
  58.9 6.9 %collective-permute-start.3 = (bf16[16,4,8,128]{3,2,1,0:T(8,128)(2,1)S(1)}, bf16[16,4,8,128]{3,2,1,0:T(8,128)(2,1)S(1)}, u32[]{:S(2)}, u32[]{:S(2)}) collective-permute-start(bf16[16,4,8,128]{3,2,1,0:T(8,128)(2,1)S(1)} %fusion), channel_id=1, source_target_pairs={{0,4},{2,6},{4,8},{6,10},{8,12},{10,14},{1,5},{3,7},{5,9},{7,11},{... | collective-permute-start | bytes 393224 | tf_op jit(solution)/shard_map/ppermute | solution.py:20
  65.8 9.4 %collective-permute-start.4 = (bf16[16,4,8,128]{3,2,1,0:T(8,128)(2,1)S(1)}, bf16[16,4,8,128]{3,2,1,0:T(8,128)(2,1)S(1)}, u32[]{:S(2)}, u32[]{:S(2)}) collective-permute-start(bf16[16,4,8,128]{3,2,1,0:T(8,128)(2,1)S(1)} %get-tuple-element.13), channel_id=1, source_target_pairs={{0,8},{2,10},{4,12},{6,14},{1,9},{3,11},{5,13},{7,15},{16,24},{18,... | collective-permute-start | bytes 393224 | tf_op jit(solution)/shard_map/ppermute | solution.py:20

commit v12 on v11

--- a/solution.py
+++ b/solution.py
@@ -52,7 +52,7 @@
 def medium_call(inputs, gate_medium, key_medium, rim, taps):
     channels, length = inputs.shape
     per_group = channels // taps.shape[0]
-    block = 512
+    block = 1024
     tap_block = block // per_group
     big = pl.BlockSpec((block, length), lambda b: (b, 0))
     return pl.pallas_call(

time: 84.6 us -> 82.4 us (0.974)
  Pallas kernels: 22.4 us -> 20.2 us
    pallas_call x1, Pallas kernels: 7.91 us -> 5.77 us  [medium_call(): pl.pallas_call(medium_kernel, grid=(channels // block,), in_specs=[big, b...]
where the time goes in v12:
time: 82.4 us; the launch traced here: 81.6 us
  waiting for transfers between devices  40.7 us (49%)
  Pallas kernels  20.2 us (25%)
  starting transfers between devices  9.76 us (12%)
  local copies, waits for them, and re-layouts  4.63 us (6%)
  other arithmetic  3.55 us (4%)
  blocking collectives  2.57 us (3%)
    ppermute x5, waiting for transfers between devices, shifted(): return lax.ppermute(block, axis, route)  40.7 us
    ppermute x5, starting transfers between devices, shifted(): return lax.ppermute(block, axis, route)  9.76 us
    pallas_call x1, Pallas kernels, output_call(): pl.pallas_call(output_kernel, grid=(channels // TILE,), in_specs=[big, pl...  7.75 us
    pallas_call x1, Pallas kernels, final_state_call(): pl.pallas_call(final_state_kernel, grid=(channels // TILE,), in_specs=[bi...  6.72 us
    pallas_call x1, Pallas kernels, medium_call(): pl.pallas_call(medium_kernel, grid=(channels // block,), in_specs=[big, b...  5.77 us
    unnamed x13, local copies, waits for them, and re-layouts  2.65 us
    psum x1, blocking collectives, on_device(): totals = lax.psum(partial, 'tensor')  2.57 us
    broadcast_in_dim x1, local copies, waits for them, and re-layouts, on_device(): gain = norm_gain[:, None]  1.98 us
  transfers between devices with their start and end apart: 5, of which 5 were waited for; matrix products, arithmetic and copies ran while one was open for 5% of the time, Pallas kernels for 0%

profile of v12, /device:TPU:24, one launch (start us, length us, event | category | flops | bytes accessed | tf_op | source)
XLA Modules:
  0.0 81.6 jit_solution(9443248962260216102)
XLA Ops:
  0.0 0.0 copy-start.2
  0.0 0.0 copy-start.1
  0.0 0.0 copy-start.3
  0.0 1.9 %multiply_convert_fusion = bf16[4096,128]{1,0:T(8,128)(2,1)S(1)} fusion(bf16[4096,128]{1,0:T(8,128)(2,1)} %x_ref.1, bf16[4096,128]{1,0:T(8,128)(2,1)} %km_ref.1), kind=kLoop, calls=%fused_computation | loop fusion | flops 2097152 | bytes 3145728 | tf_op jit(solution)/shard_map/convert_element_type | solution.py:175
  1.9 3.4 %collective-permute-start = (bf16[4096,128]{1,0:T(8,128)(2,1)S(1)}, bf16[4096,128]{1,0:T(8,128)(2,1)S(1)}, u32[]{:S(2)}, u32[]{:S(2)}) collective-permute-start(bf16[4096,128]{1,0:T(8,128)(2,1)S(1)} %multiply_convert_fusion), channel_id=1, source_target_pairs={{0,2},{2,4},{4,6},{6,8},{8,10},{10,12},{12,14},{1,3},{3,5},{5,7},{... | collective-permute-start | bytes 3145736 | tf_op jit(solution)/shard_map/ppermute | solution.py:20
  5.3 0.0 copy-done.2
  5.3 0.0 copy-done.1
  5.3 0.2 exponential_bitcast_fusion
  5.5 0.8 copy.11
  6.3 0.0 copy-done.3
  6.3 2.0 %copy.10.g_ref = f32[4096,1]{1,0:T(8,128)} copy(f32[4096,1]{0,1:T(1,128)S(1)} %bitcast.33) | data formatting | bytes 32768 | tf_op jit(solution)/shard_map/broadcast_in_dim | solution.py:180
  8.2 21.3 %collective-permute-done.rim_ref = bf16[4096,128]{1,0:T(8,128)(2,1)S(1)} collective-permute-done((bf16[4096,128]{1,0:T(8,128)(2,1)S(1)}, bf16[4096,128]{1,0:T(8,128)(2,1)S(1)}, u32[]{:S(2)}, u32[]{:S(2)}) %collective-permute-start) | collective-permute-done | bytes 1048608 | tf_op jit(solution)/shard_map/ppermute | solution.py:20
  29.6 0.0 copy-start
  29.6 1.0 %copy-done = bf16[4096,128]{1,0:T(8,128)(2,1)} copy-done((bf16[4096,128]{1,0:T(8,128)(2,1)}, bf16[4096,128]{1,0:T(8,128)(2,1)S(1)}, u32[]{:S(2)}) %copy-start) | copy-done | bytes 1048600
  30.5 5.8 %shard_map.91 = (f32[4096,128]{1,0:T(8,128)}, f32[1,128]{1,0:T(1,128)}) custom-call(bf16[4096,128]{1,0:T(8,128)(2,1)} %x_ref.1, bf16[4096,128]{1,0:T(8,128)(2,1)} %gm_ref.1, bf16[4096,128]{1,0:T(8,128)(2,1)} %km_ref.1, bf16[4096,128]{1,0:T(8,128)(2,1)} %copy-done, bf16[256,128]{1,0:T(8,128)(2,1)} %taps_ref.1), custom_call_target="tpu_custom_call" | custom-call | tf_op jit(solution)/shard_map/pallas_call | solution.py:58
  36.3 2.6 %psum.7 = f32[1,128]{1,0:T(1,128)S(1)} all-reduce(f32[1,128]{1,0:T(1,128)} %get-tuple-element.10), channel_id=1, replica_groups=mesh['groups'=2,'context'=8,'tensor'=2] {'tensor'}, use_global_device_ids=true, to_apply=%region_0.0 | all-reduce | flops 128 | bytes 1024 | tf_op jit(solution)/shard_map/psum | solution.py:178
  38.9 0.6 add_rsqrt_fusion.r_ref
  39.5 6.7 %shard_map.92 = (bf16[16,4,8,128]{3,2,1,0:T(8,128)(2,1)}, f32[4096,128]{1,0:T(8,128)}) custom-call(f32[4096,128]{1,0:T(8,128)} %get-tuple-element.9.am_ref, bf16[4096,128]{1,0:T(8,128)(2,1)} %kl_ref.1, f32[4096,1]{1,0:T(8,128)} %copy.10.g_ref, f32[1,128]{1,0:T(1,128)} %add_rsqrt_fusion.r_ref, f32[16,4,8,128]{3,2,1,0:T(8,128)} %bitcast.26), custom_call_target="tpu_custom_call" | custom-call | tf_op jit(solution)/shard_map/pallas_call | solution.py:129
  46.2 1.3 %collective-permute-start.2 = (bf16[16,4,8,128]{3,2,1,0:T(8,128)(2,1)}, bf16[16,4,8,128]{3,2,1,0:T(8,128)(2,1)S(1)}, u32[]{:S(2)}, u32[]{:S(2)}) collective-permute-start(bf16[16,4,8,128]{3,2,1,0:T(8,128)(2,1)} %get-tuple-element.12), channel_id=1, source_target_pairs={{0,4},{2,6},{4,8},{6,10},{8,12},{10,14},{1,5},{3,7},{5,9},{7,11},{... | collective-permute-start | bytes 393224 | tf_op jit(solution)/shard_map/ppermute | solution.py:20
  47.5 2.5 %collective-permute-start.1 = (bf16[16,4,8,128]{3,2,1,0:T(8,128)(2,1)}, bf16[16,4,8,128]{3,2,1,0:T(8,128)(2,1)S(1)}, u32[]{:S(2)}, u32[]{:S(2)}) collective-permute-start(bf16[16,4,8,128]{3,2,1,0:T(8,128)(2,1)} %get-tuple-element.12), channel_id=1, source_target_pairs={{0,2},{2,4},{4,6},{6,8},{8,10},{10,12},{12,14},{1,3},{3,5},{5,7},{... | collective-permute-start | bytes 393224 | tf_op jit(solution)/shard_map/ppermute | solution.py:20
  50.0 0.1 copy.13
  50.1 3.8 %collective-permute-done.2 = bf16[16,4,8,128]{3,2,1,0:T(8,128)(2,1)S(1)} collective-permute-done((bf16[16,4,8,128]{3,2,1,0:T(8,128)(2,1)}, bf16[16,4,8,128]{3,2,1,0:T(8,128)(2,1)S(1)}, u32[]{:S(2)}, u32[]{:S(2)}) %collective-permute-start.2) | collective-permute-done | bytes 131104 | tf_op jit(solution)/shard_map/ppermute | solution.py:20
  53.9 2.8 %collective-permute-done.1 = bf16[16,4,8,128]{3,2,1,0:T(8,128)(2,1)S(1)} collective-permute-done((bf16[16,4,8,128]{3,2,1,0:T(8,128)(2,1)}, bf16[16,4,8,128]{3,2,1,0:T(8,128)(2,1)S(1)}, u32[]{:S(2)}, u32[]{:S(2)}) %collective-permute-start.1) | collective-permute-done | bytes 131104 | tf_op jit(solution)/shard_map/ppermute | solution.py:20
  56.8 1.3 %collective-permute-start.3 = (bf16[16,4,8,128]{3,2,1,0:T(8,128)(2,1)S(1)}, bf16[16,4,8,128]{3,2,1,0:T(8,128)(2,1)S(1)}, u32[]{:S(2)}, u32[]{:S(2)}) collective-permute-start(bf16[16,4,8,128]{3,2,1,0:T(8,128)(2,1)S(1)} %fusion), channel_id=1, source_target_pairs={{0,4},{2,6},{4,8},{6,10},{8,12},{10,14},{1,5},{3,7},{5,9},{7,11},{... | collective-permute-start | bytes 393224 | tf_op jit(solution)/shard_map/ppermute | solution.py:20
  58.1 0.1 copy.14
  58.1 5.5 %collective-permute-done.3 = bf16[16,4,8,128]{3,2,1,0:T(8,128)(2,1)S(1)} collective-permute-done((bf16[16,4,8,128]{3,2,1,0:T(8,128)(2,1)S(1)}, bf16[16,4,8,128]{3,2,1,0:T(8,128)(2,1)S(1)}, u32[]{:S(2)}, u32[]{:S(2)}) %collective-permute-start.3) | collective-permute-done | bytes 131104 | tf_op jit(solution)/shard_map/ppermute | solution.py:20
  63.6 0.1 fusion.1
  63.7 1.3 %collective-permute-start.4 = (bf16[16,4,8,128]{3,2,1,0:T(8,128)(2,1)S(1)}, bf16[16,4,8,128]{3,2,1,0:T(8,128)(2,1)S(1)}, u32[]{:S(2)}, u32[]{:S(2)}) collective-permute-start(bf16[16,4,8,128]{3,2,1,0:T(8,128)(2,1)S(1)} %get-tuple-element.13), channel_id=1, source_target_pairs={{0,8},{2,10},{4,12},{6,14},{1,9},{3,11},{5,13},{7,15},{16,24},{18,... | collective-permute-start | bytes 393224 | tf_op jit(solution)/shard_map/ppermute | solution.py:20
  65.0 0.1 copy.15
  65.1 0.7 copy.12
  65.8 7.3 %collective-permute-done.4 = bf16[16,4,8,128]{3,2,1,0:T(8,128)(2,1)S(1)} collective-permute-done((bf16[16,4,8,128]{3,2,1,0:T(8,128)(2,1)S(1)}, bf16[16,4,8,128]{3,2,1,0:T(8,128)(2,1)S(1)}, u32[]{:S(2)}, u32[]{:S(2)}) %collective-permute-start.4) | collective-permute-done | bytes 131104 | tf_op jit(solution)/shard_map/ppermute | solution.py:20
  73.1 0.8 multiply_add_fusion.h0_ref
  73.9 7.8 %shard_map.93 = bf16[4096,128]{1,0:T(8,128)(2,1)} custom-call(f32[4096,128]{1,0:T(8,128)} %get-tuple-element.9.am_ref, f32[4096,128]{1,0:T(8,128)} %get-tuple-element.11.vt_ref, bf16[4096,128]{1,0:T(8,128)(2,1)} %gl_ref.1, f32[16,4,8,128]{3,2,1,0:T(8,128)} %bitcast.27, f32[16,4,8,128]{3,2,1,0:T(8,128)} %bitcast.30, f32[16,4,8,128]{3,2,1,0:T(8,128)} %multiply_add_fusion.h0_ref), custom_call_target="tpu_custom_call" | custom-call | tf_op jit(solution)/shard_map/pallas_call | solution.py:145
  (1 shorter events, 0.0 us)
Async XLA Ops:
  0.0 5.3 %copy-start.2 = (f32[4096,16]{0,1:T(8,128)S(1)}, f32[4096,16]{0,1:T(8,128)}, u32[]{:S(2)}) copy-start(f32[4096,16]{0,1:T(8,128)} %param.16) | copy-start | bytes 786436
  0.0 5.3 %copy-start.1 = (f32[4096,16]{0,1:T(8,128)S(1)}, f32[4096,16]{0,1:T(8,128)}, u32[]{:S(2)}) copy-start(f32[4096,16]{0,1:T(8,128)} %param.15) | copy-start | bytes 786436
  0.0 6.3 %copy-start.3 = (f32[4096]{0:T(1024)S(1)}, f32[4096]{0:T(1024)}, u32[]{:S(2)}) copy-start(f32[4096]{0:T(1024)} %param.17) | copy-start | bytes 49156
  1.9 27.7 %collective-permute-start = (bf16[4096,128]{1,0:T(8,128)(2,1)S(1)}, bf16[4096,128]{1,0:T(8,128)(2,1)S(1)}, u32[]{:S(2)}, u32[]{:S(2)}) collective-permute-start(bf16[4096,128]{1,0:T(8,128)(2,1)S(1)} %multiply_convert_fusion), channel_id=1, source_target_pairs={{0,2},{2,4},{4,6},{6,8},{8,10},{10,12},{12,14},{1,3},{3,5},{5,7},{... | collective-permute-start | bytes 3145736 | tf_op jit(solution)/shard_map/ppermute | solution.py:20
  29.6 1.0 %copy-start = (bf16[4096,128]{1,0:T(8,128)(2,1)}, bf16[4096,128]{1,0:T(8,128)(2,1)S(1)}, u32[]{:S(2)}) copy-start(bf16[4096,128]{1,0:T(8,128)(2,1)S(1)} %collective-permute-done.rim_ref) | copy-start | bytes 3145732
  46.2 7.7 %collective-permute-start.2 = (bf16[16,4,8,128]{3,2,1,0:T(8,128)(2,1)}, bf16[16,4,8,128]{3,2,1,0:T(8,128)(2,1)S(1)}, u32[]{:S(2)}, u32[]{:S(2)}) collective-permute-start(bf16[16,4,8,128]{3,2,1,0:T(8,128)(2,1)} %get-tuple-element.12), channel_id=1, source_target_pairs={{0,4},{2,6},{4,8},{6,10},{8,12},{10,14},{1,5},{3,7},{5,9},{7,11},{... | collective-permute-start | bytes 393224 | tf_op jit(solution)/shard_map/ppermute | solution.py:20
  47.5 9.2 %collective-permute-start.1 = (bf16[16,4,8,128]{3,2,1,0:T(8,128)(2,1)}, bf16[16,4,8,128]{3,2,1,0:T(8,128)(2,1)S(1)}, u32[]{:S(2)}, u32[]{:S(2)}) collective-permute-start(bf16[16,4,8,128]{3,2,1,0:T(8,128)(2,1)} %get-tuple-element.12), channel_id=1, source_target_pairs={{0,2},{2,4},{4,6},{6,8},{8,10},{10,12},{12,14},{1,3},{3,5},{5,7},{... | collective-permute-start | bytes 393224 | tf_op jit(solution)/shard_map/ppermute | solution.py:20
  56.8 6.9 %collective-permute-start.3 = (bf16[16,4,8,128]{3,2,1,0:T(8,128)(2,1)S(1)}, bf16[16,4,8,128]{3,2,1,0:T(8,128)(2,1)S(1)}, u32[]{:S(2)}, u32[]{:S(2)}) collective-permute-start(bf16[16,4,8,128]{3,2,1,0:T(8,128)(2,1)S(1)} %fusion), channel_id=1, source_target_pairs={{0,4},{2,6},{4,8},{6,10},{8,12},{10,14},{1,5},{3,7},{5,9},{7,11},{... | collective-permute-start | bytes 393224 | tf_op jit(solution)/shard_map/ppermute | solution.py:20
  63.7 9.4 %collective-permute-start.4 = (bf16[16,4,8,128]{3,2,1,0:T(8,128)(2,1)S(1)}, bf16[16,4,8,128]{3,2,1,0:T(8,128)(2,1)S(1)}, u32[]{:S(2)}, u32[]{:S(2)}) collective-permute-start(bf16[16,4,8,128]{3,2,1,0:T(8,128)(2,1)S(1)} %get-tuple-element.13), channel_id=1, source_target_pairs={{0,8},{2,10},{4,12},{6,14},{1,9},{3,11},{5,13},{7,15},{16,24},{18,... | collective-permute-start | bytes 393224 | tf_op jit(solution)/shard_map/ppermute | solution.py:20

commit v13 on v12

--- a/solution.py
+++ b/solution.py
@@ -52,7 +52,7 @@
 def medium_call(inputs, gate_medium, key_medium, rim, taps):
     channels, length = inputs.shape
     per_group = channels // taps.shape[0]
-    block = 1024
+    block = 2048
     tap_block = block // per_group
     big = pl.BlockSpec((block, length), lambda b: (b, 0))
     return pl.pallas_call(

time: 82.4 us -> 81.8 us (level)
  no operation moved by 1% of the time
where the time goes in v13:
time: 81.8 us; the launch traced here: 81 us
  waiting for transfers between devices  40.7 us (50%)
  Pallas kernels  19.7 us (24%)
  starting transfers between devices  9.76 us (12%)
  local copies, waits for them, and re-layouts  4.63 us (6%)
  other arithmetic  3.55 us (4%)
  blocking collectives  2.57 us (3%)
    ppermute x5, waiting for transfers between devices, shifted(): return lax.ppermute(block, axis, route)  40.7 us
    ppermute x5, starting transfers between devices, shifted(): return lax.ppermute(block, axis, route)  9.76 us
    pallas_call x1, Pallas kernels, output_call(): pl.pallas_call(output_kernel, grid=(channels // TILE,), in_specs=[big, pl...  7.75 us
    pallas_call x1, Pallas kernels, final_state_call(): pl.pallas_call(final_state_kernel, grid=(channels // TILE,), in_specs=[bi...  6.72 us
    pallas_call x1, Pallas kernels, medium_call(): pl.pallas_call(medium_kernel, grid=(channels // block,), in_specs=[big, b...  5.19 us
    unnamed x13, local copies, waits for them, and re-layouts  2.65 us
    psum x1, blocking collectives, on_device(): totals = lax.psum(partial, 'tensor')  2.57 us
    broadcast_in_dim x1, local copies, waits for them, and re-layouts, on_device(): gain = norm_gain[:, None]  1.98 us
  transfers between devices with their start and end apart: 5, of which 5 were waited for; matrix products, arithmetic and copies ran while one was open for 5% of the time, Pallas kernels for 0%

profile of v13, /device:TPU:24, one launch (start us, length us, event | category | flops | bytes accessed | tf_op | source)
XLA Modules:
  0.0 81.0 jit_solution(246160705261183003)
XLA Ops:
  0.0 0.0 copy-start.2
  0.0 0.0 copy-start.1
  0.0 0.0 copy-start.3
  0.0 1.9 %multiply_convert_fusion = bf16[4096,128]{1,0:T(8,128)(2,1)S(1)} fusion(bf16[4096,128]{1,0:T(8,128)(2,1)} %x_ref.1, bf16[4096,128]{1,0:T(8,128)(2,1)} %km_ref.1), kind=kLoop, calls=%fused_computation | loop fusion | flops 2097152 | bytes 3145728 | tf_op jit(solution)/shard_map/convert_element_type | solution.py:175
  1.9 3.4 %collective-permute-start = (bf16[4096,128]{1,0:T(8,128)(2,1)S(1)}, bf16[4096,128]{1,0:T(8,128)(2,1)S(1)}, u32[]{:S(2)}, u32[]{:S(2)}) collective-permute-start(bf16[4096,128]{1,0:T(8,128)(2,1)S(1)} %multiply_convert_fusion), channel_id=1, source_target_pairs={{0,2},{2,4},{4,6},{6,8},{8,10},{10,12},{12,14},{1,3},{3,5},{5,7},{... | collective-permute-start | bytes 3145736 | tf_op jit(solution)/shard_map/ppermute | solution.py:20
  5.3 0.0 copy-done.2
  5.3 0.0 copy-done.1
  5.3 0.2 exponential_bitcast_fusion
  5.5 0.8 copy.11
  6.3 0.0 copy-done.3
  6.3 2.0 %copy.10.g_ref = f32[4096,1]{1,0:T(8,128)} copy(f32[4096,1]{0,1:T(1,128)S(1)} %bitcast.33) | data formatting | bytes 32768 | tf_op jit(solution)/shard_map/broadcast_in_dim | solution.py:180
  8.2 21.3 %collective-permute-done.rim_ref = bf16[4096,128]{1,0:T(8,128)(2,1)S(1)} collective-permute-done((bf16[4096,128]{1,0:T(8,128)(2,1)S(1)}, bf16[4096,128]{1,0:T(8,128)(2,1)S(1)}, u32[]{:S(2)}, u32[]{:S(2)}) %collective-permute-start) | collective-permute-done | bytes 1048608 | tf_op jit(solution)/shard_map/ppermute | solution.py:20
  29.6 0.0 copy-start
  29.6 1.0 %copy-done = bf16[4096,128]{1,0:T(8,128)(2,1)} copy-done((bf16[4096,128]{1,0:T(8,128)(2,1)}, bf16[4096,128]{1,0:T(8,128)(2,1)S(1)}, u32[]{:S(2)}) %copy-start) | copy-done | bytes 1048600
  30.5 5.2 %shard_map.91 = (f32[4096,128]{1,0:T(8,128)}, f32[1,128]{1,0:T(1,128)}) custom-call(bf16[4096,128]{1,0:T(8,128)(2,1)} %x_ref.1, bf16[4096,128]{1,0:T(8,128)(2,1)} %gm_ref.1, bf16[4096,128]{1,0:T(8,128)(2,1)} %km_ref.1, bf16[4096,128]{1,0:T(8,128)(2,1)} %copy-done, bf16[256,128]{1,0:T(8,128)(2,1)} %taps_ref.1), custom_call_target="tpu_custom_call" | custom-call | tf_op jit(solution)/shard_map/pallas_call | solution.py:58
  35.7 2.6 %psum.7 = f32[1,128]{1,0:T(1,128)S(1)} all-reduce(f32[1,128]{1,0:T(1,128)} %get-tuple-element.10), channel_id=1, replica_groups=mesh['groups'=2,'context'=8,'tensor'=2] {'tensor'}, use_global_device_ids=true, to_apply=%region_0.0 | all-reduce | flops 128 | bytes 1024 | tf_op jit(solution)/shard_map/psum | solution.py:178
  38.3 0.6 add_rsqrt_fusion.r_ref
  38.9 6.7 %shard_map.92 = (bf16[16,4,8,128]{3,2,1,0:T(8,128)(2,1)}, f32[4096,128]{1,0:T(8,128)}) custom-call(f32[4096,128]{1,0:T(8,128)} %get-tuple-element.9.am_ref, bf16[4096,128]{1,0:T(8,128)(2,1)} %kl_ref.1, f32[4096,1]{1,0:T(8,128)} %copy.10.g_ref, f32[1,128]{1,0:T(1,128)} %add_rsqrt_fusion.r_ref, f32[16,4,8,128]{3,2,1,0:T(8,128)} %bitcast.26), custom_call_target="tpu_custom_call" | custom-call | tf_op jit(solution)/shard_map/pallas_call | solution.py:129
  45.6 1.3 %collective-permute-start.2 = (bf16[16,4,8,128]{3,2,1,0:T(8,128)(2,1)}, bf16[16,4,8,128]{3,2,1,0:T(8,128)(2,1)S(1)}, u32[]{:S(2)}, u32[]{:S(2)}) collective-permute-start(bf16[16,4,8,128]{3,2,1,0:T(8,128)(2,1)} %get-tuple-element.12), channel_id=1, source_target_pairs={{0,4},{2,6},{4,8},{6,10},{8,12},{10,14},{1,5},{3,7},{5,9},{7,11},{... | collective-permute-start | bytes 393224 | tf_op jit(solution)/shard_map/ppermute | solution.py:20
  46.9 2.5 %collective-permute-start.1 = (bf16[16,4,8,128]{3,2,1,0:T(8,128)(2,1)}, bf16[16,4,8,128]{3,2,1,0:T(8,128)(2,1)S(1)}, u32[]{:S(2)}, u32[]{:S(2)}) collective-permute-start(bf16[16,4,8,128]{3,2,1,0:T(8,128)(2,1)} %get-tuple-element.12), channel_id=1, source_target_pairs={{0,2},{2,4},{4,6},{6,8},{8,10},{10,12},{12,14},{1,3},{3,5},{5,7},{... | collective-permute-start | bytes 393224 | tf_op jit(solution)/shard_map/ppermute | solution.py:20
  49.4 0.1 copy.13
  49.5 3.8 %collective-permute-done.2 = bf16[16,4,8,128]{3,2,1,0:T(8,128)(2,1)S(1)} collective-permute-done((bf16[16,4,8,128]{3,2,1,0:T(8,128)(2,1)}, bf16[16,4,8,128]{3,2,1,0:T(8,128)(2,1)S(1)}, u32[]{:S(2)}, u32[]{:S(2)}) %collective-permute-start.2) | collective-permute-done | bytes 131104 | tf_op jit(solution)/shard_map/ppermute | solution.py:20
  53.3 2.8 %collective-permute-done.1 = bf16[16,4,8,128]{3,2,1,0:T(8,128)(2,1)S(1)} collective-permute-done((bf16[16,4,8,128]{3,2,1,0:T(8,128)(2,1)}, bf16[16,4,8,128]{3,2,1,0:T(8,128)(2,1)S(1)}, u32[]{:S(2)}, u32[]{:S(2)}) %collective-permute-start.1) | collective-permute-done | bytes 131104 | tf_op jit(solution)/shard_map/ppermute | solution.py:20
  56.2 1.3 %collective-permute-start.3 = (bf16[16,4,8,128]{3,2,1,0:T(8,128)(2,1)S(1)}, bf16[16,4,8,128]{3,2,1,0:T(8,128)(2,1)S(1)}, u32[]{:S(2)}, u32[]{:S(2)}) collective-permute-start(bf16[16,4,8,128]{3,2,1,0:T(8,128)(2,1)S(1)} %fusion), channel_id=1, source_target_pairs={{0,4},{2,6},{4,8},{6,10},{8,12},{10,14},{1,5},{3,7},{5,9},{7,11},{... | collective-permute-start | bytes 393224 | tf_op jit(solution)/shard_map/ppermute | solution.py:20
  57.5 0.1 copy.14
  57.5 5.5 %collective-permute-done.3 = bf16[16,4,8,128]{3,2,1,0:T(8,128)(2,1)S(1)} collective-permute-done((bf16[16,4,8,128]{3,2,1,0:T(8,128)(2,1)S(1)}, bf16[16,4,8,128]{3,2,1,0:T(8,128)(2,1)S(1)}, u32[]{:S(2)}, u32[]{:S(2)}) %collective-permute-start.3) | collective-permute-done | bytes 131104 | tf_op jit(solution)/shard_map/ppermute | solution.py:20
  63.1 0.1 fusion.1
  63.1 1.3 %collective-permute-start.4 = (bf16[16,4,8,128]{3,2,1,0:T(8,128)(2,1)S(1)}, bf16[16,4,8,128]{3,2,1,0:T(8,128)(2,1)S(1)}, u32[]{:S(2)}, u32[]{:S(2)}) collective-permute-start(bf16[16,4,8,128]{3,2,1,0:T(8,128)(2,1)S(1)} %get-tuple-element.13), channel_id=1, source_target_pairs={{0,8},{2,10},{4,12},{6,14},{1,9},{3,11},{5,13},{7,15},{16,24},{18,... | collective-permute-start | bytes 393224 | tf_op jit(solution)/shard_map/ppermute | solution.py:20
  64.4 0.1 copy.15
  64.5 0.7 copy.12
  65.2 7.3 %collective-permute-done.4 = bf16[16,4,8,128]{3,2,1,0:T(8,128)(2,1)S(1)} collective-permute-done((bf16[16,4,8,128]{3,2,1,0:T(8,128)(2,1)S(1)}, bf16[16,4,8,128]{3,2,1,0:T(8,128)(2,1)S(1)}, u32[]{:S(2)}, u32[]{:S(2)}) %collective-permute-start.4) | collective-permute-done | bytes 131104 | tf_op jit(solution)/shard_map/ppermute | solution.py:20
  72.5 0.8 multiply_add_fusion.h0_ref
  73.3 7.8 %shard_map.93 = bf16[4096,128]{1,0:T(8,128)(2,1)} custom-call(f32[4096,128]{1,0:T(8,128)} %get-tuple-element.9.am_ref, f32[4096,128]{1,0:T(8,128)} %get-tuple-element.11.vt_ref, bf16[4096,128]{1,0:T(8,128)(2,1)} %gl_ref.1, f32[16,4,8,128]{3,2,1,0:T(8,128)} %bitcast.27, f32[16,4,8,128]{3,2,1,0:T(8,128)} %bitcast.30, f32[16,4,8,128]{3,2,1,0:T(8,128)} %multiply_add_fusion.h0_ref), custom_call_target="tpu_custom_call" | custom-call | tf_op jit(solution)/shard_map/pallas_call | solution.py:145
  (1 shorter events, 0.0 us)
Async XLA Ops:
  0.0 5.3 %copy-start.2 = (f32[4096,16]{0,1:T(8,128)S(1)}, f32[4096,16]{0,1:T(8,128)}, u32[]{:S(2)}) copy-start(f32[4096,16]{0,1:T(8,128)} %param.16) | copy-start | bytes 786436
  0.0 5.3 %copy-start.1 = (f32[4096,16]{0,1:T(8,128)S(1)}, f32[4096,16]{0,1:T(8,128)}, u32[]{:S(2)}) copy-start(f32[4096,16]{0,1:T(8,128)} %param.15) | copy-start | bytes 786436
  0.0 6.3 %copy-start.3 = (f32[4096]{0:T(1024)S(1)}, f32[4096]{0:T(1024)}, u32[]{:S(2)}) copy-start(f32[4096]{0:T(1024)} %param.17) | copy-start | bytes 49156
  1.9 27.7 %collective-permute-start = (bf16[4096,128]{1,0:T(8,128)(2,1)S(1)}, bf16[4096,128]{1,0:T(8,128)(2,1)S(1)}, u32[]{:S(2)}, u32[]{:S(2)}) collective-permute-start(bf16[4096,128]{1,0:T(8,128)(2,1)S(1)} %multiply_convert_fusion), channel_id=1, source_target_pairs={{0,2},{2,4},{4,6},{6,8},{8,10},{10,12},{12,14},{1,3},{3,5},{5,7},{... | collective-permute-start | bytes 3145736 | tf_op jit(solution)/shard_map/ppermute | solution.py:20
  29.6 1.0 %copy-start = (bf16[4096,128]{1,0:T(8,128)(2,1)}, bf16[4096,128]{1,0:T(8,128)(2,1)S(1)}, u32[]{:S(2)}) copy-start(bf16[4096,128]{1,0:T(8,128)(2,1)S(1)} %collective-permute-done.rim_ref) | copy-start | bytes 3145732
  45.6 7.7 %collective-permute-start.2 = (bf16[16,4,8,128]{3,2,1,0:T(8,128)(2,1)}, bf16[16,4,8,128]{3,2,1,0:T(8,128)(2,1)S(1)}, u32[]{:S(2)}, u32[]{:S(2)}) collective-permute-start(bf16[16,4,8,128]{3,2,1,0:T(8,128)(2,1)} %get-tuple-element.12), channel_id=1, source_target_pairs={{0,4},{2,6},{4,8},{6,10},{8,12},{10,14},{1,5},{3,7},{5,9},{7,11},{... | collective-permute-start | bytes 393224 | tf_op jit(solution)/shard_map/ppermute | solution.py:20
  46.9 9.2 %collective-permute-start.1 = (bf16[16,4,8,128]{3,2,1,0:T(8,128)(2,1)}, bf16[16,4,8,128]{3,2,1,0:T(8,128)(2,1)S(1)}, u32[]{:S(2)}, u32[]{:S(2)}) collective-permute-start(bf16[16,4,8,128]{3,2,1,0:T(8,128)(2,1)} %get-tuple-element.12), channel_id=1, source_target_pairs={{0,2},{2,4},{4,6},{6,8},{8,10},{10,12},{12,14},{1,3},{3,5},{5,7},{... | collective-permute-start | bytes 393224 | tf_op jit(solution)/shard_map/ppermute | solution.py:20
  56.2 6.9 %collective-permute-start.3 = (bf16[16,4,8,128]{3,2,1,0:T(8,128)(2,1)S(1)}, bf16[16,4,8,128]{3,2,1,0:T(8,128)(2,1)S(1)}, u32[]{:S(2)}, u32[]{:S(2)}) collective-permute-start(bf16[16,4,8,128]{3,2,1,0:T(8,128)(2,1)S(1)} %fusion), channel_id=1, source_target_pairs={{0,4},{2,6},{4,8},{6,10},{8,12},{10,14},{1,5},{3,7},{5,9},{7,11},{... | collective-permute-start | bytes 393224 | tf_op jit(solution)/shard_map/ppermute | solution.py:20
  63.1 9.4 %collective-permute-start.4 = (bf16[16,4,8,128]{3,2,1,0:T(8,128)(2,1)S(1)}, bf16[16,4,8,128]{3,2,1,0:T(8,128)(2,1)S(1)}, u32[]{:S(2)}, u32[]{:S(2)}) collective-permute-start(bf16[16,4,8,128]{3,2,1,0:T(8,128)(2,1)S(1)} %get-tuple-element.13), channel_id=1, source_target_pairs={{0,8},{2,10},{4,12},{6,14},{1,9},{3,11},{5,13},{7,15},{16,24},{18,... | collective-permute-start | bytes 393224 | tf_op jit(solution)/shard_map/ppermute | solution.py:20

commit v14 on v13

--- a/solution.py
+++ b/solution.py
@@ -68,69 +68,79 @@
     )(inputs, gate_medium, key_medium, rim, taps)
 
 
-def load_values(am_ref, kl_ref, g_ref, r_ref, vt_ref):
+def load_values(am_ref, kl_ref, g_ref, r_ref, vt_ref, sb):
     r = r_ref[...]
+    length = am_ref.shape[1]
     for i in range(SUB):
-        rows = slice(i * LANE, (i + 1) * LANE)
+        rows = slice(sb * TILE + i * LANE, sb * TILE + (i + 1) * LANE)
         normed = am_ref[rows, :] * r * g_ref[rows, :]
         v = (kl_ref[rows, :].astype(F32) * normed).astype(BF16).astype(F32)
-        vt_ref[pl.ds(i, LANE, stride=SUB), :] = v.T
-
-
-def token_tile(ref, t):
-    return ref[pl.ds(pl.multiple_of(t * SUB, SUB), SUB), :]
+        vt_ref[pl.ds(sb * length * SUB + i, LANE, stride=SUB), :] = v.T
+
+
+def token_tile(ref, base, t):
+    return ref[pl.ds(pl.multiple_of(base + t * SUB, SUB), SUB), :]
 
 
 def final_state_kernel(am_ref, kl_ref, g_ref, r_ref, lam_ref, f_ref, vt_ref):
-    modes = lam_ref.shape[0]
+    modes, subs = lam_ref.shape[0], lam_ref.shape[1]
     length = am_ref.shape[1]
-    load_values(am_ref, kl_ref, g_ref, r_ref, vt_ref)
-    lam = [lam_ref[m] for m in range(modes)]
-
-    def body(t, h):
-        v = token_tile(vt_ref, t)
-        return tuple(lam[m] * h[m] + v for m in range(modes))
-
-    h = lax.fori_loop(0, length, body, tuple(jnp.zeros((SUB, LANE), F32) for _ in range(modes)), unroll=8)
-    for m in range(modes):
-        f_ref[m] = h[m].astype(f_ref.dtype)
+    for sb in range(subs):
+        load_values(am_ref, kl_ref, g_ref, r_ref, vt_ref, sb)
+        lam = [lam_ref[m, sb] for m in range(modes)]
+        base = sb * length * SUB
+
+        def body(t, h):
+            v = token_tile(vt_ref, base, t)
+            return tuple(lam[m] * h[m] + v for m in range(modes))
+
+        h = lax.fori_loop(0, length, body, tuple(jnp.zeros((SUB, LANE), F32) for _ in range(modes)), unroll=8)
+        for m in range(modes):
+            f_ref[m, sb] = h[m].astype(f_ref.dtype)
 
 
 def output_kernel(am_ref, vt_ref, gl_ref, lam_ref, w_ref, h0_ref, out_ref, yt_ref):
-    modes = lam_ref.shape[0]
+    modes, subs = lam_ref.shape[0], lam_ref.shape[1]
     length = am_ref.shape[1]
-    lam = [lam_ref[m] for m in range(modes)]
-    w = [w_ref[m] for m in range(modes)]
-
-    def body(t, h):
-        v = token_tile(vt_ref, t)
-        h = tuple(lam[m] * h[m] + v for m in range(modes))
-        y = w[0] * h[0]
-        for m in range(1, modes):
-            y = y + w[m] * h[m]
-        yt_ref[pl.ds(pl.multiple_of(t * SUB, SUB), SUB), :] = y
-        return h
-
-    lax.fori_loop(0, length, body, tuple(h0_ref[m] for m in range(modes)), unroll=8)
-    for i in range(SUB):
-        rows = slice(i * LANE, (i + 1) * LANE)
-        long_out = yt_ref[pl.ds(i, LANE, stride=SUB), :].T.astype(BF16).astype(F32)
-        out_ref[rows, :] = (am_ref[rows, :] + gl_ref[rows, :].astype(F32) * long_out).astype(BF16)
-
-
-def tiled_spec(lead):
-    return pl.BlockSpec((lead, None, SUB, LANE), lambda b: (0, b, 0, 0))
+    for sb in range(subs):
+        lam = [lam_ref[m, sb] for m in range(modes)]
+        w = [w_ref[m, sb] for m in range(modes)]
+        base = sb * length * SUB
+
+        def body(t, h):
+            v = token_tile(vt_ref, base, t)
+            h = tuple(lam[m] * h[m] + v for m in range(modes))
+            y = w[0] * h[0]
+            for m in range(1, modes):
+                y = y + w[m] * h[m]
+            yt_ref[pl.ds(pl.multiple_of(t * SUB, SUB), SUB), :] = y
+            return h
+
+        lax.fori_loop(0, length, body, tuple(h0_ref[m, sb] for m in range(modes)), unroll=8)
+        for i in range(SUB):
+            rows = slice(sb * TILE + i * LANE, sb * TILE + (i + 1) * LANE)
+            long_out = yt_ref[pl.ds(i, LANE, stride=SUB), :].T.astype(BF16).astype(F32)
+            out_ref[rows, :] = (am_ref[rows, :] + gl_ref[rows, :].astype(F32) * long_out).astype(BF16)
+
+
+SUBS = 2
+
+
+def tiled_spec(lead, subs):
+    return pl.BlockSpec((lead, subs, SUB, LANE), lambda b: (0, b, 0, 0))
 
 
 def final_state_call(am, kl, gain, r, lam):
     channels, length = am.shape
     modes = lam.shape[0]
-    big = pl.BlockSpec((TILE, length), lambda b: (b, 0))
+    subs = min(SUBS, channels // TILE)
+    rows = subs * TILE
+    big = pl.BlockSpec((rows, length), lambda b: (b, 0))
     return pl.pallas_call(
         final_state_kernel,
-        grid=(channels // TILE,),
-        in_specs=[big, big, pl.BlockSpec((TILE, 1), lambda b: (b, 0)), pl.BlockSpec((1, length), lambda b: (0, 0)), tiled_spec(modes)],
-        out_specs=[tiled_spec(modes), pl.BlockSpec((length * SUB, LANE), lambda b: (b, 0))],
+        grid=(channels // rows,),
+        in_specs=[big, big, pl.BlockSpec((rows, 1), lambda b: (b, 0)), pl.BlockSpec((1, length), lambda b: (0, 0)), tiled_spec(modes, subs)],
+        out_specs=[tiled_spec(modes, subs), pl.BlockSpec((subs * length * SUB, LANE), lambda b: (b, 0))],
         out_shape=[
             jax.ShapeDtypeStruct(lam.shape, BF16),
             jax.ShapeDtypeStruct((channels // TILE * length * SUB, LANE), F32),
@@ -141,11 +151,14 @@
 def output_call(am, vt, gl, lam, w, h0):
     channels, length = am.shape
     modes = lam.shape[0]
-    big = pl.BlockSpec((TILE, length), lambda b: (b, 0))
+    subs = min(SUBS, channels // TILE)
+    rows = subs * TILE
+    big = pl.BlockSpec((rows, length), lambda b: (b, 0))
+    tiles = tiled_spec(modes, subs)
     return pl.pallas_call(
         output_kernel,
-        grid=(channels // TILE,),
-        in_specs=[big, pl.BlockSpec((length * SUB, LANE), lambda b: (b, 0)), big, tiled_spec(modes), tiled_spec(modes), tiled_spec(modes)],
+        grid=(channels // rows,),
+        in_specs=[big, pl.BlockSpec((subs * length * SUB, LANE), lambda b: (b, 0)), big, tiles, tiles, tiles],
         out_specs=big,
         out_shape=jax.ShapeDtypeStruct((channels, length), BF16),
         scratch_shapes=[pltpu.VMEM((length * SUB, LANE), F32)],

time: 81.8 us -> 82.1 us (level)
  no operation moved by 1% of the time
where the time goes in v14:
time: 82.1 us; the launch traced here: 81.5 us
  waiting for transfers between devices  40.7 us (50%)
  Pallas kernels  20.1 us (24%)
  starting transfers between devices  9.76 us (12%)
  local copies, waits for them, and re-layouts  4.63 us (6%)
  other arithmetic  3.55 us (4%)
  blocking collectives  2.57 us (3%)
    ppermute x5, waiting for transfers between devices, shifted(): return lax.ppermute(block, axis, route)  40.7 us
    ppermute x5, starting transfers between devices, shifted(): return lax.ppermute(block, axis, route)  9.76 us
    pallas_call x1, Pallas kernels, output_call(): pl.pallas_call(output_kernel, grid=(channels // rows,), in_specs=[big, pl...  8.22 us
    pallas_call x1, Pallas kernels, final_state_call(): pl.pallas_call(final_state_kernel, grid=(channels // rows,), in_specs=[bi...  6.73 us
    pallas_call x1, Pallas kernels, medium_call(): pl.pallas_call(medium_kernel, grid=(channels // block,), in_specs=[big, b...  5.19 us
    unnamed x13, local copies, waits for them, and re-layouts  2.65 us
    psum x1, blocking collectives, on_device(): totals = lax.psum(partial, 'tensor')  2.57 us
    broadcast_in_dim x1, local copies, waits for them, and re-layouts, on_device(): gain = norm_gain[:, None]  1.98 us
  transfers between devices with their start and end apart: 5, of which 5 were waited for; matrix products, arithmetic and copies ran while one was open for 5% of the time, Pallas kernels for 0%

profile of v14, /device:TPU:24, one launch (start us, length us, event | category | flops | bytes accessed | tf_op | source)
XLA Modules:
  0.0 81.5 jit_solution(12970987889018482145)
XLA Ops:
  0.0 0.0 copy-start.2
  0.0 0.0 copy-start.1
  0.0 0.0 copy-start.3
  0.0 1.9 %multiply_convert_fusion = bf16[4096,128]{1,0:T(8,128)(2,1)S(1)} fusion(bf16[4096,128]{1,0:T(8,128)(2,1)} %x_ref.1, bf16[4096,128]{1,0:T(8,128)(2,1)} %km_ref.1), kind=kLoop, calls=%fused_computation | loop fusion | flops 2097152 | bytes 3145728 | tf_op jit(solution)/shard_map/convert_element_type | solution.py:188
  1.9 3.4 %collective-permute-start = (bf16[4096,128]{1,0:T(8,128)(2,1)S(1)}, bf16[4096,128]{1,0:T(8,128)(2,1)S(1)}, u32[]{:S(2)}, u32[]{:S(2)}) collective-permute-start(bf16[4096,128]{1,0:T(8,128)(2,1)S(1)} %multiply_convert_fusion), channel_id=1, source_target_pairs={{0,2},{2,4},{4,6},{6,8},{8,10},{10,12},{12,14},{1,3},{3,5},{5,7},{... | collective-permute-start | bytes 3145736 | tf_op jit(solution)/shard_map/ppermute | solution.py:20
  5.3 0.0 copy-done.2
  5.3 0.0 copy-done.1
  5.3 0.2 exponential_bitcast_fusion
  5.5 0.8 copy.11
  6.3 0.0 copy-done.3
  6.3 2.0 %copy.10.g_ref = f32[4096,1]{1,0:T(8,128)} copy(f32[4096,1]{0,1:T(1,128)S(1)} %bitcast.33) | data formatting | bytes 32768 | tf_op jit(solution)/shard_map/broadcast_in_dim | solution.py:193
  8.2 21.3 %collective-permute-done.rim_ref = bf16[4096,128]{1,0:T(8,128)(2,1)S(1)} collective-permute-done((bf16[4096,128]{1,0:T(8,128)(2,1)S(1)}, bf16[4096,128]{1,0:T(8,128)(2,1)S(1)}, u32[]{:S(2)}, u32[]{:S(2)}) %collective-permute-start) | collective-permute-done | bytes 1048608 | tf_op jit(solution)/shard_map/ppermute | solution.py:20
  29.6 0.0 copy-start
  29.6 1.0 %copy-done = bf16[4096,128]{1,0:T(8,128)(2,1)} copy-done((bf16[4096,128]{1,0:T(8,128)(2,1)}, bf16[4096,128]{1,0:T(8,128)(2,1)S(1)}, u32[]{:S(2)}) %copy-start) | copy-done | bytes 1048600
  30.5 5.2 %shard_map.91 = (f32[4096,128]{1,0:T(8,128)}, f32[1,128]{1,0:T(1,128)}) custom-call(bf16[4096,128]{1,0:T(8,128)(2,1)} %x_ref.1, bf16[4096,128]{1,0:T(8,128)(2,1)} %gm_ref.1, bf16[4096,128]{1,0:T(8,128)(2,1)} %km_ref.1, bf16[4096,128]{1,0:T(8,128)(2,1)} %copy-done, bf16[256,128]{1,0:T(8,128)(2,1)} %taps_ref.1), custom_call_target="tpu_custom_call" | custom-call | tf_op jit(solution)/shard_map/pallas_call | solution.py:58
  35.7 2.6 %psum.7 = f32[1,128]{1,0:T(1,128)S(1)} all-reduce(f32[1,128]{1,0:T(1,128)} %get-tuple-element.10), channel_id=1, replica_groups=mesh['groups'=2,'context'=8,'tensor'=2] {'tensor'}, use_global_device_ids=true, to_apply=%region_0.0 | all-reduce | flops 128 | bytes 1024 | tf_op jit(solution)/shard_map/psum | solution.py:191
  38.3 0.6 add_rsqrt_fusion.r_ref
  38.9 6.7 %shard_map.92 = (bf16[16,4,8,128]{3,2,1,0:T(8,128)(2,1)}, f32[4096,128]{1,0:T(8,128)}) custom-call(f32[4096,128]{1,0:T(8,128)} %get-tuple-element.9.am_ref, bf16[4096,128]{1,0:T(8,128)(2,1)} %kl_ref.1, f32[4096,1]{1,0:T(8,128)} %copy.10.g_ref, f32[1,128]{1,0:T(1,128)} %add_rsqrt_fusion.r_ref, f32[16,4,8,128]{3,2,1,0:T(8,128)} %bitcast.26), custom_call_target="tpu_custom_call" | custom-call | tf_op jit(solution)/shard_map/pallas_call | solution.py:139
  45.6 1.3 %collective-permute-start.2 = (bf16[16,4,8,128]{3,2,1,0:T(8,128)(2,1)}, bf16[16,4,8,128]{3,2,1,0:T(8,128)(2,1)S(1)}, u32[]{:S(2)}, u32[]{:S(2)}) collective-permute-start(bf16[16,4,8,128]{3,2,1,0:T(8,128)(2,1)} %get-tuple-element.12), channel_id=1, source_target_pairs={{0,4},{2,6},{4,8},{6,10},{8,12},{10,14},{1,5},{3,7},{5,9},{7,11},{... | collective-permute-start | bytes 393224 | tf_op jit(solution)/shard_map/ppermute | solution.py:20
  46.9 2.5 %collective-permute-start.1 = (bf16[16,4,8,128]{3,2,1,0:T(8,128)(2,1)}, bf16[16,4,8,128]{3,2,1,0:T(8,128)(2,1)S(1)}, u32[]{:S(2)}, u32[]{:S(2)}) collective-permute-start(bf16[16,4,8,128]{3,2,1,0:T(8,128)(2,1)} %get-tuple-element.12), channel_id=1, source_target_pairs={{0,2},{2,4},{4,6},{6,8},{8,10},{10,12},{12,14},{1,3},{3,5},{5,7},{... | collective-permute-start | bytes 393224 | tf_op jit(solution)/shard_map/ppermute | solution.py:20
  49.4 0.1 copy.13
  49.5 3.8 %collective-permute-done.2 = bf16[16,4,8,128]{3,2,1,0:T(8,128)(2,1)S(1)} collective-permute-done((bf16[16,4,8,128]{3,2,1,0:T(8,128)(2,1)}, bf16[16,4,8,128]{3,2,1,0:T(8,128)(2,1)S(1)}, u32[]{:S(2)}, u32[]{:S(2)}) %collective-permute-start.2) | collective-permute-done | bytes 131104 | tf_op jit(solution)/shard_map/ppermute | solution.py:20
  53.3 2.8 %collective-permute-done.1 = bf16[16,4,8,128]{3,2,1,0:T(8,128)(2,1)S(1)} collective-permute-done((bf16[16,4,8,128]{3,2,1,0:T(8,128)(2,1)}, bf16[16,4,8,128]{3,2,1,0:T(8,128)(2,1)S(1)}, u32[]{:S(2)}, u32[]{:S(2)}) %collective-permute-start.1) | collective-permute-done | bytes 131104 | tf_op jit(solution)/shard_map/ppermute | solution.py:20
  56.2 1.3 %collective-permute-start.3 = (bf16[16,4,8,128]{3,2,1,0:T(8,128)(2,1)S(1)}, bf16[16,4,8,128]{3,2,1,0:T(8,128)(2,1)S(1)}, u32[]{:S(2)}, u32[]{:S(2)}) collective-permute-start(bf16[16,4,8,128]{3,2,1,0:T(8,128)(2,1)S(1)} %fusion), channel_id=1, source_target_pairs={{0,4},{2,6},{4,8},{6,10},{8,12},{10,14},{1,5},{3,7},{5,9},{7,11},{... | collective-permute-start | bytes 393224 | tf_op jit(solution)/shard_map/ppermute | solution.py:20
  57.5 0.1 copy.14
  57.6 5.5 %collective-permute-done.3 = bf16[16,4,8,128]{3,2,1,0:T(8,128)(2,1)S(1)} collective-permute-done((bf16[16,4,8,128]{3,2,1,0:T(8,128)(2,1)S(1)}, bf16[16,4,8,128]{3,2,1,0:T(8,128)(2,1)S(1)}, u32[]{:S(2)}, u32[]{:S(2)}) %collective-permute-start.3) | collective-permute-done | bytes 131104 | tf_op jit(solution)/shard_map/ppermute | solution.py:20
  63.1 0.1 fusion.1
  63.1 1.3 %collective-permute-start.4 = (bf16[16,4,8,128]{3,2,1,0:T(8,128)(2,1)S(1)}, bf16[16,4,8,128]{3,2,1,0:T(8,128)(2,1)S(1)}, u32[]{:S(2)}, u32[]{:S(2)}) collective-permute-start(bf16[16,4,8,128]{3,2,1,0:T(8,128)(2,1)S(1)} %get-tuple-element.13), channel_id=1, source_target_pairs={{0,8},{2,10},{4,12},{6,14},{1,9},{3,11},{5,13},{7,15},{16,24},{18,... | collective-permute-start | bytes 393224 | tf_op jit(solution)/shard_map/ppermute | solution.py:20
  64.4 0.1 copy.15
  64.5 0.7 copy.12
  65.3 7.3 %collective-permute-done.4 = bf16[16,4,8,128]{3,2,1,0:T(8,128)(2,1)S(1)} collective-permute-done((bf16[16,4,8,128]{3,2,1,0:T(8,128)(2,1)S(1)}, bf16[16,4,8,128]{3,2,1,0:T(8,128)(2,1)S(1)}, u32[]{:S(2)}, u32[]{:S(2)}) %collective-permute-start.4) | collective-permute-done | bytes 131104 | tf_op jit(solution)/shard_map/ppermute | solution.py:20
  72.5 0.8 multiply_add_fusion.h0_ref
  73.3 8.2 %shard_map.93 = bf16[4096,128]{1,0:T(8,128)(2,1)} custom-call(f32[4096,128]{1,0:T(8,128)} %get-tuple-element.9.am_ref, f32[4096,128]{1,0:T(8,128)} %get-tuple-element.11.vt_ref, bf16[4096,128]{1,0:T(8,128)(2,1)} %gl_ref.1, f32[16,4,8,128]{3,2,1,0:T(8,128)} %bitcast.27, f32[16,4,8,128]{3,2,1,0:T(8,128)} %bitcast.30, f32[16,4,8,128]{3,2,1,0:T(8,128)} %multiply_add_fusion.h0_ref), custom_call_target="tpu_custom_call" | custom-call | tf_op jit(solution)/shard_map/pallas_call | solution.py:158
  (1 shorter events, 0.0 us)
Async XLA Ops:
  0.0 5.3 %copy-start.2 = (f32[4096,16]{0,1:T(8,128)S(1)}, f32[4096,16]{0,1:T(8,128)}, u32[]{:S(2)}) copy-start(f32[4096,16]{0,1:T(8,128)} %param.16) | copy-start | bytes 786436
  0.0 5.3 %copy-start.1 = (f32[4096,16]{0,1:T(8,128)S(1)}, f32[4096,16]{0,1:T(8,128)}, u32[]{:S(2)}) copy-start(f32[4096,16]{0,1:T(8,128)} %param.15) | copy-start | bytes 786436
  0.0 6.3 %copy-start.3 = (f32[4096]{0:T(1024)S(1)}, f32[4096]{0:T(1024)}, u32[]{:S(2)}) copy-start(f32[4096]{0:T(1024)} %param.17) | copy-start | bytes 49156
  1.9 27.7 %collective-permute-start = (bf16[4096,128]{1,0:T(8,128)(2,1)S(1)}, bf16[4096,128]{1,0:T(8,128)(2,1)S(1)}, u32[]{:S(2)}, u32[]{:S(2)}) collective-permute-start(bf16[4096,128]{1,0:T(8,128)(2,1)S(1)} %multiply_convert_fusion), channel_id=1, source_target_pairs={{0,2},{2,4},{4,6},{6,8},{8,10},{10,12},{12,14},{1,3},{3,5},{5,7},{... | collective-permute-start | bytes 3145736 | tf_op jit(solution)/shard_map/ppermute | solution.py:20
  29.6 1.0 %copy-start = (bf16[4096,128]{1,0:T(8,128)(2,1)}, bf16[4096,128]{1,0:T(8,128)(2,1)S(1)}, u32[]{:S(2)}) copy-start(bf16[4096,128]{1,0:T(8,128)(2,1)S(1)} %collective-permute-done.rim_ref) | copy-start | bytes 3145732
  45.6 7.7 %collective-permute-start.2 = (bf16[16,4,8,128]{3,2,1,0:T(8,128)(2,1)}, bf16[16,4,8,128]{3,2,1,0:T(8,128)(2,1)S(1)}, u32[]{:S(2)}, u32[]{:S(2)}) collective-permute-start(bf16[16,4,8,128]{3,2,1,0:T(8,128)(2,1)} %get-tuple-element.12), channel_id=1, source_target_pairs={{0,4},{2,6},{4,8},{6,10},{8,12},{10,14},{1,5},{3,7},{5,9},{7,11},{... | collective-permute-start | bytes 393224 | tf_op jit(solution)/shard_map/ppermute | solution.py:20
  46.9 9.2 %collective-permute-start.1 = (bf16[16,4,8,128]{3,2,1,0:T(8,128)(2,1)}, bf16[16,4,8,128]{3,2,1,0:T(8,128)(2,1)S(1)}, u32[]{:S(2)}, u32[]{:S(2)}) collective-permute-start(bf16[16,4,8,128]{3,2,1,0:T(8,128)(2,1)} %get-tuple-element.12), channel_id=1, source_target_pairs={{0,2},{2,4},{4,6},{6,8},{8,10},{10,12},{12,14},{1,3},{3,5},{5,7},{... | collective-permute-start | bytes 393224 | tf_op jit(solution)/shard_map/ppermute | solution.py:20
  56.2 6.9 %collective-permute-start.3 = (bf16[16,4,8,128]{3,2,1,0:T(8,128)(2,1)S(1)}, bf16[16,4,8,128]{3,2,1,0:T(8,128)(2,1)S(1)}, u32[]{:S(2)}, u32[]{:S(2)}) collective-permute-start(bf16[16,4,8,128]{3,2,1,0:T(8,128)(2,1)S(1)} %fusion), channel_id=1, source_target_pairs={{0,4},{2,6},{4,8},{6,10},{8,12},{10,14},{1,5},{3,7},{5,9},{7,11},{... | collective-permute-start | bytes 393224 | tf_op jit(solution)/shard_map/ppermute | solution.py:20
  63.1 9.4 %collective-permute-start.4 = (bf16[16,4,8,128]{3,2,1,0:T(8,128)(2,1)S(1)}, bf16[16,4,8,128]{3,2,1,0:T(8,128)(2,1)S(1)}, u32[]{:S(2)}, u32[]{:S(2)}) collective-permute-start(bf16[16,4,8,128]{3,2,1,0:T(8,128)(2,1)S(1)} %get-tuple-element.13), channel_id=1, source_target_pairs={{0,8},{2,10},{4,12},{6,14},{1,9},{3,11},{5,13},{7,15},{16,24},{18,... | collective-permute-start | bytes 393224 | tf_op jit(solution)/shard_map/ppermute | solution.py:20

commit v15 on v13

--- a/solution.py
+++ b/solution.py
@@ -96,7 +96,7 @@
         f_ref[m] = h[m].astype(f_ref.dtype)
 
 
-def output_kernel(am_ref, vt_ref, gl_ref, lam_ref, w_ref, h0_ref, out_ref, yt_ref):
+def output_kernel(am_ref, vt_ref, gl_ref, lam_ref, w_ref, base_ref, decay_ref, recv_ref, out_ref, yt_ref):
     modes = lam_ref.shape[0]
     length = am_ref.shape[1]
     lam = [lam_ref[m] for m in range(modes)]
@@ -111,7 +111,8 @@
         yt_ref[pl.ds(pl.multiple_of(t * SUB, SUB), SUB), :] = y
         return h
 
-    lax.fori_loop(0, length, body, tuple(h0_ref[m] for m in range(modes)), unroll=8)
+    h0 = tuple(base_ref[m] + decay_ref[m] * recv_ref[m].astype(F32) for m in range(modes))
+    lax.fori_loop(0, length, body, h0, unroll=8)
     for i in range(SUB):
         rows = slice(i * LANE, (i + 1) * LANE)
         long_out = yt_ref[pl.ds(i, LANE, stride=SUB), :].T.astype(BF16).astype(F32)
@@ -138,18 +139,18 @@
     )(am, kl, gain, r, lam)
 
 
-def output_call(am, vt, gl, lam, w, h0):
+def output_call(am, vt, gl, lam, w, base, decay, recv):
     channels, length = am.shape
     modes = lam.shape[0]
     big = pl.BlockSpec((TILE, length), lambda b: (b, 0))
     return pl.pallas_call(
         output_kernel,
         grid=(channels // TILE,),
-        in_specs=[big, pl.BlockSpec((length * SUB, LANE), lambda b: (b, 0)), big, tiled_spec(modes), tiled_spec(modes), tiled_spec(modes)],
+        in_specs=[big, pl.BlockSpec((length * SUB, LANE), lambda b: (b, 0)), big] + [tiled_spec(modes)] * 5,
         out_specs=big,
         out_shape=jax.ShapeDtypeStruct((channels, length), BF16),
         scratch_shapes=[pltpu.VMEM((length * SUB, LANE), F32)],
-    )(am, vt, gl, lam, w, h0)
+    )(am, vt, gl, lam, w, base, decay, recv)
 
 
 def to_tiles(a):
@@ -190,12 +191,18 @@
         decay = jnp.exp(-length * a_t)
         carried = carried + decay * shifted(sent, "context", 2).astype(F32)
         distance = 2
+    decay = jnp.zeros_like(a_t)
+    received = jnp.zeros(a_t.shape, BF16)
     while distance < lax.axis_size("context"):
-        decay = jnp.exp(-(length * distance) * a_t)
-        carried = carried + decay * shifted(carried.astype(BF16), "context", distance).astype(F32)
+        if distance * 2 < lax.axis_size("context"):
+            decay = jnp.exp(-(length * distance) * a_t)
+            carried = carried + decay * shifted(carried.astype(BF16), "context", distance).astype(F32)
+        else:
+            decay = jnp.exp(-(length * distance) * a_t)
+            received = shifted(carried.astype(BF16), "context", distance)
         distance *= 2
 
-    return output_call(after_medium, vt, gate_long, lam, w, carried)
+    return output_call(after_medium, vt, gate_long, lam, w, carried, decay, received)
 
 
 def solution(mesh):

time: 81.8 us -> 82.3 us (level)
  local copies, waits for them, and re-layouts: 4.63 us -> 5.98 us
    unnamed x13 -> x15, local copies, waits for them, and re-layouts: 2.65 us -> 4.01 us
  transfers between devices with their start and end apart: 5 -> 5, of which waited for: 5 -> 5; matrix products, arithmetic and copies ran while one was open for 5% -> 6% of each run, Pallas kernels for 0% -> 0%
where the time goes in v15:
time: 82.3 us; the launch traced here: 81.6 us
  waiting for transfers between devices  40.1 us (49%)
  Pallas kernels  19.7 us (24%)
  starting transfers between devices  9.75 us (12%)
  local copies, waits for them, and re-layouts  5.98 us (7%)
  other arithmetic  3.42 us (4%)
  blocking collectives  2.57 us (3%)
    ppermute x5, waiting for transfers between devices, shifted(): return lax.ppermute(block, axis, route)  40.1 us
    ppermute x5, starting transfers between devices, shifted(): return lax.ppermute(block, axis, route)  9.75 us
    pallas_call x1, Pallas kernels, output_call(): pl.pallas_call(output_kernel, grid=(channels // TILE,), in_specs=[big, pl...  7.81 us
    pallas_call x1, Pallas kernels, final_state_call(): pl.pallas_call(final_state_kernel, grid=(channels // TILE,), in_specs=[bi...  6.74 us
    pallas_call x1, Pallas kernels, medium_call(): pl.pallas_call(medium_kernel, grid=(channels // block,), in_specs=[big, b...  5.17 us
    unnamed x15, local copies, waits for them, and re-layouts  4.01 us
    psum x1, blocking collectives, on_device(): totals = lax.psum(partial, 'tensor')  2.57 us
    broadcast_in_dim x1, local copies, waits for them, and re-layouts, on_device(): gain = norm_gain[:, None]  1.98 us
  transfers between devices with their start and end apart: 5, of which 5 were waited for; matrix products, arithmetic and copies ran while one was open for 6% of the time, Pallas kernels for 0%

profile of v15, /device:TPU:24, one launch (start us, length us, event | category | flops | bytes accessed | tf_op | source)
XLA Modules:
  0.0 81.6 jit_solution(17559148653632776408)
XLA Ops:
  0.0 0.0 copy-start.2
  0.0 0.0 copy-start.1
  0.0 0.0 copy-start.4
  0.0 1.9 %multiply_convert_fusion = bf16[4096,128]{1,0:T(8,128)(2,1)S(1)} fusion(bf16[4096,128]{1,0:T(8,128)(2,1)} %x_ref.1, bf16[4096,128]{1,0:T(8,128)(2,1)} %km_ref.1), kind=kLoop, calls=%fused_computation | loop fusion | flops 2097152 | bytes 3145728 | tf_op jit(solution)/shard_map/convert_element_type | solution.py:176
  1.9 3.4 %collective-permute-start = (bf16[4096,128]{1,0:T(8,128)(2,1)S(1)}, bf16[4096,128]{1,0:T(8,128)(2,1)S(1)}, u32[]{:S(2)}, u32[]{:S(2)}) collective-permute-start(bf16[4096,128]{1,0:T(8,128)(2,1)S(1)} %multiply_convert_fusion), channel_id=1, source_target_pairs={{0,2},{2,4},{4,6},{6,8},{8,10},{10,12},{12,14},{1,3},{3,5},{5,7},{... | collective-permute-start | bytes 3145736 | tf_op jit(solution)/shard_map/ppermute | solution.py:20
  5.3 0.0 copy-done.2
  5.3 0.0 copy-done.1
  5.3 0.2 exponential_bitcast_fusion
  5.5 0.7 copy.11
  6.2 0.0 copy-done.4
  6.3 2.0 %copy.10.g_ref = f32[4096,1]{1,0:T(8,128)} copy(f32[4096,1]{0,1:T(1,128)S(1)} %bitcast.33) | data formatting | bytes 32768 | tf_op jit(solution)/shard_map/broadcast_in_dim | solution.py:181
  8.2 21.3 %collective-permute-done.rim_ref = bf16[4096,128]{1,0:T(8,128)(2,1)S(1)} collective-permute-done((bf16[4096,128]{1,0:T(8,128)(2,1)S(1)}, bf16[4096,128]{1,0:T(8,128)(2,1)S(1)}, u32[]{:S(2)}, u32[]{:S(2)}) %collective-permute-start) | collective-permute-done | bytes 1048608 | tf_op jit(solution)/shard_map/ppermute | solution.py:20
  29.6 0.0 copy-start
  29.6 1.0 %copy-done = bf16[4096,128]{1,0:T(8,128)(2,1)} copy-done((bf16[4096,128]{1,0:T(8,128)(2,1)}, bf16[4096,128]{1,0:T(8,128)(2,1)S(1)}, u32[]{:S(2)}) %copy-start) | copy-done | bytes 1048600
  30.5 5.2 %shard_map.91 = (f32[4096,128]{1,0:T(8,128)}, f32[1,128]{1,0:T(1,128)}) custom-call(bf16[4096,128]{1,0:T(8,128)(2,1)} %x_ref.1, bf16[4096,128]{1,0:T(8,128)(2,1)} %gm_ref.1, bf16[4096,128]{1,0:T(8,128)(2,1)} %km_ref.1, bf16[4096,128]{1,0:T(8,128)(2,1)} %copy-done, bf16[256,128]{1,0:T(8,128)(2,1)} %taps_ref.1), custom_call_target="tpu_custom_call" | custom-call | tf_op jit(solution)/shard_map/pallas_call | solution.py:58
  35.7 2.6 %psum.7 = f32[1,128]{1,0:T(1,128)S(1)} all-reduce(f32[1,128]{1,0:T(1,128)} %get-tuple-element.10), channel_id=1, replica_groups=mesh['groups'=2,'context'=8,'tensor'=2] {'tensor'}, use_global_device_ids=true, to_apply=%region_0.0 | all-reduce | flops 128 | bytes 1024 | tf_op jit(solution)/shard_map/psum | solution.py:179
  38.3 0.5 add_rsqrt_fusion.r_ref
  38.8 6.7 %shard_map.92 = (bf16[16,4,8,128]{3,2,1,0:T(8,128)(2,1)}, f32[4096,128]{1,0:T(8,128)}) custom-call(f32[4096,128]{1,0:T(8,128)} %get-tuple-element.9.am_ref, bf16[4096,128]{1,0:T(8,128)(2,1)} %kl_ref.1, f32[4096,1]{1,0:T(8,128)} %copy.10.g_ref, f32[1,128]{1,0:T(1,128)} %add_rsqrt_fusion.r_ref, f32[16,4,8,128]{3,2,1,0:T(8,128)} %bitcast.26), custom_call_target="tpu_custom_call" | custom-call | tf_op jit(solution)/shard_map/pallas_call | solution.py:130
  45.6 1.3 %collective-permute-start.2 = (bf16[16,4,8,128]{3,2,1,0:T(8,128)(2,1)}, bf16[16,4,8,128]{3,2,1,0:T(8,128)(2,1)S(1)}, u32[]{:S(2)}, u32[]{:S(2)}) collective-permute-start(bf16[16,4,8,128]{3,2,1,0:T(8,128)(2,1)} %get-tuple-element.12), channel_id=1, source_target_pairs={{0,4},{2,6},{4,8},{6,10},{8,12},{10,14},{1,5},{3,7},{5,9},{7,11},{... | collective-permute-start | bytes 393224 | tf_op jit(solution)/shard_map/ppermute | solution.py:20
  46.9 2.5 %collective-permute-start.1 = (bf16[16,4,8,128]{3,2,1,0:T(8,128)(2,1)}, bf16[16,4,8,128]{3,2,1,0:T(8,128)(2,1)S(1)}, u32[]{:S(2)}, u32[]{:S(2)}) collective-permute-start(bf16[16,4,8,128]{3,2,1,0:T(8,128)(2,1)} %get-tuple-element.12), channel_id=1, source_target_pairs={{0,2},{2,4},{4,6},{6,8},{8,10},{10,12},{12,14},{1,3},{3,5},{5,7},{... | collective-permute-start | bytes 393224 | tf_op jit(solution)/shard_map/ppermute | solution.py:20
  49.4 0.1 copy.13
  49.4 3.8 %collective-permute-done.2 = bf16[16,4,8,128]{3,2,1,0:T(8,128)(2,1)S(1)} collective-permute-done((bf16[16,4,8,128]{3,2,1,0:T(8,128)(2,1)}, bf16[16,4,8,128]{3,2,1,0:T(8,128)(2,1)S(1)}, u32[]{:S(2)}, u32[]{:S(2)}) %collective-permute-start.2) | collective-permute-done | bytes 131104 | tf_op jit(solution)/shard_map/ppermute | solution.py:20
  53.2 2.8 %collective-permute-done.1 = bf16[16,4,8,128]{3,2,1,0:T(8,128)(2,1)S(1)} collective-permute-done((bf16[16,4,8,128]{3,2,1,0:T(8,128)(2,1)}, bf16[16,4,8,128]{3,2,1,0:T(8,128)(2,1)S(1)}, u32[]{:S(2)}, u32[]{:S(2)}) %collective-permute-start.1) | collective-permute-done | bytes 131104 | tf_op jit(solution)/shard_map/ppermute | solution.py:20
  56.1 1.3 %collective-permute-start.3 = (bf16[16,4,8,128]{3,2,1,0:T(8,128)(2,1)S(1)}, bf16[16,4,8,128]{3,2,1,0:T(8,128)(2,1)S(1)}, u32[]{:S(2)}, u32[]{:S(2)}) collective-permute-start(bf16[16,4,8,128]{3,2,1,0:T(8,128)(2,1)S(1)} %fusion), channel_id=1, source_target_pairs={{0,4},{2,6},{4,8},{6,10},{8,12},{10,14},{1,5},{3,7},{5,9},{7,11},{... | collective-permute-start | bytes 393224 | tf_op jit(solution)/shard_map/ppermute | solution.py:20
  57.4 0.1 copy.14
  57.5 5.5 %collective-permute-done.3 = bf16[16,4,8,128]{3,2,1,0:T(8,128)(2,1)S(1)} collective-permute-done((bf16[16,4,8,128]{3,2,1,0:T(8,128)(2,1)S(1)}, bf16[16,4,8,128]{3,2,1,0:T(8,128)(2,1)S(1)}, u32[]{:S(2)}, u32[]{:S(2)}) %collective-permute-start.3) | collective-permute-done | bytes 131104 | tf_op jit(solution)/shard_map/ppermute | solution.py:20
  63.0 0.8 fusion.1
  63.8 1.3 %collective-permute-start.4 = (bf16[16,4,8,128]{3,2,1,0:T(8,128)(2,1)S(1)}, bf16[16,4,8,128]{3,2,1,0:T(8,128)(2,1)S(1)}, u32[]{:S(2)}, u32[]{:S(2)}) collective-permute-start(bf16[16,4,8,128]{3,2,1,0:T(8,128)(2,1)S(1)} %get-tuple-element.13), channel_id=1, source_target_pairs={{0,8},{2,10},{4,12},{6,14},{1,9},{3,11},{5,13},{7,15},{16,24},{18,... | collective-permute-start | bytes 393224 | tf_op jit(solution)/shard_map/ppermute | solution.py:20
  65.1 0.8 copy.15
  65.8 0.8 copy.12
  66.6 6.6 %collective-permute-done.4.recv_ref = bf16[16,4,8,128]{3,2,1,0:T(8,128)(2,1)S(1)} collective-permute-done((bf16[16,4,8,128]{3,2,1,0:T(8,128)(2,1)S(1)}, bf16[16,4,8,128]{3,2,1,0:T(8,128)(2,1)S(1)}, u32[]{:S(2)}, u32[]{:S(2)}) %collective-permute-start.4) | collective-permute-done | bytes 131104 | tf_op jit(solution)/shard_map/ppermute | solution.py:20
  73.1 0.0 copy-start.3
  73.1 0.7 copy-done.3
  73.8 7.8 %shard_map.93 = bf16[4096,128]{1,0:T(8,128)(2,1)} custom-call(f32[4096,128]{1,0:T(8,128)} %get-tuple-element.9.am_ref, f32[4096,128]{1,0:T(8,128)} %get-tuple-element.11.vt_ref, bf16[4096,128]{1,0:T(8,128)(2,1)} %gl_ref.1, f32[16,4,8,128]{3,2,1,0:T(8,128)} %bitcast.27, f32[16,4,8,128]{3,2,1,0:T(8,128)} %bitcast.31, ...), custom_call_target="tpu_custom_call" | custom-call | tf_op jit(solution)/shard_map/pallas_call | solution.py:146
  (1 shorter events, 0.0 us)
Async XLA Ops:
  0.0 5.3 %copy-start.2 = (f32[4096,16]{0,1:T(8,128)S(1)}, f32[4096,16]{0,1:T(8,128)}, u32[]{:S(2)}) copy-start(f32[4096,16]{0,1:T(8,128)} %param.16) | copy-start | bytes 786436
  0.0 5.3 %copy-start.1 = (f32[4096,16]{0,1:T(8,128)S(1)}, f32[4096,16]{0,1:T(8,128)}, u32[]{:S(2)}) copy-start(f32[4096,16]{0,1:T(8,128)} %param.15) | copy-start | bytes 786436
  0.0 6.2 %copy-start.4 = (f32[4096]{0:T(1024)S(1)}, f32[4096]{0:T(1024)}, u32[]{:S(2)}) copy-start(f32[4096]{0:T(1024)} %param.17) | copy-start | bytes 49156
  1.9 27.7 %collective-permute-start = (bf16[4096,128]{1,0:T(8,128)(2,1)S(1)}, bf16[4096,128]{1,0:T(8,128)(2,1)S(1)}, u32[]{:S(2)}, u32[]{:S(2)}) collective-permute-start(bf16[4096,128]{1,0:T(8,128)(2,1)S(1)} %multiply_convert_fusion), channel_id=1, source_target_pairs={{0,2},{2,4},{4,6},{6,8},{8,10},{10,12},{12,14},{1,3},{3,5},{5,7},{... | collective-permute-start | bytes 3145736 | tf_op jit(solution)/shard_map/ppermute | solution.py:20
  29.6 1.0 %copy-start = (bf16[4096,128]{1,0:T(8,128)(2,1)}, bf16[4096,128]{1,0:T(8,128)(2,1)S(1)}, u32[]{:S(2)}) copy-start(bf16[4096,128]{1,0:T(8,128)(2,1)S(1)} %collective-permute-done.rim_ref) | copy-start | bytes 3145732
  45.6 7.7 %collective-permute-start.2 = (bf16[16,4,8,128]{3,2,1,0:T(8,128)(2,1)}, bf16[16,4,8,128]{3,2,1,0:T(8,128)(2,1)S(1)}, u32[]{:S(2)}, u32[]{:S(2)}) collective-permute-start(bf16[16,4,8,128]{3,2,1,0:T(8,128)(2,1)} %get-tuple-element.12), channel_id=1, source_target_pairs={{0,4},{2,6},{4,8},{6,10},{8,12},{10,14},{1,5},{3,7},{5,9},{7,11},{... | collective-permute-start | bytes 393224 | tf_op jit(solution)/shard_map/ppermute | solution.py:20
  46.9 9.2 %collective-permute-start.1 = (bf16[16,4,8,128]{3,2,1,0:T(8,128)(2,1)}, bf16[16,4,8,128]{3,2,1,0:T(8,128)(2,1)S(1)}, u32[]{:S(2)}, u32[]{:S(2)}) collective-permute-start(bf16[16,4,8,128]{3,2,1,0:T(8,128)(2,1)} %get-tuple-element.12), channel_id=1, source_target_pairs={{0,2},{2,4},{4,6},{6,8},{8,10},{10,12},{12,14},{1,3},{3,5},{5,7},{... | collective-permute-start | bytes 393224 | tf_op jit(solution)/shard_map/ppermute | solution.py:20
  56.1 6.9 %collective-permute-start.3 = (bf16[16,4,8,128]{3,2,1,0:T(8,128)(2,1)S(1)}, bf16[16,4,8,128]{3,2,1,0:T(8,128)(2,1)S(1)}, u32[]{:S(2)}, u32[]{:S(2)}) collective-permute-start(bf16[16,4,8,128]{3,2,1,0:T(8,128)(2,1)S(1)} %fusion), channel_id=1, source_target_pairs={{0,4},{2,6},{4,8},{6,10},{8,12},{10,14},{1,5},{3,7},{5,9},{7,11},{... | collective-permute-start | bytes 393224 | tf_op jit(solution)/shard_map/ppermute | solution.py:20
  63.8 9.4 %collective-permute-start.4 = (bf16[16,4,8,128]{3,2,1,0:T(8,128)(2,1)S(1)}, bf16[16,4,8,128]{3,2,1,0:T(8,128)(2,1)S(1)}, u32[]{:S(2)}, u32[]{:S(2)}) collective-permute-start(bf16[16,4,8,128]{3,2,1,0:T(8,128)(2,1)S(1)} %get-tuple-element.13), channel_id=1, source_target_pairs={{0,8},{2,10},{4,12},{6,14},{1,9},{3,11},{5,13},{7,15},{16,24},{18,... | collective-permute-start | bytes 393224 | tf_op jit(solution)/shard_map/ppermute | solution.py:20
  73.1 0.7 copy-start.3

commit v16 on v13

--- a/solution.py
+++ b/solution.py
@@ -68,8 +68,8 @@
     )(inputs, gate_medium, key_medium, rim, taps)
 
 
-def load_values(am_ref, kl_ref, g_ref, r_ref, vt_ref):
-    r = r_ref[...]
+def load_values(am_ref, kl_ref, g_ref, r_ref, vt_ref, width):
+    r = lax.rsqrt(r_ref[...] / width + EPS)
     for i in range(SUB):
         rows = slice(i * LANE, (i + 1) * LANE)
         normed = am_ref[rows, :] * r * g_ref[rows, :]
@@ -81,10 +81,10 @@
     return ref[pl.ds(pl.multiple_of(t * SUB, SUB), SUB), :]
 
 
-def final_state_kernel(am_ref, kl_ref, g_ref, r_ref, lam_ref, f_ref, vt_ref):
+def final_state_kernel(width, am_ref, kl_ref, g_ref, r_ref, lam_ref, f_ref, vt_ref):
     modes = lam_ref.shape[0]
     length = am_ref.shape[1]
-    load_values(am_ref, kl_ref, g_ref, r_ref, vt_ref)
+    load_values(am_ref, kl_ref, g_ref, r_ref, vt_ref, width)
     lam = [lam_ref[m] for m in range(modes)]
 
     def body(t, h):
@@ -122,12 +122,12 @@
     return pl.BlockSpec((lead, None, SUB, LANE), lambda b: (0, b, 0, 0))
 
 
-def final_state_call(am, kl, gain, r, lam):
+def final_state_call(am, kl, gain, totals, lam, width):
     channels, length = am.shape
     modes = lam.shape[0]
     big = pl.BlockSpec((TILE, length), lambda b: (b, 0))
     return pl.pallas_call(
-        final_state_kernel,
+        functools.partial(final_state_kernel, float(width)),
         grid=(channels // TILE,),
         in_specs=[big, big, pl.BlockSpec((TILE, 1), lambda b: (b, 0)), pl.BlockSpec((1, length), lambda b: (0, 0)), tiled_spec(modes)],
         out_specs=[tiled_spec(modes), pl.BlockSpec((length * SUB, LANE), lambda b: (b, 0))],
@@ -135,7 +135,7 @@
             jax.ShapeDtypeStruct(lam.shape, BF16),
             jax.ShapeDtypeStruct((channels // TILE * length * SUB, LANE), F32),
         ],
-    )(am, kl, gain, r, lam)
+    )(am, kl, gain, totals, lam)
 
 
 def output_call(am, vt, gl, lam, w, h0):
@@ -176,12 +176,11 @@
     rim = shifted(values_medium, "context", 1)
     after_medium, partial = medium_call(inputs, gate_medium, key_medium, rim, medium_taps)
     totals = lax.psum(partial, "tensor")
-    r = lax.rsqrt(totals / width + EPS)
     gain = norm_gain[:, None]
     a_t = to_tiles(log_decay)
     lam = jnp.exp(-a_t)
     w = to_tiles(residues * jnp.sqrt(2.0 * log_decay))
-    finals, vt = final_state_call(after_medium, key_long, gain, r, lam)
+    finals, vt = final_state_call(after_medium, key_long, gain, totals, lam, width)
 
     sent = finals
     carried = shifted(sent, "context", 1).astype(F32)

time: 81.8 us -> 81.8 us (level)
  no operation moved by 1% of the time
where the time goes in v16:
time: 81.8 us; the launch traced here: 81 us
  waiting for transfers between devices  40.7 us (50%)
  Pallas kernels  19.7 us (24%)
  starting transfers between devices  9.76 us (12%)
  local copies, waits for them, and re-layouts  4.63 us (6%)
  blocking collectives  3.16 us (4%)
  other arithmetic  2.95 us (4%)
    ppermute x5, waiting for transfers between devices, shifted(): return lax.ppermute(block, axis, route)  40.7 us
    ppermute x5, starting transfers between devices, shifted(): return lax.ppermute(block, axis, route)  9.76 us
    pallas_call x1, Pallas kernels, output_call(): pl.pallas_call(output_kernel, grid=(channels // TILE,), in_specs=[big, pl...  7.75 us
    pallas_call x1, Pallas kernels, final_state_call(): pl.pallas_call(functools.partial(final_state_kernel, float(width)), grid=...  6.72 us
    pallas_call x1, Pallas kernels, medium_call(): pl.pallas_call(medium_kernel, grid=(channels // block,), in_specs=[big, b...  5.19 us
    psum x1, blocking collectives, on_device(): totals = lax.psum(partial, 'tensor')  3.16 us
    unnamed x13, local copies, waits for them, and re-layouts  2.65 us
    broadcast_in_dim x1, local copies, waits for them, and re-layouts, on_device(): gain = norm_gain[:, None]  1.98 us
  transfers between devices with their start and end apart: 5, of which 5 were waited for; matrix products, arithmetic and copies ran while one was open for 5% of the time, Pallas kernels for 0%

profile of v16, /device:TPU:24, one launch (start us, length us, event | category | flops | bytes accessed | tf_op | source)
XLA Modules:
  0.0 81.0 jit_solution(9411470058431095607)
XLA Ops:
  0.0 0.0 copy-start.2
  0.0 0.0 copy-start.1
  0.0 0.0 copy-start.3
  0.0 1.9 %multiply_convert_fusion = bf16[4096,128]{1,0:T(8,128)(2,1)S(1)} fusion(bf16[4096,128]{1,0:T(8,128)(2,1)} %x_ref.1, bf16[4096,128]{1,0:T(8,128)(2,1)} %km_ref.1), kind=kLoop, calls=%fused_computation | loop fusion | flops 2097152 | bytes 3145728 | tf_op jit(solution)/shard_map/convert_element_type | solution.py:175
  1.9 3.4 %collective-permute-start = (bf16[4096,128]{1,0:T(8,128)(2,1)S(1)}, bf16[4096,128]{1,0:T(8,128)(2,1)S(1)}, u32[]{:S(2)}, u32[]{:S(2)}) collective-permute-start(bf16[4096,128]{1,0:T(8,128)(2,1)S(1)} %multiply_convert_fusion), channel_id=1, source_target_pairs={{0,2},{2,4},{4,6},{6,8},{8,10},{10,12},{12,14},{1,3},{3,5},{5,7},{... | collective-permute-start | bytes 3145736 | tf_op jit(solution)/shard_map/ppermute | solution.py:20
  5.3 0.0 copy-done.2
  5.3 0.0 copy-done.1
  5.3 0.2 exponential_bitcast_fusion
  5.5 0.8 copy.11
  6.3 0.0 copy-done.3
  6.3 2.0 %copy.10.g_ref = f32[4096,1]{1,0:T(8,128)} copy(f32[4096,1]{0,1:T(1,128)S(1)} %bitcast.33) | data formatting | bytes 32768 | tf_op jit(solution)/shard_map/broadcast_in_dim | solution.py:179
  8.2 21.3 %collective-permute-done.rim_ref = bf16[4096,128]{1,0:T(8,128)(2,1)S(1)} collective-permute-done((bf16[4096,128]{1,0:T(8,128)(2,1)S(1)}, bf16[4096,128]{1,0:T(8,128)(2,1)S(1)}, u32[]{:S(2)}, u32[]{:S(2)}) %collective-permute-start) | collective-permute-done | bytes 1048608 | tf_op jit(solution)/shard_map/ppermute | solution.py:20
  29.6 0.0 copy-start
  29.6 1.0 %copy-done = bf16[4096,128]{1,0:T(8,128)(2,1)} copy-done((bf16[4096,128]{1,0:T(8,128)(2,1)}, bf16[4096,128]{1,0:T(8,128)(2,1)S(1)}, u32[]{:S(2)}) %copy-start) | copy-done | bytes 1048600
  30.5 5.2 %shard_map.91 = (f32[4096,128]{1,0:T(8,128)}, f32[1,128]{1,0:T(1,128)}) custom-call(bf16[4096,128]{1,0:T(8,128)(2,1)} %x_ref.1, bf16[4096,128]{1,0:T(8,128)(2,1)} %gm_ref.1, bf16[4096,128]{1,0:T(8,128)(2,1)} %km_ref.1, bf16[4096,128]{1,0:T(8,128)(2,1)} %copy-done, bf16[256,128]{1,0:T(8,128)(2,1)} %taps_ref.1), custom_call_target="tpu_custom_call" | custom-call | tf_op jit(solution)/shard_map/pallas_call | solution.py:58
  35.7 3.2 %psum.7.r_ref = f32[1,128]{1,0:T(1,128)} all-reduce(f32[1,128]{1,0:T(1,128)} %get-tuple-element.10), channel_id=1, replica_groups=mesh['groups'=2,'context'=8,'tensor'=2] {'tensor'}, use_global_device_ids=true, to_apply=%region_0.0 | all-reduce | flops 128 | bytes 1024 | tf_op jit(solution)/shard_map/psum | solution.py:178
  38.9 6.7 %shard_map.92 = (bf16[16,4,8,128]{3,2,1,0:T(8,128)(2,1)}, f32[4096,128]{1,0:T(8,128)}) custom-call(f32[4096,128]{1,0:T(8,128)} %get-tuple-element.9.am_ref, bf16[4096,128]{1,0:T(8,128)(2,1)} %kl_ref.1, f32[4096,1]{1,0:T(8,128)} %copy.10.g_ref, f32[1,128]{1,0:T(1,128)} %psum.7.r_ref, f32[16,4,8,128]{3,2,1,0:T(8,128)} %bitcast.26), custom_call_target="tpu_custom_call" | custom-call | tf_op jit(solution)/shard_map/pallas_call | solution.py:129
  45.6 1.3 %collective-permute-start.2 = (bf16[16,4,8,128]{3,2,1,0:T(8,128)(2,1)}, bf16[16,4,8,128]{3,2,1,0:T(8,128)(2,1)S(1)}, u32[]{:S(2)}, u32[]{:S(2)}) collective-permute-start(bf16[16,4,8,128]{3,2,1,0:T(8,128)(2,1)} %get-tuple-element.12), channel_id=1, source_target_pairs={{0,4},{2,6},{4,8},{6,10},{8,12},{10,14},{1,5},{3,7},{5,9},{7,11},{... | collective-permute-start | bytes 393224 | tf_op jit(solution)/shard_map/ppermute | solution.py:20
  46.9 2.5 %collective-permute-start.1 = (bf16[16,4,8,128]{3,2,1,0:T(8,128)(2,1)}, bf16[16,4,8,128]{3,2,1,0:T(8,128)(2,1)S(1)}, u32[]{:S(2)}, u32[]{:S(2)}) collective-permute-start(bf16[16,4,8,128]{3,2,1,0:T(8,128)(2,1)} %get-tuple-element.12), channel_id=1, source_target_pairs={{0,2},{2,4},{4,6},{6,8},{8,10},{10,12},{12,14},{1,3},{3,5},{5,7},{... | collective-permute-start | bytes 393224 | tf_op jit(solution)/shard_map/ppermute | solution.py:20
  49.4 0.1 copy.13
  49.5 3.8 %collective-permute-done.2 = bf16[16,4,8,128]{3,2,1,0:T(8,128)(2,1)S(1)} collective-permute-done((bf16[16,4,8,128]{3,2,1,0:T(8,128)(2,1)}, bf16[16,4,8,128]{3,2,1,0:T(8,128)(2,1)S(1)}, u32[]{:S(2)}, u32[]{:S(2)}) %collective-permute-start.2) | collective-permute-done | bytes 131104 | tf_op jit(solution)/shard_map/ppermute | solution.py:20
  53.3 2.8 %collective-permute-done.1 = bf16[16,4,8,128]{3,2,1,0:T(8,128)(2,1)S(1)} collective-permute-done((bf16[16,4,8,128]{3,2,1,0:T(8,128)(2,1)}, bf16[16,4,8,128]{3,2,1,0:T(8,128)(2,1)S(1)}, u32[]{:S(2)}, u32[]{:S(2)}) %collective-permute-start.1) | collective-permute-done | bytes 131104 | tf_op jit(solution)/shard_map/ppermute | solution.py:20
  56.2 1.3 %collective-permute-start.3 = (bf16[16,4,8,128]{3,2,1,0:T(8,128)(2,1)S(1)}, bf16[16,4,8,128]{3,2,1,0:T(8,128)(2,1)S(1)}, u32[]{:S(2)}, u32[]{:S(2)}) collective-permute-start(bf16[16,4,8,128]{3,2,1,0:T(8,128)(2,1)S(1)} %fusion), channel_id=1, source_target_pairs={{0,4},{2,6},{4,8},{6,10},{8,12},{10,14},{1,5},{3,7},{5,9},{7,11},{... | collective-permute-start | bytes 393224 | tf_op jit(solution)/shard_map/ppermute | solution.py:20
  57.5 0.1 copy.14
  57.5 5.5 %collective-permute-done.3 = bf16[16,4,8,128]{3,2,1,0:T(8,128)(2,1)S(1)} collective-permute-done((bf16[16,4,8,128]{3,2,1,0:T(8,128)(2,1)S(1)}, bf16[16,4,8,128]{3,2,1,0:T(8,128)(2,1)S(1)}, u32[]{:S(2)}, u32[]{:S(2)}) %collective-permute-start.3) | collective-permute-done | bytes 131104 | tf_op jit(solution)/shard_map/ppermute | solution.py:20
  63.0 0.1 fusion.1
  63.1 1.3 %collective-permute-start.4 = (bf16[16,4,8,128]{3,2,1,0:T(8,128)(2,1)S(1)}, bf16[16,4,8,128]{3,2,1,0:T(8,128)(2,1)S(1)}, u32[]{:S(2)}, u32[]{:S(2)}) collective-permute-start(bf16[16,4,8,128]{3,2,1,0:T(8,128)(2,1)S(1)} %get-tuple-element.13), channel_id=1, source_target_pairs={{0,8},{2,10},{4,12},{6,14},{1,9},{3,11},{5,13},{7,15},{16,24},{18,... | collective-permute-start | bytes 393224 | tf_op jit(solution)/shard_map/ppermute | solution.py:20
  64.4 0.1 copy.15
  64.5 0.7 copy.12
  65.2 7.3 %collective-permute-done.4 = bf16[16,4,8,128]{3,2,1,0:T(8,128)(2,1)S(1)} collective-permute-done((bf16[16,4,8,128]{3,2,1,0:T(8,128)(2,1)S(1)}, bf16[16,4,8,128]{3,2,1,0:T(8,128)(2,1)S(1)}, u32[]{:S(2)}, u32[]{:S(2)}) %collective-permute-start.4) | collective-permute-done | bytes 131104 | tf_op jit(solution)/shard_map/ppermute | solution.py:20
  72.5 0.8 multiply_add_fusion.h0_ref
  73.3 7.8 %shard_map.93 = bf16[4096,128]{1,0:T(8,128)(2,1)} custom-call(f32[4096,128]{1,0:T(8,128)} %get-tuple-element.9.am_ref, f32[4096,128]{1,0:T(8,128)} %get-tuple-element.11.vt_ref, bf16[4096,128]{1,0:T(8,128)(2,1)} %gl_ref.1, f32[16,4,8,128]{3,2,1,0:T(8,128)} %bitcast.27, f32[16,4,8,128]{3,2,1,0:T(8,128)} %bitcast.30, f32[16,4,8,128]{3,2,1,0:T(8,128)} %multiply_add_fusion.h0_ref), custom_call_target="tpu_custom_call" | custom-call | tf_op jit(solution)/shard_map/pallas_call | solution.py:145
  (1 shorter events, 0.0 us)
Async XLA Ops:
  0.0 5.3 %copy-start.2 = (f32[4096,16]{0,1:T(8,128)S(1)}, f32[4096,16]{0,1:T(8,128)}, u32[]{:S(2)}) copy-start(f32[4096,16]{0,1:T(8,128)} %param.16) | copy-start | bytes 786436
  0.0 5.3 %copy-start.1 = (f32[4096,16]{0,1:T(8,128)S(1)}, f32[4096,16]{0,1:T(8,128)}, u32[]{:S(2)}) copy-start(f32[4096,16]{0,1:T(8,128)} %param.15) | copy-start | bytes 786436
  0.0 6.3 %copy-start.3 = (f32[4096]{0:T(1024)S(1)}, f32[4096]{0:T(1024)}, u32[]{:S(2)}) copy-start(f32[4096]{0:T(1024)} %param.17) | copy-start | bytes 49156
  1.9 27.7 %collective-permute-start = (bf16[4096,128]{1,0:T(8,128)(2,1)S(1)}, bf16[4096,128]{1,0:T(8,128)(2,1)S(1)}, u32[]{:S(2)}, u32[]{:S(2)}) collective-permute-start(bf16[4096,128]{1,0:T(8,128)(2,1)S(1)} %multiply_convert_fusion), channel_id=1, source_target_pairs={{0,2},{2,4},{4,6},{6,8},{8,10},{10,12},{12,14},{1,3},{3,5},{5,7},{... | collective-permute-start | bytes 3145736 | tf_op jit(solution)/shard_map/ppermute | solution.py:20
  29.6 1.0 %copy-start = (bf16[4096,128]{1,0:T(8,128)(2,1)}, bf16[4096,128]{1,0:T(8,128)(2,1)S(1)}, u32[]{:S(2)}) copy-start(bf16[4096,128]{1,0:T(8,128)(2,1)S(1)} %collective-permute-done.rim_ref) | copy-start | bytes 3145732
  45.6 7.7 %collective-permute-start.2 = (bf16[16,4,8,128]{3,2,1,0:T(8,128)(2,1)}, bf16[16,4,8,128]{3,2,1,0:T(8,128)(2,1)S(1)}, u32[]{:S(2)}, u32[]{:S(2)}) collective-permute-start(bf16[16,4,8,128]{3,2,1,0:T(8,128)(2,1)} %get-tuple-element.12), channel_id=1, source_target_pairs={{0,4},{2,6},{4,8},{6,10},{8,12},{10,14},{1,5},{3,7},{5,9},{7,11},{... | collective-permute-start | bytes 393224 | tf_op jit(solution)/shard_map/ppermute | solution.py:20
  46.9 9.2 %collective-permute-start.1 = (bf16[16,4,8,128]{3,2,1,0:T(8,128)(2,1)}, bf16[16,4,8,128]{3,2,1,0:T(8,128)(2,1)S(1)}, u32[]{:S(2)}, u32[]{:S(2)}) collective-permute-start(bf16[16,4,8,128]{3,2,1,0:T(8,128)(2,1)} %get-tuple-element.12), channel_id=1, source_target_pairs={{0,2},{2,4},{4,6},{6,8},{8,10},{10,12},{12,14},{1,3},{3,5},{5,7},{... | collective-permute-start | bytes 393224 | tf_op jit(solution)/shard_map/ppermute | solution.py:20
  56.2 6.9 %collective-permute-start.3 = (bf16[16,4,8,128]{3,2,1,0:T(8,128)(2,1)S(1)}, bf16[16,4,8,128]{3,2,1,0:T(8,128)(2,1)S(1)}, u32[]{:S(2)}, u32[]{:S(2)}) collective-permute-start(bf16[16,4,8,128]{3,2,1,0:T(8,128)(2,1)S(1)} %fusion), channel_id=1, source_target_pairs={{0,4},{2,6},{4,8},{6,10},{8,12},{10,14},{1,5},{3,7},{5,9},{7,11},{... | collective-permute-start | bytes 393224 | tf_op jit(solution)/shard_map/ppermute | solution.py:20
  63.1 9.4 %collective-permute-start.4 = (bf16[16,4,8,128]{3,2,1,0:T(8,128)(2,1)S(1)}, bf16[16,4,8,128]{3,2,1,0:T(8,128)(2,1)S(1)}, u32[]{:S(2)}, u32[]{:S(2)}) collective-permute-start(bf16[16,4,8,128]{3,2,1,0:T(8,128)(2,1)S(1)} %get-tuple-element.13), channel_id=1, source_target_pairs={{0,8},{2,10},{4,12},{6,14},{1,9},{3,11},{5,13},{7,15},{16,24},{18,... | collective-permute-start | bytes 393224 | tf_op jit(solution)/shard_map/ppermute | solution.py:20

commit v17 on v13

--- a/solution.py
+++ b/solution.py
@@ -175,7 +175,10 @@
     values_medium = (key_medium.astype(F32) * source).astype(BF16)
     rim = shifted(values_medium, "context", 1)
     after_medium, partial = medium_call(inputs, gate_medium, key_medium, rim, medium_taps)
-    totals = lax.psum(partial, "tensor")
+    if lax.axis_size("tensor") == 2:
+        totals = partial + lax.ppermute(partial, "tensor", [(0, 1), (1, 0)])
+    else:
+        totals = lax.psum(partial, "tensor")
     r = lax.rsqrt(totals / width + EPS)
     gain = norm_gain[:, None]
     a_t = to_tiles(log_decay)

time: 81.8 us -> 82.7 us (1.011)
  waiting for transfers between devices: 40.7 us -> 44.5 us
  blocking collectives: 2.57 us -> 0 us
    ppermute x5, waiting for transfers between devices: 40.7 us -> 44.5 us  [shifted(): return lax.ppermute(block, axis, route)]
    psum x1 -> x0, blocking collectives: 2.57 us -> none  [on_device(): totals = lax.psum(partial, 'tensor')]
    unnamed x13 -> x15, local copies, waits for them, and re-layouts: 2.65 us -> 2.66 us
  transfers between devices with their start and end apart: 5 -> 6, of which waited for: 5 -> 5; matrix products, arithmetic and copies ran while one was open for 5% -> 5% of each run, Pallas kernels for 0% -> 0%
where the time goes in v17:
time: 82.7 us; the launch traced here: 82.3 us
  waiting for transfers between devices  44.5 us (54%)
  Pallas kernels  19.6 us (24%)
  starting transfers between devices  9.97 us (12%)
  local copies, waits for them, and re-layouts  4.65 us (6%)
  other arithmetic  3.42 us (4%)
    ppermute x5, waiting for transfers between devices, shifted(): return lax.ppermute(block, axis, route)  44.5 us
    ppermute x5, starting transfers between devices, shifted(): return lax.ppermute(block, axis, route)  9.9 us
    pallas_call x1, Pallas kernels, output_call(): pl.pallas_call(output_kernel, grid=(channels // TILE,), in_specs=[big, pl...  7.75 us
    pallas_call x1, Pallas kernels, final_state_call(): pl.pallas_call(final_state_kernel, grid=(channels // TILE,), in_specs=[bi...  6.68 us
    pallas_call x1, Pallas kernels, medium_call(): pl.pallas_call(medium_kernel, grid=(channels // block,), in_specs=[big, b...  5.17 us
    unnamed x15, local copies, waits for them, and re-layouts  2.66 us
    broadcast_in_dim x1, local copies, waits for them, and re-layouts, on_device(): gain = norm_gain[:, None]  1.99 us
    convert_element_type x1, other arithmetic, on_device(): values_medium = (key_medium.astype(F32) * source).astype(BF16)  1.81 us
  transfers between devices with their start and end apart: 6, of which 5 were waited for; matrix products, arithmetic and copies ran while one was open for 5% of the time, Pallas kernels for 0%

profile of v17, /device:TPU:24, one launch (start us, length us, event | category | flops | bytes accessed | tf_op | source)
XLA Modules:
  0.0 82.3 jit_solution(8338589419323785054)
XLA Ops:
  0.0 1.8 %multiply_convert_fusion = bf16[4096,128]{1,0:T(8,128)(2,1)S(1)} fusion(bf16[4096,128]{1,0:T(8,128)(2,1)} %x_ref.1, bf16[4096,128]{1,0:T(8,128)(2,1)} %km_ref.1), kind=kLoop, calls=%fused_computation | loop fusion | flops 2097152 | bytes 3145728 | tf_op jit(solution)/shard_map/convert_element_type | solution.py:175
  1.8 0.0 copy-start.1
  1.8 0.0 copy-start.2
  1.8 3.5 %collective-permute-start = (bf16[4096,128]{1,0:T(8,128)(2,1)S(1)}, bf16[4096,128]{1,0:T(8,128)(2,1)S(1)}, u32[]{:S(2)}, u32[]{:S(2)}) collective-permute-start(bf16[4096,128]{1,0:T(8,128)(2,1)S(1)} %multiply_convert_fusion), channel_id=1, source_target_pairs={{0,2},{2,4},{4,6},{6,8},{8,10},{10,12},{12,14},{1,3},{3,5},{5,7},{... | collective-permute-start | bytes 3145736 | tf_op jit(solution)/shard_map/ppermute | solution.py:20
  5.4 24.3 %collective-permute-done.rim_ref = bf16[4096,128]{1,0:T(8,128)(2,1)S(1)} collective-permute-done((bf16[4096,128]{1,0:T(8,128)(2,1)S(1)}, bf16[4096,128]{1,0:T(8,128)(2,1)S(1)}, u32[]{:S(2)}, u32[]{:S(2)}) %collective-permute-start) | collective-permute-done | bytes 1048608 | tf_op jit(solution)/shard_map/ppermute | solution.py:20
  29.7 0.0 copy-start
  29.7 1.0 %copy-done = bf16[4096,128]{1,0:T(8,128)(2,1)} copy-done((bf16[4096,128]{1,0:T(8,128)(2,1)}, bf16[4096,128]{1,0:T(8,128)(2,1)S(1)}, u32[]{:S(2)}) %copy-start) | copy-done | bytes 1048600
  30.6 5.2 %shard_map.91 = (f32[4096,128]{1,0:T(8,128)}, f32[1,128]{1,0:T(1,128)}) custom-call(bf16[4096,128]{1,0:T(8,128)(2,1)} %x_ref.1, bf16[4096,128]{1,0:T(8,128)(2,1)} %gm_ref.1, bf16[4096,128]{1,0:T(8,128)(2,1)} %km_ref.1, bf16[4096,128]{1,0:T(8,128)(2,1)} %copy-done, bf16[256,128]{1,0:T(8,128)(2,1)} %taps_ref.1), custom_call_target="tpu_custom_call" | custom-call | tf_op jit(solution)/shard_map/pallas_call | solution.py:58
  35.8 0.0 copy-start.3
  35.8 0.0 copy-start.4
  35.8 0.1 collective-permute-start.1
  35.9 0.0 copy-done.1
  35.9 0.0 copy-done.2
  35.9 0.2 exponential_bitcast_fusion
  36.1 0.7 copy.11
  36.8 0.0 copy-done.3
  36.9 2.0 %copy.10.g_ref = f32[4096,1]{1,0:T(8,128)} copy(f32[4096,1]{0,1:T(1,128)S(1)} %bitcast.33) | data formatting | bytes 32768 | tf_op jit(solution)/shard_map/broadcast_in_dim | solution.py:183
  38.8 0.0 collective-permute-done.1
  38.8 0.0 copy-done.4
  38.8 0.5 add_rsqrt_fusion.r_ref
  39.4 6.7 %shard_map.92 = (bf16[16,4,8,128]{3,2,1,0:T(8,128)(2,1)}, f32[4096,128]{1,0:T(8,128)}) custom-call(f32[4096,128]{1,0:T(8,128)} %get-tuple-element.9.am_ref, bf16[4096,128]{1,0:T(8,128)(2,1)} %kl_ref.1, f32[4096,1]{1,0:T(8,128)} %copy.10.g_ref, f32[1,128]{1,0:T(1,128)} %add_rsqrt_fusion.r_ref, f32[16,4,8,128]{3,2,1,0:T(8,128)} %bitcast.26), custom_call_target="tpu_custom_call" | custom-call | tf_op jit(solution)/shard_map/pallas_call | solution.py:129
  46.1 1.3 %collective-permute-start.3 = (bf16[16,4,8,128]{3,2,1,0:T(8,128)(2,1)}, bf16[16,4,8,128]{3,2,1,0:T(8,128)(2,1)S(1)}, u32[]{:S(2)}, u32[]{:S(2)}) collective-permute-start(bf16[16,4,8,128]{3,2,1,0:T(8,128)(2,1)} %get-tuple-element.12), channel_id=1, source_target_pairs={{0,4},{2,6},{4,8},{6,10},{8,12},{10,14},{1,5},{3,7},{5,9},{7,11},{... | collective-permute-start | bytes 393224 | tf_op jit(solution)/shard_map/ppermute | solution.py:20
  47.4 2.5 %collective-permute-start.2 = (bf16[16,4,8,128]{3,2,1,0:T(8,128)(2,1)}, bf16[16,4,8,128]{3,2,1,0:T(8,128)(2,1)S(1)}, u32[]{:S(2)}, u32[]{:S(2)}) collective-permute-start(bf16[16,4,8,128]{3,2,1,0:T(8,128)(2,1)} %get-tuple-element.12), channel_id=1, source_target_pairs={{0,2},{2,4},{4,6},{6,8},{8,10},{10,12},{12,14},{1,3},{3,5},{5,7},{... | collective-permute-start | bytes 393224 | tf_op jit(solution)/shard_map/ppermute | solution.py:20
  49.9 0.1 copy.13
  49.9 4.1 %collective-permute-done.3 = bf16[16,4,8,128]{3,2,1,0:T(8,128)(2,1)S(1)} collective-permute-done((bf16[16,4,8,128]{3,2,1,0:T(8,128)(2,1)}, bf16[16,4,8,128]{3,2,1,0:T(8,128)(2,1)S(1)}, u32[]{:S(2)}, u32[]{:S(2)}) %collective-permute-start.3) | collective-permute-done | bytes 131104 | tf_op jit(solution)/shard_map/ppermute | solution.py:20
  54.0 2.8 %collective-permute-done.2 = bf16[16,4,8,128]{3,2,1,0:T(8,128)(2,1)S(1)} collective-permute-done((bf16[16,4,8,128]{3,2,1,0:T(8,128)(2,1)}, bf16[16,4,8,128]{3,2,1,0:T(8,128)(2,1)S(1)}, u32[]{:S(2)}, u32[]{:S(2)}) %collective-permute-start.2) | collective-permute-done | bytes 131104 | tf_op jit(solution)/shard_map/ppermute | solution.py:20
  56.9 1.3 %collective-permute-start.4 = (bf16[16,4,8,128]{3,2,1,0:T(8,128)(2,1)S(1)}, bf16[16,4,8,128]{3,2,1,0:T(8,128)(2,1)S(1)}, u32[]{:S(2)}, u32[]{:S(2)}) collective-permute-start(bf16[16,4,8,128]{3,2,1,0:T(8,128)(2,1)S(1)} %fusion), channel_id=1, source_target_pairs={{0,4},{2,6},{4,8},{6,10},{8,12},{10,14},{1,5},{3,7},{5,9},{7,11},{... | collective-permute-start | bytes 393224 | tf_op jit(solution)/shard_map/ppermute | solution.py:20
  58.2 0.1 copy.14
  58.3 5.6 %collective-permute-done.4 = bf16[16,4,8,128]{3,2,1,0:T(8,128)(2,1)S(1)} collective-permute-done((bf16[16,4,8,128]{3,2,1,0:T(8,128)(2,1)S(1)}, bf16[16,4,8,128]{3,2,1,0:T(8,128)(2,1)S(1)}, u32[]{:S(2)}, u32[]{:S(2)}) %collective-permute-start.4) | collective-permute-done | bytes 131104 | tf_op jit(solution)/shard_map/ppermute | solution.py:20
  63.9 0.1 fusion.1
  64.0 1.3 %collective-permute-start.5 = (bf16[16,4,8,128]{3,2,1,0:T(8,128)(2,1)S(1)}, bf16[16,4,8,128]{3,2,1,0:T(8,128)(2,1)S(1)}, u32[]{:S(2)}, u32[]{:S(2)}) collective-permute-start(bf16[16,4,8,128]{3,2,1,0:T(8,128)(2,1)S(1)} %get-tuple-element.13), channel_id=1, source_target_pairs={{0,8},{2,10},{4,12},{6,14},{1,9},{3,11},{5,13},{7,15},{16,24},{18,... | collective-permute-start | bytes 393224 | tf_op jit(solution)/shard_map/ppermute | solution.py:20
  65.3 0.1 copy.15
  65.4 0.8 copy.12
  66.1 7.7 %collective-permute-done.5 = bf16[16,4,8,128]{3,2,1,0:T(8,128)(2,1)S(1)} collective-permute-done((bf16[16,4,8,128]{3,2,1,0:T(8,128)(2,1)S(1)}, bf16[16,4,8,128]{3,2,1,0:T(8,128)(2,1)S(1)}, u32[]{:S(2)}, u32[]{:S(2)}) %collective-permute-start.5) | collective-permute-done | bytes 131104 | tf_op jit(solution)/shard_map/ppermute | solution.py:20
  73.8 0.8 multiply_add_fusion.h0_ref
  74.6 7.8 %shard_map.93 = bf16[4096,128]{1,0:T(8,128)(2,1)} custom-call(f32[4096,128]{1,0:T(8,128)} %get-tuple-element.9.am_ref, f32[4096,128]{1,0:T(8,128)} %get-tuple-element.11.vt_ref, bf16[4096,128]{1,0:T(8,128)(2,1)} %gl_ref.1, f32[16,4,8,128]{3,2,1,0:T(8,128)} %bitcast.27, f32[16,4,8,128]{3,2,1,0:T(8,128)} %bitcast.30, f32[16,4,8,128]{3,2,1,0:T(8,128)} %multiply_add_fusion.h0_ref), custom_call_target="tpu_custom_call" | custom-call | tf_op jit(solution)/shard_map/pallas_call | solution.py:145
  (1 shorter events, 0.0 us)
Async XLA Ops:
  1.8 34.1 %copy-start.1 = (f32[4096,16]{0,1:T(8,128)S(1)}, f32[4096,16]{0,1:T(8,128)}, u32[]{:S(2)}) copy-start(f32[4096,16]{0,1:T(8,128)} %param.15) | copy-start | bytes 786436
  1.8 34.1 %copy-start.2 = (f32[4096,16]{0,1:T(8,128)S(1)}, f32[4096,16]{0,1:T(8,128)}, u32[]{:S(2)}) copy-start(f32[4096,16]{0,1:T(8,128)} %param.16) | copy-start | bytes 786436
  1.8 27.8 %collective-permute-start = (bf16[4096,128]{1,0:T(8,128)(2,1)S(1)}, bf16[4096,128]{1,0:T(8,128)(2,1)S(1)}, u32[]{:S(2)}, u32[]{:S(2)}) collective-permute-start(bf16[4096,128]{1,0:T(8,128)(2,1)S(1)} %multiply_convert_fusion), channel_id=1, source_target_pairs={{0,2},{2,4},{4,6},{6,8},{8,10},{10,12},{12,14},{1,3},{3,5},{5,7},{... | collective-permute-start | bytes 3145736 | tf_op jit(solution)/shard_map/ppermute | solution.py:20
  29.7 1.0 %copy-start = (bf16[4096,128]{1,0:T(8,128)(2,1)}, bf16[4096,128]{1,0:T(8,128)(2,1)S(1)}, u32[]{:S(2)}) copy-start(bf16[4096,128]{1,0:T(8,128)(2,1)S(1)} %collective-permute-done.rim_ref) | copy-start | bytes 3145732
  35.8 1.0 %copy-start.3 = (f32[4096]{0:T(1024)S(1)}, f32[4096]{0:T(1024)}, u32[]{:S(2)}) copy-start(f32[4096]{0:T(1024)} %param.17) | copy-start | bytes 49156
  35.8 3.0 %copy-start.4 = (f32[1,128]{1,0:T(1,128)S(1)}, f32[1,128]{1,0:T(1,128)}, u32[]{:S(2)}) copy-start(f32[1,128]{1,0:T(1,128)} %get-tuple-element.10) | copy-start | bytes 1540
  35.8 3.0 %collective-permute-start.1 = (f32[1,128]{1,0:T(1,128)}, f32[1,128]{1,0:T(1,128)S(1)}, u32[]{:S(2)}, u32[]{:S(2)}) collective-permute-start(f32[1,128]{1,0:T(1,128)} %get-tuple-element.10), channel_id=1, source_target_pairs={{0,1},{1,0},{2,3},{3,2},{4,5},{5,4},{6,7},{7,6},{8,9},{9,8},{10,11... | collective-permute-start | bytes 1544 | tf_op jit(solution)/shard_map/ppermute | solution.py:179
  46.1 8.0 %collective-permute-start.3 = (bf16[16,4,8,128]{3,2,1,0:T(8,128)(2,1)}, bf16[16,4,8,128]{3,2,1,0:T(8,128)(2,1)S(1)}, u32[]{:S(2)}, u32[]{:S(2)}) collective-permute-start(bf16[16,4,8,128]{3,2,1,0:T(8,128)(2,1)} %get-tuple-element.12), channel_id=1, source_target_pairs={{0,4},{2,6},{4,8},{6,10},{8,12},{10,14},{1,5},{3,7},{5,9},{7,11},{... | collective-permute-start | bytes 393224 | tf_op jit(solution)/shard_map/ppermute | solution.py:20
  47.4 9.5 %collective-permute-start.2 = (bf16[16,4,8,128]{3,2,1,0:T(8,128)(2,1)}, bf16[16,4,8,128]{3,2,1,0:T(8,128)(2,1)S(1)}, u32[]{:S(2)}, u32[]{:S(2)}) collective-permute-start(bf16[16,4,8,128]{3,2,1,0:T(8,128)(2,1)} %get-tuple-element.12), channel_id=1, source_target_pairs={{0,2},{2,4},{4,6},{6,8},{8,10},{10,12},{12,14},{1,3},{3,5},{5,7},{... | collective-permute-start | bytes 393224 | tf_op jit(solution)/shard_map/ppermute | solution.py:20
  56.9 7.0 %collective-permute-start.4 = (bf16[16,4,8,128]{3,2,1,0:T(8,128)(2,1)S(1)}, bf16[16,4,8,128]{3,2,1,0:T(8,128)(2,1)S(1)}, u32[]{:S(2)}, u32[]{:S(2)}) collective-permute-start(bf16[16,4,8,128]{3,2,1,0:T(8,128)(2,1)S(1)} %fusion), channel_id=1, source_target_pairs={{0,4},{2,6},{4,8},{6,10},{8,12},{10,14},{1,5},{3,7},{5,9},{7,11},{... | collective-permute-start | bytes 393224 | tf_op jit(solution)/shard_map/ppermute | solution.py:20
  64.0 9.8 %collective-permute-start.5 = (bf16[16,4,8,128]{3,2,1,0:T(8,128)(2,1)S(1)}, bf16[16,4,8,128]{3,2,1,0:T(8,128)(2,1)S(1)}, u32[]{:S(2)}, u32[]{:S(2)}) collective-permute-start(bf16[16,4,8,128]{3,2,1,0:T(8,128)(2,1)S(1)} %get-tuple-element.13), channel_id=1, source_target_pairs={{0,8},{2,10},{4,12},{6,14},{1,9},{3,11},{5,13},{7,15},{16,24},{18,... | collective-permute-start | bytes 393224 | tf_op jit(solution)/shard_map/ppermute | solution.py:20

commit v18 on v17

--- a/solution.py
+++ b/solution.py
@@ -129,7 +129,7 @@
     return pl.pallas_call(
         final_state_kernel,
         grid=(channels // TILE,),
-        in_specs=[big, big, pl.BlockSpec((TILE, 1), lambda b: (b, 0)), pl.BlockSpec((1, length), lambda b: (0, 0)), tiled_spec(modes)],
+        in_specs=[big, big, big, pl.BlockSpec((1, length), lambda b: (0, 0)), tiled_spec(modes)],
         out_specs=[tiled_spec(modes), pl.BlockSpec((length * SUB, LANE), lambda b: (b, 0))],
         out_shape=[
             jax.ShapeDtypeStruct(lam.shape, BF16),
@@ -174,16 +174,17 @@
     source = inputs.astype(F32)
     values_medium = (key_medium.astype(F32) * source).astype(BF16)
     rim = shifted(values_medium, "context", 1)
+    gain = jnp.broadcast_to(norm_gain[:, None], inputs.shape)
+    a_t = to_tiles(log_decay)
+    lam = jnp.exp(-a_t)
+    w = to_tiles(residues * jnp.sqrt(2.0 * log_decay))
+    rim, gain, a_t, lam, w = lax.optimization_barrier((rim, gain, a_t, lam, w))
     after_medium, partial = medium_call(inputs, gate_medium, key_medium, rim, medium_taps)
     if lax.axis_size("tensor") == 2:
         totals = partial + lax.ppermute(partial, "tensor", [(0, 1), (1, 0)])
     else:
         totals = lax.psum(partial, "tensor")
     r = lax.rsqrt(totals / width + EPS)
-    gain = norm_gain[:, None]
-    a_t = to_tiles(log_decay)
-    lam = jnp.exp(-a_t)
-    w = to_tiles(residues * jnp.sqrt(2.0 * log_decay))
     finals, vt = final_state_call(after_medium, key_long, gain, r, lam)
 
     sent = finals

time: 82.7 us -> 81.3 us (0.983)
  local copies, waits for them, and re-layouts: 4.65 us -> 2.75 us
  other arithmetic: 3.42 us -> 4.93 us
    unnamed x15 -> x10, local copies, waits for them, and re-layouts: 2.66 us -> 0.82 us
    ppermute x5, waiting for transfers between devices: 44.5 us -> 43 us  [shifted(): return lax.ppermute(block, axis, route)]
    ppermute x1, waiting for transfers between devices: 0.01 us -> 1.18 us  [on_device(): totals = partial + lax.ppermute(partial, 'tensor', [(0, 1), (1, 0)])]
  transfers between devices with their start and end apart: 6 -> 6, of which waited for: 5 -> 6; matrix products, arithmetic and copies ran while one was open for 5% -> 2% of each run, Pallas kernels for 0% -> 0%
where the time goes in v18:
time: 81.3 us; the launch traced here: 80.6 us
  waiting for transfers between devices  44.2 us (54%)
  Pallas kernels  18.9 us (23%)
  starting transfers between devices  9.77 us (12%)
  other arithmetic  4.93 us (6%)
  local copies, waits for them, and re-layouts  2.75 us (3%)
    ppermute x5, waiting for transfers between devices, shifted(): return lax.ppermute(block, axis, route)  43 us
    ppermute x5, starting transfers between devices, shifted(): return lax.ppermute(block, axis, route)  9.76 us
    pallas_call x1, Pallas kernels, output_call(): pl.pallas_call(output_kernel, grid=(channels // TILE,), in_specs=[big, pl...  7.75 us
    pallas_call x1, Pallas kernels, final_state_call(): pl.pallas_call(final_state_kernel, grid=(channels // TILE,), in_specs=[bi...  5.94 us
    pallas_call x1, Pallas kernels, medium_call(): pl.pallas_call(medium_kernel, grid=(channels // block,), in_specs=[big, b...  5.17 us
    broadcast_in_dim x1, local copies, waits for them, and re-layouts, on_device(): gain = jnp.broadcast_to(norm_gain[:, None], inputs.shape)  1.93 us
    convert_element_type x1, other arithmetic, on_device(): values_medium = (key_medium.astype(F32) * source).astype(BF16)  1.87 us
  transfers between devices with their start and end apart: 6, of which 6 were waited for; matrix products, arithmetic and copies ran while one was open for 2% of the time, Pallas kernels for 0%

profile of v18, /device:TPU:24, one launch (start us, length us, event | category | flops | bytes accessed | tf_op | source)
XLA Modules:
  0.0 80.6 jit_solution(9111838533897103868)
XLA Ops:
  0.0 0.0 copy-start
  0.0 0.0 copy-start.2
  0.0 0.0 copy-start.3
  0.0 1.9 %multiply_convert_fusion = bf16[4096,128]{1,0:T(8,128)(2,1)S(1)} fusion(bf16[4096,128]{1,0:T(8,128)(2,1)} %x_ref.1, bf16[4096,128]{1,0:T(8,128)(2,1)} %km_ref.1), kind=kLoop, calls=%fused_computation | loop fusion | flops 2097152 | bytes 3145728 | tf_op jit(solution)/shard_map/convert_element_type | solution.py:175
  1.9 3.4 %collective-permute-start = (bf16[4096,128]{1,0:T(8,128)(2,1)S(1)}, bf16[4096,128]{1,0:T(8,128)(2,1)S(1)}, u32[]{:S(2)}, u32[]{:S(2)}) collective-permute-start(bf16[4096,128]{1,0:T(8,128)(2,1)S(1)} %multiply_convert_fusion), channel_id=1, source_target_pairs={{0,2},{2,4},{4,6},{6,8},{8,10},{10,12},{12,14},{1,3},{3,5},{5,7},{... | collective-permute-start | bytes 3145736 | tf_op jit(solution)/shard_map/ppermute | solution.py:20
  5.3 0.0 copy-done
  5.3 0.0 copy-done.2
  5.3 0.1 multiply_bitcast_fusion
  5.4 0.8 copy.11
  6.2 0.1 copy.10
  6.2 0.7 negate_exponential_fusion.lam_ref
  7.0 22.6 %collective-permute-done.rim_ref = bf16[4096,128]{1,0:T(8,128)(2,1)S(1)} collective-permute-done((bf16[4096,128]{1,0:T(8,128)(2,1)S(1)}, bf16[4096,128]{1,0:T(8,128)(2,1)S(1)}, u32[]{:S(2)}, u32[]{:S(2)}) %collective-permute-start) | collective-permute-done | bytes 1048608 | tf_op jit(solution)/shard_map/ppermute | solution.py:20
  29.6 0.0 copy-start.1
  29.6 0.0 copy-done.3
  29.6 1.9 %broadcast_in_dim.2.g_ref = f32[4096,128]{1,0:T(8,128)} broadcast(f32[4096]{0:T(1024)S(1)} %copy-done.3), dimensions={0} | broadcast | bytes 2113536 | tf_op jit(solution)/shard_map/broadcast_in_dim | solution.py:177
  31.5 0.0 copy-done.1
  31.5 5.2 %shard_map.91 = (f32[4096,128]{1,0:T(8,128)}, f32[1,128]{1,0:T(1,128)}) custom-call(bf16[4096,128]{1,0:T(8,128)(2,1)} %x_ref.1, bf16[4096,128]{1,0:T(8,128)(2,1)} %gm_ref.1, bf16[4096,128]{1,0:T(8,128)(2,1)} %km_ref.1, bf16[4096,128]{1,0:T(8,128)(2,1)} %copy-done.1, bf16[256,128]{1,0:T(8,128)(2,1)} %taps_ref.1), custom_call_target="tpu_custom_call" | custom-call | tf_op jit(solution)/shard_map/pallas_call | solution.py:58
  36.7 0.0 collective-permute-start.1
  36.7 1.2 %collective-permute-done.1 = f32[1,128]{1,0:T(1,128)S(1)} collective-permute-done((f32[1,128]{1,0:T(1,128)}, f32[1,128]{1,0:T(1,128)S(1)}, u32[]{:S(2)}, u32[]{:S(2)}) %collective-permute-start.1) | collective-permute-done | bytes 544 | tf_op jit(solution)/shard_map/ppermute | solution.py:184
  37.9 1.2 %add_rsqrt_fusion.r_ref = f32[1,128]{1,0:T(1,128)} fusion(f32[1,128]{1,0:T(1,128)} %get-tuple-element.17, f32[1,128]{1,0:T(1,128)S(1)} %collective-permute-done.1), kind=kLoop, calls=%fused_computation.8 | loop fusion | flops 384 | bytes 1536 | tf_op jit(solution)/shard_map/rsqrt | solution.py:187
  39.0 5.9 %shard_map.92 = (bf16[16,4,8,128]{3,2,1,0:T(8,128)(2,1)}, f32[4096,128]{1,0:T(8,128)}) custom-call(f32[4096,128]{1,0:T(8,128)} %get-tuple-element.15.am_ref, bf16[4096,128]{1,0:T(8,128)(2,1)} %kl_ref.1, f32[4096,128]{1,0:T(8,128)} %broadcast_in_dim.2.g_ref, f32[1,128]{1,0:T(1,128)} %add_rsqrt_fusion.r_ref, f32[16,4,8,128]{3,2,1,0:T(8,128)} %negate_exponential_fusion.lam_ref), custom_call_target="tpu_custom_call" | custom-call | tf_op jit(solution)/shard_map/pallas_call | solution.py:129
  45.0 1.3 %collective-permute-start.3 = (bf16[16,4,8,128]{3,2,1,0:T(8,128)(2,1)}, bf16[16,4,8,128]{3,2,1,0:T(8,128)(2,1)S(1)}, u32[]{:S(2)}, u32[]{:S(2)}) collective-permute-start(bf16[16,4,8,128]{3,2,1,0:T(8,128)(2,1)} %get-tuple-element.21), channel_id=1, source_target_pairs={{0,4},{2,6},{4,8},{6,10},{8,12},{10,14},{1,5},{3,7},{5,9},{7,11},{... | collective-permute-start | bytes 393224 | tf_op jit(solution)/shard_map/ppermute | solution.py:20
  46.2 2.5 %collective-permute-start.2 = (bf16[16,4,8,128]{3,2,1,0:T(8,128)(2,1)}, bf16[16,4,8,128]{3,2,1,0:T(8,128)(2,1)S(1)}, u32[]{:S(2)}, u32[]{:S(2)}) collective-permute-start(bf16[16,4,8,128]{3,2,1,0:T(8,128)(2,1)} %get-tuple-element.21), channel_id=1, source_target_pairs={{0,2},{2,4},{4,6},{6,8},{8,10},{10,12},{12,14},{1,3},{3,5},{5,7},{... | collective-permute-start | bytes 393224 | tf_op jit(solution)/shard_map/ppermute | solution.py:20
  48.8 3.9 %collective-permute-done.3 = bf16[16,4,8,128]{3,2,1,0:T(8,128)(2,1)S(1)} collective-permute-done((bf16[16,4,8,128]{3,2,1,0:T(8,128)(2,1)}, bf16[16,4,8,128]{3,2,1,0:T(8,128)(2,1)S(1)}, u32[]{:S(2)}, u32[]{:S(2)}) %collective-permute-start.3) | collective-permute-done | bytes 131104 | tf_op jit(solution)/shard_map/ppermute | solution.py:20
  52.7 2.8 %collective-permute-done.2 = bf16[16,4,8,128]{3,2,1,0:T(8,128)(2,1)S(1)} collective-permute-done((bf16[16,4,8,128]{3,2,1,0:T(8,128)(2,1)}, bf16[16,4,8,128]{3,2,1,0:T(8,128)(2,1)S(1)}, u32[]{:S(2)}, u32[]{:S(2)}) %collective-permute-start.2) | collective-permute-done | bytes 131104 | tf_op jit(solution)/shard_map/ppermute | solution.py:20
  55.5 0.1 fusion
  55.6 1.3 %collective-permute-start.4 = (bf16[16,4,8,128]{3,2,1,0:T(8,128)(2,1)S(1)}, bf16[16,4,8,128]{3,2,1,0:T(8,128)(2,1)S(1)}, u32[]{:S(2)}, u32[]{:S(2)}) collective-permute-start(bf16[16,4,8,128]{3,2,1,0:T(8,128)(2,1)S(1)} %fusion), channel_id=1, source_target_pairs={{0,4},{2,6},{4,8},{6,10},{8,12},{10,14},{1,5},{3,7},{5,9},{7,11},{... | collective-permute-start | bytes 393224 | tf_op jit(solution)/shard_map/ppermute | solution.py:20
  56.9 5.6 %collective-permute-done.4 = bf16[16,4,8,128]{3,2,1,0:T(8,128)(2,1)S(1)} collective-permute-done((bf16[16,4,8,128]{3,2,1,0:T(8,128)(2,1)S(1)}, bf16[16,4,8,128]{3,2,1,0:T(8,128)(2,1)S(1)}, u32[]{:S(2)}, u32[]{:S(2)}) %collective-permute-start.4) | collective-permute-done | bytes 131104 | tf_op jit(solution)/shard_map/ppermute | solution.py:20
  62.4 0.1 fusion.1
  62.6 1.3 %collective-permute-start.5 = (bf16[16,4,8,128]{3,2,1,0:T(8,128)(2,1)S(1)}, bf16[16,4,8,128]{3,2,1,0:T(8,128)(2,1)S(1)}, u32[]{:S(2)}, u32[]{:S(2)}) collective-permute-start(bf16[16,4,8,128]{3,2,1,0:T(8,128)(2,1)S(1)} %fusion.1), channel_id=1, source_target_pairs={{0,8},{2,10},{4,12},{6,14},{1,9},{3,11},{5,13},{7,15},{16,24},{18,... | collective-permute-start | bytes 393224 | tf_op jit(solution)/shard_map/ppermute | solution.py:20
  63.9 8.1 %collective-permute-done.5 = bf16[16,4,8,128]{3,2,1,0:T(8,128)(2,1)S(1)} collective-permute-done((bf16[16,4,8,128]{3,2,1,0:T(8,128)(2,1)S(1)}, bf16[16,4,8,128]{3,2,1,0:T(8,128)(2,1)S(1)}, u32[]{:S(2)}, u32[]{:S(2)}) %collective-permute-start.5) | collective-permute-done | bytes 131104 | tf_op jit(solution)/shard_map/ppermute | solution.py:20
  72.0 0.9 %multiply_add_fusion.h0_ref = f32[16,4,8,128]{3,2,1,0:T(8,128)} fusion(bf16[16,4,8,128]{3,2,1,0:T(8,128)(2,1)S(1)} %collective-permute-done.5, f32[16,4,8,128]{3,2,1,0:T(8,128)S(1)} %bitcast.12, bf16[16,4,8,128]{3,2,1,0:T(8,128)(2,1)S(1)} %collective-permute-done.4, bf16[16,4,8,128]{3,2,1,0:T(8,128)(2,1)S(1)} %collective-permute-done.3, ...), kind=kLoop, calls=%fused_computation.1 | loop fusion | flops 851968 | bytes 1048576 | tf_op jit(solution)/shard_map/add | solution.py:199
  72.8 7.8 %shard_map.93 = bf16[4096,128]{1,0:T(8,128)(2,1)} custom-call(f32[4096,128]{1,0:T(8,128)} %get-tuple-element.15.am_ref, f32[4096,128]{1,0:T(8,128)} %get-tuple-element.19.vt_ref, bf16[4096,128]{1,0:T(8,128)(2,1)} %gl_ref.1, f32[16,4,8,128]{3,2,1,0:T(8,128)} %negate_exponential_fusion.lam_ref, f32[16,4,8,128]{3,2,1,0:T(8,128)} %bitcast.13, ...), custom_call_target="tpu_custom_call" | custom-call | tf_op jit(solution)/shard_map/pallas_call | solution.py:145
Async XLA Ops:
  0.0 5.3 %copy-start = (f32[4096,16]{0,1:T(8,128)S(1)}, f32[4096,16]{0,1:T(8,128)}, u32[]{:S(2)}) copy-start(f32[4096,16]{0,1:T(8,128)} %param.15) | copy-start | bytes 786436
  0.0 5.3 %copy-start.2 = (f32[4096,16]{0,1:T(8,128)S(1)}, f32[4096,16]{0,1:T(8,128)}, u32[]{:S(2)}) copy-start(f32[4096,16]{0,1:T(8,128)} %param.16) | copy-start | bytes 786436
  0.0 29.6 %copy-start.3 = (f32[4096]{0:T(1024)S(1)}, f32[4096]{0:T(1024)}, u32[]{:S(2)}) copy-start(f32[4096]{0:T(1024)} %param.17) | copy-start | bytes 49156
  1.9 27.7 %collective-permute-start = (bf16[4096,128]{1,0:T(8,128)(2,1)S(1)}, bf16[4096,128]{1,0:T(8,128)(2,1)S(1)}, u32[]{:S(2)}, u32[]{:S(2)}) collective-permute-start(bf16[4096,128]{1,0:T(8,128)(2,1)S(1)} %multiply_convert_fusion), channel_id=1, source_target_pairs={{0,2},{2,4},{4,6},{6,8},{8,10},{10,12},{12,14},{1,3},{3,5},{5,7},{... | collective-permute-start | bytes 3145736 | tf_op jit(solution)/shard_map/ppermute | solution.py:20
  29.6 1.9 %copy-start.1 = (bf16[4096,128]{1,0:T(8,128)(2,1)}, bf16[4096,128]{1,0:T(8,128)(2,1)S(1)}, u32[]{:S(2)}) copy-start(bf16[4096,128]{1,0:T(8,128)(2,1)S(1)} %collective-permute-done.rim_ref) | copy-start | bytes 3145732
  36.7 1.2 %collective-permute-start.1 = (f32[1,128]{1,0:T(1,128)}, f32[1,128]{1,0:T(1,128)S(1)}, u32[]{:S(2)}, u32[]{:S(2)}) collective-permute-start(f32[1,128]{1,0:T(1,128)} %get-tuple-element.17), channel_id=1, source_target_pairs={{0,1},{1,0},{2,3},{3,2},{4,5},{5,4},{6,7},{7,6},{8,9},{9,8},{10,11... | collective-permute-start | bytes 1544 | tf_op jit(solution)/shard_map/ppermute | solution.py:184
  45.0 7.7 %collective-permute-start.3 = (bf16[16,4,8,128]{3,2,1,0:T(8,128)(2,1)}, bf16[16,4,8,128]{3,2,1,0:T(8,128)(2,1)S(1)}, u32[]{:S(2)}, u32[]{:S(2)}) collective-permute-start(bf16[16,4,8,128]{3,2,1,0:T(8,128)(2,1)} %get-tuple-element.21), channel_id=1, source_target_pairs={{0,4},{2,6},{4,8},{6,10},{8,12},{10,14},{1,5},{3,7},{5,9},{7,11},{... | collective-permute-start | bytes 393224 | tf_op jit(solution)/shard_map/ppermute | solution.py:20
  46.2 9.3 %collective-permute-start.2 = (bf16[16,4,8,128]{3,2,1,0:T(8,128)(2,1)}, bf16[16,4,8,128]{3,2,1,0:T(8,128)(2,1)S(1)}, u32[]{:S(2)}, u32[]{:S(2)}) collective-permute-start(bf16[16,4,8,128]{3,2,1,0:T(8,128)(2,1)} %get-tuple-element.21), channel_id=1, source_target_pairs={{0,2},{2,4},{4,6},{6,8},{8,10},{10,12},{12,14},{1,3},{3,5},{5,7},{... | collective-permute-start | bytes 393224 | tf_op jit(solution)/shard_map/ppermute | solution.py:20
  55.6 6.9 %collective-permute-start.4 = (bf16[16,4,8,128]{3,2,1,0:T(8,128)(2,1)S(1)}, bf16[16,4,8,128]{3,2,1,0:T(8,128)(2,1)S(1)}, u32[]{:S(2)}, u32[]{:S(2)}) collective-permute-start(bf16[16,4,8,128]{3,2,1,0:T(8,128)(2,1)S(1)} %fusion), channel_id=1, source_target_pairs={{0,4},{2,6},{4,8},{6,10},{8,12},{10,14},{1,5},{3,7},{5,9},{7,11},{... | collective-permute-start | bytes 393224 | tf_op jit(solution)/shard_map/ppermute | solution.py:20
  62.6 9.4 %collective-permute-start.5 = (bf16[16,4,8,128]{3,2,1,0:T(8,128)(2,1)S(1)}, bf16[16,4,8,128]{3,2,1,0:T(8,128)(2,1)S(1)}, u32[]{:S(2)}, u32[]{:S(2)}) collective-permute-start(bf16[16,4,8,128]{3,2,1,0:T(8,128)(2,1)S(1)} %fusion.1), channel_id=1, source_target_pairs={{0,8},{2,10},{4,12},{6,14},{1,9},{3,11},{5,13},{7,15},{16,24},{18,... | collective-permute-start | bytes 393224 | tf_op jit(solution)/shard_map/ppermute | solution.py:20

commit v19 on v18

--- a/solution.py
+++ b/solution.py
@@ -72,7 +72,8 @@
     r = r_ref[...]
     for i in range(SUB):
         rows = slice(i * LANE, (i + 1) * LANE)
-        normed = am_ref[rows, :] * r * g_ref[rows, :]
+        gain = jnp.broadcast_to(g_ref[i : i + 1, :], (LANE, LANE)).T
+        normed = am_ref[rows, :] * r * gain
         v = (kl_ref[rows, :].astype(F32) * normed).astype(BF16).astype(F32)
         vt_ref[pl.ds(i, LANE, stride=SUB), :] = v.T
 
@@ -129,7 +130,7 @@
     return pl.pallas_call(
         final_state_kernel,
         grid=(channels // TILE,),
-        in_specs=[big, big, big, pl.BlockSpec((1, length), lambda b: (0, 0)), tiled_spec(modes)],
+        in_specs=[big, big, pl.BlockSpec((SUB, LANE), lambda b: (b, 0)), pl.BlockSpec((1, length), lambda b: (0, 0)), tiled_spec(modes)],
         out_specs=[tiled_spec(modes), pl.BlockSpec((length * SUB, LANE), lambda b: (b, 0))],
         out_shape=[
             jax.ShapeDtypeStruct(lam.shape, BF16),
@@ -174,11 +175,11 @@
     source = inputs.astype(F32)
     values_medium = (key_medium.astype(F32) * source).astype(BF16)
     rim = shifted(values_medium, "context", 1)
-    gain = jnp.broadcast_to(norm_gain[:, None], inputs.shape)
+    gain = norm_gain.reshape(channels // LANE, LANE)
     a_t = to_tiles(log_decay)
     lam = jnp.exp(-a_t)
     w = to_tiles(residues * jnp.sqrt(2.0 * log_decay))
-    rim, gain, a_t, lam, w = lax.optimization_barrier((rim, gain, a_t, lam, w))
+    rim, a_t, lam, w = lax.optimization_barrier((rim, a_t, lam, w))
     after_medium, partial = medium_call(inputs, gate_medium, key_medium, rim, medium_taps)
     if lax.axis_size("tensor") == 2:
         totals = partial + lax.ppermute(partial, "tensor", [(0, 1), (1, 0)])

time: 81.3 us -> 81.1 us (level)
  local copies, waits for them, and re-layouts: 2.75 us -> 1.79 us
    broadcast_in_dim x1 -> x0, local copies, waits for them, and re-layouts: 1.93 us -> none  [on_device(): gain = jnp.broadcast_to(norm_gain[:, None], inputs.shape)]
    unnamed x10 -> x8, local copies, waits for them, and re-layouts: 0.82 us -> 1.79 us
where the time goes in v19:
time: 81.1 us; the launch traced here: 80.4 us
  waiting for transfers between devices  44.2 us (55%)
  Pallas kernels  19.5 us (24%)
  starting transfers between devices  9.77 us (12%)
  other arithmetic  5.03 us (6%)
  local copies, waits for them, and re-layouts  1.79 us (2%)
    ppermute x5, waiting for transfers between devices, shifted(): return lax.ppermute(block, axis, route)  43 us
    ppermute x5, starting transfers between devices, shifted(): return lax.ppermute(block, axis, route)  9.76 us
    pallas_call x1, Pallas kernels, output_call(): pl.pallas_call(output_kernel, grid=(channels // TILE,), in_specs=[big, pl...  7.75 us
    pallas_call x1, Pallas kernels, final_state_call(): pl.pallas_call(final_state_kernel, grid=(channels // TILE,), in_specs=[bi...  6.57 us
    pallas_call x1, Pallas kernels, medium_call(): pl.pallas_call(medium_kernel, grid=(channels // block,), in_specs=[big, b...  5.19 us
    convert_element_type x1, other arithmetic, on_device(): values_medium = (key_medium.astype(F32) * source).astype(BF16)  1.87 us
    unnamed x8, local copies, waits for them, and re-layouts  1.79 us
  transfers between devices with their start and end apart: 6, of which 6 were waited for; matrix products, arithmetic and copies ran while one was open for 2% of the time, Pallas kernels for 0%

profile of v19, /device:TPU:24, one launch (start us, length us, event | category | flops | bytes accessed | tf_op | source)
XLA Modules:
  0.0 80.4 jit_solution(1309536325454517899)
XLA Ops:
  0.0 0.0 copy-start
  0.0 0.0 copy-start.2
  0.0 1.9 %multiply_convert_fusion = bf16[4096,128]{1,0:T(8,128)(2,1)S(1)} fusion(bf16[4096,128]{1,0:T(8,128)(2,1)} %x_ref.1, bf16[4096,128]{1,0:T(8,128)(2,1)} %km_ref.1), kind=kLoop, calls=%fused_computation | loop fusion | flops 2097152 | bytes 3145728 | tf_op jit(solution)/shard_map/convert_element_type | solution.py:176
  1.9 3.4 %collective-permute-start = (bf16[4096,128]{1,0:T(8,128)(2,1)S(1)}, bf16[4096,128]{1,0:T(8,128)(2,1)S(1)}, u32[]{:S(2)}, u32[]{:S(2)}) collective-permute-start(bf16[4096,128]{1,0:T(8,128)(2,1)S(1)} %multiply_convert_fusion), channel_id=1, source_target_pairs={{0,2},{2,4},{4,6},{6,8},{8,10},{10,12},{12,14},{1,3},{3,5},{5,7},{... | collective-permute-start | bytes 3145736 | tf_op jit(solution)/shard_map/ppermute | solution.py:20
  5.3 0.0 copy-done
  5.3 0.0 copy-done.2
  5.3 0.1 multiply_bitcast_fusion
  5.4 0.8 copy.11
  6.2 0.1 copy.10
  6.2 0.7 negate_exponential_fusion.lam_ref
  7.0 22.6 %collective-permute-done.rim_ref = bf16[4096,128]{1,0:T(8,128)(2,1)S(1)} collective-permute-done((bf16[4096,128]{1,0:T(8,128)(2,1)S(1)}, bf16[4096,128]{1,0:T(8,128)(2,1)S(1)}, u32[]{:S(2)}, u32[]{:S(2)}) %collective-permute-start) | collective-permute-done | bytes 1048608 | tf_op jit(solution)/shard_map/ppermute | solution.py:20
  29.6 0.0 copy-start.1
  29.6 1.0 %copy-done.1 = bf16[4096,128]{1,0:T(8,128)(2,1)} copy-done((bf16[4096,128]{1,0:T(8,128)(2,1)}, bf16[4096,128]{1,0:T(8,128)(2,1)S(1)}, u32[]{:S(2)}) %copy-start.1) | copy-done | bytes 1048600
  30.5 5.2 %shard_map.91 = (f32[4096,128]{1,0:T(8,128)}, f32[1,128]{1,0:T(1,128)}) custom-call(bf16[4096,128]{1,0:T(8,128)(2,1)} %x_ref.1, bf16[4096,128]{1,0:T(8,128)(2,1)} %gm_ref.1, bf16[4096,128]{1,0:T(8,128)(2,1)} %km_ref.1, bf16[4096,128]{1,0:T(8,128)(2,1)} %copy-done.1, bf16[256,128]{1,0:T(8,128)(2,1)} %taps_ref.1), custom_call_target="tpu_custom_call" | custom-call | tf_op jit(solution)/shard_map/pallas_call | solution.py:58
  35.7 0.0 collective-permute-start.1
  35.7 1.2 %collective-permute-done.1 = f32[1,128]{1,0:T(1,128)S(1)} collective-permute-done((f32[1,128]{1,0:T(1,128)}, f32[1,128]{1,0:T(1,128)S(1)}, u32[]{:S(2)}, u32[]{:S(2)}) %collective-permute-start.1) | collective-permute-done | bytes 544 | tf_op jit(solution)/shard_map/ppermute | solution.py:185
  36.9 1.2 %add_rsqrt_fusion.r_ref = f32[1,128]{1,0:T(1,128)} fusion(f32[1,128]{1,0:T(1,128)} %get-tuple-element.15, f32[1,128]{1,0:T(1,128)S(1)} %collective-permute-done.1), kind=kLoop, calls=%fused_computation.8 | loop fusion | flops 384 | bytes 1536 | tf_op jit(solution)/shard_map/rsqrt | solution.py:188
  38.2 6.6 %shard_map.92 = (bf16[16,4,8,128]{3,2,1,0:T(8,128)(2,1)}, f32[4096,128]{1,0:T(8,128)}) custom-call(f32[4096,128]{1,0:T(8,128)} %get-tuple-element.14.am_ref, bf16[4096,128]{1,0:T(8,128)(2,1)} %kl_ref.1, f32[32,128]{1,0:T(8,128)} %bitcast.16, f32[1,128]{1,0:T(1,128)} %add_rsqrt_fusion.r_ref, f32[16,4,8,128]{3,2,1,0:T(8,128)} %negate_exponential_fusion.lam_ref), custom_call_target="tpu_custom_call" | custom-call | tf_op jit(solution)/shard_map/pallas_call | solution.py:130
  44.7 1.3 %collective-permute-start.3 = (bf16[16,4,8,128]{3,2,1,0:T(8,128)(2,1)}, bf16[16,4,8,128]{3,2,1,0:T(8,128)(2,1)S(1)}, u32[]{:S(2)}, u32[]{:S(2)}) collective-permute-start(bf16[16,4,8,128]{3,2,1,0:T(8,128)(2,1)} %get-tuple-element.19), channel_id=1, source_target_pairs={{0,4},{2,6},{4,8},{6,10},{8,12},{10,14},{1,5},{3,7},{5,9},{7,11},{... | collective-permute-start | bytes 393224 | tf_op jit(solution)/shard_map/ppermute | solution.py:20
  46.0 2.5 %collective-permute-start.2 = (bf16[16,4,8,128]{3,2,1,0:T(8,128)(2,1)}, bf16[16,4,8,128]{3,2,1,0:T(8,128)(2,1)S(1)}, u32[]{:S(2)}, u32[]{:S(2)}) collective-permute-start(bf16[16,4,8,128]{3,2,1,0:T(8,128)(2,1)} %get-tuple-element.19), channel_id=1, source_target_pairs={{0,2},{2,4},{4,6},{6,8},{8,10},{10,12},{12,14},{1,3},{3,5},{5,7},{... | collective-permute-start | bytes 393224 | tf_op jit(solution)/shard_map/ppermute | solution.py:20
  48.5 3.9 %collective-permute-done.3 = bf16[16,4,8,128]{3,2,1,0:T(8,128)(2,1)S(1)} collective-permute-done((bf16[16,4,8,128]{3,2,1,0:T(8,128)(2,1)}, bf16[16,4,8,128]{3,2,1,0:T(8,128)(2,1)S(1)}, u32[]{:S(2)}, u32[]{:S(2)}) %collective-permute-start.3) | collective-permute-done | bytes 131104 | tf_op jit(solution)/shard_map/ppermute | solution.py:20
  52.4 2.8 %collective-permute-done.2 = bf16[16,4,8,128]{3,2,1,0:T(8,128)(2,1)S(1)} collective-permute-done((bf16[16,4,8,128]{3,2,1,0:T(8,128)(2,1)}, bf16[16,4,8,128]{3,2,1,0:T(8,128)(2,1)S(1)}, u32[]{:S(2)}, u32[]{:S(2)}) %collective-permute-start.2) | collective-permute-done | bytes 131104 | tf_op jit(solution)/shard_map/ppermute | solution.py:20
  55.3 0.1 fusion
  55.3 1.3 %collective-permute-start.4 = (bf16[16,4,8,128]{3,2,1,0:T(8,128)(2,1)S(1)}, bf16[16,4,8,128]{3,2,1,0:T(8,128)(2,1)S(1)}, u32[]{:S(2)}, u32[]{:S(2)}) collective-permute-start(bf16[16,4,8,128]{3,2,1,0:T(8,128)(2,1)S(1)} %fusion), channel_id=1, source_target_pairs={{0,4},{2,6},{4,8},{6,10},{8,12},{10,14},{1,5},{3,7},{5,9},{7,11},{... | collective-permute-start | bytes 393224 | tf_op jit(solution)/shard_map/ppermute | solution.py:20
  56.6 5.6 %collective-permute-done.4 = bf16[16,4,8,128]{3,2,1,0:T(8,128)(2,1)S(1)} collective-permute-done((bf16[16,4,8,128]{3,2,1,0:T(8,128)(2,1)S(1)}, bf16[16,4,8,128]{3,2,1,0:T(8,128)(2,1)S(1)}, u32[]{:S(2)}, u32[]{:S(2)}) %collective-permute-start.4) | collective-permute-done | bytes 131104 | tf_op jit(solution)/shard_map/ppermute | solution.py:20
  62.2 0.1 fusion.1
  62.3 1.3 %collective-permute-start.5 = (bf16[16,4,8,128]{3,2,1,0:T(8,128)(2,1)S(1)}, bf16[16,4,8,128]{3,2,1,0:T(8,128)(2,1)S(1)}, u32[]{:S(2)}, u32[]{:S(2)}) collective-permute-start(bf16[16,4,8,128]{3,2,1,0:T(8,128)(2,1)S(1)} %fusion.1), channel_id=1, source_target_pairs={{0,8},{2,10},{4,12},{6,14},{1,9},{3,11},{5,13},{7,15},{16,24},{18,... | collective-permute-start | bytes 393224 | tf_op jit(solution)/shard_map/ppermute | solution.py:20
  63.6 8.1 %collective-permute-done.5 = bf16[16,4,8,128]{3,2,1,0:T(8,128)(2,1)S(1)} collective-permute-done((bf16[16,4,8,128]{3,2,1,0:T(8,128)(2,1)S(1)}, bf16[16,4,8,128]{3,2,1,0:T(8,128)(2,1)S(1)}, u32[]{:S(2)}, u32[]{:S(2)}) %collective-permute-start.5) | collective-permute-done | bytes 131104 | tf_op jit(solution)/shard_map/ppermute | solution.py:20
  71.7 0.9 %multiply_add_fusion.h0_ref = f32[16,4,8,128]{3,2,1,0:T(8,128)} fusion(bf16[16,4,8,128]{3,2,1,0:T(8,128)(2,1)S(1)} %collective-permute-done.5, f32[16,4,8,128]{3,2,1,0:T(8,128)S(1)} %bitcast.13, bf16[16,4,8,128]{3,2,1,0:T(8,128)(2,1)S(1)} %collective-permute-done.4, bf16[16,4,8,128]{3,2,1,0:T(8,128)(2,1)S(1)} %collective-permute-done.3, ...), kind=kLoop, calls=%fused_computation.1 | loop fusion | flops 851968 | bytes 1048576 | tf_op jit(solution)/shard_map/add | solution.py:200
  72.6 7.8 %shard_map.93 = bf16[4096,128]{1,0:T(8,128)(2,1)} custom-call(f32[4096,128]{1,0:T(8,128)} %get-tuple-element.14.am_ref, f32[4096,128]{1,0:T(8,128)} %get-tuple-element.17.vt_ref, bf16[4096,128]{1,0:T(8,128)(2,1)} %gl_ref.1, f32[16,4,8,128]{3,2,1,0:T(8,128)} %negate_exponential_fusion.lam_ref, f32[16,4,8,128]{3,2,1,0:T(8,128)} %bitcast.14, ...), custom_call_target="tpu_custom_call" | custom-call | tf_op jit(solution)/shard_map/pallas_call | solution.py:146
Async XLA Ops:
  0.0 5.3 %copy-start = (f32[4096,16]{0,1:T(8,128)S(1)}, f32[4096,16]{0,1:T(8,128)}, u32[]{:S(2)}) copy-start(f32[4096,16]{0,1:T(8,128)} %param.15) | copy-start | bytes 786436
  0.0 5.3 %copy-start.2 = (f32[4096,16]{0,1:T(8,128)S(1)}, f32[4096,16]{0,1:T(8,128)}, u32[]{:S(2)}) copy-start(f32[4096,16]{0,1:T(8,128)} %param.16) | copy-start | bytes 786436
  1.9 27.7 %collective-permute-start = (bf16[4096,128]{1,0:T(8,128)(2,1)S(1)}, bf16[4096,128]{1,0:T(8,128)(2,1)S(1)}, u32[]{:S(2)}, u32[]{:S(2)}) collective-permute-start(bf16[4096,128]{1,0:T(8,128)(2,1)S(1)} %multiply_convert_fusion), channel_id=1, source_target_pairs={{0,2},{2,4},{4,6},{6,8},{8,10},{10,12},{12,14},{1,3},{3,5},{5,7},{... | collective-permute-start | bytes 3145736 | tf_op jit(solution)/shard_map/ppermute | solution.py:20
  29.6 1.0 %copy-start.1 = (bf16[4096,128]{1,0:T(8,128)(2,1)}, bf16[4096,128]{1,0:T(8,128)(2,1)S(1)}, u32[]{:S(2)}) copy-start(bf16[4096,128]{1,0:T(8,128)(2,1)S(1)} %collective-permute-done.rim_ref) | copy-start | bytes 3145732
  35.7 1.2 %collective-permute-start.1 = (f32[1,128]{1,0:T(1,128)}, f32[1,128]{1,0:T(1,128)S(1)}, u32[]{:S(2)}, u32[]{:S(2)}) collective-permute-start(f32[1,128]{1,0:T(1,128)} %get-tuple-element.15), channel_id=1, source_target_pairs={{0,1},{1,0},{2,3},{3,2},{4,5},{5,4},{6,7},{7,6},{8,9},{9,8},{10,11... | collective-permute-start | bytes 1544 | tf_op jit(solution)/shard_map/ppermute | solution.py:185
  44.7 7.7 %collective-permute-start.3 = (bf16[16,4,8,128]{3,2,1,0:T(8,128)(2,1)}, bf16[16,4,8,128]{3,2,1,0:T(8,128)(2,1)S(1)}, u32[]{:S(2)}, u32[]{:S(2)}) collective-permute-start(bf16[16,4,8,128]{3,2,1,0:T(8,128)(2,1)} %get-tuple-element.19), channel_id=1, source_target_pairs={{0,4},{2,6},{4,8},{6,10},{8,12},{10,14},{1,5},{3,7},{5,9},{7,11},{... | collective-permute-start | bytes 393224 | tf_op jit(solution)/shard_map/ppermute | solution.py:20
  46.0 9.3 %collective-permute-start.2 = (bf16[16,4,8,128]{3,2,1,0:T(8,128)(2,1)}, bf16[16,4,8,128]{3,2,1,0:T(8,128)(2,1)S(1)}, u32[]{:S(2)}, u32[]{:S(2)}) collective-permute-start(bf16[16,4,8,128]{3,2,1,0:T(8,128)(2,1)} %get-tuple-element.19), channel_id=1, source_target_pairs={{0,2},{2,4},{4,6},{6,8},{8,10},{10,12},{12,14},{1,3},{3,5},{5,7},{... | collective-permute-start | bytes 393224 | tf_op jit(solution)/shard_map/ppermute | solution.py:20
  55.3 6.9 %collective-permute-start.4 = (bf16[16,4,8,128]{3,2,1,0:T(8,128)(2,1)S(1)}, bf16[16,4,8,128]{3,2,1,0:T(8,128)(2,1)S(1)}, u32[]{:S(2)}, u32[]{:S(2)}) collective-permute-start(bf16[16,4,8,128]{3,2,1,0:T(8,128)(2,1)S(1)} %fusion), channel_id=1, source_target_pairs={{0,4},{2,6},{4,8},{6,10},{8,12},{10,14},{1,5},{3,7},{5,9},{7,11},{... | collective-permute-start | bytes 393224 | tf_op jit(solution)/shard_map/ppermute | solution.py:20
  62.3 9.4 %collective-permute-start.5 = (bf16[16,4,8,128]{3,2,1,0:T(8,128)(2,1)S(1)}, bf16[16,4,8,128]{3,2,1,0:T(8,128)(2,1)S(1)}, u32[]{:S(2)}, u32[]{:S(2)}) collective-permute-start(bf16[16,4,8,128]{3,2,1,0:T(8,128)(2,1)S(1)} %fusion.1), channel_id=1, source_target_pairs={{0,8},{2,10},{4,12},{6,14},{1,9},{3,11},{5,13},{7,15},{16,24},{18,... | collective-permute-start | bytes 393224 | tf_op jit(solution)/shard_map/ppermute | solution.py:20

commit v20 on v19

--- a/solution.py
+++ b/solution.py
@@ -68,8 +68,8 @@
     )(inputs, gate_medium, key_medium, rim, taps)
 
 
-def load_values(am_ref, kl_ref, g_ref, r_ref, vt_ref):
-    r = r_ref[...]
+def load_values(am_ref, kl_ref, g_ref, p_ref, q_ref, vt_ref, width):
+    r = lax.rsqrt((p_ref[...] + q_ref[...]) / width + EPS)
     for i in range(SUB):
         rows = slice(i * LANE, (i + 1) * LANE)
         gain = jnp.broadcast_to(g_ref[i : i + 1, :], (LANE, LANE)).T
@@ -82,10 +82,10 @@
     return ref[pl.ds(pl.multiple_of(t * SUB, SUB), SUB), :]
 
 
-def final_state_kernel(am_ref, kl_ref, g_ref, r_ref, lam_ref, f_ref, vt_ref):
+def final_state_kernel(width, am_ref, kl_ref, g_ref, p_ref, q_ref, lam_ref, f_ref, vt_ref):
     modes = lam_ref.shape[0]
     length = am_ref.shape[1]
-    load_values(am_ref, kl_ref, g_ref, r_ref, vt_ref)
+    load_values(am_ref, kl_ref, g_ref, p_ref, q_ref, vt_ref, width)
     lam = [lam_ref[m] for m in range(modes)]
 
     def body(t, h):
@@ -123,20 +123,21 @@
     return pl.BlockSpec((lead, None, SUB, LANE), lambda b: (0, b, 0, 0))
 
 
-def final_state_call(am, kl, gain, r, lam):
+def final_state_call(am, kl, gain, mine, other, lam, width):
     channels, length = am.shape
     modes = lam.shape[0]
     big = pl.BlockSpec((TILE, length), lambda b: (b, 0))
+    row = pl.BlockSpec((1, length), lambda b: (0, 0))
     return pl.pallas_call(
-        final_state_kernel,
+        functools.partial(final_state_kernel, float(width)),
         grid=(channels // TILE,),
-        in_specs=[big, big, pl.BlockSpec((SUB, LANE), lambda b: (b, 0)), pl.BlockSpec((1, length), lambda b: (0, 0)), tiled_spec(modes)],
+        in_specs=[big, big, pl.BlockSpec((SUB, LANE), lambda b: (b, 0)), row, row, tiled_spec(modes)],
         out_specs=[tiled_spec(modes), pl.BlockSpec((length * SUB, LANE), lambda b: (b, 0))],
         out_shape=[
             jax.ShapeDtypeStruct(lam.shape, BF16),
             jax.ShapeDtypeStruct((channels // TILE * length * SUB, LANE), F32),
         ],
-    )(am, kl, gain, r, lam)
+    )(am, kl, gain, mine, other, lam)
 
 
 def output_call(am, vt, gl, lam, w, h0):
@@ -182,11 +183,10 @@
     rim, a_t, lam, w = lax.optimization_barrier((rim, a_t, lam, w))
     after_medium, partial = medium_call(inputs, gate_medium, key_medium, rim, medium_taps)
     if lax.axis_size("tensor") == 2:
-        totals = partial + lax.ppermute(partial, "tensor", [(0, 1), (1, 0)])
+        other = lax.ppermute(partial, "tensor", [(0, 1), (1, 0)])
     else:
-        totals = lax.psum(partial, "tensor")
-    r = lax.rsqrt(totals / width + EPS)
-    finals, vt = final_state_call(after_medium, key_long, gain, r, lam)
+        partial, other = lax.psum(partial, "tensor"), jnp.zeros_like(partial)
+    finals, vt = final_state_call(after_medium, key_long, gain, partial, other, lam, width)
 
     sent = finals
     carried = shifted(sent, "context", 1).astype(F32)

time: 81.1 us -> 80.6 us (level)
  other arithmetic: 5.03 us -> 3.79 us
    rsqrt x1 -> x0, other arithmetic: 1.24 us -> none  [on_device(): r = lax.rsqrt(totals / width + EPS)]
    unnamed x8 -> x10, local copies, waits for them, and re-layouts: 1.79 us -> 2.38 us
where the time goes in v20:
time: 80.6 us; the launch traced here: 79.9 us
  waiting for transfers between devices  44.3 us (55%)
  Pallas kernels  19.5 us (24%)
  starting transfers between devices  9.77 us (12%)
  other arithmetic  3.79 us (5%)
  local copies, waits for them, and re-layouts  2.38 us (3%)
    ppermute x5, waiting for transfers between devices, shifted(): return lax.ppermute(block, axis, route)  43 us
    ppermute x5, starting transfers between devices, shifted(): return lax.ppermute(block, axis, route)  9.76 us
    pallas_call x1, Pallas kernels, output_call(): pl.pallas_call(output_kernel, grid=(channels // TILE,), in_specs=[big, pl...  7.75 us
    pallas_call x1, Pallas kernels, final_state_call(): pl.pallas_call(functools.partial(final_state_kernel, float(width)), grid=...  6.6 us
    pallas_call x1, Pallas kernels, medium_call(): pl.pallas_call(medium_kernel, grid=(channels // block,), in_specs=[big, b...  5.17 us
    unnamed x10, local copies, waits for them, and re-layouts  2.38 us
    convert_element_type x1, other arithmetic, on_device(): values_medium = (key_medium.astype(F32) * source).astype(BF16)  1.87 us
  transfers between devices with their start and end apart: 6, of which 6 were waited for; matrix products, arithmetic and copies ran while one was open for 2% of the time, Pallas kernels for 0%

profile of v20, /device:TPU:24, one launch (start us, length us, event | category | flops | bytes accessed | tf_op | source)
XLA Modules:
  0.0 79.9 jit_solution(8740015911972128267)
XLA Ops:
  0.0 0.0 copy-start
  0.0 0.0 copy-start.2
  0.0 1.9 %multiply_convert_fusion = bf16[4096,128]{1,0:T(8,128)(2,1)S(1)} fusion(bf16[4096,128]{1,0:T(8,128)(2,1)} %x_ref.1, bf16[4096,128]{1,0:T(8,128)(2,1)} %km_ref.1), kind=kLoop, calls=%fused_computation | loop fusion | flops 2097152 | bytes 3145728 | tf_op jit(solution)/shard_map/convert_element_type | solution.py:177
  1.9 3.4 %collective-permute-start = (bf16[4096,128]{1,0:T(8,128)(2,1)S(1)}, bf16[4096,128]{1,0:T(8,128)(2,1)S(1)}, u32[]{:S(2)}, u32[]{:S(2)}) collective-permute-start(bf16[4096,128]{1,0:T(8,128)(2,1)S(1)} %multiply_convert_fusion), channel_id=1, source_target_pairs={{0,2},{2,4},{4,6},{6,8},{8,10},{10,12},{12,14},{1,3},{3,5},{5,7},{... | collective-permute-start | bytes 3145736 | tf_op jit(solution)/shard_map/ppermute | solution.py:20
  5.3 0.0 copy-done
  5.3 0.0 copy-done.2
  5.3 0.1 multiply_bitcast_fusion
  5.4 0.8 copy.11
  6.2 0.1 copy.10
  6.2 0.7 negate_exponential_fusion.lam_ref
  7.0 22.6 %collective-permute-done.rim_ref = bf16[4096,128]{1,0:T(8,128)(2,1)S(1)} collective-permute-done((bf16[4096,128]{1,0:T(8,128)(2,1)S(1)}, bf16[4096,128]{1,0:T(8,128)(2,1)S(1)}, u32[]{:S(2)}, u32[]{:S(2)}) %collective-permute-start) | collective-permute-done | bytes 1048608 | tf_op jit(solution)/shard_map/ppermute | solution.py:20
  29.6 0.0 copy-start.1
  29.6 1.0 %copy-done.1 = bf16[4096,128]{1,0:T(8,128)(2,1)} copy-done((bf16[4096,128]{1,0:T(8,128)(2,1)}, bf16[4096,128]{1,0:T(8,128)(2,1)S(1)}, u32[]{:S(2)}) %copy-start.1) | copy-done | bytes 1048600
  30.5 5.2 %shard_map.91 = (f32[4096,128]{1,0:T(8,128)}, f32[1,128]{1,0:T(1,128)}) custom-call(bf16[4096,128]{1,0:T(8,128)(2,1)} %x_ref.1, bf16[4096,128]{1,0:T(8,128)(2,1)} %gm_ref.1, bf16[4096,128]{1,0:T(8,128)(2,1)} %km_ref.1, bf16[4096,128]{1,0:T(8,128)(2,1)} %copy-done.1, bf16[256,128]{1,0:T(8,128)(2,1)} %taps_ref.1), custom_call_target="tpu_custom_call" | custom-call | tf_op jit(solution)/shard_map/pallas_call | solution.py:58
  35.7 0.0 collective-permute-start.1
  35.7 1.3 %collective-permute-done.1.q_ref = f32[1,128]{1,0:T(1,128)S(1)} collective-permute-done((f32[1,128]{1,0:T(1,128)}, f32[1,128]{1,0:T(1,128)S(1)}, u32[]{:S(2)}, u32[]{:S(2)}) %collective-permute-start.1) | collective-permute-done | bytes 544 | tf_op jit(solution)/shard_map/ppermute | solution.py:186
  37.0 0.0 copy-start.3
  37.0 0.6 copy-done.3
  37.6 6.6 %shard_map.92 = (bf16[16,4,8,128]{3,2,1,0:T(8,128)(2,1)}, f32[4096,128]{1,0:T(8,128)}) custom-call(f32[4096,128]{1,0:T(8,128)} %get-tuple-element.14.am_ref, bf16[4096,128]{1,0:T(8,128)(2,1)} %kl_ref.1, f32[32,128]{1,0:T(8,128)} %bitcast.16, f32[1,128]{1,0:T(1,128)} %get-tuple-element.15.p_ref, f32[1,128]{1,0:T(1,128)} %copy-done.3, ...), custom_call_target="tpu_custom_call" | custom-call | tf_op jit(solution)/shard_map/pallas_call | solution.py:131
  44.2 1.3 %collective-permute-start.3 = (bf16[16,4,8,128]{3,2,1,0:T(8,128)(2,1)}, bf16[16,4,8,128]{3,2,1,0:T(8,128)(2,1)S(1)}, u32[]{:S(2)}, u32[]{:S(2)}) collective-permute-start(bf16[16,4,8,128]{3,2,1,0:T(8,128)(2,1)} %get-tuple-element.19), channel_id=1, source_target_pairs={{0,4},{2,6},{4,8},{6,10},{8,12},{10,14},{1,5},{3,7},{5,9},{7,11},{... | collective-permute-start | bytes 393224 | tf_op jit(solution)/shard_map/ppermute | solution.py:20
  45.5 2.5 %collective-permute-start.2 = (bf16[16,4,8,128]{3,2,1,0:T(8,128)(2,1)}, bf16[16,4,8,128]{3,2,1,0:T(8,128)(2,1)S(1)}, u32[]{:S(2)}, u32[]{:S(2)}) collective-permute-start(bf16[16,4,8,128]{3,2,1,0:T(8,128)(2,1)} %get-tuple-element.19), channel_id=1, source_target_pairs={{0,2},{2,4},{4,6},{6,8},{8,10},{10,12},{12,14},{1,3},{3,5},{5,7},{... | collective-permute-start | bytes 393224 | tf_op jit(solution)/shard_map/ppermute | solution.py:20
  48.0 3.9 %collective-permute-done.3 = bf16[16,4,8,128]{3,2,1,0:T(8,128)(2,1)S(1)} collective-permute-done((bf16[16,4,8,128]{3,2,1,0:T(8,128)(2,1)}, bf16[16,4,8,128]{3,2,1,0:T(8,128)(2,1)S(1)}, u32[]{:S(2)}, u32[]{:S(2)}) %collective-permute-start.3) | collective-permute-done | bytes 131104 | tf_op jit(solution)/shard_map/ppermute | solution.py:20
  51.9 2.8 %collective-permute-done.2 = bf16[16,4,8,128]{3,2,1,0:T(8,128)(2,1)S(1)} collective-permute-done((bf16[16,4,8,128]{3,2,1,0:T(8,128)(2,1)}, bf16[16,4,8,128]{3,2,1,0:T(8,128)(2,1)S(1)}, u32[]{:S(2)}, u32[]{:S(2)}) %collective-permute-start.2) | collective-permute-done | bytes 131104 | tf_op jit(solution)/shard_map/ppermute | solution.py:20
  54.8 0.1 fusion
  54.9 1.3 %collective-permute-start.4 = (bf16[16,4,8,128]{3,2,1,0:T(8,128)(2,1)S(1)}, bf16[16,4,8,128]{3,2,1,0:T(8,128)(2,1)S(1)}, u32[]{:S(2)}, u32[]{:S(2)}) collective-permute-start(bf16[16,4,8,128]{3,2,1,0:T(8,128)(2,1)S(1)} %fusion), channel_id=1, source_target_pairs={{0,4},{2,6},{4,8},{6,10},{8,12},{10,14},{1,5},{3,7},{5,9},{7,11},{... | collective-permute-start | bytes 393224 | tf_op jit(solution)/shard_map/ppermute | solution.py:20
  56.2 5.6 %collective-permute-done.4 = bf16[16,4,8,128]{3,2,1,0:T(8,128)(2,1)S(1)} collective-permute-done((bf16[16,4,8,128]{3,2,1,0:T(8,128)(2,1)S(1)}, bf16[16,4,8,128]{3,2,1,0:T(8,128)(2,1)S(1)}, u32[]{:S(2)}, u32[]{:S(2)}) %collective-permute-start.4) | collective-permute-done | bytes 131104 | tf_op jit(solution)/shard_map/ppermute | solution.py:20
  61.7 0.1 fusion.1
  61.9 1.3 %collective-permute-start.5 = (bf16[16,4,8,128]{3,2,1,0:T(8,128)(2,1)S(1)}, bf16[16,4,8,128]{3,2,1,0:T(8,128)(2,1)S(1)}, u32[]{:S(2)}, u32[]{:S(2)}) collective-permute-start(bf16[16,4,8,128]{3,2,1,0:T(8,128)(2,1)S(1)} %fusion.1), channel_id=1, source_target_pairs={{0,8},{2,10},{4,12},{6,14},{1,9},{3,11},{5,13},{7,15},{16,24},{18,... | collective-permute-start | bytes 393224 | tf_op jit(solution)/shard_map/ppermute | solution.py:20
  63.2 8.1 %collective-permute-done.5 = bf16[16,4,8,128]{3,2,1,0:T(8,128)(2,1)S(1)} collective-permute-done((bf16[16,4,8,128]{3,2,1,0:T(8,128)(2,1)S(1)}, bf16[16,4,8,128]{3,2,1,0:T(8,128)(2,1)S(1)}, u32[]{:S(2)}, u32[]{:S(2)}) %collective-permute-start.5) | collective-permute-done | bytes 131104 | tf_op jit(solution)/shard_map/ppermute | solution.py:20
  71.2 0.9 %multiply_add_fusion.h0_ref = f32[16,4,8,128]{3,2,1,0:T(8,128)} fusion(bf16[16,4,8,128]{3,2,1,0:T(8,128)(2,1)S(1)} %collective-permute-done.5, f32[16,4,8,128]{3,2,1,0:T(8,128)S(1)} %bitcast.13, bf16[16,4,8,128]{3,2,1,0:T(8,128)(2,1)S(1)} %collective-permute-done.4, bf16[16,4,8,128]{3,2,1,0:T(8,128)(2,1)S(1)} %collective-permute-done.3, ...), kind=kLoop, calls=%fused_computation.1 | loop fusion | flops 851968 | bytes 1048576 | tf_op jit(solution)/shard_map/add | solution.py:200
  72.1 7.8 %shard_map.93 = bf16[4096,128]{1,0:T(8,128)(2,1)} custom-call(f32[4096,128]{1,0:T(8,128)} %get-tuple-element.14.am_ref, f32[4096,128]{1,0:T(8,128)} %get-tuple-element.17.vt_ref, bf16[4096,128]{1,0:T(8,128)(2,1)} %gl_ref.1, f32[16,4,8,128]{3,2,1,0:T(8,128)} %negate_exponential_fusion.lam_ref, f32[16,4,8,128]{3,2,1,0:T(8,128)} %bitcast.14, ...), custom_call_target="tpu_custom_call" | custom-call | tf_op jit(solution)/shard_map/pallas_call | solution.py:147
Async XLA Ops:
  0.0 5.3 %copy-start = (f32[4096,16]{0,1:T(8,128)S(1)}, f32[4096,16]{0,1:T(8,128)}, u32[]{:S(2)}) copy-start(f32[4096,16]{0,1:T(8,128)} %param.15) | copy-start | bytes 786436
  0.0 5.3 %copy-start.2 = (f32[4096,16]{0,1:T(8,128)S(1)}, f32[4096,16]{0,1:T(8,128)}, u32[]{:S(2)}) copy-start(f32[4096,16]{0,1:T(8,128)} %param.16) | copy-start | bytes 786436
  1.9 27.7 %collective-permute-start = (bf16[4096,128]{1,0:T(8,128)(2,1)S(1)}, bf16[4096,128]{1,0:T(8,128)(2,1)S(1)}, u32[]{:S(2)}, u32[]{:S(2)}) collective-permute-start(bf16[4096,128]{1,0:T(8,128)(2,1)S(1)} %multiply_convert_fusion), channel_id=1, source_target_pairs={{0,2},{2,4},{4,6},{6,8},{8,10},{10,12},{12,14},{1,3},{3,5},{5,7},{... | collective-permute-start | bytes 3145736 | tf_op jit(solution)/shard_map/ppermute | solution.py:20
  29.6 1.0 %copy-start.1 = (bf16[4096,128]{1,0:T(8,128)(2,1)}, bf16[4096,128]{1,0:T(8,128)(2,1)S(1)}, u32[]{:S(2)}) copy-start(bf16[4096,128]{1,0:T(8,128)(2,1)S(1)} %collective-permute-done.rim_ref) | copy-start | bytes 3145732
  35.7 1.3 %collective-permute-start.1 = (f32[1,128]{1,0:T(1,128)}, f32[1,128]{1,0:T(1,128)S(1)}, u32[]{:S(2)}, u32[]{:S(2)}) collective-permute-start(f32[1,128]{1,0:T(1,128)} %get-tuple-element.15.p_ref), channel_id=1, source_target_pairs={{0,1},{1,0},{2,3},{3,2},{4,5},{5,4},{6,7},{7,6},{8,9},{9,8},{10,11... | collective-permute-start | bytes 1544 | tf_op jit(solution)/shard_map/ppermute | solution.py:186
  37.0 0.6 copy-start.3
  44.2 7.7 %collective-permute-start.3 = (bf16[16,4,8,128]{3,2,1,0:T(8,128)(2,1)}, bf16[16,4,8,128]{3,2,1,0:T(8,128)(2,1)S(1)}, u32[]{:S(2)}, u32[]{:S(2)}) collective-permute-start(bf16[16,4,8,128]{3,2,1,0:T(8,128)(2,1)} %get-tuple-element.19), channel_id=1, source_target_pairs={{0,4},{2,6},{4,8},{6,10},{8,12},{10,14},{1,5},{3,7},{5,9},{7,11},{... | collective-permute-start | bytes 393224 | tf_op jit(solution)/shard_map/ppermute | solution.py:20
  45.5 9.3 %collective-permute-start.2 = (bf16[16,4,8,128]{3,2,1,0:T(8,128)(2,1)}, bf16[16,4,8,128]{3,2,1,0:T(8,128)(2,1)S(1)}, u32[]{:S(2)}, u32[]{:S(2)}) collective-permute-start(bf16[16,4,8,128]{3,2,1,0:T(8,128)(2,1)} %get-tuple-element.19), channel_id=1, source_target_pairs={{0,2},{2,4},{4,6},{6,8},{8,10},{10,12},{12,14},{1,3},{3,5},{5,7},{... | collective-permute-start | bytes 393224 | tf_op jit(solution)/shard_map/ppermute | solution.py:20
  54.9 6.9 %collective-permute-start.4 = (bf16[16,4,8,128]{3,2,1,0:T(8,128)(2,1)S(1)}, bf16[16,4,8,128]{3,2,1,0:T(8,128)(2,1)S(1)}, u32[]{:S(2)}, u32[]{:S(2)}) collective-permute-start(bf16[16,4,8,128]{3,2,1,0:T(8,128)(2,1)S(1)} %fusion), channel_id=1, source_target_pairs={{0,4},{2,6},{4,8},{6,10},{8,12},{10,14},{1,5},{3,7},{5,9},{7,11},{... | collective-permute-start | bytes 393224 | tf_op jit(solution)/shard_map/ppermute | solution.py:20
  61.9 9.4 %collective-permute-start.5 = (bf16[16,4,8,128]{3,2,1,0:T(8,128)(2,1)S(1)}, bf16[16,4,8,128]{3,2,1,0:T(8,128)(2,1)S(1)}, u32[]{:S(2)}, u32[]{:S(2)}) collective-permute-start(bf16[16,4,8,128]{3,2,1,0:T(8,128)(2,1)S(1)} %fusion.1), channel_id=1, source_target_pairs={{0,8},{2,10},{4,12},{6,14},{1,9},{3,11},{5,13},{7,15},{16,24},{18,... | collective-permute-start | bytes 393224 | tf_op jit(solution)/shard_map/ppermute | solution.py:20

commit v21 on v20

--- a/solution.py
+++ b/solution.py
@@ -70,9 +70,10 @@
 
 def load_values(am_ref, kl_ref, g_ref, p_ref, q_ref, vt_ref, width):
     r = lax.rsqrt((p_ref[...] + q_ref[...]) / width + EPS)
+    columns = g_ref[...].T
     for i in range(SUB):
         rows = slice(i * LANE, (i + 1) * LANE)
-        gain = jnp.broadcast_to(g_ref[i : i + 1, :], (LANE, LANE)).T
+        gain = jnp.broadcast_to(columns[:, i : i + 1], (LANE, LANE))
         normed = am_ref[rows, :] * r * gain
         v = (kl_ref[rows, :].astype(F32) * normed).astype(BF16).astype(F32)
         vt_ref[pl.ds(i, LANE, stride=SUB), :] = v.T

time: 80.6 us -> 80.8 us (level)
  no operation moved by 1% of the time
where the time goes in v21:
time: 80.8 us; the launch traced here: 80.1 us
  waiting for transfers between devices  44.3 us (55%)
  Pallas kernels  19.7 us (24%)
  starting transfers between devices  9.77 us (12%)
  other arithmetic  3.79 us (5%)
  local copies, waits for them, and re-layouts  2.38 us (3%)
    ppermute x5, waiting for transfers between devices, shifted(): return lax.ppermute(block, axis, route)  43 us
    ppermute x5, starting transfers between devices, shifted(): return lax.ppermute(block, axis, route)  9.76 us
    pallas_call x1, Pallas kernels, output_call(): pl.pallas_call(output_kernel, grid=(channels // TILE,), in_specs=[big, pl...  7.75 us
    pallas_call x1, Pallas kernels, final_state_call(): pl.pallas_call(functools.partial(final_state_kernel, float(width)), grid=...  6.8 us
    pallas_call x1, Pallas kernels, medium_call(): pl.pallas_call(medium_kernel, grid=(channels // block,), in_specs=[big, b...  5.17 us
    unnamed x10, local copies, waits for them, and re-layouts  2.38 us
    convert_element_type x1, other arithmetic, on_device(): values_medium = (key_medium.astype(F32) * source).astype(BF16)  1.87 us
  transfers between devices with their start and end apart: 6, of which 6 were waited for; matrix products, arithmetic and copies ran while one was open for 2% of the time, Pallas kernels for 0%

profile of v21, /device:TPU:24, one launch (start us, length us, event | category | flops | bytes accessed | tf_op | source)
XLA Modules:
  0.0 80.1 jit_solution(16287137506213868286)
XLA Ops:
  0.0 0.0 copy-start
  0.0 0.0 copy-start.2
  0.0 1.9 %multiply_convert_fusion = bf16[4096,128]{1,0:T(8,128)(2,1)S(1)} fusion(bf16[4096,128]{1,0:T(8,128)(2,1)} %x_ref.1, bf16[4096,128]{1,0:T(8,128)(2,1)} %km_ref.1), kind=kLoop, calls=%fused_computation | loop fusion | flops 2097152 | bytes 3145728 | tf_op jit(solution)/shard_map/convert_element_type | solution.py:178
  1.9 3.4 %collective-permute-start = (bf16[4096,128]{1,0:T(8,128)(2,1)S(1)}, bf16[4096,128]{1,0:T(8,128)(2,1)S(1)}, u32[]{:S(2)}, u32[]{:S(2)}) collective-permute-start(bf16[4096,128]{1,0:T(8,128)(2,1)S(1)} %multiply_convert_fusion), channel_id=1, source_target_pairs={{0,2},{2,4},{4,6},{6,8},{8,10},{10,12},{12,14},{1,3},{3,5},{5,7},{... | collective-permute-start | bytes 3145736 | tf_op jit(solution)/shard_map/ppermute | solution.py:20
  5.3 0.0 copy-done
  5.3 0.0 copy-done.2
  5.3 0.1 multiply_bitcast_fusion
  5.4 0.8 copy.11
  6.2 0.1 copy.10
  6.2 0.7 negate_exponential_fusion.lam_ref
  7.0 22.6 %collective-permute-done.rim_ref = bf16[4096,128]{1,0:T(8,128)(2,1)S(1)} collective-permute-done((bf16[4096,128]{1,0:T(8,128)(2,1)S(1)}, bf16[4096,128]{1,0:T(8,128)(2,1)S(1)}, u32[]{:S(2)}, u32[]{:S(2)}) %collective-permute-start) | collective-permute-done | bytes 1048608 | tf_op jit(solution)/shard_map/ppermute | solution.py:20
  29.6 0.0 copy-start.1
  29.6 1.0 %copy-done.1 = bf16[4096,128]{1,0:T(8,128)(2,1)} copy-done((bf16[4096,128]{1,0:T(8,128)(2,1)}, bf16[4096,128]{1,0:T(8,128)(2,1)S(1)}, u32[]{:S(2)}) %copy-start.1) | copy-done | bytes 1048600
  30.5 5.2 %shard_map.91 = (f32[4096,128]{1,0:T(8,128)}, f32[1,128]{1,0:T(1,128)}) custom-call(bf16[4096,128]{1,0:T(8,128)(2,1)} %x_ref.1, bf16[4096,128]{1,0:T(8,128)(2,1)} %gm_ref.1, bf16[4096,128]{1,0:T(8,128)(2,1)} %km_ref.1, bf16[4096,128]{1,0:T(8,128)(2,1)} %copy-done.1, bf16[256,128]{1,0:T(8,128)(2,1)} %taps_ref.1), custom_call_target="tpu_custom_call" | custom-call | tf_op jit(solution)/shard_map/pallas_call | solution.py:58
  35.7 0.0 collective-permute-start.1
  35.7 1.3 %collective-permute-done.1.q_ref = f32[1,128]{1,0:T(1,128)S(1)} collective-permute-done((f32[1,128]{1,0:T(1,128)}, f32[1,128]{1,0:T(1,128)S(1)}, u32[]{:S(2)}, u32[]{:S(2)}) %collective-permute-start.1) | collective-permute-done | bytes 544 | tf_op jit(solution)/shard_map/ppermute | solution.py:187
  37.0 0.0 copy-start.3
  37.0 0.6 copy-done.3
  37.6 6.8 %shard_map.92 = (bf16[16,4,8,128]{3,2,1,0:T(8,128)(2,1)}, f32[4096,128]{1,0:T(8,128)}) custom-call(f32[4096,128]{1,0:T(8,128)} %get-tuple-element.14.am_ref, bf16[4096,128]{1,0:T(8,128)(2,1)} %kl_ref.1, f32[32,128]{1,0:T(8,128)} %bitcast.16, f32[1,128]{1,0:T(1,128)} %get-tuple-element.15.p_ref, f32[1,128]{1,0:T(1,128)} %copy-done.3, ...), custom_call_target="tpu_custom_call" | custom-call | tf_op jit(solution)/shard_map/pallas_call | solution.py:132
  44.4 1.3 %collective-permute-start.3 = (bf16[16,4,8,128]{3,2,1,0:T(8,128)(2,1)}, bf16[16,4,8,128]{3,2,1,0:T(8,128)(2,1)S(1)}, u32[]{:S(2)}, u32[]{:S(2)}) collective-permute-start(bf16[16,4,8,128]{3,2,1,0:T(8,128)(2,1)} %get-tuple-element.19), channel_id=1, source_target_pairs={{0,4},{2,6},{4,8},{6,10},{8,12},{10,14},{1,5},{3,7},{5,9},{7,11},{... | collective-permute-start | bytes 393224 | tf_op jit(solution)/shard_map/ppermute | solution.py:20
  45.7 2.5 %collective-permute-start.2 = (bf16[16,4,8,128]{3,2,1,0:T(8,128)(2,1)}, bf16[16,4,8,128]{3,2,1,0:T(8,128)(2,1)S(1)}, u32[]{:S(2)}, u32[]{:S(2)}) collective-permute-start(bf16[16,4,8,128]{3,2,1,0:T(8,128)(2,1)} %get-tuple-element.19), channel_id=1, source_target_pairs={{0,2},{2,4},{4,6},{6,8},{8,10},{10,12},{12,14},{1,3},{3,5},{5,7},{... | collective-permute-start | bytes 393224 | tf_op jit(solution)/shard_map/ppermute | solution.py:20
  48.2 3.9 %collective-permute-done.3 = bf16[16,4,8,128]{3,2,1,0:T(8,128)(2,1)S(1)} collective-permute-done((bf16[16,4,8,128]{3,2,1,0:T(8,128)(2,1)}, bf16[16,4,8,128]{3,2,1,0:T(8,128)(2,1)S(1)}, u32[]{:S(2)}, u32[]{:S(2)}) %collective-permute-start.3) | collective-permute-done | bytes 131104 | tf_op jit(solution)/shard_map/ppermute | solution.py:20
  52.1 2.8 %collective-permute-done.2 = bf16[16,4,8,128]{3,2,1,0:T(8,128)(2,1)S(1)} collective-permute-done((bf16[16,4,8,128]{3,2,1,0:T(8,128)(2,1)}, bf16[16,4,8,128]{3,2,1,0:T(8,128)(2,1)S(1)}, u32[]{:S(2)}, u32[]{:S(2)}) %collective-permute-start.2) | collective-permute-done | bytes 131104 | tf_op jit(solution)/shard_map/ppermute | solution.py:20
  55.0 0.1 fusion
  55.1 1.3 %collective-permute-start.4 = (bf16[16,4,8,128]{3,2,1,0:T(8,128)(2,1)S(1)}, bf16[16,4,8,128]{3,2,1,0:T(8,128)(2,1)S(1)}, u32[]{:S(2)}, u32[]{:S(2)}) collective-permute-start(bf16[16,4,8,128]{3,2,1,0:T(8,128)(2,1)S(1)} %fusion), channel_id=1, source_target_pairs={{0,4},{2,6},{4,8},{6,10},{8,12},{10,14},{1,5},{3,7},{5,9},{7,11},{... | collective-permute-start | bytes 393224 | tf_op jit(solution)/shard_map/ppermute | solution.py:20
  56.4 5.6 %collective-permute-done.4 = bf16[16,4,8,128]{3,2,1,0:T(8,128)(2,1)S(1)} collective-permute-done((bf16[16,4,8,128]{3,2,1,0:T(8,128)(2,1)S(1)}, bf16[16,4,8,128]{3,2,1,0:T(8,128)(2,1)S(1)}, u32[]{:S(2)}, u32[]{:S(2)}) %collective-permute-start.4) | collective-permute-done | bytes 131104 | tf_op jit(solution)/shard_map/ppermute | solution.py:20
  61.9 0.1 fusion.1
  62.1 1.3 %collective-permute-start.5 = (bf16[16,4,8,128]{3,2,1,0:T(8,128)(2,1)S(1)}, bf16[16,4,8,128]{3,2,1,0:T(8,128)(2,1)S(1)}, u32[]{:S(2)}, u32[]{:S(2)}) collective-permute-start(bf16[16,4,8,128]{3,2,1,0:T(8,128)(2,1)S(1)} %fusion.1), channel_id=1, source_target_pairs={{0,8},{2,10},{4,12},{6,14},{1,9},{3,11},{5,13},{7,15},{16,24},{18,... | collective-permute-start | bytes 393224 | tf_op jit(solution)/shard_map/ppermute | solution.py:20
  63.4 8.1 %collective-permute-done.5 = bf16[16,4,8,128]{3,2,1,0:T(8,128)(2,1)S(1)} collective-permute-done((bf16[16,4,8,128]{3,2,1,0:T(8,128)(2,1)S(1)}, bf16[16,4,8,128]{3,2,1,0:T(8,128)(2,1)S(1)}, u32[]{:S(2)}, u32[]{:S(2)}) %collective-permute-start.5) | collective-permute-done | bytes 131104 | tf_op jit(solution)/shard_map/ppermute | solution.py:20
  71.4 0.9 %multiply_add_fusion.h0_ref = f32[16,4,8,128]{3,2,1,0:T(8,128)} fusion(bf16[16,4,8,128]{3,2,1,0:T(8,128)(2,1)S(1)} %collective-permute-done.5, f32[16,4,8,128]{3,2,1,0:T(8,128)S(1)} %bitcast.13, bf16[16,4,8,128]{3,2,1,0:T(8,128)(2,1)S(1)} %collective-permute-done.4, bf16[16,4,8,128]{3,2,1,0:T(8,128)(2,1)S(1)} %collective-permute-done.3, ...), kind=kLoop, calls=%fused_computation.1 | loop fusion | flops 851968 | bytes 1048576 | tf_op jit(solution)/shard_map/add | solution.py:201
  72.3 7.8 %shard_map.93 = bf16[4096,128]{1,0:T(8,128)(2,1)} custom-call(f32[4096,128]{1,0:T(8,128)} %get-tuple-element.14.am_ref, f32[4096,128]{1,0:T(8,128)} %get-tuple-element.17.vt_ref, bf16[4096,128]{1,0:T(8,128)(2,1)} %gl_ref.1, f32[16,4,8,128]{3,2,1,0:T(8,128)} %negate_exponential_fusion.lam_ref, f32[16,4,8,128]{3,2,1,0:T(8,128)} %bitcast.14, ...), custom_call_target="tpu_custom_call" | custom-call | tf_op jit(solution)/shard_map/pallas_call | solution.py:148
Async XLA Ops:
  0.0 5.3 %copy-start = (f32[4096,16]{0,1:T(8,128)S(1)}, f32[4096,16]{0,1:T(8,128)}, u32[]{:S(2)}) copy-start(f32[4096,16]{0,1:T(8,128)} %param.15) | copy-start | bytes 786436
  0.0 5.3 %copy-start.2 = (f32[4096,16]{0,1:T(8,128)S(1)}, f32[4096,16]{0,1:T(8,128)}, u32[]{:S(2)}) copy-start(f32[4096,16]{0,1:T(8,128)} %param.16) | copy-start | bytes 786436
  1.9 27.7 %collective-permute-start = (bf16[4096,128]{1,0:T(8,128)(2,1)S(1)}, bf16[4096,128]{1,0:T(8,128)(2,1)S(1)}, u32[]{:S(2)}, u32[]{:S(2)}) collective-permute-start(bf16[4096,128]{1,0:T(8,128)(2,1)S(1)} %multiply_convert_fusion), channel_id=1, source_target_pairs={{0,2},{2,4},{4,6},{6,8},{8,10},{10,12},{12,14},{1,3},{3,5},{5,7},{... | collective-permute-start | bytes 3145736 | tf_op jit(solution)/shard_map/ppermute | solution.py:20
  29.6 1.0 %copy-start.1 = (bf16[4096,128]{1,0:T(8,128)(2,1)}, bf16[4096,128]{1,0:T(8,128)(2,1)S(1)}, u32[]{:S(2)}) copy-start(bf16[4096,128]{1,0:T(8,128)(2,1)S(1)} %collective-permute-done.rim_ref) | copy-start | bytes 3145732
  35.7 1.3 %collective-permute-start.1 = (f32[1,128]{1,0:T(1,128)}, f32[1,128]{1,0:T(1,128)S(1)}, u32[]{:S(2)}, u32[]{:S(2)}) collective-permute-start(f32[1,128]{1,0:T(1,128)} %get-tuple-element.15.p_ref), channel_id=1, source_target_pairs={{0,1},{1,0},{2,3},{3,2},{4,5},{5,4},{6,7},{7,6},{8,9},{9,8},{10,11... | collective-permute-start | bytes 1544 | tf_op jit(solution)/shard_map/ppermute | solution.py:187
  37.0 0.6 copy-start.3
  44.4 7.7 %collective-permute-start.3 = (bf16[16,4,8,128]{3,2,1,0:T(8,128)(2,1)}, bf16[16,4,8,128]{3,2,1,0:T(8,128)(2,1)S(1)}, u32[]{:S(2)}, u32[]{:S(2)}) collective-permute-start(bf16[16,4,8,128]{3,2,1,0:T(8,128)(2,1)} %get-tuple-element.19), channel_id=1, source_target_pairs={{0,4},{2,6},{4,8},{6,10},{8,12},{10,14},{1,5},{3,7},{5,9},{7,11},{... | collective-permute-start | bytes 393224 | tf_op jit(solution)/shard_map/ppermute | solution.py:20
  45.7 9.3 %collective-permute-start.2 = (bf16[16,4,8,128]{3,2,1,0:T(8,128)(2,1)}, bf16[16,4,8,128]{3,2,1,0:T(8,128)(2,1)S(1)}, u32[]{:S(2)}, u32[]{:S(2)}) collective-permute-start(bf16[16,4,8,128]{3,2,1,0:T(8,128)(2,1)} %get-tuple-element.19), channel_id=1, source_target_pairs={{0,2},{2,4},{4,6},{6,8},{8,10},{10,12},{12,14},{1,3},{3,5},{5,7},{... | collective-permute-start | bytes 393224 | tf_op jit(solution)/shard_map/ppermute | solution.py:20
  55.1 6.9 %collective-permute-start.4 = (bf16[16,4,8,128]{3,2,1,0:T(8,128)(2,1)S(1)}, bf16[16,4,8,128]{3,2,1,0:T(8,128)(2,1)S(1)}, u32[]{:S(2)}, u32[]{:S(2)}) collective-permute-start(bf16[16,4,8,128]{3,2,1,0:T(8,128)(2,1)S(1)} %fusion), channel_id=1, source_target_pairs={{0,4},{2,6},{4,8},{6,10},{8,12},{10,14},{1,5},{3,7},{5,9},{7,11},{... | collective-permute-start | bytes 393224 | tf_op jit(solution)/shard_map/ppermute | solution.py:20
  62.1 9.4 %collective-permute-start.5 = (bf16[16,4,8,128]{3,2,1,0:T(8,128)(2,1)S(1)}, bf16[16,4,8,128]{3,2,1,0:T(8,128)(2,1)S(1)}, u32[]{:S(2)}, u32[]{:S(2)}) collective-permute-start(bf16[16,4,8,128]{3,2,1,0:T(8,128)(2,1)S(1)} %fusion.1), channel_id=1, source_target_pairs={{0,8},{2,10},{4,12},{6,14},{1,9},{3,11},{5,13},{7,15},{16,24},{18,... | collective-permute-start | bytes 393224 | tf_op jit(solution)/shard_map/ppermute | solution.py:20

commit v22 on v20

--- a/solution.py
+++ b/solution.py
@@ -52,7 +52,7 @@
 def medium_call(inputs, gate_medium, key_medium, rim, taps):
     channels, length = inputs.shape
     per_group = channels // taps.shape[0]
-    block = 2048
+    block = 4096
     tap_block = block // per_group
     big = pl.BlockSpec((block, length), lambda b: (b, 0))
     return pl.pallas_call(

time: 80.6 us -> 81.3 us (level)
  no operation moved by 1% of the time
where the time goes in v22:
time: 81.3 us; the launch traced here: 80.6 us
  waiting for transfers between devices  44.3 us (54%)
  Pallas kernels  20.3 us (25%)
  starting transfers between devices  9.77 us (12%)
  other arithmetic  3.79 us (5%)
  local copies, waits for them, and re-layouts  2.38 us (3%)
    ppermute x5, waiting for transfers between devices, shifted(): return lax.ppermute(block, axis, route)  43 us
    ppermute x5, starting transfers between devices, shifted(): return lax.ppermute(block, axis, route)  9.76 us
    pallas_call x1, Pallas kernels, output_call(): pl.pallas_call(output_kernel, grid=(channels // TILE,), in_specs=[big, pl...  7.75 us
    pallas_call x1, Pallas kernels, final_state_call(): pl.pallas_call(functools.partial(final_state_kernel, float(width)), grid=...  6.6 us
    pallas_call x1, Pallas kernels, medium_call(): pl.pallas_call(medium_kernel, grid=(channels // block,), in_specs=[big, b...  5.9 us
    unnamed x10, local copies, waits for them, and re-layouts  2.38 us
    convert_element_type x1, other arithmetic, on_device(): values_medium = (key_medium.astype(F32) * source).astype(BF16)  1.87 us
  transfers between devices with their start and end apart: 6, of which 6 were waited for; matrix products, arithmetic and copies ran while one was open for 2% of the time, Pallas kernels for 0%

profile of v22, /device:TPU:24, one launch (start us, length us, event | category | flops | bytes accessed | tf_op | source)
XLA Modules:
  0.0 80.6 jit_solution(14744829792203544024)
XLA Ops:
  0.0 0.0 copy-start
  0.0 0.0 copy-start.2
  0.0 1.9 %multiply_convert_fusion = bf16[4096,128]{1,0:T(8,128)(2,1)S(1)} fusion(bf16[4096,128]{1,0:T(8,128)(2,1)} %x_ref.1, bf16[4096,128]{1,0:T(8,128)(2,1)} %km_ref.1), kind=kLoop, calls=%fused_computation | loop fusion | flops 2097152 | bytes 3145728 | tf_op jit(solution)/shard_map/convert_element_type | solution.py:177
  1.9 3.4 %collective-permute-start = (bf16[4096,128]{1,0:T(8,128)(2,1)S(1)}, bf16[4096,128]{1,0:T(8,128)(2,1)S(1)}, u32[]{:S(2)}, u32[]{:S(2)}) collective-permute-start(bf16[4096,128]{1,0:T(8,128)(2,1)S(1)} %multiply_convert_fusion), channel_id=1, source_target_pairs={{0,2},{2,4},{4,6},{6,8},{8,10},{10,12},{12,14},{1,3},{3,5},{5,7},{... | collective-permute-start | bytes 3145736 | tf_op jit(solution)/shard_map/ppermute | solution.py:20
  5.3 0.0 copy-done
  5.3 0.0 copy-done.2
  5.3 0.1 multiply_bitcast_fusion
  5.4 0.8 copy.11
  6.2 0.1 copy.10
  6.2 0.7 negate_exponential_fusion.lam_ref
  7.0 22.6 %collective-permute-done.rim_ref = bf16[4096,128]{1,0:T(8,128)(2,1)S(1)} collective-permute-done((bf16[4096,128]{1,0:T(8,128)(2,1)S(1)}, bf16[4096,128]{1,0:T(8,128)(2,1)S(1)}, u32[]{:S(2)}, u32[]{:S(2)}) %collective-permute-start) | collective-permute-done | bytes 1048608 | tf_op jit(solution)/shard_map/ppermute | solution.py:20
  29.6 0.0 copy-start.1
  29.6 1.0 %copy-done.1 = bf16[4096,128]{1,0:T(8,128)(2,1)} copy-done((bf16[4096,128]{1,0:T(8,128)(2,1)}, bf16[4096,128]{1,0:T(8,128)(2,1)S(1)}, u32[]{:S(2)}) %copy-start.1) | copy-done | bytes 1048600
  30.5 5.9 %shard_map.91 = (f32[4096,128]{1,0:T(8,128)}, f32[1,128]{1,0:T(1,128)}) custom-call(bf16[4096,128]{1,0:T(8,128)(2,1)} %x_ref.1, bf16[4096,128]{1,0:T(8,128)(2,1)} %gm_ref.1, bf16[4096,128]{1,0:T(8,128)(2,1)} %km_ref.1, bf16[4096,128]{1,0:T(8,128)(2,1)} %copy-done.1, bf16[256,128]{1,0:T(8,128)(2,1)} %taps_ref.1), custom_call_target="tpu_custom_call" | custom-call | tf_op jit(solution)/shard_map/pallas_call | solution.py:58
  36.4 0.0 collective-permute-start.1
  36.4 1.3 %collective-permute-done.1.q_ref = f32[1,128]{1,0:T(1,128)S(1)} collective-permute-done((f32[1,128]{1,0:T(1,128)}, f32[1,128]{1,0:T(1,128)S(1)}, u32[]{:S(2)}, u32[]{:S(2)}) %collective-permute-start.1) | collective-permute-done | bytes 544 | tf_op jit(solution)/shard_map/ppermute | solution.py:186
  37.8 0.0 copy-start.3
  37.8 0.6 copy-done.3
  38.4 6.6 %shard_map.92 = (bf16[16,4,8,128]{3,2,1,0:T(8,128)(2,1)}, f32[4096,128]{1,0:T(8,128)}) custom-call(f32[4096,128]{1,0:T(8,128)} %get-tuple-element.14.am_ref, bf16[4096,128]{1,0:T(8,128)(2,1)} %kl_ref.1, f32[32,128]{1,0:T(8,128)} %bitcast.16, f32[1,128]{1,0:T(1,128)} %get-tuple-element.15.p_ref, f32[1,128]{1,0:T(1,128)} %copy-done.3, ...), custom_call_target="tpu_custom_call" | custom-call | tf_op jit(solution)/shard_map/pallas_call | solution.py:131
  45.0 1.3 %collective-permute-start.3 = (bf16[16,4,8,128]{3,2,1,0:T(8,128)(2,1)}, bf16[16,4,8,128]{3,2,1,0:T(8,128)(2,1)S(1)}, u32[]{:S(2)}, u32[]{:S(2)}) collective-permute-start(bf16[16,4,8,128]{3,2,1,0:T(8,128)(2,1)} %get-tuple-element.19), channel_id=1, source_target_pairs={{0,4},{2,6},{4,8},{6,10},{8,12},{10,14},{1,5},{3,7},{5,9},{7,11},{... | collective-permute-start | bytes 393224 | tf_op jit(solution)/shard_map/ppermute | solution.py:20
  46.3 2.5 %collective-permute-start.2 = (bf16[16,4,8,128]{3,2,1,0:T(8,128)(2,1)}, bf16[16,4,8,128]{3,2,1,0:T(8,128)(2,1)S(1)}, u32[]{:S(2)}, u32[]{:S(2)}) collective-permute-start(bf16[16,4,8,128]{3,2,1,0:T(8,128)(2,1)} %get-tuple-element.19), channel_id=1, source_target_pairs={{0,2},{2,4},{4,6},{6,8},{8,10},{10,12},{12,14},{1,3},{3,5},{5,7},{... | collective-permute-start | bytes 393224 | tf_op jit(solution)/shard_map/ppermute | solution.py:20
  48.8 3.9 %collective-permute-done.3 = bf16[16,4,8,128]{3,2,1,0:T(8,128)(2,1)S(1)} collective-permute-done((bf16[16,4,8,128]{3,2,1,0:T(8,128)(2,1)}, bf16[16,4,8,128]{3,2,1,0:T(8,128)(2,1)S(1)}, u32[]{:S(2)}, u32[]{:S(2)}) %collective-permute-start.3) | collective-permute-done | bytes 131104 | tf_op jit(solution)/shard_map/ppermute | solution.py:20
  52.7 2.8 %collective-permute-done.2 = bf16[16,4,8,128]{3,2,1,0:T(8,128)(2,1)S(1)} collective-permute-done((bf16[16,4,8,128]{3,2,1,0:T(8,128)(2,1)}, bf16[16,4,8,128]{3,2,1,0:T(8,128)(2,1)S(1)}, u32[]{:S(2)}, u32[]{:S(2)}) %collective-permute-start.2) | collective-permute-done | bytes 131104 | tf_op jit(solution)/shard_map/ppermute | solution.py:20
  55.5 0.1 fusion
  55.6 1.3 %collective-permute-start.4 = (bf16[16,4,8,128]{3,2,1,0:T(8,128)(2,1)S(1)}, bf16[16,4,8,128]{3,2,1,0:T(8,128)(2,1)S(1)}, u32[]{:S(2)}, u32[]{:S(2)}) collective-permute-start(bf16[16,4,8,128]{3,2,1,0:T(8,128)(2,1)S(1)} %fusion), channel_id=1, source_target_pairs={{0,4},{2,6},{4,8},{6,10},{8,12},{10,14},{1,5},{3,7},{5,9},{7,11},{... | collective-permute-start | bytes 393224 | tf_op jit(solution)/shard_map/ppermute | solution.py:20
  56.9 5.6 %collective-permute-done.4 = bf16[16,4,8,128]{3,2,1,0:T(8,128)(2,1)S(1)} collective-permute-done((bf16[16,4,8,128]{3,2,1,0:T(8,128)(2,1)S(1)}, bf16[16,4,8,128]{3,2,1,0:T(8,128)(2,1)S(1)}, u32[]{:S(2)}, u32[]{:S(2)}) %collective-permute-start.4) | collective-permute-done | bytes 131104 | tf_op jit(solution)/shard_map/ppermute | solution.py:20
  62.5 0.1 fusion.1
  62.6 1.3 %collective-permute-start.5 = (bf16[16,4,8,128]{3,2,1,0:T(8,128)(2,1)S(1)}, bf16[16,4,8,128]{3,2,1,0:T(8,128)(2,1)S(1)}, u32[]{:S(2)}, u32[]{:S(2)}) collective-permute-start(bf16[16,4,8,128]{3,2,1,0:T(8,128)(2,1)S(1)} %fusion.1), channel_id=1, source_target_pairs={{0,8},{2,10},{4,12},{6,14},{1,9},{3,11},{5,13},{7,15},{16,24},{18,... | collective-permute-start | bytes 393224 | tf_op jit(solution)/shard_map/ppermute | solution.py:20
  63.9 8.1 %collective-permute-done.5 = bf16[16,4,8,128]{3,2,1,0:T(8,128)(2,1)S(1)} collective-permute-done((bf16[16,4,8,128]{3,2,1,0:T(8,128)(2,1)S(1)}, bf16[16,4,8,128]{3,2,1,0:T(8,128)(2,1)S(1)}, u32[]{:S(2)}, u32[]{:S(2)}) %collective-permute-start.5) | collective-permute-done | bytes 131104 | tf_op jit(solution)/shard_map/ppermute | solution.py:20
  72.0 0.9 %multiply_add_fusion.h0_ref = f32[16,4,8,128]{3,2,1,0:T(8,128)} fusion(bf16[16,4,8,128]{3,2,1,0:T(8,128)(2,1)S(1)} %collective-permute-done.5, f32[16,4,8,128]{3,2,1,0:T(8,128)S(1)} %bitcast.13, bf16[16,4,8,128]{3,2,1,0:T(8,128)(2,1)S(1)} %collective-permute-done.4, bf16[16,4,8,128]{3,2,1,0:T(8,128)(2,1)S(1)} %collective-permute-done.3, ...), kind=kLoop, calls=%fused_computation.1 | loop fusion | flops 851968 | bytes 1048576 | tf_op jit(solution)/shard_map/add | solution.py:200
  72.8 7.8 %shard_map.93 = bf16[4096,128]{1,0:T(8,128)(2,1)} custom-call(f32[4096,128]{1,0:T(8,128)} %get-tuple-element.14.am_ref, f32[4096,128]{1,0:T(8,128)} %get-tuple-element.17.vt_ref, bf16[4096,128]{1,0:T(8,128)(2,1)} %gl_ref.1, f32[16,4,8,128]{3,2,1,0:T(8,128)} %negate_exponential_fusion.lam_ref, f32[16,4,8,128]{3,2,1,0:T(8,128)} %bitcast.14, ...), custom_call_target="tpu_custom_call" | custom-call | tf_op jit(solution)/shard_map/pallas_call | solution.py:147
Async XLA Ops:
  0.0 5.3 %copy-start = (f32[4096,16]{0,1:T(8,128)S(1)}, f32[4096,16]{0,1:T(8,128)}, u32[]{:S(2)}) copy-start(f32[4096,16]{0,1:T(8,128)} %param.15) | copy-start | bytes 786436
  0.0 5.3 %copy-start.2 = (f32[4096,16]{0,1:T(8,128)S(1)}, f32[4096,16]{0,1:T(8,128)}, u32[]{:S(2)}) copy-start(f32[4096,16]{0,1:T(8,128)} %param.16) | copy-start | bytes 786436
  1.9 27.7 %collective-permute-start = (bf16[4096,128]{1,0:T(8,128)(2,1)S(1)}, bf16[4096,128]{1,0:T(8,128)(2,1)S(1)}, u32[]{:S(2)}, u32[]{:S(2)}) collective-permute-start(bf16[4096,128]{1,0:T(8,128)(2,1)S(1)} %multiply_convert_fusion), channel_id=1, source_target_pairs={{0,2},{2,4},{4,6},{6,8},{8,10},{10,12},{12,14},{1,3},{3,5},{5,7},{... | collective-permute-start | bytes 3145736 | tf_op jit(solution)/shard_map/ppermute | solution.py:20
  29.6 1.0 %copy-start.1 = (bf16[4096,128]{1,0:T(8,128)(2,1)}, bf16[4096,128]{1,0:T(8,128)(2,1)S(1)}, u32[]{:S(2)}) copy-start(bf16[4096,128]{1,0:T(8,128)(2,1)S(1)} %collective-permute-done.rim_ref) | copy-start | bytes 3145732
  36.4 1.3 %collective-permute-start.1 = (f32[1,128]{1,0:T(1,128)}, f32[1,128]{1,0:T(1,128)S(1)}, u32[]{:S(2)}, u32[]{:S(2)}) collective-permute-start(f32[1,128]{1,0:T(1,128)} %get-tuple-element.15.p_ref), channel_id=1, source_target_pairs={{0,1},{1,0},{2,3},{3,2},{4,5},{5,4},{6,7},{7,6},{8,9},{9,8},{10,11... | collective-permute-start | bytes 1544 | tf_op jit(solution)/shard_map/ppermute | solution.py:186
  37.8 0.6 copy-start.3
  45.0 7.7 %collective-permute-start.3 = (bf16[16,4,8,128]{3,2,1,0:T(8,128)(2,1)}, bf16[16,4,8,128]{3,2,1,0:T(8,128)(2,1)S(1)}, u32[]{:S(2)}, u32[]{:S(2)}) collective-permute-start(bf16[16,4,8,128]{3,2,1,0:T(8,128)(2,1)} %get-tuple-element.19), channel_id=1, source_target_pairs={{0,4},{2,6},{4,8},{6,10},{8,12},{10,14},{1,5},{3,7},{5,9},{7,11},{... | collective-permute-start | bytes 393224 | tf_op jit(solution)/shard_map/ppermute | solution.py:20
  46.3 9.3 %collective-permute-start.2 = (bf16[16,4,8,128]{3,2,1,0:T(8,128)(2,1)}, bf16[16,4,8,128]{3,2,1,0:T(8,128)(2,1)S(1)}, u32[]{:S(2)}, u32[]{:S(2)}) collective-permute-start(bf16[16,4,8,128]{3,2,1,0:T(8,128)(2,1)} %get-tuple-element.19), channel_id=1, source_target_pairs={{0,2},{2,4},{4,6},{6,8},{8,10},{10,12},{12,14},{1,3},{3,5},{5,7},{... | collective-permute-start | bytes 393224 | tf_op jit(solution)/shard_map/ppermute | solution.py:20
  55.6 6.9 %collective-permute-start.4 = (bf16[16,4,8,128]{3,2,1,0:T(8,128)(2,1)S(1)}, bf16[16,4,8,128]{3,2,1,0:T(8,128)(2,1)S(1)}, u32[]{:S(2)}, u32[]{:S(2)}) collective-permute-start(bf16[16,4,8,128]{3,2,1,0:T(8,128)(2,1)S(1)} %fusion), channel_id=1, source_target_pairs={{0,4},{2,6},{4,8},{6,10},{8,12},{10,14},{1,5},{3,7},{5,9},{7,11},{... | collective-permute-start | bytes 393224 | tf_op jit(solution)/shard_map/ppermute | solution.py:20
  62.6 9.4 %collective-permute-start.5 = (bf16[16,4,8,128]{3,2,1,0:T(8,128)(2,1)S(1)}, bf16[16,4,8,128]{3,2,1,0:T(8,128)(2,1)S(1)}, u32[]{:S(2)}, u32[]{:S(2)}) collective-permute-start(bf16[16,4,8,128]{3,2,1,0:T(8,128)(2,1)S(1)} %fusion.1), channel_id=1, source_target_pairs={{0,8},{2,10},{4,12},{6,14},{1,9},{3,11},{5,13},{7,15},{16,24},{18,... | collective-permute-start | bytes 393224 | tf_op jit(solution)/shard_map/ppermute | solution.py:20

commit v23 on v20

--- a/solution.py
+++ b/solution.py
@@ -92,7 +92,7 @@
         v = token_tile(vt_ref, t)
         return tuple(lam[m] * h[m] + v for m in range(modes))
 
-    h = lax.fori_loop(0, length, body, tuple(jnp.zeros((SUB, LANE), F32) for _ in range(modes)), unroll=8)
+    h = lax.fori_loop(0, length, body, tuple(jnp.zeros((SUB, LANE), F32) for _ in range(modes)), unroll=16)
     for m in range(modes):
         f_ref[m] = h[m].astype(f_ref.dtype)
 
@@ -112,7 +112,7 @@
         yt_ref[pl.ds(pl.multiple_of(t * SUB, SUB), SUB), :] = y
         return h
 
-    lax.fori_loop(0, length, body, tuple(h0_ref[m] for m in range(modes)), unroll=8)
+    lax.fori_loop(0, length, body, tuple(h0_ref[m] for m in range(modes)), unroll=16)
     for i in range(SUB):
         rows = slice(i * LANE, (i + 1) * LANE)
         long_out = yt_ref[pl.ds(i, LANE, stride=SUB), :].T.astype(BF16).astype(F32)

time: 80.6 us -> 80.2 us (level)
  no operation moved by 1% of the time
where the time goes in v23:
time: 80.2 us; the launch traced here: 79.5 us
  waiting for transfers between devices  44.3 us (55%)
  Pallas kernels  19.1 us (24%)
  starting transfers between devices  9.77 us (12%)
  other arithmetic  3.79 us (5%)
  local copies, waits for them, and re-layouts  2.38 us (3%)
    ppermute x5, waiting for transfers between devices, shifted(): return lax.ppermute(block, axis, route)  43 us
    ppermute x5, starting transfers between devices, shifted(): return lax.ppermute(block, axis, route)  9.76 us
    pallas_call x1, Pallas kernels, output_call(): pl.pallas_call(output_kernel, grid=(channels // TILE,), in_specs=[big, pl...  7.43 us
    pallas_call x1, Pallas kernels, final_state_call(): pl.pallas_call(functools.partial(final_state_kernel, float(width)), grid=...  6.51 us
    pallas_call x1, Pallas kernels, medium_call(): pl.pallas_call(medium_kernel, grid=(channels // block,), in_specs=[big, b...  5.17 us
    unnamed x10, local copies, waits for them, and re-layouts  2.38 us
    convert_element_type x1, other arithmetic, on_device(): values_medium = (key_medium.astype(F32) * source).astype(BF16)  1.87 us
  transfers between devices with their start and end apart: 6, of which 6 were waited for; matrix products, arithmetic and copies ran while one was open for 2% of the time, Pallas kernels for 0%

profile of v23, /device:TPU:24, one launch (start us, length us, event | category | flops | bytes accessed | tf_op | source)
XLA Modules:
  0.0 79.5 jit_solution(534837895349194994)
XLA Ops:
  0.0 0.0 copy-start
  0.0 0.0 copy-start.2
  0.0 1.9 %multiply_convert_fusion = bf16[4096,128]{1,0:T(8,128)(2,1)S(1)} fusion(bf16[4096,128]{1,0:T(8,128)(2,1)} %x_ref.1, bf16[4096,128]{1,0:T(8,128)(2,1)} %km_ref.1), kind=kLoop, calls=%fused_computation | loop fusion | flops 2097152 | bytes 3145728 | tf_op jit(solution)/shard_map/convert_element_type | solution.py:177
  1.9 3.4 %collective-permute-start = (bf16[4096,128]{1,0:T(8,128)(2,1)S(1)}, bf16[4096,128]{1,0:T(8,128)(2,1)S(1)}, u32[]{:S(2)}, u32[]{:S(2)}) collective-permute-start(bf16[4096,128]{1,0:T(8,128)(2,1)S(1)} %multiply_convert_fusion), channel_id=1, source_target_pairs={{0,2},{2,4},{4,6},{6,8},{8,10},{10,12},{12,14},{1,3},{3,5},{5,7},{... | collective-permute-start | bytes 3145736 | tf_op jit(solution)/shard_map/ppermute | solution.py:20
  5.3 0.0 copy-done
  5.3 0.0 copy-done.2
  5.3 0.1 multiply_bitcast_fusion
  5.4 0.8 copy.11
  6.2 0.1 copy.10
  6.2 0.7 negate_exponential_fusion.lam_ref
  7.0 22.6 %collective-permute-done.rim_ref = bf16[4096,128]{1,0:T(8,128)(2,1)S(1)} collective-permute-done((bf16[4096,128]{1,0:T(8,128)(2,1)S(1)}, bf16[4096,128]{1,0:T(8,128)(2,1)S(1)}, u32[]{:S(2)}, u32[]{:S(2)}) %collective-permute-start) | collective-permute-done | bytes 1048608 | tf_op jit(solution)/shard_map/ppermute | solution.py:20
  29.6 0.0 copy-start.1
  29.6 1.0 %copy-done.1 = bf16[4096,128]{1,0:T(8,128)(2,1)} copy-done((bf16[4096,128]{1,0:T(8,128)(2,1)}, bf16[4096,128]{1,0:T(8,128)(2,1)S(1)}, u32[]{:S(2)}) %copy-start.1) | copy-done | bytes 1048600
  30.5 5.2 %shard_map.91 = (f32[4096,128]{1,0:T(8,128)}, f32[1,128]{1,0:T(1,128)}) custom-call(bf16[4096,128]{1,0:T(8,128)(2,1)} %x_ref.1, bf16[4096,128]{1,0:T(8,128)(2,1)} %gm_ref.1, bf16[4096,128]{1,0:T(8,128)(2,1)} %km_ref.1, bf16[4096,128]{1,0:T(8,128)(2,1)} %copy-done.1, bf16[256,128]{1,0:T(8,128)(2,1)} %taps_ref.1), custom_call_target="tpu_custom_call" | custom-call | tf_op jit(solution)/shard_map/pallas_call | solution.py:58
  35.7 0.0 collective-permute-start.1
  35.7 1.3 %collective-permute-done.1.q_ref = f32[1,128]{1,0:T(1,128)S(1)} collective-permute-done((f32[1,128]{1,0:T(1,128)}, f32[1,128]{1,0:T(1,128)S(1)}, u32[]{:S(2)}, u32[]{:S(2)}) %collective-permute-start.1) | collective-permute-done | bytes 544 | tf_op jit(solution)/shard_map/ppermute | solution.py:186
  37.0 0.0 copy-start.3
  37.0 0.6 copy-done.3
  37.6 6.5 %shard_map.92 = (bf16[16,4,8,128]{3,2,1,0:T(8,128)(2,1)}, f32[4096,128]{1,0:T(8,128)}) custom-call(f32[4096,128]{1,0:T(8,128)} %get-tuple-element.14.am_ref, bf16[4096,128]{1,0:T(8,128)(2,1)} %kl_ref.1, f32[32,128]{1,0:T(8,128)} %bitcast.16, f32[1,128]{1,0:T(1,128)} %get-tuple-element.15.p_ref, f32[1,128]{1,0:T(1,128)} %copy-done.3, ...), custom_call_target="tpu_custom_call" | custom-call | tf_op jit(solution)/shard_map/pallas_call | solution.py:131
  44.1 1.3 %collective-permute-start.3 = (bf16[16,4,8,128]{3,2,1,0:T(8,128)(2,1)}, bf16[16,4,8,128]{3,2,1,0:T(8,128)(2,1)S(1)}, u32[]{:S(2)}, u32[]{:S(2)}) collective-permute-start(bf16[16,4,8,128]{3,2,1,0:T(8,128)(2,1)} %get-tuple-element.19), channel_id=1, source_target_pairs={{0,4},{2,6},{4,8},{6,10},{8,12},{10,14},{1,5},{3,7},{5,9},{7,11},{... | collective-permute-start | bytes 393224 | tf_op jit(solution)/shard_map/ppermute | solution.py:20
  45.4 2.5 %collective-permute-start.2 = (bf16[16,4,8,128]{3,2,1,0:T(8,128)(2,1)}, bf16[16,4,8,128]{3,2,1,0:T(8,128)(2,1)S(1)}, u32[]{:S(2)}, u32[]{:S(2)}) collective-permute-start(bf16[16,4,8,128]{3,2,1,0:T(8,128)(2,1)} %get-tuple-element.19), channel_id=1, source_target_pairs={{0,2},{2,4},{4,6},{6,8},{8,10},{10,12},{12,14},{1,3},{3,5},{5,7},{... | collective-permute-start | bytes 393224 | tf_op jit(solution)/shard_map/ppermute | solution.py:20
  47.9 3.9 %collective-permute-done.3 = bf16[16,4,8,128]{3,2,1,0:T(8,128)(2,1)S(1)} collective-permute-done((bf16[16,4,8,128]{3,2,1,0:T(8,128)(2,1)}, bf16[16,4,8,128]{3,2,1,0:T(8,128)(2,1)S(1)}, u32[]{:S(2)}, u32[]{:S(2)}) %collective-permute-start.3) | collective-permute-done | bytes 131104 | tf_op jit(solution)/shard_map/ppermute | solution.py:20
  51.9 2.8 %collective-permute-done.2 = bf16[16,4,8,128]{3,2,1,0:T(8,128)(2,1)S(1)} collective-permute-done((bf16[16,4,8,128]{3,2,1,0:T(8,128)(2,1)}, bf16[16,4,8,128]{3,2,1,0:T(8,128)(2,1)S(1)}, u32[]{:S(2)}, u32[]{:S(2)}) %collective-permute-start.2) | collective-permute-done | bytes 131104 | tf_op jit(solution)/shard_map/ppermute | solution.py:20
  54.7 0.1 fusion
  54.8 1.3 %collective-permute-start.4 = (bf16[16,4,8,128]{3,2,1,0:T(8,128)(2,1)S(1)}, bf16[16,4,8,128]{3,2,1,0:T(8,128)(2,1)S(1)}, u32[]{:S(2)}, u32[]{:S(2)}) collective-permute-start(bf16[16,4,8,128]{3,2,1,0:T(8,128)(2,1)S(1)} %fusion), channel_id=1, source_target_pairs={{0,4},{2,6},{4,8},{6,10},{8,12},{10,14},{1,5},{3,7},{5,9},{7,11},{... | collective-permute-start | bytes 393224 | tf_op jit(solution)/shard_map/ppermute | solution.py:20
  56.1 5.6 %collective-permute-done.4 = bf16[16,4,8,128]{3,2,1,0:T(8,128)(2,1)S(1)} collective-permute-done((bf16[16,4,8,128]{3,2,1,0:T(8,128)(2,1)S(1)}, bf16[16,4,8,128]{3,2,1,0:T(8,128)(2,1)S(1)}, u32[]{:S(2)}, u32[]{:S(2)}) %collective-permute-start.4) | collective-permute-done | bytes 131104 | tf_op jit(solution)/shard_map/ppermute | solution.py:20
  61.6 0.1 fusion.1
  61.8 1.3 %collective-permute-start.5 = (bf16[16,4,8,128]{3,2,1,0:T(8,128)(2,1)S(1)}, bf16[16,4,8,128]{3,2,1,0:T(8,128)(2,1)S(1)}, u32[]{:S(2)}, u32[]{:S(2)}) collective-permute-start(bf16[16,4,8,128]{3,2,1,0:T(8,128)(2,1)S(1)} %fusion.1), channel_id=1, source_target_pairs={{0,8},{2,10},{4,12},{6,14},{1,9},{3,11},{5,13},{7,15},{16,24},{18,... | collective-permute-start | bytes 393224 | tf_op jit(solution)/shard_map/ppermute | solution.py:20
  63.1 8.1 %collective-permute-done.5 = bf16[16,4,8,128]{3,2,1,0:T(8,128)(2,1)S(1)} collective-permute-done((bf16[16,4,8,128]{3,2,1,0:T(8,128)(2,1)S(1)}, bf16[16,4,8,128]{3,2,1,0:T(8,128)(2,1)S(1)}, u32[]{:S(2)}, u32[]{:S(2)}) %collective-permute-start.5) | collective-permute-done | bytes 131104 | tf_op jit(solution)/shard_map/ppermute | solution.py:20
  71.2 0.9 %multiply_add_fusion.h0_ref = f32[16,4,8,128]{3,2,1,0:T(8,128)} fusion(bf16[16,4,8,128]{3,2,1,0:T(8,128)(2,1)S(1)} %collective-permute-done.5, f32[16,4,8,128]{3,2,1,0:T(8,128)S(1)} %bitcast.13, bf16[16,4,8,128]{3,2,1,0:T(8,128)(2,1)S(1)} %collective-permute-done.4, bf16[16,4,8,128]{3,2,1,0:T(8,128)(2,1)S(1)} %collective-permute-done.3, ...), kind=kLoop, calls=%fused_computation.1 | loop fusion | flops 851968 | bytes 1048576 | tf_op jit(solution)/shard_map/add | solution.py:200
  72.0 7.4 %shard_map.93 = bf16[4096,128]{1,0:T(8,128)(2,1)} custom-call(f32[4096,128]{1,0:T(8,128)} %get-tuple-element.14.am_ref, f32[4096,128]{1,0:T(8,128)} %get-tuple-element.17.vt_ref, bf16[4096,128]{1,0:T(8,128)(2,1)} %gl_ref.1, f32[16,4,8,128]{3,2,1,0:T(8,128)} %negate_exponential_fusion.lam_ref, f32[16,4,8,128]{3,2,1,0:T(8,128)} %bitcast.14, ...), custom_call_target="tpu_custom_call" | custom-call | tf_op jit(solution)/shard_map/pallas_call | solution.py:147
Async XLA Ops:
  0.0 5.3 %copy-start = (f32[4096,16]{0,1:T(8,128)S(1)}, f32[4096,16]{0,1:T(8,128)}, u32[]{:S(2)}) copy-start(f32[4096,16]{0,1:T(8,128)} %param.15) | copy-start | bytes 786436
  0.0 5.3 %copy-start.2 = (f32[4096,16]{0,1:T(8,128)S(1)}, f32[4096,16]{0,1:T(8,128)}, u32[]{:S(2)}) copy-start(f32[4096,16]{0,1:T(8,128)} %param.16) | copy-start | bytes 786436
  1.9 27.7 %collective-permute-start = (bf16[4096,128]{1,0:T(8,128)(2,1)S(1)}, bf16[4096,128]{1,0:T(8,128)(2,1)S(1)}, u32[]{:S(2)}, u32[]{:S(2)}) collective-permute-start(bf16[4096,128]{1,0:T(8,128)(2,1)S(1)} %multiply_convert_fusion), channel_id=1, source_target_pairs={{0,2},{2,4},{4,6},{6,8},{8,10},{10,12},{12,14},{1,3},{3,5},{5,7},{... | collective-permute-start | bytes 3145736 | tf_op jit(solution)/shard_map/ppermute | solution.py:20
  29.6 1.0 %copy-start.1 = (bf16[4096,128]{1,0:T(8,128)(2,1)}, bf16[4096,128]{1,0:T(8,128)(2,1)S(1)}, u32[]{:S(2)}) copy-start(bf16[4096,128]{1,0:T(8,128)(2,1)S(1)} %collective-permute-done.rim_ref) | copy-start | bytes 3145732
  35.7 1.3 %collective-permute-start.1 = (f32[1,128]{1,0:T(1,128)}, f32[1,128]{1,0:T(1,128)S(1)}, u32[]{:S(2)}, u32[]{:S(2)}) collective-permute-start(f32[1,128]{1,0:T(1,128)} %get-tuple-element.15.p_ref), channel_id=1, source_target_pairs={{0,1},{1,0},{2,3},{3,2},{4,5},{5,4},{6,7},{7,6},{8,9},{9,8},{10,11... | collective-permute-start | bytes 1544 | tf_op jit(solution)/shard_map/ppermute | solution.py:186
  37.0 0.6 copy-start.3
  44.1 7.7 %collective-permute-start.3 = (bf16[16,4,8,128]{3,2,1,0:T(8,128)(2,1)}, bf16[16,4,8,128]{3,2,1,0:T(8,128)(2,1)S(1)}, u32[]{:S(2)}, u32[]{:S(2)}) collective-permute-start(bf16[16,4,8,128]{3,2,1,0:T(8,128)(2,1)} %get-tuple-element.19), channel_id=1, source_target_pairs={{0,4},{2,6},{4,8},{6,10},{8,12},{10,14},{1,5},{3,7},{5,9},{7,11},{... | collective-permute-start | bytes 393224 | tf_op jit(solution)/shard_map/ppermute | solution.py:20
  45.4 9.3 %collective-permute-start.2 = (bf16[16,4,8,128]{3,2,1,0:T(8,128)(2,1)}, bf16[16,4,8,128]{3,2,1,0:T(8,128)(2,1)S(1)}, u32[]{:S(2)}, u32[]{:S(2)}) collective-permute-start(bf16[16,4,8,128]{3,2,1,0:T(8,128)(2,1)} %get-tuple-element.19), channel_id=1, source_target_pairs={{0,2},{2,4},{4,6},{6,8},{8,10},{10,12},{12,14},{1,3},{3,5},{5,7},{... | collective-permute-start | bytes 393224 | tf_op jit(solution)/shard_map/ppermute | solution.py:20
  54.8 6.9 %collective-permute-start.4 = (bf16[16,4,8,128]{3,2,1,0:T(8,128)(2,1)S(1)}, bf16[16,4,8,128]{3,2,1,0:T(8,128)(2,1)S(1)}, u32[]{:S(2)}, u32[]{:S(2)}) collective-permute-start(bf16[16,4,8,128]{3,2,1,0:T(8,128)(2,1)S(1)} %fusion), channel_id=1, source_target_pairs={{0,4},{2,6},{4,8},{6,10},{8,12},{10,14},{1,5},{3,7},{5,9},{7,11},{... | collective-permute-start | bytes 393224 | tf_op jit(solution)/shard_map/ppermute | solution.py:20
  61.8 9.4 %collective-permute-start.5 = (bf16[16,4,8,128]{3,2,1,0:T(8,128)(2,1)S(1)}, bf16[16,4,8,128]{3,2,1,0:T(8,128)(2,1)S(1)}, u32[]{:S(2)}, u32[]{:S(2)}) collective-permute-start(bf16[16,4,8,128]{3,2,1,0:T(8,128)(2,1)S(1)} %fusion.1), channel_id=1, source_target_pairs={{0,8},{2,10},{4,12},{6,14},{1,9},{3,11},{5,13},{7,15},{16,24},{18,... | collective-permute-start | bytes 393224 | tf_op jit(solution)/shard_map/ppermute | solution.py:20

commit v24 on v23

--- a/solution.py
+++ b/solution.py
@@ -92,7 +92,7 @@
         v = token_tile(vt_ref, t)
         return tuple(lam[m] * h[m] + v for m in range(modes))
 
-    h = lax.fori_loop(0, length, body, tuple(jnp.zeros((SUB, LANE), F32) for _ in range(modes)), unroll=16)
+    h = lax.fori_loop(0, length, body, tuple(jnp.zeros((SUB, LANE), F32) for _ in range(modes)), unroll=32)
     for m in range(modes):
         f_ref[m] = h[m].astype(f_ref.dtype)
 
@@ -112,7 +112,7 @@
         yt_ref[pl.ds(pl.multiple_of(t * SUB, SUB), SUB), :] = y
         return h
 
-    lax.fori_loop(0, length, body, tuple(h0_ref[m] for m in range(modes)), unroll=16)
+    lax.fori_loop(0, length, body, tuple(h0_ref[m] for m in range(modes)), unroll=32)
     for i in range(SUB):
         rows = slice(i * LANE, (i + 1) * LANE)
         long_out = yt_ref[pl.ds(i, LANE, stride=SUB), :].T.astype(BF16).astype(F32)

time: 80.2 us -> 80.1 us (level)
  no operation moved by 1% of the time
where the time goes in v24:
time: 80.1 us; the launch traced here: 79.3 us
  waiting for transfers between devices  44.3 us (55%)
  Pallas kernels  19 us (24%)
  starting transfers between devices  9.77 us (12%)
  other arithmetic  3.79 us (5%)
  local copies, waits for them, and re-layouts  2.38 us (3%)
    ppermute x5, waiting for transfers between devices, shifted(): return lax.ppermute(block, axis, route)  43 us
    ppermute x5, starting transfers between devices, shifted(): return lax.ppermute(block, axis, route)  9.76 us
    pallas_call x1, Pallas kernels, output_call(): pl.pallas_call(output_kernel, grid=(channels // TILE,), in_specs=[big, pl...  7.32 us
    pallas_call x1, Pallas kernels, final_state_call(): pl.pallas_call(functools.partial(final_state_kernel, float(width)), grid=...  6.46 us
    pallas_call x1, Pallas kernels, medium_call(): pl.pallas_call(medium_kernel, grid=(channels // block,), in_specs=[big, b...  5.17 us
    unnamed x10, local copies, waits for them, and re-layouts  2.38 us
    convert_element_type x1, other arithmetic, on_device(): values_medium = (key_medium.astype(F32) * source).astype(BF16)  1.87 us
  transfers between devices with their start and end apart: 6, of which 6 were waited for; matrix products, arithmetic and copies ran while one was open for 2% of the time, Pallas kernels for 0%

profile of v24, /device:TPU:24, one launch (start us, length us, event | category | flops | bytes accessed | tf_op | source)
XLA Modules:
  0.0 79.3 jit_solution(159038988581610718)
XLA Ops:
  0.0 0.0 copy-start
  0.0 0.0 copy-start.2
  0.0 1.9 %multiply_convert_fusion = bf16[4096,128]{1,0:T(8,128)(2,1)S(1)} fusion(bf16[4096,128]{1,0:T(8,128)(2,1)} %x_ref.1, bf16[4096,128]{1,0:T(8,128)(2,1)} %km_ref.1), kind=kLoop, calls=%fused_computation | loop fusion | flops 2097152 | bytes 3145728 | tf_op jit(solution)/shard_map/convert_element_type | solution.py:177
  1.9 3.4 %collective-permute-start = (bf16[4096,128]{1,0:T(8,128)(2,1)S(1)}, bf16[4096,128]{1,0:T(8,128)(2,1)S(1)}, u32[]{:S(2)}, u32[]{:S(2)}) collective-permute-start(bf16[4096,128]{1,0:T(8,128)(2,1)S(1)} %multiply_convert_fusion), channel_id=1, source_target_pairs={{0,2},{2,4},{4,6},{6,8},{8,10},{10,12},{12,14},{1,3},{3,5},{5,7},{... | collective-permute-start | bytes 3145736 | tf_op jit(solution)/shard_map/ppermute | solution.py:20
  5.3 0.0 copy-done
  5.3 0.0 copy-done.2
  5.3 0.1 multiply_bitcast_fusion
  5.4 0.8 copy.11
  6.2 0.1 copy.10
  6.2 0.7 negate_exponential_fusion.lam_ref
  7.0 22.6 %collective-permute-done.rim_ref = bf16[4096,128]{1,0:T(8,128)(2,1)S(1)} collective-permute-done((bf16[4096,128]{1,0:T(8,128)(2,1)S(1)}, bf16[4096,128]{1,0:T(8,128)(2,1)S(1)}, u32[]{:S(2)}, u32[]{:S(2)}) %collective-permute-start) | collective-permute-done | bytes 1048608 | tf_op jit(solution)/shard_map/ppermute | solution.py:20
  29.6 0.0 copy-start.1
  29.6 1.0 %copy-done.1 = bf16[4096,128]{1,0:T(8,128)(2,1)} copy-done((bf16[4096,128]{1,0:T(8,128)(2,1)}, bf16[4096,128]{1,0:T(8,128)(2,1)S(1)}, u32[]{:S(2)}) %copy-start.1) | copy-done | bytes 1048600
  30.5 5.2 %shard_map.91 = (f32[4096,128]{1,0:T(8,128)}, f32[1,128]{1,0:T(1,128)}) custom-call(bf16[4096,128]{1,0:T(8,128)(2,1)} %x_ref.1, bf16[4096,128]{1,0:T(8,128)(2,1)} %gm_ref.1, bf16[4096,128]{1,0:T(8,128)(2,1)} %km_ref.1, bf16[4096,128]{1,0:T(8,128)(2,1)} %copy-done.1, bf16[256,128]{1,0:T(8,128)(2,1)} %taps_ref.1), custom_call_target="tpu_custom_call" | custom-call | tf_op jit(solution)/shard_map/pallas_call | solution.py:58
  35.7 0.0 collective-permute-start.1
  35.7 1.3 %collective-permute-done.1.q_ref = f32[1,128]{1,0:T(1,128)S(1)} collective-permute-done((f32[1,128]{1,0:T(1,128)}, f32[1,128]{1,0:T(1,128)S(1)}, u32[]{:S(2)}, u32[]{:S(2)}) %collective-permute-start.1) | collective-permute-done | bytes 544 | tf_op jit(solution)/shard_map/ppermute | solution.py:186
  37.0 0.0 copy-start.3
  37.0 0.6 copy-done.3
  37.6 6.5 %shard_map.92 = (bf16[16,4,8,128]{3,2,1,0:T(8,128)(2,1)}, f32[4096,128]{1,0:T(8,128)}) custom-call(f32[4096,128]{1,0:T(8,128)} %get-tuple-element.14.am_ref, bf16[4096,128]{1,0:T(8,128)(2,1)} %kl_ref.1, f32[32,128]{1,0:T(8,128)} %bitcast.16, f32[1,128]{1,0:T(1,128)} %get-tuple-element.15.p_ref, f32[1,128]{1,0:T(1,128)} %copy-done.3, ...), custom_call_target="tpu_custom_call" | custom-call | tf_op jit(solution)/shard_map/pallas_call | solution.py:131
  44.1 1.3 %collective-permute-start.3 = (bf16[16,4,8,128]{3,2,1,0:T(8,128)(2,1)}, bf16[16,4,8,128]{3,2,1,0:T(8,128)(2,1)S(1)}, u32[]{:S(2)}, u32[]{:S(2)}) collective-permute-start(bf16[16,4,8,128]{3,2,1,0:T(8,128)(2,1)} %get-tuple-element.19), channel_id=1, source_target_pairs={{0,4},{2,6},{4,8},{6,10},{8,12},{10,14},{1,5},{3,7},{5,9},{7,11},{... | collective-permute-start | bytes 393224 | tf_op jit(solution)/shard_map/ppermute | solution.py:20
  45.4 2.5 %collective-permute-start.2 = (bf16[16,4,8,128]{3,2,1,0:T(8,128)(2,1)}, bf16[16,4,8,128]{3,2,1,0:T(8,128)(2,1)S(1)}, u32[]{:S(2)}, u32[]{:S(2)}) collective-permute-start(bf16[16,4,8,128]{3,2,1,0:T(8,128)(2,1)} %get-tuple-element.19), channel_id=1, source_target_pairs={{0,2},{2,4},{4,6},{6,8},{8,10},{10,12},{12,14},{1,3},{3,5},{5,7},{... | collective-permute-start | bytes 393224 | tf_op jit(solution)/shard_map/ppermute | solution.py:20
  47.9 3.9 %collective-permute-done.3 = bf16[16,4,8,128]{3,2,1,0:T(8,128)(2,1)S(1)} collective-permute-done((bf16[16,4,8,128]{3,2,1,0:T(8,128)(2,1)}, bf16[16,4,8,128]{3,2,1,0:T(8,128)(2,1)S(1)}, u32[]{:S(2)}, u32[]{:S(2)}) %collective-permute-start.3) | collective-permute-done | bytes 131104 | tf_op jit(solution)/shard_map/ppermute | solution.py:20
  51.8 2.8 %collective-permute-done.2 = bf16[16,4,8,128]{3,2,1,0:T(8,128)(2,1)S(1)} collective-permute-done((bf16[16,4,8,128]{3,2,1,0:T(8,128)(2,1)}, bf16[16,4,8,128]{3,2,1,0:T(8,128)(2,1)S(1)}, u32[]{:S(2)}, u32[]{:S(2)}) %collective-permute-start.2) | collective-permute-done | bytes 131104 | tf_op jit(solution)/shard_map/ppermute | solution.py:20
  54.6 0.1 fusion
  54.7 1.3 %collective-permute-start.4 = (bf16[16,4,8,128]{3,2,1,0:T(8,128)(2,1)S(1)}, bf16[16,4,8,128]{3,2,1,0:T(8,128)(2,1)S(1)}, u32[]{:S(2)}, u32[]{:S(2)}) collective-permute-start(bf16[16,4,8,128]{3,2,1,0:T(8,128)(2,1)S(1)} %fusion), channel_id=1, source_target_pairs={{0,4},{2,6},{4,8},{6,10},{8,12},{10,14},{1,5},{3,7},{5,9},{7,11},{... | collective-permute-start | bytes 393224 | tf_op jit(solution)/shard_map/ppermute | solution.py:20
  56.0 5.6 %collective-permute-done.4 = bf16[16,4,8,128]{3,2,1,0:T(8,128)(2,1)S(1)} collective-permute-done((bf16[16,4,8,128]{3,2,1,0:T(8,128)(2,1)S(1)}, bf16[16,4,8,128]{3,2,1,0:T(8,128)(2,1)S(1)}, u32[]{:S(2)}, u32[]{:S(2)}) %collective-permute-start.4) | collective-permute-done | bytes 131104 | tf_op jit(solution)/shard_map/ppermute | solution.py:20
  61.6 0.1 fusion.1
  61.7 1.3 %collective-permute-start.5 = (bf16[16,4,8,128]{3,2,1,0:T(8,128)(2,1)S(1)}, bf16[16,4,8,128]{3,2,1,0:T(8,128)(2,1)S(1)}, u32[]{:S(2)}, u32[]{:S(2)}) collective-permute-start(bf16[16,4,8,128]{3,2,1,0:T(8,128)(2,1)S(1)} %fusion.1), channel_id=1, source_target_pairs={{0,8},{2,10},{4,12},{6,14},{1,9},{3,11},{5,13},{7,15},{16,24},{18,... | collective-permute-start | bytes 393224 | tf_op jit(solution)/shard_map/ppermute | solution.py:20
  63.0 8.1 %collective-permute-done.5 = bf16[16,4,8,128]{3,2,1,0:T(8,128)(2,1)S(1)} collective-permute-done((bf16[16,4,8,128]{3,2,1,0:T(8,128)(2,1)S(1)}, bf16[16,4,8,128]{3,2,1,0:T(8,128)(2,1)S(1)}, u32[]{:S(2)}, u32[]{:S(2)}) %collective-permute-start.5) | collective-permute-done | bytes 131104 | tf_op jit(solution)/shard_map/ppermute | solution.py:20
  71.1 0.9 %multiply_add_fusion.h0_ref = f32[16,4,8,128]{3,2,1,0:T(8,128)} fusion(bf16[16,4,8,128]{3,2,1,0:T(8,128)(2,1)S(1)} %collective-permute-done.5, f32[16,4,8,128]{3,2,1,0:T(8,128)S(1)} %bitcast.13, bf16[16,4,8,128]{3,2,1,0:T(8,128)(2,1)S(1)} %collective-permute-done.4, bf16[16,4,8,128]{3,2,1,0:T(8,128)(2,1)S(1)} %collective-permute-done.3, ...), kind=kLoop, calls=%fused_computation.1 | loop fusion | flops 851968 | bytes 1048576 | tf_op jit(solution)/shard_map/add | solution.py:200
  72.0 7.3 %shard_map.93 = bf16[4096,128]{1,0:T(8,128)(2,1)} custom-call(f32[4096,128]{1,0:T(8,128)} %get-tuple-element.14.am_ref, f32[4096,128]{1,0:T(8,128)} %get-tuple-element.17.vt_ref, bf16[4096,128]{1,0:T(8,128)(2,1)} %gl_ref.1, f32[16,4,8,128]{3,2,1,0:T(8,128)} %negate_exponential_fusion.lam_ref, f32[16,4,8,128]{3,2,1,0:T(8,128)} %bitcast.14, ...), custom_call_target="tpu_custom_call" | custom-call | tf_op jit(solution)/shard_map/pallas_call | solution.py:147
Async XLA Ops:
  0.0 5.3 %copy-start = (f32[4096,16]{0,1:T(8,128)S(1)}, f32[4096,16]{0,1:T(8,128)}, u32[]{:S(2)}) copy-start(f32[4096,16]{0,1:T(8,128)} %param.15) | copy-start | bytes 786436
  0.0 5.3 %copy-start.2 = (f32[4096,16]{0,1:T(8,128)S(1)}, f32[4096,16]{0,1:T(8,128)}, u32[]{:S(2)}) copy-start(f32[4096,16]{0,1:T(8,128)} %param.16) | copy-start | bytes 786436
  1.9 27.7 %collective-permute-start = (bf16[4096,128]{1,0:T(8,128)(2,1)S(1)}, bf16[4096,128]{1,0:T(8,128)(2,1)S(1)}, u32[]{:S(2)}, u32[]{:S(2)}) collective-permute-start(bf16[4096,128]{1,0:T(8,128)(2,1)S(1)} %multiply_convert_fusion), channel_id=1, source_target_pairs={{0,2},{2,4},{4,6},{6,8},{8,10},{10,12},{12,14},{1,3},{3,5},{5,7},{... | collective-permute-start | bytes 3145736 | tf_op jit(solution)/shard_map/ppermute | solution.py:20
  29.6 1.0 %copy-start.1 = (bf16[4096,128]{1,0:T(8,128)(2,1)}, bf16[4096,128]{1,0:T(8,128)(2,1)S(1)}, u32[]{:S(2)}) copy-start(bf16[4096,128]{1,0:T(8,128)(2,1)S(1)} %collective-permute-done.rim_ref) | copy-start | bytes 3145732
  35.7 1.3 %collective-permute-start.1 = (f32[1,128]{1,0:T(1,128)}, f32[1,128]{1,0:T(1,128)S(1)}, u32[]{:S(2)}, u32[]{:S(2)}) collective-permute-start(f32[1,128]{1,0:T(1,128)} %get-tuple-element.15.p_ref), channel_id=1, source_target_pairs={{0,1},{1,0},{2,3},{3,2},{4,5},{5,4},{6,7},{7,6},{8,9},{9,8},{10,11... | collective-permute-start | bytes 1544 | tf_op jit(solution)/shard_map/ppermute | solution.py:186
  37.0 0.6 copy-start.3
  44.1 7.7 %collective-permute-start.3 = (bf16[16,4,8,128]{3,2,1,0:T(8,128)(2,1)}, bf16[16,4,8,128]{3,2,1,0:T(8,128)(2,1)S(1)}, u32[]{:S(2)}, u32[]{:S(2)}) collective-permute-start(bf16[16,4,8,128]{3,2,1,0:T(8,128)(2,1)} %get-tuple-element.19), channel_id=1, source_target_pairs={{0,4},{2,6},{4,8},{6,10},{8,12},{10,14},{1,5},{3,7},{5,9},{7,11},{... | collective-permute-start | bytes 393224 | tf_op jit(solution)/shard_map/ppermute | solution.py:20
  45.4 9.3 %collective-permute-start.2 = (bf16[16,4,8,128]{3,2,1,0:T(8,128)(2,1)}, bf16[16,4,8,128]{3,2,1,0:T(8,128)(2,1)S(1)}, u32[]{:S(2)}, u32[]{:S(2)}) collective-permute-start(bf16[16,4,8,128]{3,2,1,0:T(8,128)(2,1)} %get-tuple-element.19), channel_id=1, source_target_pairs={{0,2},{2,4},{4,6},{6,8},{8,10},{10,12},{12,14},{1,3},{3,5},{5,7},{... | collective-permute-start | bytes 393224 | tf_op jit(solution)/shard_map/ppermute | solution.py:20
  54.7 6.9 %collective-permute-start.4 = (bf16[16,4,8,128]{3,2,1,0:T(8,128)(2,1)S(1)}, bf16[16,4,8,128]{3,2,1,0:T(8,128)(2,1)S(1)}, u32[]{:S(2)}, u32[]{:S(2)}) collective-permute-start(bf16[16,4,8,128]{3,2,1,0:T(8,128)(2,1)S(1)} %fusion), channel_id=1, source_target_pairs={{0,4},{2,6},{4,8},{6,10},{8,12},{10,14},{1,5},{3,7},{5,9},{7,11},{... | collective-permute-start | bytes 393224 | tf_op jit(solution)/shard_map/ppermute | solution.py:20
  61.7 9.4 %collective-permute-start.5 = (bf16[16,4,8,128]{3,2,1,0:T(8,128)(2,1)S(1)}, bf16[16,4,8,128]{3,2,1,0:T(8,128)(2,1)S(1)}, u32[]{:S(2)}, u32[]{:S(2)}) collective-permute-start(bf16[16,4,8,128]{3,2,1,0:T(8,128)(2,1)S(1)} %fusion.1), channel_id=1, source_target_pairs={{0,8},{2,10},{4,12},{6,14},{1,9},{3,11},{5,13},{7,15},{16,24},{18,... | collective-permute-start | bytes 393224 | tf_op jit(solution)/shard_map/ppermute | solution.py:20

commit v25 on v24

--- a/solution.py
+++ b/solution.py
@@ -92,7 +92,7 @@
         v = token_tile(vt_ref, t)
         return tuple(lam[m] * h[m] + v for m in range(modes))
 
-    h = lax.fori_loop(0, length, body, tuple(jnp.zeros((SUB, LANE), F32) for _ in range(modes)), unroll=32)
+    h = lax.fori_loop(0, length, body, tuple(jnp.zeros((SUB, LANE), F32) for _ in range(modes)), unroll=64)
     for m in range(modes):
         f_ref[m] = h[m].astype(f_ref.dtype)
 
@@ -112,7 +112,7 @@
         yt_ref[pl.ds(pl.multiple_of(t * SUB, SUB), SUB), :] = y
         return h
 
-    lax.fori_loop(0, length, body, tuple(h0_ref[m] for m in range(modes)), unroll=32)
+    lax.fori_loop(0, length, body, tuple(h0_ref[m] for m in range(modes)), unroll=64)
     for i in range(SUB):
         rows = slice(i * LANE, (i + 1) * LANE)
         long_out = yt_ref[pl.ds(i, LANE, stride=SUB), :].T.astype(BF16).astype(F32)

time: 80.1 us -> 80 us (level)
  no operation moved by 1% of the time
where the time goes in v25:
time: 80 us; the launch traced here: 79.2 us
  waiting for transfers between devices  44.3 us (55%)
  Pallas kernels  18.9 us (24%)
  starting transfers between devices  9.77 us (12%)
  other arithmetic  3.79 us (5%)
  local copies, waits for them, and re-layouts  2.38 us (3%)
    ppermute x5, waiting for transfers between devices, shifted(): return lax.ppermute(block, axis, route)  43 us
    ppermute x5, starting transfers between devices, shifted(): return lax.ppermute(block, axis, route)  9.76 us
    pallas_call x1, Pallas kernels, output_call(): pl.pallas_call(output_kernel, grid=(channels // TILE,), in_specs=[big, pl...  7.27 us
    pallas_call x1, Pallas kernels, final_state_call(): pl.pallas_call(functools.partial(final_state_kernel, float(width)), grid=...  6.44 us
    pallas_call x1, Pallas kernels, medium_call(): pl.pallas_call(medium_kernel, grid=(channels // block,), in_specs=[big, b...  5.17 us
    unnamed x10, local copies, waits for them, and re-layouts  2.38 us
    convert_element_type x1, other arithmetic, on_device(): values_medium = (key_medium.astype(F32) * source).astype(BF16)  1.87 us
  transfers between devices with their start and end apart: 6, of which 6 were waited for; matrix products, arithmetic and copies ran while one was open for 2% of the time, Pallas kernels for 0%

profile of v25, /device:TPU:24, one launch (start us, length us, event | category | flops | bytes accessed | tf_op | source)
XLA Modules:
  0.0 79.2 jit_solution(11346144006531158400)
XLA Ops:
  0.0 0.0 copy-start
  0.0 0.0 copy-start.2
  0.0 1.9 %multiply_convert_fusion = bf16[4096,128]{1,0:T(8,128)(2,1)S(1)} fusion(bf16[4096,128]{1,0:T(8,128)(2,1)} %x_ref.1, bf16[4096,128]{1,0:T(8,128)(2,1)} %km_ref.1), kind=kLoop, calls=%fused_computation | loop fusion | flops 2097152 | bytes 3145728 | tf_op jit(solution)/shard_map/convert_element_type | solution.py:177
  1.9 3.4 %collective-permute-start = (bf16[4096,128]{1,0:T(8,128)(2,1)S(1)}, bf16[4096,128]{1,0:T(8,128)(2,1)S(1)}, u32[]{:S(2)}, u32[]{:S(2)}) collective-permute-start(bf16[4096,128]{1,0:T(8,128)(2,1)S(1)} %multiply_convert_fusion), channel_id=1, source_target_pairs={{0,2},{2,4},{4,6},{6,8},{8,10},{10,12},{12,14},{1,3},{3,5},{5,7},{... | collective-permute-start | bytes 3145736 | tf_op jit(solution)/shard_map/ppermute | solution.py:20
  5.3 0.0 copy-done
  5.3 0.0 copy-done.2
  5.3 0.1 multiply_bitcast_fusion
  5.4 0.8 copy.11
  6.2 0.1 copy.10
  6.2 0.7 negate_exponential_fusion.lam_ref
  7.0 22.6 %collective-permute-done.rim_ref = bf16[4096,128]{1,0:T(8,128)(2,1)S(1)} collective-permute-done((bf16[4096,128]{1,0:T(8,128)(2,1)S(1)}, bf16[4096,128]{1,0:T(8,128)(2,1)S(1)}, u32[]{:S(2)}, u32[]{:S(2)}) %collective-permute-start) | collective-permute-done | bytes 1048608 | tf_op jit(solution)/shard_map/ppermute | solution.py:20
  29.6 0.0 copy-start.1
  29.6 1.0 %copy-done.1 = bf16[4096,128]{1,0:T(8,128)(2,1)} copy-done((bf16[4096,128]{1,0:T(8,128)(2,1)}, bf16[4096,128]{1,0:T(8,128)(2,1)S(1)}, u32[]{:S(2)}) %copy-start.1) | copy-done | bytes 1048600
  30.5 5.2 %shard_map.91 = (f32[4096,128]{1,0:T(8,128)}, f32[1,128]{1,0:T(1,128)}) custom-call(bf16[4096,128]{1,0:T(8,128)(2,1)} %x_ref.1, bf16[4096,128]{1,0:T(8,128)(2,1)} %gm_ref.1, bf16[4096,128]{1,0:T(8,128)(2,1)} %km_ref.1, bf16[4096,128]{1,0:T(8,128)(2,1)} %copy-done.1, bf16[256,128]{1,0:T(8,128)(2,1)} %taps_ref.1), custom_call_target="tpu_custom_call" | custom-call | tf_op jit(solution)/shard_map/pallas_call | solution.py:58
  35.7 0.0 collective-permute-start.1
  35.7 1.3 %collective-permute-done.1.q_ref = f32[1,128]{1,0:T(1,128)S(1)} collective-permute-done((f32[1,128]{1,0:T(1,128)}, f32[1,128]{1,0:T(1,128)S(1)}, u32[]{:S(2)}, u32[]{:S(2)}) %collective-permute-start.1) | collective-permute-done | bytes 544 | tf_op jit(solution)/shard_map/ppermute | solution.py:186
  37.0 0.0 copy-start.3
  37.0 0.6 copy-done.3
  37.6 6.4 %shard_map.92 = (bf16[16,4,8,128]{3,2,1,0:T(8,128)(2,1)}, f32[4096,128]{1,0:T(8,128)}) custom-call(f32[4096,128]{1,0:T(8,128)} %get-tuple-element.14.am_ref, bf16[4096,128]{1,0:T(8,128)(2,1)} %kl_ref.1, f32[32,128]{1,0:T(8,128)} %bitcast.16, f32[1,128]{1,0:T(1,128)} %get-tuple-element.15.p_ref, f32[1,128]{1,0:T(1,128)} %copy-done.3, ...), custom_call_target="tpu_custom_call" | custom-call | tf_op jit(solution)/shard_map/pallas_call | solution.py:131
  44.1 1.3 %collective-permute-start.3 = (bf16[16,4,8,128]{3,2,1,0:T(8,128)(2,1)}, bf16[16,4,8,128]{3,2,1,0:T(8,128)(2,1)S(1)}, u32[]{:S(2)}, u32[]{:S(2)}) collective-permute-start(bf16[16,4,8,128]{3,2,1,0:T(8,128)(2,1)} %get-tuple-element.19), channel_id=1, source_target_pairs={{0,4},{2,6},{4,8},{6,10},{8,12},{10,14},{1,5},{3,7},{5,9},{7,11},{... | collective-permute-start | bytes 393224 | tf_op jit(solution)/shard_map/ppermute | solution.py:20
  45.4 2.5 %collective-permute-start.2 = (bf16[16,4,8,128]{3,2,1,0:T(8,128)(2,1)}, bf16[16,4,8,128]{3,2,1,0:T(8,128)(2,1)S(1)}, u32[]{:S(2)}, u32[]{:S(2)}) collective-permute-start(bf16[16,4,8,128]{3,2,1,0:T(8,128)(2,1)} %get-tuple-element.19), channel_id=1, source_target_pairs={{0,2},{2,4},{4,6},{6,8},{8,10},{10,12},{12,14},{1,3},{3,5},{5,7},{... | collective-permute-start | bytes 393224 | tf_op jit(solution)/shard_map/ppermute | solution.py:20
  47.9 3.9 %collective-permute-done.3 = bf16[16,4,8,128]{3,2,1,0:T(8,128)(2,1)S(1)} collective-permute-done((bf16[16,4,8,128]{3,2,1,0:T(8,128)(2,1)}, bf16[16,4,8,128]{3,2,1,0:T(8,128)(2,1)S(1)}, u32[]{:S(2)}, u32[]{:S(2)}) %collective-permute-start.3) | collective-permute-done | bytes 131104 | tf_op jit(solution)/shard_map/ppermute | solution.py:20
  51.8 2.8 %collective-permute-done.2 = bf16[16,4,8,128]{3,2,1,0:T(8,128)(2,1)S(1)} collective-permute-done((bf16[16,4,8,128]{3,2,1,0:T(8,128)(2,1)}, bf16[16,4,8,128]{3,2,1,0:T(8,128)(2,1)S(1)}, u32[]{:S(2)}, u32[]{:S(2)}) %collective-permute-start.2) | collective-permute-done | bytes 131104 | tf_op jit(solution)/shard_map/ppermute | solution.py:20
  54.6 0.1 fusion
  54.7 1.3 %collective-permute-start.4 = (bf16[16,4,8,128]{3,2,1,0:T(8,128)(2,1)S(1)}, bf16[16,4,8,128]{3,2,1,0:T(8,128)(2,1)S(1)}, u32[]{:S(2)}, u32[]{:S(2)}) collective-permute-start(bf16[16,4,8,128]{3,2,1,0:T(8,128)(2,1)S(1)} %fusion), channel_id=1, source_target_pairs={{0,4},{2,6},{4,8},{6,10},{8,12},{10,14},{1,5},{3,7},{5,9},{7,11},{... | collective-permute-start | bytes 393224 | tf_op jit(solution)/shard_map/ppermute | solution.py:20
  56.0 5.6 %collective-permute-done.4 = bf16[16,4,8,128]{3,2,1,0:T(8,128)(2,1)S(1)} collective-permute-done((bf16[16,4,8,128]{3,2,1,0:T(8,128)(2,1)S(1)}, bf16[16,4,8,128]{3,2,1,0:T(8,128)(2,1)S(1)}, u32[]{:S(2)}, u32[]{:S(2)}) %collective-permute-start.4) | collective-permute-done | bytes 131104 | tf_op jit(solution)/shard_map/ppermute | solution.py:20
  61.6 0.1 fusion.1
  61.7 1.3 %collective-permute-start.5 = (bf16[16,4,8,128]{3,2,1,0:T(8,128)(2,1)S(1)}, bf16[16,4,8,128]{3,2,1,0:T(8,128)(2,1)S(1)}, u32[]{:S(2)}, u32[]{:S(2)}) collective-permute-start(bf16[16,4,8,128]{3,2,1,0:T(8,128)(2,1)S(1)} %fusion.1), channel_id=1, source_target_pairs={{0,8},{2,10},{4,12},{6,14},{1,9},{3,11},{5,13},{7,15},{16,24},{18,... | collective-permute-start | bytes 393224 | tf_op jit(solution)/shard_map/ppermute | solution.py:20
  63.0 8.1 %collective-permute-done.5 = bf16[16,4,8,128]{3,2,1,0:T(8,128)(2,1)S(1)} collective-permute-done((bf16[16,4,8,128]{3,2,1,0:T(8,128)(2,1)S(1)}, bf16[16,4,8,128]{3,2,1,0:T(8,128)(2,1)S(1)}, u32[]{:S(2)}, u32[]{:S(2)}) %collective-permute-start.5) | collective-permute-done | bytes 131104 | tf_op jit(solution)/shard_map/ppermute | solution.py:20
  71.1 0.9 %multiply_add_fusion.h0_ref = f32[16,4,8,128]{3,2,1,0:T(8,128)} fusion(bf16[16,4,8,128]{3,2,1,0:T(8,128)(2,1)S(1)} %collective-permute-done.5, f32[16,4,8,128]{3,2,1,0:T(8,128)S(1)} %bitcast.13, bf16[16,4,8,128]{3,2,1,0:T(8,128)(2,1)S(1)} %collective-permute-done.4, bf16[16,4,8,128]{3,2,1,0:T(8,128)(2,1)S(1)} %collective-permute-done.3, ...), kind=kLoop, calls=%fused_computation.1 | loop fusion | flops 851968 | bytes 1048576 | tf_op jit(solution)/shard_map/add | solution.py:200
  72.0 7.3 %shard_map.93 = bf16[4096,128]{1,0:T(8,128)(2,1)} custom-call(f32[4096,128]{1,0:T(8,128)} %get-tuple-element.14.am_ref, f32[4096,128]{1,0:T(8,128)} %get-tuple-element.17.vt_ref, bf16[4096,128]{1,0:T(8,128)(2,1)} %gl_ref.1, f32[16,4,8,128]{3,2,1,0:T(8,128)} %negate_exponential_fusion.lam_ref, f32[16,4,8,128]{3,2,1,0:T(8,128)} %bitcast.14, ...), custom_call_target="tpu_custom_call" | custom-call | tf_op jit(solution)/shard_map/pallas_call | solution.py:147
Async XLA Ops:
  0.0 5.3 %copy-start = (f32[4096,16]{0,1:T(8,128)S(1)}, f32[4096,16]{0,1:T(8,128)}, u32[]{:S(2)}) copy-start(f32[4096,16]{0,1:T(8,128)} %param.15) | copy-start | bytes 786436
  0.0 5.3 %copy-start.2 = (f32[4096,16]{0,1:T(8,128)S(1)}, f32[4096,16]{0,1:T(8,128)}, u32[]{:S(2)}) copy-start(f32[4096,16]{0,1:T(8,128)} %param.16) | copy-start | bytes 786436
  1.9 27.7 %collective-permute-start = (bf16[4096,128]{1,0:T(8,128)(2,1)S(1)}, bf16[4096,128]{1,0:T(8,128)(2,1)S(1)}, u32[]{:S(2)}, u32[]{:S(2)}) collective-permute-start(bf16[4096,128]{1,0:T(8,128)(2,1)S(1)} %multiply_convert_fusion), channel_id=1, source_target_pairs={{0,2},{2,4},{4,6},{6,8},{8,10},{10,12},{12,14},{1,3},{3,5},{5,7},{... | collective-permute-start | bytes 3145736 | tf_op jit(solution)/shard_map/ppermute | solution.py:20
  29.6 1.0 %copy-start.1 = (bf16[4096,128]{1,0:T(8,128)(2,1)}, bf16[4096,128]{1,0:T(8,128)(2,1)S(1)}, u32[]{:S(2)}) copy-start(bf16[4096,128]{1,0:T(8,128)(2,1)S(1)} %collective-permute-done.rim_ref) | copy-start | bytes 3145732
  35.7 1.3 %collective-permute-start.1 = (f32[1,128]{1,0:T(1,128)}, f32[1,128]{1,0:T(1,128)S(1)}, u32[]{:S(2)}, u32[]{:S(2)}) collective-permute-start(f32[1,128]{1,0:T(1,128)} %get-tuple-element.15.p_ref), channel_id=1, source_target_pairs={{0,1},{1,0},{2,3},{3,2},{4,5},{5,4},{6,7},{7,6},{8,9},{9,8},{10,11... | collective-permute-start | bytes 1544 | tf_op jit(solution)/shard_map/ppermute | solution.py:186
  37.0 0.6 copy-start.3
  44.1 7.7 %collective-permute-start.3 = (bf16[16,4,8,128]{3,2,1,0:T(8,128)(2,1)}, bf16[16,4,8,128]{3,2,1,0:T(8,128)(2,1)S(1)}, u32[]{:S(2)}, u32[]{:S(2)}) collective-permute-start(bf16[16,4,8,128]{3,2,1,0:T(8,128)(2,1)} %get-tuple-element.19), channel_id=1, source_target_pairs={{0,4},{2,6},{4,8},{6,10},{8,12},{10,14},{1,5},{3,7},{5,9},{7,11},{... | collective-permute-start | bytes 393224 | tf_op jit(solution)/shard_map/ppermute | solution.py:20
  45.4 9.3 %collective-permute-start.2 = (bf16[16,4,8,128]{3,2,1,0:T(8,128)(2,1)}, bf16[16,4,8,128]{3,2,1,0:T(8,128)(2,1)S(1)}, u32[]{:S(2)}, u32[]{:S(2)}) collective-permute-start(bf16[16,4,8,128]{3,2,1,0:T(8,128)(2,1)} %get-tuple-element.19), channel_id=1, source_target_pairs={{0,2},{2,4},{4,6},{6,8},{8,10},{10,12},{12,14},{1,3},{3,5},{5,7},{... | collective-permute-start | bytes 393224 | tf_op jit(solution)/shard_map/ppermute | solution.py:20
  54.7 6.9 %collective-permute-start.4 = (bf16[16,4,8,128]{3,2,1,0:T(8,128)(2,1)S(1)}, bf16[16,4,8,128]{3,2,1,0:T(8,128)(2,1)S(1)}, u32[]{:S(2)}, u32[]{:S(2)}) collective-permute-start(bf16[16,4,8,128]{3,2,1,0:T(8,128)(2,1)S(1)} %fusion), channel_id=1, source_target_pairs={{0,4},{2,6},{4,8},{6,10},{8,12},{10,14},{1,5},{3,7},{5,9},{7,11},{... | collective-permute-start | bytes 393224 | tf_op jit(solution)/shard_map/ppermute | solution.py:20
  61.7 9.4 %collective-permute-start.5 = (bf16[16,4,8,128]{3,2,1,0:T(8,128)(2,1)S(1)}, bf16[16,4,8,128]{3,2,1,0:T(8,128)(2,1)S(1)}, u32[]{:S(2)}, u32[]{:S(2)}) collective-permute-start(bf16[16,4,8,128]{3,2,1,0:T(8,128)(2,1)S(1)} %fusion.1), channel_id=1, source_target_pairs={{0,8},{2,10},{4,12},{6,14},{1,9},{3,11},{5,13},{7,15},{16,24},{18,... | collective-permute-start | bytes 393224 | tf_op jit(solution)/shard_map/ppermute | solution.py:20
